TPU v7x, 512 devices: a whole 4x4x16 slice. The times are simulated.
512 devices in a mesh: req: 128 (over x, z, core), tp: 4 (over y).
Axes of the slice: x: 4, y: 4, z: 16, core: 2. Of those that a mesh axis runs over, the one named last changes fastest.
Arguments:
- queries: bfloat16 [1024, 4096], P('req', 'tp'), may hold values from -320 to 320, as said below
- new_kv: bfloat16 [1024, 2, 512], P('req', None, 'tp'), may hold values from -6 to 6
- own_kv: bfloat16 [1024, 128, 2, 512], P('req', None, None, 'tp'), may hold values from -6 to 6
- prompt_kv: bfloat16 [128, 512, 2, 512], P('req', None, None, 'tp'), may hold values from -6 to 6
- out_weight: bfloat16 [4096, 2048], P('tp'), may hold values from -0.09375 to 0.09375
- parents: int32 [1024], replicated, may hold values from 0 to 1023, as said below
- own_len: int32 [1024], replicated, may hold values from 1 to 128, as said below
- first_beam: int32 [1024], replicated, may hold values from 0 to 1023, as said below
Outputs:
- mixed_out: bfloat16 [1024, 2048], P('req', 'tp')
Inputs may be any that keep to these rules, and one draw needn't show every extreme that they name: Beams of one request are consecutive; first_beam[b] is the first of them; every request but the last holds 8 to 16 beams, and one holds exactly 16. parents[b] is a beam of the same request as b. `own_len`: some beam has exactly 128 valid positions. queries are real-valued, with row scales that may differ widely.
All inputs are finite; a program needn't handle non-finite values.
Results may differ from a plain program's by a relative error of at most 0.015.
Values may be sent and summed in bfloat16 or wider, within the bound.
No kernel may reach another device: no remote copies, remote signals or barrier semaphores. Data moves between devices by JAX's collectives and lax.ppermute only.
A program may use at most 64 MiB of HBM per device.

v0:
```python
import jax
import jax.numpy as jnp
from jax import lax
from jax.sharding import PartitionSpec as P

HD = 128
MOST_BEAMS = 16


MASKED_SCORE = -1e30


def from_behind(block, axis, distance):
    devices = range(lax.axis_size(axis))
    route = [(i - distance, i) for i in devices if i - distance in devices]
    return lax.ppermute(block, axis, route)


def partial_block(query_block, key_block, value_block, allowed):
    score_scale = query_block.shape[-1] ** (-0.5)
    scores = jnp.einsum(
        "nkgd,nskd->nkgs", query_block, key_block, preferred_element_type=jnp.float32
    )
    scores = scores * score_scale
    masked = allowed[:, None, None, :]
    scores = jnp.where(masked, scores, MASKED_SCORE)
    peaks = jnp.max(scores, axis=-1)
    weights = jnp.where(masked, jnp.exp(scores - peaks[..., None]), 0.0)
    totals = jnp.sum(weights, axis=-1)
    formula = "nkgs,nskd->nkgd"
    weighted = jnp.einsum(
        formula, weights, value_block.astype(jnp.float32), precision=lax.Precision.HIGHEST
    )
    return (weighted, peaks, totals)


def merge_parts(left_part, right_part):
    peaks = jnp.maximum(left_part[1], right_part[1])
    scale_left = jnp.exp(left_part[1] - peaks)
    scale_right = jnp.exp(right_part[1] - peaks)
    weighted = left_part[0] * scale_left[..., None] + right_part[0] * scale_right[..., None]
    return (weighted, peaks, left_part[2] * scale_left + right_part[2] * scale_right)


def split_rows(rows, kv_heads_local, head_dim):
    count_rows = rows.shape[0]
    return (
        rows[:, :, 0].reshape(count_rows, -1, kv_heads_local, head_dim),
        rows[:, :, 1].reshape(count_rows, -1, kv_heads_local, head_dim),
    )


def local(queries, new_kv, own_kv, prompt_kv, out_weight, parents, own_len, first_beam):
    per_dev = queries.shape[0]
    head_dim = HD
    kv_heads_local = new_kv.shape[2] // head_dim
    q_heads_local = queries.shape[1] // head_dim
    group_size = q_heads_local // kv_heads_local
    own_size = own_kv.shape[1]
    dev_index = lax.axis_index("req")
    reach_dev = (MOST_BEAMS - 2) // per_dev + 1
    offsets = list(range(-reach_dev, reach_dev + 1))
    slot_ids = jnp.arange(per_dev, dtype=jnp.int32)
    my_beams = dev_index * per_dev + slot_ids
    own_positions = jnp.arange(own_size, dtype=jnp.int32)
    query_block = queries.reshape(per_dev, kv_heads_local, group_size, head_dim)
    fresh_keys, fresh_values = split_rows(new_kv[:, None], kv_heads_local, head_dim)
    fresh_allowed = jnp.ones((per_dev, 1), bool)
    merged = partial_block(query_block, fresh_keys, fresh_values, fresh_allowed)
    home_gap = dev_index - first_beam[my_beams] // per_dev
    prompt_list = [prompt_kv[0]]
    for offset in range(1, reach_dev + 1):
        prompt_list.append(from_behind(prompt_kv, "req", offset)[0])
    prompt_stack = jnp.stack(prompt_list)
    beam_prompt = prompt_stack[home_gap]
    pieces = []
    for offset in offsets:
        if offset == 0:
            pieces.append(own_kv)
        else:
            pieces.append(from_behind(own_kv, "req", -offset))
    stacked = jnp.concatenate(pieces, axis=0)
    parent = parents[my_beams]
    picked = (parent // per_dev - dev_index + reach_dev) * per_dev + parent % per_dev
    parent_cache = stacked[picked]
    lengths = own_len[parent]
    allowed = own_positions[None, :] < lengths[:, None]
    allowed_all = jnp.concatenate(
        [jnp.ones((per_dev, beam_prompt.shape[1]), bool), allowed], axis=1
    )
    key_rows, value_rows = split_rows(
        jnp.concatenate([beam_prompt, parent_cache], axis=1), kv_heads_local, head_dim
    )
    merged = merge_parts(merged, partial_block(query_block, key_rows, value_rows, allowed_all))
    weighted, peaks, totals = merged
    attended = (
        (weighted / totals[..., None])
        .reshape(per_dev, q_heads_local * head_dim)
        .astype(jnp.bfloat16)
    )
    partial_term = jnp.dot(attended, out_weight, preferred_element_type=jnp.float32)
    return lax.psum_scatter(
        partial_term.astype(jnp.bfloat16), "tp", scatter_dimension=1, tiled=True
    )


def solution(mesh):
    in_specs = (
        P("req", "tp"),
        P("req", None, "tp"),
        P("req", None, None, "tp"),
        P("req", None, None, "tp"),
        P("tp", None),
        P(),
        P(),
        P(),
    )
    out_specs = P("req", "tp")
    return jax.shard_map(local, mesh=mesh, in_specs=in_specs, out_specs=out_specs, check_vma=False)
```

profile of v0, /device:TPU:6, one launch (start us, length us, event | category | flops | bytes accessed | tf_op | source)
XLA Modules:
  0.0 98.1 jit_solution(13976824975334852017)
XLA Ops:
  6.5 0.0 copy-start
  6.5 0.0 copy-start.1
  6.5 0.0 copy-start.5
  6.5 0.0 reduce-scatter.2.cloned.1.call-start
  6.6 2.0 %copy.14 = bf16[8,128,2,128]{3,1,2,0:T(8,128)(2,1)} copy(bf16[8,128,2,128]{3,2,1,0:T(2,128)(2,1)} %param.10) | data formatting | bytes 1048576 | tf_op args[2]
  8.6 3.8 %collective-permute-start.2 = (bf16[8,128,2,128]{3,1,2,0:T(8,128)(2,1)}, bf16[8,128,2,128]{3,1,2,0:T(8,128)(2,1)S(1)}, u32[]{:S(2)}, u32[]{:S(2)}) collective-permute-start(bf16[8,128,2,128]{3,1,2,0:T(8,128)(2,1)} %copy.14), channel_id=1, source_target_pairs={{0,8},{4,12},{8,16},{12,20},{16,24},{20,28},{24,32},{28,36},{32,40... | collective-permute-start | bytes 1572872 | tf_op jit(solution)/shard_map/ppermute | solution.py:16
  12.4 1.9 %collective-permute-start.3 = (bf16[8,128,2,128]{3,1,2,0:T(8,128)(2,1)}, bf16[8,128,2,128]{3,1,2,0:T(8,128)(2,1)}, u32[]{:S(2)}, u32[]{:S(2)}) collective-permute-start(bf16[8,128,2,128]{3,1,2,0:T(8,128)(2,1)} %copy.14), channel_id=1, source_target_pairs={{0,4},{4,8},{8,12},{12,16},{16,20},{20,24},{24,28},{28,32},{32,36}... | collective-permute-start | bytes 1572872 | tf_op jit(solution)/shard_map/ppermute | solution.py:16
  14.3 9.2 %collective-permute-start.4 = (bf16[8,128,2,128]{3,1,2,0:T(8,128)(2,1)}, bf16[8,128,2,128]{3,1,2,0:T(8,128)(2,1)}, u32[]{:S(2)}, u32[]{:S(2)}) collective-permute-start(bf16[8,128,2,128]{3,1,2,0:T(8,128)(2,1)} %copy.14), channel_id=1, source_target_pairs={{4,0},{8,4},{12,8},{16,12},{20,16},{24,20},{28,24},{32,28},{36,32}... | collective-permute-start | bytes 1572872 | tf_op jit(solution)/shard_map/ppermute | solution.py:16
  23.5 1.0 %copy.13 = bf16[1,512,2,128]{3,1,2,0:T(8,128)(2,1)S(1)} copy(bf16[1,512,2,128]{3,2,1,0:T(2,128)(2,1)} %param.11) | data formatting | bytes 524288 | tf_op args[3]
  24.5 1.9 %collective-permute-start = (bf16[1,512,2,128]{3,1,2,0:T(8,128)(2,1)S(1)}, bf16[1,512,2,128]{3,1,2,0:T(8,128)(2,1)S(1)}, u32[]{:S(2)}, u32[]{:S(2)}) collective-permute-start(bf16[1,512,2,128]{3,1,2,0:T(8,128)(2,1)S(1)} %copy.13), channel_id=1, source_target_pairs={{0,4},{4,8},{8,12},{12,16},{16,20},{20,24},{24,28},{28,32},{32,36}... | collective-permute-start | bytes 786440 | tf_op jit(solution)/shard_map/ppermute | solution.py:16
  26.5 1.9 %collective-permute-start.1 = (bf16[1,512,2,128]{3,1,2,0:T(8,128)(2,1)S(1)}, bf16[1,512,2,128]{3,1,2,0:T(8,128)(2,1)S(1)}, u32[]{:S(2)}, u32[]{:S(2)}) collective-permute-start(bf16[1,512,2,128]{3,1,2,0:T(8,128)(2,1)S(1)} %copy.13), channel_id=1, source_target_pairs={{0,8},{4,12},{8,16},{12,20},{16,24},{20,28},{24,32},{28,36},{32,40... | collective-permute-start | bytes 786440 | tf_op jit(solution)/shard_map/ppermute | solution.py:16
  28.4 0.0 copy-done
  28.4 0.6 gather_fusion
  29.1 1.3 %gather_fusion.2 = s32[8]{0:T(128)S(1)} fusion(s32[1024]{0:T(1024)} %param.15, s32[1024]{0:T(1024)S(1)} %pad_clamp_fusion.3), kind=kCustom, calls=%fused_computation.2 | custom fusion | bytes 96 | tf_op jit(solution)/shard_map/gather | solution.py:70
  30.4 0.0 copy-done.1
  30.4 0.6 gather_fusion.1
  31.1 0.1 iota_compare_fusion
  31.1 0.0 copy-done.5
  31.2 0.0 copy-done.6
  31.2 0.1 fusion.16
  31.3 12.2 %collective-permute-done = bf16[1,512,2,128]{3,1,2,0:T(8,128)(2,1)S(1)} collective-permute-done((bf16[1,512,2,128]{3,1,2,0:T(8,128)(2,1)S(1)}, bf16[1,512,2,128]{3,1,2,0:T(8,128)(2,1)S(1)}, u32[]{:S(2)}, u32[]{:S(2)}) %collective-permute-start) | collective-permute-done | bytes 262176 | tf_op jit(solution)/shard_map/ppermute | solution.py:16
  43.6 3.6 %collective-permute-start.5 = (bf16[8,128,2,128]{3,1,2,0:T(8,128)(2,1)}, bf16[8,128,2,128]{3,1,2,0:T(8,128)(2,1)}, u32[]{:S(2)}, u32[]{:S(2)}) collective-permute-start(bf16[8,128,2,128]{3,1,2,0:T(8,128)(2,1)} %copy.14), channel_id=1, source_target_pairs={{8,0},{12,4},{16,8},{20,12},{24,16},{28,20},{32,24},{36,28},{40,32... | collective-permute-start | bytes 1572872 | tf_op jit(solution)/shard_map/ppermute | solution.py:16
  47.2 0.0 collective-permute-done.1
  47.2 0.1 pad_maximum_fusion
  47.3 1.0 gather_fusion.3
  48.3 0.0 copy-start.3
  48.3 1.7 %constant_dynamic-update-slice_fusion.6 = bf16[8,640,2,128]{3,1,2,0:T(8,128)(2,1)} fusion(bf16[8,512,2,128]{3,1,2,0:T(8,128)(2,1)S(1)} %gather_fusion.3), kind=kLoop, calls=%fused_computation.35 | loop fusion | bytes 4194304
  50.0 0.0 collective-permute-done.2
  50.0 0.8 constant_dynamic-update-slice_fusion.4
  50.9 0.0 collective-permute-done.3
  50.9 2.1 %constant_dynamic-update-slice_fusion.3 = bf16[40,128,2,128]{3,1,2,0:T(8,128)(2,1)} fusion(bf16[40,128,2,128]{3,1,2,0:T(8,128)(2,1)} %constant_dynamic-update-slice_fusion.4, bf16[8,128,2,128]{3,1,2,0:T(8,128)(2,1)} %collective-permute-done.3), kind=kLoop, calls=%fused_computation.32 | loop fusion | bytes 1048576
  52.9 0.0 copy-done.3
  52.9 0.9 constant_dynamic-update-slice_fusion.2
  53.8 0.0 collective-permute-done.4
  53.8 1.9 %constant_dynamic-update-slice_fusion.1 = bf16[40,128,2,128]{3,1,2,0:T(8,128)(2,1)} fusion(bf16[40,128,2,128]{3,1,2,0:T(8,128)(2,1)} %constant_dynamic-update-slice_fusion.2, bf16[8,128,2,128]{3,1,2,0:T(8,128)(2,1)} %collective-permute-done.4), kind=kLoop, calls=%fused_computation.30 | loop fusion | bytes 1048576
  55.7 1.1 %collective-permute-done.5 = bf16[8,128,2,128]{3,1,2,0:T(8,128)(2,1)} collective-permute-done((bf16[8,128,2,128]{3,1,2,0:T(8,128)(2,1)}, bf16[8,128,2,128]{3,1,2,0:T(8,128)(2,1)}, u32[]{:S(2)}, u32[]{:S(2)}) %collective-permute-start.5) | collective-permute-done | bytes 524320 | tf_op jit(solution)/shard_map/ppermute | solution.py:16
  56.8 1.9 %constant_dynamic-update-slice_fusion = bf16[40,128,2,128]{3,1,2,0:T(8,128)(2,1)} fusion(bf16[40,128,2,128]{3,1,2,0:T(8,128)(2,1)} %constant_dynamic-update-slice_fusion.1, bf16[8,128,2,128]{3,1,2,0:T(8,128)(2,1)} %collective-permute-done.5), kind=kLoop, calls=%fused_computation.29 | loop fusion | bytes 1048576 | tf_op jit(solution)/shard_map/concatenate | solution.py:82
  58.7 2.4 %gather_fusion.4 = bf16[8,128,2,128]{3,1,2,0:T(8,128)(2,1)S(1)} fusion(bf16[40,128,2,128]{3,1,2,0:T(8,128)(2,1)} %constant_dynamic-update-slice_fusion, s32[1024]{0:T(1024)S(1)} %pad_clamp_fusion), kind=kCustom, calls=%fused_computation.4 | custom fusion | bytes 1048608 | tf_op jit(solution)/shard_map/gather | solution.py:85
  61.1 0.0 copy-done.4
  61.1 0.0 copy-start.2
  61.1 0.1 constant_dynamic-update-slice_fusion.5
  61.2 0.6 fusion.31
  61.8 0.2 fusion.10
  62.0 0.8 fusion.9
  62.8 0.5 copy-done.2
  63.3 1.3 %convolution_convert_fusion = bf16[8,2048]{1,0:T(8,128)(2,1)} fusion(bf16[1024,2048]{1,0:T(8,128)(2,1)S(1)} %copy-done.2, bf16[1,8,8,128]{3,2,1,0:T(8,128)(2,1)S(1)} %fusion.9), kind=kOutput, calls=%fused_computation.5 | convolution fusion | flops 33570816 | bytes 4243456 | tf_op jit(solution)/shard_map/dot_general | solution.py:101
  64.5 0.0 reduce-scatter.2.cloned.1.call-update
  64.6 26.7 %reduce-scatter.2.cloned.1.call-done = bf16[8,512]{1,0:T(8,128)(2,1)} async-done(((bf16[8,2048]{1,0:T(8,128)(2,1)}), bf16[8,512]{1,0:T(8,128)(2,1)}) %reduce-scatter.2.cloned.1.call-update) | async-done | bytes 8208 | tf_op jit(solution)/shard_map/reduce_scatter | solution.py:102
  (13 shorter events, 0.1 us)
Async XLA Ops:
  6.5 21.9 %copy-start = (s32[1024]{0:T(1024)S(1)}, s32[1024]{0:T(1024)}, u32[]{:S(2)}) copy-start(s32[1024]{0:T(1024)} %param.13) | copy-start | bytes 12292
  6.5 23.9 %copy-start.1 = (s32[1024]{0:T(1024)S(1)}, s32[1024]{0:T(1024)}, u32[]{:S(2)}) copy-start(s32[1024]{0:T(1024)} %param.14) | copy-start | bytes 12292
  6.5 24.6 %copy-start.5 = (bf16[8,2,128]{2,1,0:T(2,128)(2,1)S(1)}, bf16[8,2,128]{2,1,0:T(2,128)(2,1)}, u32[]{:S(2)}) copy-start(bf16[8,2,128]{2,1,0:T(2,128)(2,1)} %param.9) | copy-start | bytes 12292
  6.5 24.6 %copy-start.6 = (bf16[8,1024]{1,0:T(8,128)(2,1)S(1)}, bf16[8,1024]{1,0:T(8,128)(2,1)}, u32[]{:S(2)}) copy-start(bf16[8,1024]{1,0:T(8,128)(2,1)} %param.8) | copy-start | bytes 49156
  6.5 84.7 %reduce-scatter.2.cloned.1.call-start = ((), (), s32[]{:S(2)}) async-start(), calls=%async_computation.1 | async-start | bytes 40960 | tf_op jit(solution)/shard_map/reduce_scatter | solution.py:102
  8.6 41.4 %collective-permute-start.2 = (bf16[8,128,2,128]{3,1,2,0:T(8,128)(2,1)}, bf16[8,128,2,128]{3,1,2,0:T(8,128)(2,1)S(1)}, u32[]{:S(2)}, u32[]{:S(2)}) collective-permute-start(bf16[8,128,2,128]{3,1,2,0:T(8,128)(2,1)} %copy.14), channel_id=1, source_target_pairs={{0,8},{4,12},{8,16},{12,20},{16,24},{20,28},{24,32},{28,36},{32,40... | collective-permute-start | bytes 1572872 | tf_op jit(solution)/shard_map/ppermute | solution.py:16
  12.4 38.5 %collective-permute-start.3 = (bf16[8,128,2,128]{3,1,2,0:T(8,128)(2,1)}, bf16[8,128,2,128]{3,1,2,0:T(8,128)(2,1)}, u32[]{:S(2)}, u32[]{:S(2)}) collective-permute-start(bf16[8,128,2,128]{3,1,2,0:T(8,128)(2,1)} %copy.14), channel_id=1, source_target_pairs={{0,4},{4,8},{8,12},{12,16},{16,20},{20,24},{24,28},{28,32},{32,36}... | collective-permute-start | bytes 1572872 | tf_op jit(solution)/shard_map/ppermute | solution.py:16
  14.3 39.5 %collective-permute-start.4 = (bf16[8,128,2,128]{3,1,2,0:T(8,128)(2,1)}, bf16[8,128,2,128]{3,1,2,0:T(8,128)(2,1)}, u32[]{:S(2)}, u32[]{:S(2)}) collective-permute-start(bf16[8,128,2,128]{3,1,2,0:T(8,128)(2,1)} %copy.14), channel_id=1, source_target_pairs={{4,0},{8,4},{12,8},{16,12},{20,16},{24,20},{28,24},{32,28},{36,32}... | collective-permute-start | bytes 1572872 | tf_op jit(solution)/shard_map/ppermute | solution.py:16
  24.5 19.1 %collective-permute-start = (bf16[1,512,2,128]{3,1,2,0:T(8,128)(2,1)S(1)}, bf16[1,512,2,128]{3,1,2,0:T(8,128)(2,1)S(1)}, u32[]{:S(2)}, u32[]{:S(2)}) collective-permute-start(bf16[1,512,2,128]{3,1,2,0:T(8,128)(2,1)S(1)} %copy.13), channel_id=1, source_target_pairs={{0,4},{4,8},{8,12},{12,16},{16,20},{20,24},{24,28},{28,32},{32,36}... | collective-permute-start | bytes 786440 | tf_op jit(solution)/shard_map/ppermute | solution.py:16
  26.5 20.8 %collective-permute-start.1 = (bf16[1,512,2,128]{3,1,2,0:T(8,128)(2,1)S(1)}, bf16[1,512,2,128]{3,1,2,0:T(8,128)(2,1)S(1)}, u32[]{:S(2)}, u32[]{:S(2)}) collective-permute-start(bf16[1,512,2,128]{3,1,2,0:T(8,128)(2,1)S(1)} %copy.13), channel_id=1, source_target_pairs={{0,8},{4,12},{8,16},{12,20},{16,24},{20,28},{24,32},{28,36},{32,40... | collective-permute-start | bytes 786440 | tf_op jit(solution)/shard_map/ppermute | solution.py:16
  43.6 13.2 %collective-permute-start.5 = (bf16[8,128,2,128]{3,1,2,0:T(8,128)(2,1)}, bf16[8,128,2,128]{3,1,2,0:T(8,128)(2,1)}, u32[]{:S(2)}, u32[]{:S(2)}) collective-permute-start(bf16[8,128,2,128]{3,1,2,0:T(8,128)(2,1)} %copy.14), channel_id=1, source_target_pairs={{8,0},{12,4},{16,8},{20,12},{24,16},{28,20},{32,24},{36,28},{40,32... | collective-permute-start | bytes 1572872 | tf_op jit(solution)/shard_map/ppermute | solution.py:16
  48.3 4.6 %copy-start.3 = (bf16[8,128,2,128]{3,2,1,0:T(2,128)(2,1)S(1)}, bf16[8,128,2,128]{3,2,1,0:T(2,128)(2,1)}, u32[]{:S(2)}) copy-start(bf16[8,128,2,128]{3,2,1,0:T(2,128)(2,1)} %param.10) | copy-start | bytes 1572868
  50.9 10.2 %copy-start.4 = (bf16[8,640,2,128]{3,1,2,0:T(8,128)(2,1)S(1)}, bf16[8,640,2,128]{3,1,2,0:T(8,128)(2,1)}, u32[]{:S(2)}) copy-start(bf16[8,640,2,128]{3,1,2,0:T(8,128)(2,1)} %constant_dynamic-update-slice_fusion.6) | copy-start | bytes 7864324
  61.1 2.2 %copy-start.2 = (bf16[1024,2048]{1,0:T(8,128)(2,1)S(1)}, bf16[1024,2048]{1,0:T(8,128)(2,1)}, u32[]{:S(2)}) copy-start(bf16[1024,2048]{1,0:T(8,128)(2,1)} %param.12) | copy-start | bytes 12582916
Sparse Core Ops, SparseCore 0:
  64.7 26.5 reduce-scatter.1
where the time goes:
time: 98.6 us; the launch traced here: 98.1 us
  waiting for transfers between devices  40 us (41%)
  starting transfers between devices  22.4 us (23%)
  local copies, waits for them, and re-layouts  18.8 us (19%)
  between operations  13.6 us (14%)
  matrix products  2.76 us (3%)
    reduce_scatter x1, waiting for transfers between devices, local(): lax.psum_scatter(partial_term.astype(jnp.bfloat16), 'tp', scatter_dimensi...  26.7 us
    ppermute x6, starting transfers between devices, from_behind(): return lax.ppermute(block, axis, route)  22.4 us
    ppermute x6, waiting for transfers between devices, from_behind(): return lax.ppermute(block, axis, route)  13.3 us
    unnamed x22, local copies, waits for them, and re-layouts  10.9 us
    gather x1, local copies, waits for them, and re-layouts, local(): parent_cache = stacked[picked]  2.39 us
  transfers between devices with their start and end apart: 7, of which 3 were waited for; matrix products, arithmetic and copies ran while one was open for 13% of the time, Pallas kernels for 0%

commit v1 on v0

v1 whole, which is shorter than its diff:
```python
import jax
import jax.numpy as jnp
from jax import lax
from jax.sharding import PartitionSpec as P

HD = 128
MOST_BEAMS = 16


MASKED_SCORE = -1e30


def shifted(block, axis, distance):
    devices = range(lax.axis_size(axis))
    route = [(i + distance, i) for i in devices if i + distance in devices]
    return lax.ppermute(block, axis, route)


def split_weights(weights):
    high = weights.astype(jnp.bfloat16)
    low = (weights - high.astype(jnp.float32)).astype(jnp.bfloat16)
    return high, low


def partial_block(query_block, key_block, value_block, allowed):
    score_scale = query_block.shape[-1] ** (-0.5)
    scores = jnp.einsum(
        "nkgd,skd->nkgs", query_block, key_block, preferred_element_type=jnp.float32
    )
    scores = scores * score_scale
    masked = allowed[:, None, None, :]
    scores = jnp.where(masked, scores, MASKED_SCORE)
    peaks = jnp.max(scores, axis=-1)
    weights = jnp.where(masked, jnp.exp(scores - peaks[..., None]), 0.0)
    totals = jnp.sum(weights, axis=-1)
    high, low = split_weights(weights)
    formula = "nkgs,skd->nkgd"
    weighted = jnp.einsum(
        formula, high, value_block, preferred_element_type=jnp.float32
    ) + jnp.einsum(formula, low, value_block, preferred_element_type=jnp.float32)
    return (weighted, peaks, totals)


def merge_all(parts):
    peaks = [jnp.where(p[2] > 0, p[1], MASKED_SCORE) for p in parts]
    top = peaks[0]
    for pk in peaks[1:]:
        top = jnp.maximum(top, pk)
    weighted = 0.0
    totals = 0.0
    for part, pk in zip(parts, peaks):
        scale = jnp.where(part[2] > 0, jnp.exp(pk - top), 0.0)
        weighted = weighted + part[0] * scale[..., None]
        totals = totals + part[2] * scale
    return (weighted, top, totals)


def pack(part):
    weighted, peaks, totals = part
    n = weighted.shape[0]
    return jnp.concatenate(
        [weighted.reshape(n, -1), peaks.reshape(n, -1), totals.reshape(n, -1)], axis=1
    )


def unpack(packed, shape):
    n, k, g, d = shape
    width = k * g * d
    weighted = packed[:, :width].reshape(n, k, g, d)
    peaks = packed[:, width : width + k * g].reshape(n, k, g)
    totals = packed[:, width + k * g :].reshape(n, k, g)
    return (weighted, peaks, totals)


def local(queries, new_kv, own_kv, prompt_kv, out_weight, parents, own_len, first_beam):
    per_dev = queries.shape[0]
    head_dim = HD
    kv_heads_local = new_kv.shape[2] // head_dim
    q_heads_local = queries.shape[1] // head_dim
    group_size = q_heads_local // kv_heads_local
    own_size = own_kv.shape[1]
    prompt_size = prompt_kv.shape[1]
    req_count = lax.axis_size("req")
    beam_count = per_dev * req_count
    dev_index = lax.axis_index("req")
    reach_dev = (MOST_BEAMS - 2) // per_dev + 1
    offsets = list(range(-reach_dev, reach_dev + 1))
    shape4 = (per_dev, kv_heads_local, group_size, head_dim)

    query_block = queries.reshape(shape4)
    hood = [query_block if k == 0 else shifted(query_block, "req", k) for k in offsets]
    hood_queries = jnp.concatenate(hood, axis=0)
    hood_count = hood_queries.shape[0]
    hood_beams = (dev_index - reach_dev) * per_dev + jnp.arange(hood_count, dtype=jnp.int32)
    in_range = (hood_beams >= 0) & (hood_beams < beam_count)
    clipped = jnp.clip(hood_beams, 0, beam_count - 1)

    parent = parents[clipped]
    lengths = own_len[parent]
    parent_here = in_range & (parent // per_dev == dev_index)
    columns = jnp.arange(per_dev * own_size, dtype=jnp.int32)
    own_allowed = (
        parent_here[:, None]
        & (columns[None, :] // own_size == (parent % per_dev)[:, None])
        & (columns[None, :] % own_size < lengths[:, None])
    )
    own_keys = own_kv[:, :, 0].reshape(per_dev * own_size, kv_heads_local, head_dim)
    own_values = own_kv[:, :, 1].reshape(per_dev * own_size, kv_heads_local, head_dim)
    own_part = partial_block(hood_queries, own_keys, own_values, own_allowed)

    start = reach_dev * per_dev
    home_here = in_range[start:] & (first_beam[clipped[start:]] // per_dev == dev_index)
    prompt_allowed = jnp.broadcast_to(home_here[:, None], (hood_count - start, prompt_size))
    prompt_keys = prompt_kv[0, :, 0].reshape(prompt_size, kv_heads_local, head_dim)
    prompt_values = prompt_kv[0, :, 1].reshape(prompt_size, kv_heads_local, head_dim)
    prompt_part = partial_block(hood_queries[start:], prompt_keys, prompt_values, prompt_allowed)

    fresh_keys = new_kv[:, 0].reshape(per_dev, 1, kv_heads_local, head_dim)
    fresh_values = new_kv[:, 1].reshape(per_dev, 1, kv_heads_local, head_dim)
    fresh_scores = jnp.einsum(
        "nkgd,nskd->nkgs", query_block, fresh_keys, preferred_element_type=jnp.float32
    ) * (head_dim ** (-0.5))
    fresh_part = (
        fresh_values[:, 0, :, None, :].astype(jnp.float32) * jnp.ones_like(fresh_scores),
        fresh_scores[..., 0],
        jnp.ones_like(fresh_scores[..., 0]),
    )

    def block_of(part, k, base):
        lo = (k + reach_dev) * per_dev - base
        return tuple(x[lo : lo + per_dev] for x in part)

    parts = [fresh_part]
    for k in offsets:
        own_k = block_of(own_part, k, 0)
        if k >= 0:
            own_k = merge_all([own_k, block_of(prompt_part, k, start)])
        if k == 0:
            parts.append(own_k)
        else:
            parts.append(unpack(shifted(pack(own_k), "req", -k), shape4))
    weighted, _, totals = merge_all(parts)
    attended = (
        (weighted / totals[..., None])
        .reshape(per_dev, q_heads_local * head_dim)
        .astype(jnp.bfloat16)
    )
    partial_term = jnp.dot(attended, out_weight, preferred_element_type=jnp.float32)

    tp_count = lax.axis_size("tp")
    tp_index = lax.axis_index("tp")
    width = partial_term.shape[1] // tp_count
    total = lax.dynamic_slice_in_dim(partial_term, tp_index * width, width, axis=1)
    for step in range(1, tp_count):
        dest = (tp_index + step) % tp_count
        chunk = lax.dynamic_slice_in_dim(partial_term, dest * width, width, axis=1)
        route = [(i, (i + step) % tp_count) for i in range(tp_count)]
        got = lax.ppermute(chunk.astype(jnp.bfloat16), "tp", route)
        total = total + got.astype(jnp.float32)
    return total.astype(jnp.bfloat16)


def solution(mesh):
    in_specs = (
        P("req", "tp"),
        P("req", None, "tp"),
        P("req", None, None, "tp"),
        P("req", None, None, "tp"),
        P("tp", None),
        P(),
        P(),
        P(),
    )
    out_specs = P("req", "tp")
    return jax.shard_map(local, mesh=mesh, in_specs=in_specs, out_specs=out_specs, check_vma=False)
```

time: 98.6 us -> 65.7 us (0.67)
  waiting for transfers between devices: 40 us -> 8.35 us
  starting transfers between devices: 22.4 us -> 42.4 us
  between operations: 13.6 us -> 0.44 us
  local copies, waits for them, and re-layouts: 18.8 us -> 5.85 us
  matrix products: 2.76 us -> 5.24 us
  other arithmetic: 0.43 us -> 2.84 us
    reduce_scatter x1 -> x0, waiting for transfers between devices: 26.7 us -> none  [local(): lax.psum_scatter(partial_term.astype(jnp.bfloat16), 'tp', scatter_dimensi...]
    ppermute x6 -> x11, starting transfers between devices: 22.4 us -> 42.4 us  [the longest x8 31.5 us: shifted(): return lax.ppermute(block, axis, route)]
    unnamed x22 -> x26, local copies, waits for them, and re-layouts: 10.9 us -> 0.97 us
    ppermute x6 -> x11, waiting for transfers between devices: 13.3 us -> 8.35 us  [the longest x8 5.23 us: shifted(): return lax.ppermute(block, axis, route)]
    gather x4 -> x2, local copies, waits for them, and re-layouts: 5.3 us -> 1.4 us  [the longest x1 0.73 us: local(): parent = parents[clipped]]
    slice x0 -> x2, local copies, waits for them, and re-layouts: none -> 2.42 us  [the longest x1 1.48 us: local(): prompt_kv[0, :, 1].reshape(prompt_size, kv_heads_local, head_dim)]
    concatenate x3 -> x5, local copies, waits for them, and re-layouts: 1.96 us -> 0.32 us  [the longest x4 0.31 us: pack(): jnp.concatenate([weighted.reshape(n, -1), peaks.reshape(n, -1), totals.re...]
    dot_general x1, matrix products: 1.26 us -> 2.84 us  [local(): jnp.dot(attended, out_weight, preferred_element_type=jnp.float32)]
  transfers between devices with their start and end apart: 7 -> 11, of which waited for: 3 -> 3; matrix products, arithmetic and copies ran while one was open for 13% -> 9% of each run, Pallas kernels for 0% -> 0%
where the time goes in v1:
time: 65.7 us; the launch traced here: 65.1 us
  starting transfers between devices  42.4 us (65%)
  waiting for transfers between devices  8.35 us (13%)
  local copies, waits for them, and re-layouts  5.85 us (9%)
  matrix products  5.24 us (8%)
  other arithmetic  2.84 us (4%)
    ppermute x8, starting transfers between devices, shifted(): return lax.ppermute(block, axis, route)  31.5 us
    ppermute x3, starting transfers between devices, local(): got = lax.ppermute(chunk.astype(jnp.bfloat16), 'tp', route)  10.9 us
    ppermute x8, waiting for transfers between devices, shifted(): return lax.ppermute(block, axis, route)  5.23 us
    ppermute x3, waiting for transfers between devices, local(): got = lax.ppermute(chunk.astype(jnp.bfloat16), 'tp', route)  3.12 us
    dot_general x1, matrix products, local(): jnp.dot(attended, out_weight, preferred_element_type=jnp.float32)  2.84 us
    slice x1, local copies, waits for them, and re-layouts, local(): prompt_kv[0, :, 1].reshape(prompt_size, kv_heads_local, head_dim)  1.48 us
  transfers between devices with their start and end apart: 11, of which 3 were waited for; matrix products, arithmetic and copies ran while one was open for 9% of the time, Pallas kernels for 0%

profile of v1, /device:TPU:6, one launch (start us, length us, event | category | flops | bytes accessed | tf_op | source)
XLA Modules:
  0.0 65.1 jit_solution(875549623571790503)
XLA Ops:
  0.0 0.8 %copy.73 = bf16[1,8,8,128]{3,2,1,0:T(8,128)(2,1)S(1)} copy(bf16[1,8,8,128]{3,1,2,0:T(8,128)(2,1)} %bitcast.191) | data formatting | bytes 32768
  0.8 11.7 %collective-permute-start.3 = (bf16[8,1,8,128]{3,2,0,1:T(8,128)(2,1)S(1)}, bf16[8,1,8,128]{3,2,0,1:T(8,128)(2,1)S(1)}, u32[]{:S(2)}, u32[]{:S(2)}) collective-permute-start(bf16[8,1,8,128]{3,2,0,1:T(8,128)(2,1)S(1)} %bitcast.195), channel_id=1, source_target_pairs={{8,0},{12,4},{16,8},{20,12},{24,16},{28,20},{32,24},{36,28},{40,32... | collective-permute-start | bytes 49160 | tf_op jit(solution)/shard_map/ppermute | solution.py:16
  12.4 2.1 %collective-permute-start.2 = (bf16[8,1,8,128]{3,2,0,1:T(8,128)(2,1)S(1)}, bf16[8,1,8,128]{3,2,0,1:T(8,128)(2,1)S(1)}, u32[]{:S(2)}, u32[]{:S(2)}) collective-permute-start(bf16[8,1,8,128]{3,2,0,1:T(8,128)(2,1)S(1)} %bitcast.196), channel_id=1, source_target_pairs={{4,0},{8,4},{12,8},{16,12},{20,16},{24,20},{28,24},{32,28},{36,32}... | collective-permute-start | bytes 49160 | tf_op jit(solution)/shard_map/ppermute | solution.py:16
  14.5 2.3 %collective-permute-start.1 = (bf16[8,1,8,128]{3,2,0,1:T(8,128)(2,1)S(1)}, bf16[8,1,8,128]{3,2,0,1:T(8,128)(2,1)S(1)}, u32[]{:S(2)}, u32[]{:S(2)}) collective-permute-start(bf16[8,1,8,128]{3,2,0,1:T(8,128)(2,1)S(1)} %bitcast.197), channel_id=1, source_target_pairs={{0,4},{4,8},{8,12},{12,16},{16,20},{20,24},{24,28},{28,32},{32,36}... | collective-permute-start | bytes 49160 | tf_op jit(solution)/shard_map/ppermute | solution.py:16
  16.8 2.6 %collective-permute-start = (bf16[8,1,8,128]{3,2,0,1:T(8,128)(2,1)S(1)}, bf16[8,1,8,128]{3,2,0,1:T(8,128)(2,1)S(1)}, u32[]{:S(2)}, u32[]{:S(2)}) collective-permute-start(bf16[8,1,8,128]{3,2,0,1:T(8,128)(2,1)S(1)} %bitcast.198), channel_id=1, source_target_pairs={{0,8},{4,12},{8,16},{12,20},{16,24},{20,28},{24,32},{28,36},{32,40... | collective-permute-start | bytes 49160 | tf_op jit(solution)/shard_map/ppermute | solution.py:16
  19.5 0.7 %gather_fusion = s32[40]{0:T(128)S(1)} fusion(s32[1024]{0:T(1024)S(1)} %copy-done, s32[1024]{0:T(1024)S(1)} %pad_clamp_fusion.2), kind=kCustom, calls=%fused_computation | custom fusion | bytes 480 | tf_op jit(solution)/shard_map/gather | solution.py:98
  20.2 0.1 compare_select_fusion
  20.3 0.8 %slice_convert_fusion = (f32[8,1,128]{2,1,0:T(1,128)S(1)}, bf16[8,1,128]{2,1,0:T(2,128)(2,1)S(1)}) fusion(bf16[8,2,128]{2,1,0:T(2,128)(2,1)} %param.9), kind=kLoop, calls=%fused_computation.139 | loop fusion | flops 1024 | bytes 10240 | tf_op jit(solution)/shard_map/convert_element_type | solution.py:124
  21.1 1.5 %fusion.80 = (bf16[1,512,1,128]{3,2,1,0:T(2,128)(2,1)S(1)}, bf16[1,512,1,128]{3,2,1,0:T(2,128)(2,1)S(1)}) fusion(bf16[1,512,2,128]{3,2,1,0:T(2,128)(2,1)} %param.11), kind=kLoop, calls=%fused_computation.181 | loop fusion | bytes 524288 | tf_op jit(solution)/shard_map/slice | solution.py:115
  22.6 0.0 copy-start.1
  22.6 0.0 copy-start.2
  22.6 0.9 %fusion.79 = (bf16[8,128,1,128]{3,2,1,0:T(2,128)(2,1)S(1)}, bf16[8,128,1,128]{3,2,1,0:T(2,128)(2,1)S(1)}) fusion(bf16[8,128,2,128]{3,2,1,0:T(2,128)(2,1)S(1)} %copy-done.3), kind=kLoop, calls=%fused_computation.180 | loop fusion | bytes 1048576 | tf_op jit(solution)/shard_map/slice | solution.py:107
  23.6 0.0 copy-start.4
  23.6 0.7 %gather_fusion.2 = s32[24]{0:T(128)S(1)} fusion(s32[1024]{0:T(1024)S(1)} %copy-done.1, s32[1024]{0:T(1024)S(1)} %get-tuple-element.63), kind=kCustom, calls=%fused_computation.2 | custom fusion | bytes 288 | tf_op jit(solution)/shard_map/gather | solution.py:112
  24.3 0.7 %gather_fusion.1 = s32[40]{0:T(128)S(1)} fusion(s32[1024]{0:T(1024)S(1)} %copy-done.2, s32[1024]{0:T(1024)S(1)} %get-tuple-element.64), kind=kCustom, calls=%fused_computation.1 | custom fusion | bytes 480 | tf_op jit(solution)/shard_map/gather | solution.py:99
  25.0 0.1 compare_and_fusion
  25.1 0.1 compare_and_fusion.1
  25.3 0.0 collective-permute-done
  25.3 0.0 collective-permute-done.1
  25.4 0.3 fusion.82
  25.7 0.2 fusion.21
  25.9 0.3 fusion.23
  26.2 0.3 fusion.6
  26.5 0.5 fusion.81
  27.0 0.5 fusion.7
  27.5 0.4 fusion.10
  27.9 0.5 fusion.5
  28.5 0.1 fusion.48
  28.6 0.1 concatenate.19
  28.7 5.3 %collective-permute-start.4 = (f32[8,1040]{1,0:T(8,128)S(1)}, f32[8,1040]{1,0:T(8,128)S(1)}, u32[]{:S(2)}, u32[]{:S(2)}) collective-permute-start(f32[8,1040]{1,0:T(8,128)S(1)} %concatenate.19), channel_id=1, source_target_pairs={{8,0},{12,4},{16,8},{20,12},{24,16},{28,20},{32,24},{36,28},{40,32... | collective-permute-start | bytes 99848 | tf_op jit(solution)/shard_map/ppermute | solution.py:16
  34.0 0.1 fusion.54
  34.2 0.1 concatenate.20
  34.3 2.7 %collective-permute-start.5 = (f32[8,1040]{1,0:T(8,128)S(1)}, f32[8,1040]{1,0:T(8,128)S(1)}, u32[]{:S(2)}, u32[]{:S(2)}) collective-permute-start(f32[8,1040]{1,0:T(8,128)S(1)} %concatenate.20), channel_id=1, source_target_pairs={{4,0},{8,4},{12,8},{16,12},{20,16},{24,20},{28,24},{32,28},{36,32}... | collective-permute-start | bytes 99848 | tf_op jit(solution)/shard_map/ppermute | solution.py:16
  37.0 0.1 concatenate.22
  37.1 1.9 %collective-permute-start.6 = (f32[8,1040]{1,0:T(8,128)S(1)}, f32[8,1040]{1,0:T(8,128)S(1)}, u32[]{:S(2)}, u32[]{:S(2)}) collective-permute-start(f32[8,1040]{1,0:T(8,128)S(1)} %concatenate.22), channel_id=1, source_target_pairs={{0,4},{4,8},{8,12},{12,16},{16,20},{20,24},{24,28},{28,32},{32,36}... | collective-permute-start | bytes 99848 | tf_op jit(solution)/shard_map/ppermute | solution.py:16
  39.0 0.1 concatenate.23
  39.1 2.9 %collective-permute-start.7 = (f32[8,1040]{1,0:T(8,128)S(1)}, f32[8,1040]{1,0:T(8,128)S(1)}, u32[]{:S(2)}, u32[]{:S(2)}) collective-permute-start(f32[8,1040]{1,0:T(8,128)S(1)} %concatenate.23), channel_id=1, source_target_pairs={{0,8},{4,12},{8,16},{12,20},{16,24},{20,28},{24,32},{28,36},{32,40... | collective-permute-start | bytes 99848 | tf_op jit(solution)/shard_map/ppermute | solution.py:16
  42.0 2.4 %collective-permute-done.6 = f32[8,1040]{1,0:T(8,128)S(1)} collective-permute-done((f32[8,1040]{1,0:T(8,128)S(1)}, f32[8,1040]{1,0:T(8,128)S(1)}, u32[]{:S(2)}, u32[]{:S(2)}) %collective-permute-start.6) | collective-permute-done | bytes 33312 | tf_op jit(solution)/shard_map/ppermute | solution.py:16
  44.5 2.8 %collective-permute-done.7 = f32[8,1040]{1,0:T(8,128)S(1)} collective-permute-done((f32[8,1040]{1,0:T(8,128)S(1)}, f32[8,1040]{1,0:T(8,128)S(1)}, u32[]{:S(2)}, u32[]{:S(2)}) %collective-permute-start.7) | collective-permute-done | bytes 33312 | tf_op jit(solution)/shard_map/ppermute | solution.py:16
  47.3 0.1 maximum_maximum_fusion
  47.3 0.1 multiply_add_fusion
  47.4 0.1 fusion.56
  47.6 2.8 %fusion.51 = f32[8,2048]{1,0:T(8,128)S(1)} fusion(bf16[1024,2048]{1,0:T(8,128)(2,1)} %param.12, bf16[1,8,8,128]{3,2,1,0:T(8,128)(2,1)S(1)} %fusion.56), kind=kOutput, calls=%fused_computation.82 | convolution fusion | flops 33554432 | bytes 4276224 | tf_op jit(solution)/shard_map/dot_general | solution.py:148
  50.4 3.5 %collective-permute-start.8 = (bf16[8,512]{1,0:T(8,128)(2,1)S(1)}, bf16[8,512]{1,0:T(8,128)(2,1)S(1)}, u32[]{:S(2)}, u32[]{:S(2)}) collective-permute-start(bf16[8,512]{1,0:T(8,128)(2,1)S(1)} %get-tuple-element.38), channel_id=1, source_target_pairs={{0,1},{1,2},{2,3},{3,0},{4,5},{5,6},{6,7},{7,4},{8,9},{9,10},{10,1... | collective-permute-start | bytes 24584 | tf_op jit(solution)/shard_map/ppermute | solution.py:158
  53.9 3.6 %collective-permute-start.10 = (bf16[8,512]{1,0:T(8,128)(2,1)S(1)}, bf16[8,512]{1,0:T(8,128)(2,1)S(1)}, u32[]{:S(2)}, u32[]{:S(2)}) collective-permute-start(bf16[8,512]{1,0:T(8,128)(2,1)S(1)} %get-tuple-element.39), channel_id=1, source_target_pairs={{0,3},{1,0},{2,1},{3,2},{4,7},{5,4},{6,5},{7,6},{8,11},{9,8},{10,9... | collective-permute-start | bytes 24584 | tf_op jit(solution)/shard_map/ppermute | solution.py:158
  57.5 3.9 %collective-permute-start.9 = (bf16[8,512]{1,0:T(8,128)(2,1)S(1)}, bf16[8,512]{1,0:T(8,128)(2,1)S(1)}, u32[]{:S(2)}, u32[]{:S(2)}) collective-permute-start(bf16[8,512]{1,0:T(8,128)(2,1)S(1)} %get-tuple-element.40), channel_id=1, source_target_pairs={{0,2},{1,3},{2,0},{3,1},{4,6},{5,7},{6,4},{7,5},{8,10},{9,11},{10,... | collective-permute-start | bytes 24584 | tf_op jit(solution)/shard_map/ppermute | solution.py:158
  61.4 3.1 %collective-permute-done.9 = bf16[8,512]{1,0:T(8,128)(2,1)S(1)} collective-permute-done((bf16[8,512]{1,0:T(8,128)(2,1)S(1)}, bf16[8,512]{1,0:T(8,128)(2,1)S(1)}, u32[]{:S(2)}, u32[]{:S(2)}) %collective-permute-start.9) | collective-permute-done | bytes 8224 | tf_op jit(solution)/shard_map/ppermute | solution.py:158
  64.5 0.6 add_convert_fusion
  (41 shorter events, 0.3 us)
Async XLA Ops:
  0.0 19.4 %copy-start = (s32[1024]{0:T(1024)S(1)}, s32[1024]{0:T(1024)}, u32[]{:S(2)}) copy-start(s32[1024]{0:T(1024)} %param.13) | copy-start | bytes 12292
  0.0 22.6 %copy-start.3 = (bf16[8,128,2,128]{3,2,1,0:T(2,128)(2,1)S(1)}, bf16[8,128,2,128]{3,2,1,0:T(2,128)(2,1)}, u32[]{:S(2)}) copy-start(bf16[8,128,2,128]{3,2,1,0:T(2,128)(2,1)} %param.10) | copy-start | bytes 1572868
  0.8 24.6 %collective-permute-start.3 = (bf16[8,1,8,128]{3,2,0,1:T(8,128)(2,1)S(1)}, bf16[8,1,8,128]{3,2,0,1:T(8,128)(2,1)S(1)}, u32[]{:S(2)}, u32[]{:S(2)}) collective-permute-start(bf16[8,1,8,128]{3,2,0,1:T(8,128)(2,1)S(1)} %bitcast.195), channel_id=1, source_target_pairs={{8,0},{12,4},{16,8},{20,12},{24,16},{28,20},{32,24},{36,28},{40,32... | collective-permute-start | bytes 49160 | tf_op jit(solution)/shard_map/ppermute | solution.py:16
  12.4 12.9 %collective-permute-start.2 = (bf16[8,1,8,128]{3,2,0,1:T(8,128)(2,1)S(1)}, bf16[8,1,8,128]{3,2,0,1:T(8,128)(2,1)S(1)}, u32[]{:S(2)}, u32[]{:S(2)}) collective-permute-start(bf16[8,1,8,128]{3,2,0,1:T(8,128)(2,1)S(1)} %bitcast.196), channel_id=1, source_target_pairs={{4,0},{8,4},{12,8},{16,12},{20,16},{24,20},{28,24},{32,28},{36,32}... | collective-permute-start | bytes 49160 | tf_op jit(solution)/shard_map/ppermute | solution.py:16
  14.5 10.8 %collective-permute-start.1 = (bf16[8,1,8,128]{3,2,0,1:T(8,128)(2,1)S(1)}, bf16[8,1,8,128]{3,2,0,1:T(8,128)(2,1)S(1)}, u32[]{:S(2)}, u32[]{:S(2)}) collective-permute-start(bf16[8,1,8,128]{3,2,0,1:T(8,128)(2,1)S(1)} %bitcast.197), channel_id=1, source_target_pairs={{0,4},{4,8},{8,12},{12,16},{16,20},{20,24},{24,28},{28,32},{32,36}... | collective-permute-start | bytes 49160 | tf_op jit(solution)/shard_map/ppermute | solution.py:16
  16.8 8.5 %collective-permute-start = (bf16[8,1,8,128]{3,2,0,1:T(8,128)(2,1)S(1)}, bf16[8,1,8,128]{3,2,0,1:T(8,128)(2,1)S(1)}, u32[]{:S(2)}, u32[]{:S(2)}) collective-permute-start(bf16[8,1,8,128]{3,2,0,1:T(8,128)(2,1)S(1)} %bitcast.198), channel_id=1, source_target_pairs={{0,8},{4,12},{8,16},{12,20},{16,24},{20,28},{24,32},{28,36},{32,40... | collective-permute-start | bytes 49160 | tf_op jit(solution)/shard_map/ppermute | solution.py:16
  22.6 1.0 %copy-start.1 = (s32[1024]{0:T(1024)S(1)}, s32[1024]{0:T(1024)}, u32[]{:S(2)}) copy-start(s32[1024]{0:T(1024)} %param.15) | copy-start | bytes 12292
  22.6 1.7 %copy-start.2 = (s32[1024]{0:T(1024)S(1)}, s32[1024]{0:T(1024)}, u32[]{:S(2)}) copy-start(s32[1024]{0:T(1024)} %param.14) | copy-start | bytes 12292
  23.6 1.8 %copy-start.4 = (bf16[8,1024]{1,0:T(8,128)(2,1)S(1)}, bf16[8,1024]{1,0:T(8,128)(2,1)}, u32[]{:S(2)}) copy-start(bf16[8,1024]{1,0:T(8,128)(2,1)} %param.8) | copy-start | bytes 49156
  28.7 13.3 %collective-permute-start.4 = (f32[8,1040]{1,0:T(8,128)S(1)}, f32[8,1040]{1,0:T(8,128)S(1)}, u32[]{:S(2)}, u32[]{:S(2)}) collective-permute-start(f32[8,1040]{1,0:T(8,128)S(1)} %concatenate.19), channel_id=1, source_target_pairs={{8,0},{12,4},{16,8},{20,12},{24,16},{28,20},{32,24},{36,28},{40,32... | collective-permute-start | bytes 99848 | tf_op jit(solution)/shard_map/ppermute | solution.py:16
  34.3 7.8 %collective-permute-start.5 = (f32[8,1040]{1,0:T(8,128)S(1)}, f32[8,1040]{1,0:T(8,128)S(1)}, u32[]{:S(2)}, u32[]{:S(2)}) collective-permute-start(f32[8,1040]{1,0:T(8,128)S(1)} %concatenate.20), channel_id=1, source_target_pairs={{4,0},{8,4},{12,8},{16,12},{20,16},{24,20},{28,24},{32,28},{36,32}... | collective-permute-start | bytes 99848 | tf_op jit(solution)/shard_map/ppermute | solution.py:16
  37.1 7.4 %collective-permute-start.6 = (f32[8,1040]{1,0:T(8,128)S(1)}, f32[8,1040]{1,0:T(8,128)S(1)}, u32[]{:S(2)}, u32[]{:S(2)}) collective-permute-start(f32[8,1040]{1,0:T(8,128)S(1)} %concatenate.22), channel_id=1, source_target_pairs={{0,4},{4,8},{8,12},{12,16},{16,20},{20,24},{24,28},{28,32},{32,36}... | collective-permute-start | bytes 99848 | tf_op jit(solution)/shard_map/ppermute | solution.py:16
  39.1 8.2 %collective-permute-start.7 = (f32[8,1040]{1,0:T(8,128)S(1)}, f32[8,1040]{1,0:T(8,128)S(1)}, u32[]{:S(2)}, u32[]{:S(2)}) collective-permute-start(f32[8,1040]{1,0:T(8,128)S(1)} %concatenate.23), channel_id=1, source_target_pairs={{0,8},{4,12},{8,16},{12,20},{16,24},{20,28},{24,32},{28,36},{32,40... | collective-permute-start | bytes 99848 | tf_op jit(solution)/shard_map/ppermute | solution.py:16
  50.4 11.0 %collective-permute-start.8 = (bf16[8,512]{1,0:T(8,128)(2,1)S(1)}, bf16[8,512]{1,0:T(8,128)(2,1)S(1)}, u32[]{:S(2)}, u32[]{:S(2)}) collective-permute-start(bf16[8,512]{1,0:T(8,128)(2,1)S(1)} %get-tuple-element.38), channel_id=1, source_target_pairs={{0,1},{1,2},{2,3},{3,0},{4,5},{5,6},{6,7},{7,4},{8,9},{9,10},{10,1... | collective-permute-start | bytes 24584 | tf_op jit(solution)/shard_map/ppermute | solution.py:158
  53.9 7.5 %collective-permute-start.10 = (bf16[8,512]{1,0:T(8,128)(2,1)S(1)}, bf16[8,512]{1,0:T(8,128)(2,1)S(1)}, u32[]{:S(2)}, u32[]{:S(2)}) collective-permute-start(bf16[8,512]{1,0:T(8,128)(2,1)S(1)} %get-tuple-element.39), channel_id=1, source_target_pairs={{0,3},{1,0},{2,1},{3,2},{4,7},{5,4},{6,5},{7,6},{8,11},{9,8},{10,9... | collective-permute-start | bytes 24584 | tf_op jit(solution)/shard_map/ppermute | solution.py:158
  57.5 7.0 %collective-permute-start.9 = (bf16[8,512]{1,0:T(8,128)(2,1)S(1)}, bf16[8,512]{1,0:T(8,128)(2,1)S(1)}, u32[]{:S(2)}, u32[]{:S(2)}) collective-permute-start(bf16[8,512]{1,0:T(8,128)(2,1)S(1)} %get-tuple-element.40), channel_id=1, source_target_pairs={{0,2},{1,3},{2,0},{3,1},{4,6},{5,7},{6,4},{7,5},{8,10},{9,11},{10,... | collective-permute-start | bytes 24584 | tf_op jit(solution)/shard_map/ppermute | solution.py:158

commit v2 on v1

--- a/solution.py
+++ b/solution.py
@@ -150,13 +150,11 @@
     tp_count = lax.axis_size("tp")
     tp_index = lax.axis_index("tp")
     width = partial_term.shape[1] // tp_count
-    total = lax.dynamic_slice_in_dim(partial_term, tp_index * width, width, axis=1)
-    for step in range(1, tp_count):
-        dest = (tp_index + step) % tp_count
-        chunk = lax.dynamic_slice_in_dim(partial_term, dest * width, width, axis=1)
-        route = [(i, (i + step) % tp_count) for i in range(tp_count)]
-        got = lax.ppermute(chunk.astype(jnp.bfloat16), "tp", route)
-        total = total + got.astype(jnp.float32)
+    chunks = partial_term.reshape(per_dev, tp_count, width).transpose(1, 0, 2)
+    got = lax.all_to_all(chunks.astype(jnp.bfloat16), "tp", 0, 0, tiled=True)
+    others = jnp.arange(tp_count, dtype=jnp.int32)[:, None, None] != tp_index
+    mine = lax.dynamic_slice_in_dim(partial_term, tp_index * width, width, axis=1)
+    total = mine + jnp.sum(jnp.where(others, got.astype(jnp.float32), 0.0), axis=0)
     return total.astype(jnp.bfloat16)
 
 

time: 65.7 us -> 62.2 us (0.947)
  starting transfers between devices: 42.4 us -> 36 us
  waiting for transfers between devices: 8.35 us -> 10.7 us
    ppermute x3 -> x0, starting transfers between devices: 10.9 us -> none  [local(): got = lax.ppermute(chunk.astype(jnp.bfloat16), 'tp', route)]
    all_to_all x0 -> x1, waiting for transfers between devices: none -> 5.44 us  [local(): got = lax.all_to_all(chunks.astype(jnp.bfloat16), 'tp', 0, 0, tiled=True)]
    all_to_all x0 -> x1, starting transfers between devices: none -> 4.47 us  [local(): got = lax.all_to_all(chunks.astype(jnp.bfloat16), 'tp', 0, 0, tiled=True)]
    ppermute x3 -> x0, waiting for transfers between devices: 3.12 us -> none  [local(): got = lax.ppermute(chunk.astype(jnp.bfloat16), 'tp', route)]
  transfers between devices with their start and end apart: 11 -> 9, of which waited for: 3 -> 3; matrix products, arithmetic and copies ran while one was open for 9% -> 10% of each run, Pallas kernels for 0% -> 0%
where the time goes in v2:
time: 62.2 us; the launch traced here: 61.6 us
  starting transfers between devices  36 us (58%)
  waiting for transfers between devices  10.7 us (17%)
  local copies, waits for them, and re-layouts  5.84 us (9%)
  matrix products  5.84 us (9%)
  other arithmetic  2.92 us (5%)
    ppermute x8, starting transfers between devices, shifted(): return lax.ppermute(block, axis, route)  31.5 us
    all_to_all x1, waiting for transfers between devices, local(): got = lax.all_to_all(chunks.astype(jnp.bfloat16), 'tp', 0, 0, tiled=True)  5.44 us
    ppermute x8, waiting for transfers between devices, shifted(): return lax.ppermute(block, axis, route)  5.23 us
    all_to_all x1, starting transfers between devices, local(): got = lax.all_to_all(chunks.astype(jnp.bfloat16), 'tp', 0, 0, tiled=True)  4.47 us
    dot_general x1, matrix products, local(): jnp.dot(attended, out_weight, preferred_element_type=jnp.float32)  3.45 us
    slice x1, local copies, waits for them, and re-layouts, local(): prompt_kv[0, :, 1].reshape(prompt_size, kv_heads_local, head_dim)  1.48 us
  transfers between devices with their start and end apart: 9, of which 3 were waited for; matrix products, arithmetic and copies ran while one was open for 10% of the time, Pallas kernels for 0%

profile of v2, /device:TPU:6, one launch (start us, length us, event | category | flops | bytes accessed | tf_op | source)
XLA Modules:
  0.0 61.6 jit_solution(8040267562724664633)
XLA Ops:
  0.0 0.8 %copy.75 = bf16[1,8,8,128]{3,2,1,0:T(8,128)(2,1)S(1)} copy(bf16[1,8,8,128]{3,1,2,0:T(8,128)(2,1)} %bitcast.196) | data formatting | bytes 32768
  0.8 11.7 %collective-permute-start.3 = (bf16[8,1,8,128]{3,2,0,1:T(8,128)(2,1)S(1)}, bf16[8,1,8,128]{3,2,0,1:T(8,128)(2,1)S(1)}, u32[]{:S(2)}, u32[]{:S(2)}) collective-permute-start(bf16[8,1,8,128]{3,2,0,1:T(8,128)(2,1)S(1)} %bitcast.200), channel_id=1, source_target_pairs={{8,0},{12,4},{16,8},{20,12},{24,16},{28,20},{32,24},{36,28},{40,32... | collective-permute-start | bytes 49160 | tf_op jit(solution)/shard_map/ppermute | solution.py:16
  12.4 2.1 %collective-permute-start.2 = (bf16[8,1,8,128]{3,2,0,1:T(8,128)(2,1)S(1)}, bf16[8,1,8,128]{3,2,0,1:T(8,128)(2,1)S(1)}, u32[]{:S(2)}, u32[]{:S(2)}) collective-permute-start(bf16[8,1,8,128]{3,2,0,1:T(8,128)(2,1)S(1)} %bitcast.201), channel_id=1, source_target_pairs={{4,0},{8,4},{12,8},{16,12},{20,16},{24,20},{28,24},{32,28},{36,32}... | collective-permute-start | bytes 49160 | tf_op jit(solution)/shard_map/ppermute | solution.py:16
  14.5 2.3 %collective-permute-start.1 = (bf16[8,1,8,128]{3,2,0,1:T(8,128)(2,1)S(1)}, bf16[8,1,8,128]{3,2,0,1:T(8,128)(2,1)S(1)}, u32[]{:S(2)}, u32[]{:S(2)}) collective-permute-start(bf16[8,1,8,128]{3,2,0,1:T(8,128)(2,1)S(1)} %bitcast.202), channel_id=1, source_target_pairs={{0,4},{4,8},{8,12},{12,16},{16,20},{20,24},{24,28},{28,32},{32,36}... | collective-permute-start | bytes 49160 | tf_op jit(solution)/shard_map/ppermute | solution.py:16
  16.8 2.6 %collective-permute-start = (bf16[8,1,8,128]{3,2,0,1:T(8,128)(2,1)S(1)}, bf16[8,1,8,128]{3,2,0,1:T(8,128)(2,1)S(1)}, u32[]{:S(2)}, u32[]{:S(2)}) collective-permute-start(bf16[8,1,8,128]{3,2,0,1:T(8,128)(2,1)S(1)} %bitcast.203), channel_id=1, source_target_pairs={{0,8},{4,12},{8,16},{12,20},{16,24},{20,28},{24,32},{28,36},{32,40... | collective-permute-start | bytes 49160 | tf_op jit(solution)/shard_map/ppermute | solution.py:16
  19.5 0.7 %gather_fusion = s32[40]{0:T(128)S(1)} fusion(s32[1024]{0:T(1024)S(1)} %copy-done, s32[1024]{0:T(1024)S(1)} %pad_clamp_fusion.2), kind=kCustom, calls=%fused_computation | custom fusion | bytes 480 | tf_op jit(solution)/shard_map/gather | solution.py:98
  20.2 0.1 compare_select_fusion
  20.3 0.8 %slice_convert_fusion = (f32[8,1,128]{2,1,0:T(1,128)S(1)}, bf16[8,1,128]{2,1,0:T(2,128)(2,1)S(1)}) fusion(bf16[8,2,128]{2,1,0:T(2,128)(2,1)} %param.9), kind=kLoop, calls=%fused_computation.137 | loop fusion | flops 1024 | bytes 10240 | tf_op jit(solution)/shard_map/convert_element_type | solution.py:124
  21.1 1.5 %fusion.80 = (bf16[1,512,1,128]{3,2,1,0:T(2,128)(2,1)S(1)}, bf16[1,512,1,128]{3,2,1,0:T(2,128)(2,1)S(1)}) fusion(bf16[1,512,2,128]{3,2,1,0:T(2,128)(2,1)} %param.11), kind=kLoop, calls=%fused_computation.180 | loop fusion | bytes 524288 | tf_op jit(solution)/shard_map/slice | solution.py:115
  22.6 0.0 copy-start.1
  22.6 0.0 copy-start.2
  22.6 0.9 %fusion.79 = (bf16[8,128,1,128]{3,2,1,0:T(2,128)(2,1)S(1)}, bf16[8,128,1,128]{3,2,1,0:T(2,128)(2,1)S(1)}) fusion(bf16[8,128,2,128]{3,2,1,0:T(2,128)(2,1)S(1)} %copy-done.3), kind=kLoop, calls=%fused_computation.179 | loop fusion | bytes 1048576 | tf_op jit(solution)/shard_map/slice | solution.py:107
  23.6 0.0 copy-start.4
  23.6 0.7 %gather_fusion.2 = s32[24]{0:T(128)S(1)} fusion(s32[1024]{0:T(1024)S(1)} %copy-done.1, s32[1024]{0:T(1024)S(1)} %get-tuple-element.62), kind=kCustom, calls=%fused_computation.2 | custom fusion | bytes 288 | tf_op jit(solution)/shard_map/gather | solution.py:112
  24.3 0.7 %gather_fusion.1 = s32[40]{0:T(128)S(1)} fusion(s32[1024]{0:T(1024)S(1)} %copy-done.2, s32[1024]{0:T(1024)S(1)} %get-tuple-element.63), kind=kCustom, calls=%fused_computation.1 | custom fusion | bytes 480 | tf_op jit(solution)/shard_map/gather | solution.py:99
  25.0 0.1 compare_and_fusion
  25.1 0.1 compare_and_fusion.1
  25.3 0.0 collective-permute-done
  25.3 0.0 collective-permute-done.1
  25.4 0.0 collective-permute-done.2
  25.4 0.3 fusion.82
  25.7 0.2 fusion.21
  25.9 0.3 fusion.23
  26.2 0.3 fusion.6
  26.5 0.5 fusion.81
  27.0 0.5 fusion.7
  27.5 0.4 fusion.10
  27.9 0.5 fusion.5
  28.5 0.1 fusion.48
  28.6 0.1 concatenate.19
  28.7 5.3 %collective-permute-start.4 = (f32[8,1040]{1,0:T(8,128)S(1)}, f32[8,1040]{1,0:T(8,128)S(1)}, u32[]{:S(2)}, u32[]{:S(2)}) collective-permute-start(f32[8,1040]{1,0:T(8,128)S(1)} %concatenate.19), channel_id=1, source_target_pairs={{8,0},{12,4},{16,8},{20,12},{24,16},{28,20},{32,24},{36,28},{40,32... | collective-permute-start | bytes 99848 | tf_op jit(solution)/shard_map/ppermute | solution.py:16
  34.0 0.1 fusion.54
  34.2 0.1 concatenate.20
  34.3 2.7 %collective-permute-start.5 = (f32[8,1040]{1,0:T(8,128)S(1)}, f32[8,1040]{1,0:T(8,128)S(1)}, u32[]{:S(2)}, u32[]{:S(2)}) collective-permute-start(f32[8,1040]{1,0:T(8,128)S(1)} %concatenate.20), channel_id=1, source_target_pairs={{4,0},{8,4},{12,8},{16,12},{20,16},{24,20},{28,24},{32,28},{36,32}... | collective-permute-start | bytes 99848 | tf_op jit(solution)/shard_map/ppermute | solution.py:16
  37.0 0.1 concatenate.22
  37.1 1.9 %collective-permute-start.6 = (f32[8,1040]{1,0:T(8,128)S(1)}, f32[8,1040]{1,0:T(8,128)S(1)}, u32[]{:S(2)}, u32[]{:S(2)}) collective-permute-start(f32[8,1040]{1,0:T(8,128)S(1)} %concatenate.22), channel_id=1, source_target_pairs={{0,4},{4,8},{8,12},{12,16},{16,20},{20,24},{24,28},{28,32},{32,36}... | collective-permute-start | bytes 99848 | tf_op jit(solution)/shard_map/ppermute | solution.py:16
  39.0 0.1 concatenate.23
  39.1 2.9 %collective-permute-start.7 = (f32[8,1040]{1,0:T(8,128)S(1)}, f32[8,1040]{1,0:T(8,128)S(1)}, u32[]{:S(2)}, u32[]{:S(2)}) collective-permute-start(f32[8,1040]{1,0:T(8,128)S(1)} %concatenate.23), channel_id=1, source_target_pairs={{0,8},{4,12},{8,16},{12,20},{16,24},{20,28},{24,32},{28,36},{32,40... | collective-permute-start | bytes 99848 | tf_op jit(solution)/shard_map/ppermute | solution.py:16
  42.0 2.4 %collective-permute-done.6 = f32[8,1040]{1,0:T(8,128)S(1)} collective-permute-done((f32[8,1040]{1,0:T(8,128)S(1)}, f32[8,1040]{1,0:T(8,128)S(1)}, u32[]{:S(2)}, u32[]{:S(2)}) %collective-permute-start.6) | collective-permute-done | bytes 33312 | tf_op jit(solution)/shard_map/ppermute | solution.py:16
  44.5 2.8 %collective-permute-done.7 = f32[8,1040]{1,0:T(8,128)S(1)} collective-permute-done((f32[8,1040]{1,0:T(8,128)S(1)}, f32[8,1040]{1,0:T(8,128)S(1)}, u32[]{:S(2)}, u32[]{:S(2)}) %collective-permute-start.7) | collective-permute-done | bytes 33312 | tf_op jit(solution)/shard_map/ppermute | solution.py:16
  47.3 0.1 maximum_maximum_fusion
  47.3 0.1 multiply_add_fusion
  47.4 0.1 fusion.56
  47.6 3.4 %fusion.83 = (bf16[8,2048]{1,0:T(8,128)(2,1)}, f32[8,2048]{1,0:T(8,128)S(1)}) fusion(bf16[1024,2048]{1,0:T(8,128)(2,1)} %param.12, bf16[1,8,8,128]{3,2,1,0:T(8,128)(2,1)S(1)} %fusion.56), kind=kOutput, calls=%fused_computation.183 | convolution fusion | flops 33570816 | bytes 4308992 | tf_op jit(solution)/shard_map/dot_general | solution.py:148
  51.0 4.5 %all-to-all-start = ((bf16[4,8,512]{2,1,0:T(8,128)(2,1)}), bf16[4,8,512]{2,1,0:T(8,128)(2,1)S(1)}, u32[]{:S(2)}, u32[]{:S(2)}) async-start(bf16[4,8,512]{2,1,0:T(8,128)(2,1)} %bitcast.42), calls=%async_computation | async-start | bytes 65536 | tf_op jit(solution)/shard_map/all_to_all | solution.py:154
  55.5 5.4 %all-to-all-done = bf16[4,8,512]{2,1,0:T(8,128)(2,1)S(1)} async-done(((bf16[4,8,512]{2,1,0:T(8,128)(2,1)}), bf16[4,8,512]{2,1,0:T(8,128)(2,1)S(1)}, u32[]{:S(2)}, u32[]{:S(2)}) %all-to-all-start) | async-done | bytes 32800 | tf_op jit(solution)/shard_map/all_to_all | solution.py:154
  60.9 0.1 select_reduce_fusion
  61.0 0.6 add_convert_fusion
  (38 shorter events, 0.3 us)
Async XLA Ops:
  0.0 19.4 %copy-start = (s32[1024]{0:T(1024)S(1)}, s32[1024]{0:T(1024)}, u32[]{:S(2)}) copy-start(s32[1024]{0:T(1024)} %param.13) | copy-start | bytes 12292
  0.0 22.6 %copy-start.3 = (bf16[8,128,2,128]{3,2,1,0:T(2,128)(2,1)S(1)}, bf16[8,128,2,128]{3,2,1,0:T(2,128)(2,1)}, u32[]{:S(2)}) copy-start(bf16[8,128,2,128]{3,2,1,0:T(2,128)(2,1)} %param.10) | copy-start | bytes 1572868
  0.8 24.6 %collective-permute-start.3 = (bf16[8,1,8,128]{3,2,0,1:T(8,128)(2,1)S(1)}, bf16[8,1,8,128]{3,2,0,1:T(8,128)(2,1)S(1)}, u32[]{:S(2)}, u32[]{:S(2)}) collective-permute-start(bf16[8,1,8,128]{3,2,0,1:T(8,128)(2,1)S(1)} %bitcast.200), channel_id=1, source_target_pairs={{8,0},{12,4},{16,8},{20,12},{24,16},{28,20},{32,24},{36,28},{40,32... | collective-permute-start | bytes 49160 | tf_op jit(solution)/shard_map/ppermute | solution.py:16
  12.4 12.9 %collective-permute-start.2 = (bf16[8,1,8,128]{3,2,0,1:T(8,128)(2,1)S(1)}, bf16[8,1,8,128]{3,2,0,1:T(8,128)(2,1)S(1)}, u32[]{:S(2)}, u32[]{:S(2)}) collective-permute-start(bf16[8,1,8,128]{3,2,0,1:T(8,128)(2,1)S(1)} %bitcast.201), channel_id=1, source_target_pairs={{4,0},{8,4},{12,8},{16,12},{20,16},{24,20},{28,24},{32,28},{36,32}... | collective-permute-start | bytes 49160 | tf_op jit(solution)/shard_map/ppermute | solution.py:16
  14.5 10.8 %collective-permute-start.1 = (bf16[8,1,8,128]{3,2,0,1:T(8,128)(2,1)S(1)}, bf16[8,1,8,128]{3,2,0,1:T(8,128)(2,1)S(1)}, u32[]{:S(2)}, u32[]{:S(2)}) collective-permute-start(bf16[8,1,8,128]{3,2,0,1:T(8,128)(2,1)S(1)} %bitcast.202), channel_id=1, source_target_pairs={{0,4},{4,8},{8,12},{12,16},{16,20},{20,24},{24,28},{28,32},{32,36}... | collective-permute-start | bytes 49160 | tf_op jit(solution)/shard_map/ppermute | solution.py:16
  16.8 8.5 %collective-permute-start = (bf16[8,1,8,128]{3,2,0,1:T(8,128)(2,1)S(1)}, bf16[8,1,8,128]{3,2,0,1:T(8,128)(2,1)S(1)}, u32[]{:S(2)}, u32[]{:S(2)}) collective-permute-start(bf16[8,1,8,128]{3,2,0,1:T(8,128)(2,1)S(1)} %bitcast.203), channel_id=1, source_target_pairs={{0,8},{4,12},{8,16},{12,20},{16,24},{20,28},{24,32},{28,36},{32,40... | collective-permute-start | bytes 49160 | tf_op jit(solution)/shard_map/ppermute | solution.py:16
  22.6 1.0 %copy-start.1 = (s32[1024]{0:T(1024)S(1)}, s32[1024]{0:T(1024)}, u32[]{:S(2)}) copy-start(s32[1024]{0:T(1024)} %param.15) | copy-start | bytes 12292
  22.6 1.7 %copy-start.2 = (s32[1024]{0:T(1024)S(1)}, s32[1024]{0:T(1024)}, u32[]{:S(2)}) copy-start(s32[1024]{0:T(1024)} %param.14) | copy-start | bytes 12292
  23.6 1.8 %copy-start.4 = (bf16[8,1024]{1,0:T(8,128)(2,1)S(1)}, bf16[8,1024]{1,0:T(8,128)(2,1)}, u32[]{:S(2)}) copy-start(bf16[8,1024]{1,0:T(8,128)(2,1)} %param.8) | copy-start | bytes 49156
  28.7 13.3 %collective-permute-start.4 = (f32[8,1040]{1,0:T(8,128)S(1)}, f32[8,1040]{1,0:T(8,128)S(1)}, u32[]{:S(2)}, u32[]{:S(2)}) collective-permute-start(f32[8,1040]{1,0:T(8,128)S(1)} %concatenate.19), channel_id=1, source_target_pairs={{8,0},{12,4},{16,8},{20,12},{24,16},{28,20},{32,24},{36,28},{40,32... | collective-permute-start | bytes 99848 | tf_op jit(solution)/shard_map/ppermute | solution.py:16
  34.3 7.8 %collective-permute-start.5 = (f32[8,1040]{1,0:T(8,128)S(1)}, f32[8,1040]{1,0:T(8,128)S(1)}, u32[]{:S(2)}, u32[]{:S(2)}) collective-permute-start(f32[8,1040]{1,0:T(8,128)S(1)} %concatenate.20), channel_id=1, source_target_pairs={{4,0},{8,4},{12,8},{16,12},{20,16},{24,20},{28,24},{32,28},{36,32}... | collective-permute-start | bytes 99848 | tf_op jit(solution)/shard_map/ppermute | solution.py:16
  37.1 7.4 %collective-permute-start.6 = (f32[8,1040]{1,0:T(8,128)S(1)}, f32[8,1040]{1,0:T(8,128)S(1)}, u32[]{:S(2)}, u32[]{:S(2)}) collective-permute-start(f32[8,1040]{1,0:T(8,128)S(1)} %concatenate.22), channel_id=1, source_target_pairs={{0,4},{4,8},{8,12},{12,16},{16,20},{20,24},{24,28},{28,32},{32,36}... | collective-permute-start | bytes 99848 | tf_op jit(solution)/shard_map/ppermute | solution.py:16
  39.1 8.2 %collective-permute-start.7 = (f32[8,1040]{1,0:T(8,128)S(1)}, f32[8,1040]{1,0:T(8,128)S(1)}, u32[]{:S(2)}, u32[]{:S(2)}) collective-permute-start(f32[8,1040]{1,0:T(8,128)S(1)} %concatenate.23), channel_id=1, source_target_pairs={{0,8},{4,12},{8,16},{12,20},{16,24},{20,28},{24,32},{28,36},{32,40... | collective-permute-start | bytes 99848 | tf_op jit(solution)/shard_map/ppermute | solution.py:16
  51.0 9.9 %all-to-all-start = ((bf16[4,8,512]{2,1,0:T(8,128)(2,1)}), bf16[4,8,512]{2,1,0:T(8,128)(2,1)S(1)}, u32[]{:S(2)}, u32[]{:S(2)}) async-start(bf16[4,8,512]{2,1,0:T(8,128)(2,1)} %bitcast.42), calls=%async_computation | async-start | bytes 65536 | tf_op jit(solution)/shard_map/all_to_all | solution.py:154

commit v3 on v2

--- a/solution.py
+++ b/solution.py
@@ -72,6 +72,11 @@
     return (weighted, peaks, totals)
 
 
+def swapped(block, axis):
+    devices = range(lax.axis_size(axis))
+    return lax.ppermute(block, axis, [(i, i ^ 1) for i in devices])
+
+
 def local(queries, new_kv, own_kv, prompt_kv, out_weight, parents, own_len, first_beam):
     per_dev = queries.shape[0]
     head_dim = HD
@@ -83,33 +88,48 @@
     req_count = lax.axis_size("req")
     beam_count = per_dev * req_count
     dev_index = lax.axis_index("req")
-    reach_dev = (MOST_BEAMS - 2) // per_dev + 1
-    offsets = list(range(-reach_dev, reach_dev + 1))
+    core = dev_index % 2
+    first_core = core == 0
+    chip_beams = 2 * per_dev
     shape4 = (per_dev, kv_heads_local, group_size, head_dim)
 
     query_block = queries.reshape(shape4)
-    hood = [query_block if k == 0 else shifted(query_block, "req", k) for k in offsets]
+    from_prev = shifted(query_block, "req", -2)
+    from_next = shifted(query_block, "req", 2)
+    mine3 = jnp.concatenate([from_prev, query_block, from_next], axis=0)
+    mate3 = swapped(mine3, "req")
+    hood = []
+    for i in range(3):
+        a = mine3[i * per_dev : (i + 1) * per_dev]
+        b = mate3[i * per_dev : (i + 1) * per_dev]
+        hood += [jnp.where(first_core, a, b), jnp.where(first_core, b, a)]
     hood_queries = jnp.concatenate(hood, axis=0)
     hood_count = hood_queries.shape[0]
-    hood_beams = (dev_index - reach_dev) * per_dev + jnp.arange(hood_count, dtype=jnp.int32)
+    chip = dev_index // 2
+    hood_start = (chip - 1) * chip_beams
+    hood_beams = hood_start + jnp.arange(hood_count, dtype=jnp.int32)
     in_range = (hood_beams >= 0) & (hood_beams < beam_count)
-    clipped = jnp.clip(hood_beams, 0, beam_count - 1)
-
-    parent = parents[clipped]
-    lengths = own_len[parent]
+    padded_parents = jnp.pad(parents, (chip_beams, chip_beams))
+    padded_first = jnp.pad(first_beam, (chip_beams, chip_beams))
+    parent = lax.dynamic_slice_in_dim(padded_parents, chip * chip_beams, hood_count)
+    hood_first = lax.dynamic_slice_in_dim(padded_first, chip * chip_beams, hood_count)
+
     parent_here = in_range & (parent // per_dev == dev_index)
+    local_len = lax.dynamic_slice_in_dim(own_len, dev_index * per_dev, per_dev)
     columns = jnp.arange(per_dev * own_size, dtype=jnp.int32)
+    column_slot = columns // own_size
+    column_len = jnp.repeat(local_len, own_size)
     own_allowed = (
         parent_here[:, None]
-        & (columns[None, :] // own_size == (parent % per_dev)[:, None])
-        & (columns[None, :] % own_size < lengths[:, None])
+        & (column_slot[None, :] == (parent % per_dev)[:, None])
+        & (columns % own_size < column_len)[None, :]
     )
     own_keys = own_kv[:, :, 0].reshape(per_dev * own_size, kv_heads_local, head_dim)
     own_values = own_kv[:, :, 1].reshape(per_dev * own_size, kv_heads_local, head_dim)
     own_part = partial_block(hood_queries, own_keys, own_values, own_allowed)
 
-    start = reach_dev * per_dev
-    home_here = in_range[start:] & (first_beam[clipped[start:]] // per_dev == dev_index)
+    start = chip_beams
+    home_here = in_range[start:] & (hood_first[start:] // per_dev == dev_index)
     prompt_allowed = jnp.broadcast_to(home_here[:, None], (hood_count - start, prompt_size))
     prompt_keys = prompt_kv[0, :, 0].reshape(prompt_size, kv_heads_local, head_dim)
     prompt_values = prompt_kv[0, :, 1].reshape(prompt_size, kv_heads_local, head_dim)
@@ -126,20 +146,33 @@
         jnp.ones_like(fresh_scores[..., 0]),
     )
 
-    def block_of(part, k, base):
-        lo = (k + reach_dev) * per_dev - base
+    def rows(part, lo):
         return tuple(x[lo : lo + per_dev] for x in part)
 
-    parts = [fresh_part]
-    for k in offsets:
-        own_k = block_of(own_part, k, 0)
-        if k >= 0:
-            own_k = merge_all([own_k, block_of(prompt_part, k, start)])
-        if k == 0:
-            parts.append(own_k)
-        else:
-            parts.append(unpack(shifted(pack(own_k), "req", -k), shape4))
-    weighted, _, totals = merge_all(parts)
+    def block_for(chip_offset, which_core):
+        lo = (chip_offset + 1) * chip_beams + which_core * per_dev
+        own_k = rows(own_part, lo)
+        if chip_offset >= 0:
+            return merge_all([own_k, rows(prompt_part, lo - start)])
+        return own_k
+
+    def pick(which_first, which_second):
+        return tuple(jnp.where(first_core, a, b) for a, b in zip(which_first, which_second))
+
+    mate_core = 1 - core
+    to_mate = [
+        pick(block_for(k, 1), block_for(k, 0)) for k in (-1, 0, 1)
+    ]
+    mine_blocks = [
+        pick(block_for(k, 0), block_for(k, 1)) for k in (-1, 0, 1)
+    ]
+    del mate_core
+    sent = swapped(jnp.concatenate([pack(b) for b in to_mate], axis=0), "req")
+    got = [unpack(sent[i * per_dev : (i + 1) * per_dev], shape4) for i in range(3)]
+    merged = [merge_all([mine_blocks[i], got[i]]) for i in range(3)]
+    back_from_next = unpack(shifted(pack(merged[0]), "req", 2), shape4)
+    back_from_prev = unpack(shifted(pack(merged[2]), "req", -2), shape4)
+    weighted, _, totals = merge_all([fresh_part, merged[1], back_from_next, back_from_prev])
     attended = (
         (weighted / totals[..., None])
         .reshape(per_dev, q_heads_local * head_dim)

time: 62.2 us -> 58.7 us (0.944)
  starting transfers between devices: 36 us -> 28.6 us
  waiting for transfers between devices: 10.7 us -> 15 us
  local copies, waits for them, and re-layouts: 5.84 us -> 4.6 us
    ppermute x8 -> x4, starting transfers between devices: 31.5 us -> 20.1 us  [shifted(): return lax.ppermute(block, axis, route)]
    ppermute x0 -> x2, starting transfers between devices: none -> 3.99 us  [swapped(): return lax.ppermute(block, axis, [(i, i ^ 1) for i in devices])]
    ppermute x8 -> x4, waiting for transfers between devices: 5.23 us -> 7.39 us  [shifted(): return lax.ppermute(block, axis, route)]
    gather x3 -> x0, local copies, waits for them, and re-layouts: 2.13 us -> none  [the longest x1 0.73 us: local(): lengths = own_len[parent]]
    ppermute x0 -> x2, waiting for transfers between devices: none -> 2.12 us  [swapped(): return lax.ppermute(block, axis, [(i, i ^ 1) for i in devices])]
    dynamic_slice x0 -> x2, local copies, waits for them, and re-layouts: none -> 0.85 us  [the longest x1 0.76 us: local(): local_len = lax.dynamic_slice_in_dim(own_len, dev_index * per_dev, per_dev)]
    and x1, other arithmetic: 0.01 us -> 0.85 us  [local(): parent_here = in_range & (parent // per_dev == dev_index)]
    convert_element_type x1, other arithmetic: 0.77 us -> 0.01 us  [local(): fresh_values[:, 0, :, None, :].astype(jnp.float32)]
  transfers between devices with their start and end apart: 9 -> 7, of which waited for: 3 -> 5; matrix products, arithmetic and copies ran while one was open for 10% -> 8% of each run, Pallas kernels for 0% -> 0%
where the time goes in v3:
time: 58.7 us; the launch traced here: 58.1 us
  starting transfers between devices  28.6 us (49%)
  waiting for transfers between devices  15 us (26%)
  matrix products  6.07 us (10%)
  local copies, waits for them, and re-layouts  4.6 us (8%)
  other arithmetic  3.54 us (6%)
    ppermute x4, starting transfers between devices, shifted(): return lax.ppermute(block, axis, route)  20.1 us
    ppermute x4, waiting for transfers between devices, shifted(): return lax.ppermute(block, axis, route)  7.39 us
    all_to_all x1, waiting for transfers between devices, local(): got = lax.all_to_all(chunks.astype(jnp.bfloat16), 'tp', 0, 0, tiled=True)  5.44 us
    all_to_all x1, starting transfers between devices, local(): got = lax.all_to_all(chunks.astype(jnp.bfloat16), 'tp', 0, 0, tiled=True)  4.47 us
    ppermute x2, starting transfers between devices, swapped(): return lax.ppermute(block, axis, [(i, i ^ 1) for i in devices])  3.99 us
    dot_general x1, matrix products, local(): jnp.dot(attended, out_weight, preferred_element_type=jnp.float32)  3.45 us
    ppermute x2, waiting for transfers between devices, swapped(): return lax.ppermute(block, axis, [(i, i ^ 1) for i in devices])  2.12 us
    slice x1, local copies, waits for them, and re-layouts, local(): prompt_kv[0, :, 1].reshape(prompt_size, kv_heads_local, head_dim)  1.49 us
  transfers between devices with their start and end apart: 7, of which 5 were waited for; matrix products, arithmetic and copies ran while one was open for 8% of the time, Pallas kernels for 0%

profile of v3, /device:TPU:6, one launch (start us, length us, event | category | flops | bytes accessed | tf_op | source)
XLA Modules:
  0.0 58.1 jit_solution(3723801559835805904)
XLA Ops:
  0.0 0.8 %copy.80 = bf16[1,8,8,128]{3,2,1,0:T(8,128)(2,1)S(1)} copy(bf16[1,8,8,128]{3,1,2,0:T(8,128)(2,1)} %bitcast.205) | data formatting | bytes 32768
  0.8 11.7 %collective-permute-start.1 = (bf16[8,1,8,128]{3,2,0,1:T(8,128)(2,1)S(1)}, bf16[8,1,8,128]{3,2,0,1:T(8,128)(2,1)S(1)}, u32[]{:S(2)}, u32[]{:S(2)}) collective-permute-start(bf16[8,1,8,128]{3,2,0,1:T(8,128)(2,1)S(1)} %bitcast.212), channel_id=1, source_target_pairs={{8,0},{12,4},{16,8},{20,12},{24,16},{28,20},{32,24},{36,28},{40,32... | collective-permute-start | bytes 49160 | tf_op jit(solution)/shard_map/ppermute | solution.py:16
  12.4 1.9 %collective-permute-start = (bf16[8,1,8,128]{3,2,0,1:T(8,128)(2,1)S(1)}, bf16[8,1,8,128]{3,2,0,1:T(8,128)(2,1)S(1)}, u32[]{:S(2)}, u32[]{:S(2)}) collective-permute-start(bf16[8,1,8,128]{3,2,0,1:T(8,128)(2,1)S(1)} %bitcast.213), channel_id=1, source_target_pairs={{0,8},{4,12},{8,16},{12,20},{16,24},{20,28},{24,32},{28,36},{32,40... | collective-permute-start | bytes 49160 | tf_op jit(solution)/shard_map/ppermute | solution.py:16
  14.4 0.8 %dynamic_slice.13 = s32[8]{0:T(128)S(1)} dynamic-slice(s32[1024]{0:T(1024)} %param.14, s32[]{:T(128)S(6)} %select_n.358), dynamic_slice_sizes={8} | dynamic-slice | bytes 68 | tf_op jit(solution)/shard_map/dynamic_slice | solution.py:118
  15.2 0.1 fusion.65
  15.3 0.8 %compare_and_fusion.1 = (pred[48]{0:T(512)(128)(4,1)S(1)}, s32[48]{0:T(128)S(1)}) fusion(s32[]{:T(128)S(6)} %axis_index.23, s32[]{:T(128)S(6)} %select_n.353, s32[1024]{0:T(1024)} %param.13, s32[]{:T(128)S(6)} %mul.356), kind=kLoop, calls=%fused_computation.198 | loop fusion | flops 1152 | bytes 4348 | tf_op jit(solution)/shard_map/and | solution.py:117
  16.1 0.0 copy-start.3
  16.1 1.5 %fusion.88 = (bf16[1,512,1,128]{3,2,1,0:T(2,128)(2,1)S(1)}, bf16[1,512,1,128]{3,2,1,0:T(2,128)(2,1)S(1)}) fusion(bf16[1,512,2,128]{3,2,1,0:T(2,128)(2,1)} %param.11), kind=kLoop, calls=%fused_computation.220 | loop fusion | bytes 524288 | tf_op jit(solution)/shard_map/slice | solution.py:135
  17.6 0.0 copy-start.1
  17.7 0.9 %fusion.87 = (bf16[8,128,1,128]{3,2,1,0:T(2,128)(2,1)S(1)}, bf16[8,128,1,128]{3,2,1,0:T(2,128)(2,1)S(1)}) fusion(bf16[8,128,2,128]{3,2,1,0:T(2,128)(2,1)S(1)} %copy-done), kind=kLoop, calls=%fused_computation.219 | loop fusion | bytes 1048576 | tf_op jit(solution)/shard_map/slice | solution.py:128
  18.6 0.1 and_and_fusion
  18.7 0.1 pad_dynamic-slice_fusion
  18.8 1.4 %collective-permute-done = bf16[8,1,8,128]{3,2,0,1:T(8,128)(2,1)S(1)} collective-permute-done((bf16[8,1,8,128]{3,2,0,1:T(8,128)(2,1)S(1)}, bf16[8,1,8,128]{3,2,0,1:T(8,128)(2,1)S(1)}, u32[]{:S(2)}, u32[]{:S(2)}) %collective-permute-start) | collective-permute-done | bytes 16416 | tf_op jit(solution)/shard_map/ppermute | solution.py:16
  20.2 1.9 %collective-permute-start.2 = (bf16[24,1,8,128]{3,2,0,1:T(8,128)(2,1)S(1)}, bf16[24,1,8,128]{3,2,0,1:T(8,128)(2,1)S(1)}, u32[]{:S(2)}, u32[]{:S(2)}) collective-permute-start(bf16[24,1,8,128]{3,2,0,1:T(8,128)(2,1)S(1)} %pad_maximum_fusion.1), channel_id=1, source_target_pairs={{0,4},{4,0},{8,12},{12,8},{16,20},{20,16},{24,28},{28,24},{32,36},... | collective-permute-start | bytes 147464 | tf_op jit(solution)/shard_map/ppermute | solution.py:77
  22.1 0.1 compare_and_fusion
  22.3 1.0 %collective-permute-done.2 = bf16[24,1,8,128]{3,2,0,1:T(8,128)(2,1)S(1)} collective-permute-done((bf16[24,1,8,128]{3,2,0,1:T(8,128)(2,1)S(1)}, bf16[24,1,8,128]{3,2,0,1:T(8,128)(2,1)S(1)}, u32[]{:S(2)}, u32[]{:S(2)}) %collective-permute-start.2) | collective-permute-done | bytes 49184 | tf_op jit(solution)/shard_map/ppermute | solution.py:77
  23.5 0.6 fusion.90
  24.0 0.5 fusion.6
  24.6 0.3 fusion.89
  24.9 0.2 fusion.19
  25.2 0.3 fusion.21
  25.4 0.3 fusion.4
  25.7 0.5 fusion.8
  26.2 0.0 copy-start.2
  26.2 0.6 fusion.3
  26.9 0.1 select_bitcast_fusion.1
  27.1 0.1 concatenate.32
  27.2 0.1 concatenate.31
  27.2 0.1 concatenate.30
  27.3 2.1 %collective-permute-start.3 = (f32[24,1040]{1,0:T(8,128)S(1)}, f32[24,1040]{1,0:T(8,128)S(1)}, u32[]{:S(2)}, u32[]{:S(2)}) collective-permute-start(f32[24,1040]{1,0:T(8,128)S(1)} %pad_maximum_fusion), channel_id=1, source_target_pairs={{0,4},{4,0},{8,12},{12,8},{16,20},{20,16},{24,28},{28,24},{32,36},... | collective-permute-start | bytes 299528 | tf_op jit(solution)/shard_map/ppermute | solution.py:77
  29.4 1.1 %collective-permute-done.3 = f32[24,1040]{1,0:T(8,128)S(1)} collective-permute-done((f32[24,1040]{1,0:T(8,128)S(1)}, f32[24,1040]{1,0:T(8,128)S(1)}, u32[]{:S(2)}, u32[]{:S(2)}) %collective-permute-start.3) | collective-permute-done | bytes 99872 | tf_op jit(solution)/shard_map/ppermute | solution.py:77
  30.5 0.1 slice_compare_fusion.4
  30.6 0.1 multiply_add_fusion.1
  30.7 0.1 fusion.46
  30.9 0.1 concatenate.34
  30.9 4.7 %collective-permute-start.4 = (f32[8,1040]{1,0:T(8,128)S(1)}, f32[8,1040]{1,0:T(8,128)S(1)}, u32[]{:S(2)}, u32[]{:S(2)}) collective-permute-start(f32[8,1040]{1,0:T(8,128)S(1)} %concatenate.34), channel_id=1, source_target_pairs={{8,0},{12,4},{16,8},{20,12},{24,16},{28,20},{32,24},{36,28},{40,32... | collective-permute-start | bytes 99848 | tf_op jit(solution)/shard_map/ppermute | solution.py:16
  35.6 0.1 fusion.56
  35.7 0.1 concatenate.35
  35.8 1.9 %collective-permute-start.5 = (f32[8,1040]{1,0:T(8,128)S(1)}, f32[8,1040]{1,0:T(8,128)S(1)}, u32[]{:S(2)}, u32[]{:S(2)}) collective-permute-start(f32[8,1040]{1,0:T(8,128)S(1)} %concatenate.35), channel_id=1, source_target_pairs={{0,8},{4,12},{8,16},{12,20},{16,24},{20,28},{24,32},{28,36},{32,40... | collective-permute-start | bytes 99848 | tf_op jit(solution)/shard_map/ppermute | solution.py:16
  37.8 6.0 %collective-permute-done.5 = f32[8,1040]{1,0:T(8,128)S(1)} collective-permute-done((f32[8,1040]{1,0:T(8,128)S(1)}, f32[8,1040]{1,0:T(8,128)S(1)}, u32[]{:S(2)}, u32[]{:S(2)}) %collective-permute-start.5) | collective-permute-done | bytes 33312 | tf_op jit(solution)/shard_map/ppermute | solution.py:16
  43.8 0.1 maximum_maximum_fusion
  43.8 0.1 multiply_add_fusion
  43.9 0.2 fusion.58
  44.1 3.4 %fusion.91 = (bf16[8,2048]{1,0:T(8,128)(2,1)}, f32[8,2048]{1,0:T(8,128)S(1)}) fusion(bf16[1024,2048]{1,0:T(8,128)(2,1)} %param.12, bf16[1,8,8,128]{3,2,1,0:T(8,128)(2,1)S(1)} %fusion.58), kind=kOutput, calls=%fused_computation.223 | convolution fusion | flops 33570816 | bytes 4308992 | tf_op jit(solution)/shard_map/dot_general | solution.py:181
  47.5 4.5 %all-to-all-start = ((bf16[4,8,512]{2,1,0:T(8,128)(2,1)}), bf16[4,8,512]{2,1,0:T(8,128)(2,1)S(1)}, u32[]{:S(2)}, u32[]{:S(2)}) async-start(bf16[4,8,512]{2,1,0:T(8,128)(2,1)} %bitcast.40), calls=%async_computation | async-start | bytes 65536 | tf_op jit(solution)/shard_map/all_to_all | solution.py:187
  52.0 5.4 %all-to-all-done = bf16[4,8,512]{2,1,0:T(8,128)(2,1)S(1)} async-done(((bf16[4,8,512]{2,1,0:T(8,128)(2,1)}), bf16[4,8,512]{2,1,0:T(8,128)(2,1)S(1)}, u32[]{:S(2)}, u32[]{:S(2)}) %all-to-all-start) | async-done | bytes 32800 | tf_op jit(solution)/shard_map/all_to_all | solution.py:187
  57.5 0.1 select_reduce_fusion
  57.5 0.6 %add_convert_fusion = bf16[8,512]{1,0:T(8,128)(2,1)} fusion(f32[8,512]{1,0:T(8,128)S(1)} %select_reduce_fusion, f32[8,2048]{1,0:T(8,128)S(1)} %get-tuple-element.89, s32[]{:T(128)S(6)} %select_n.424), kind=kLoop, calls=%fused_computation.94 | loop fusion | flops 8192 | bytes 40964 | tf_op jit(solution)/shard_map/convert_element_type | solution.py:191
  (37 shorter events, 0.4 us)
Async XLA Ops:
  0.0 17.6 %copy-start = (bf16[8,128,2,128]{3,2,1,0:T(2,128)(2,1)S(1)}, bf16[8,128,2,128]{3,2,1,0:T(2,128)(2,1)}, u32[]{:S(2)}) copy-start(bf16[8,128,2,128]{3,2,1,0:T(2,128)(2,1)} %param.10) | copy-start | bytes 1572868
  0.8 18.0 %collective-permute-start.1 = (bf16[8,1,8,128]{3,2,0,1:T(8,128)(2,1)S(1)}, bf16[8,1,8,128]{3,2,0,1:T(8,128)(2,1)S(1)}, u32[]{:S(2)}, u32[]{:S(2)}) collective-permute-start(bf16[8,1,8,128]{3,2,0,1:T(8,128)(2,1)S(1)} %bitcast.212), channel_id=1, source_target_pairs={{8,0},{12,4},{16,8},{20,12},{24,16},{28,20},{32,24},{36,28},{40,32... | collective-permute-start | bytes 49160 | tf_op jit(solution)/shard_map/ppermute | solution.py:16
  12.4 7.7 %collective-permute-start = (bf16[8,1,8,128]{3,2,0,1:T(8,128)(2,1)S(1)}, bf16[8,1,8,128]{3,2,0,1:T(8,128)(2,1)S(1)}, u32[]{:S(2)}, u32[]{:S(2)}) collective-permute-start(bf16[8,1,8,128]{3,2,0,1:T(8,128)(2,1)S(1)} %bitcast.213), channel_id=1, source_target_pairs={{0,8},{4,12},{8,16},{12,20},{16,24},{20,28},{24,32},{28,36},{32,40... | collective-permute-start | bytes 49160 | tf_op jit(solution)/shard_map/ppermute | solution.py:16
  16.1 2.6 %copy-start.3 = (s32[1024]{0:T(1024)S(1)}, s32[1024]{0:T(1024)}, u32[]{:S(2)}) copy-start(s32[1024]{0:T(1024)} %param.15) | copy-start | bytes 12292
  17.6 5.7 %copy-start.1 = (bf16[8,1024]{1,0:T(8,128)(2,1)S(1)}, bf16[8,1024]{1,0:T(8,128)(2,1)}, u32[]{:S(2)}) copy-start(bf16[8,1024]{1,0:T(8,128)(2,1)} %param.8) | copy-start | bytes 49156
  20.2 3.1 %collective-permute-start.2 = (bf16[24,1,8,128]{3,2,0,1:T(8,128)(2,1)S(1)}, bf16[24,1,8,128]{3,2,0,1:T(8,128)(2,1)S(1)}, u32[]{:S(2)}, u32[]{:S(2)}) collective-permute-start(bf16[24,1,8,128]{3,2,0,1:T(8,128)(2,1)S(1)} %pad_maximum_fusion.1), channel_id=1, source_target_pairs={{0,4},{4,0},{8,12},{12,8},{16,20},{20,16},{24,28},{28,24},{32,36},... | collective-permute-start | bytes 147464 | tf_op jit(solution)/shard_map/ppermute | solution.py:77
  26.2 3.2 %copy-start.2 = (bf16[8,2,128]{2,1,0:T(2,128)(2,1)S(1)}, bf16[8,2,128]{2,1,0:T(2,128)(2,1)}, u32[]{:S(2)}) copy-start(bf16[8,2,128]{2,1,0:T(2,128)(2,1)} %param.9) | copy-start | bytes 12292
  27.3 3.2 %collective-permute-start.3 = (f32[24,1040]{1,0:T(8,128)S(1)}, f32[24,1040]{1,0:T(8,128)S(1)}, u32[]{:S(2)}, u32[]{:S(2)}) collective-permute-start(f32[24,1040]{1,0:T(8,128)S(1)} %pad_maximum_fusion), channel_id=1, source_target_pairs={{0,4},{4,0},{8,12},{12,8},{16,20},{20,16},{24,28},{28,24},{32,36},... | collective-permute-start | bytes 299528 | tf_op jit(solution)/shard_map/ppermute | solution.py:77
  30.9 6.8 %collective-permute-start.4 = (f32[8,1040]{1,0:T(8,128)S(1)}, f32[8,1040]{1,0:T(8,128)S(1)}, u32[]{:S(2)}, u32[]{:S(2)}) collective-permute-start(f32[8,1040]{1,0:T(8,128)S(1)} %concatenate.34), channel_id=1, source_target_pairs={{8,0},{12,4},{16,8},{20,12},{24,16},{28,20},{32,24},{36,28},{40,32... | collective-permute-start | bytes 99848 | tf_op jit(solution)/shard_map/ppermute | solution.py:16
  35.8 8.0 %collective-permute-start.5 = (f32[8,1040]{1,0:T(8,128)S(1)}, f32[8,1040]{1,0:T(8,128)S(1)}, u32[]{:S(2)}, u32[]{:S(2)}) collective-permute-start(f32[8,1040]{1,0:T(8,128)S(1)} %concatenate.35), channel_id=1, source_target_pairs={{0,8},{4,12},{8,16},{12,20},{16,24},{20,28},{24,32},{28,36},{32,40... | collective-permute-start | bytes 99848 | tf_op jit(solution)/shard_map/ppermute | solution.py:16
  47.5 9.9 %all-to-all-start = ((bf16[4,8,512]{2,1,0:T(8,128)(2,1)}), bf16[4,8,512]{2,1,0:T(8,128)(2,1)S(1)}, u32[]{:S(2)}, u32[]{:S(2)}) async-start(bf16[4,8,512]{2,1,0:T(8,128)(2,1)} %bitcast.40), calls=%async_computation | async-start | bytes 65536 | tf_op jit(solution)/shard_map/all_to_all | solution.py:187

commit v4 on v3

--- a/solution.py
+++ b/solution.py
@@ -1,6 +1,7 @@
 import jax
 import jax.numpy as jnp
 from jax import lax
+from jax.experimental import pallas as pl
 from jax.sharding import PartitionSpec as P
 
 HD = 128
@@ -70,6 +71,25 @@
     peaks = packed[:, width : width + k * g].reshape(n, k, g)
     totals = packed[:, width + k * g :].reshape(n, k, g)
     return (weighted, peaks, totals)
+
+
+def project_kernel(x_ref, w_ref, o_ref):
+    o_ref[0] = jnp.dot(x_ref[...], w_ref[...], preferred_element_type=jnp.float32)
+
+
+def project(attended, weight, pieces):
+    n, inner = attended.shape
+    width = weight.shape[1] // pieces
+    return pl.pallas_call(
+        project_kernel,
+        grid=(pieces,),
+        in_specs=[
+            pl.BlockSpec((n, inner), lambda j: (0, 0)),
+            pl.BlockSpec((inner, width), lambda j: (0, j)),
+        ],
+        out_specs=pl.BlockSpec((1, n, width), lambda j: (j, 0, 0)),
+        out_shape=jax.ShapeDtypeStruct((pieces, n, width), jnp.float32),
+    )(attended, weight)
 
 
 def swapped(block, axis):
@@ -94,10 +114,12 @@
     shape4 = (per_dev, kv_heads_local, group_size, head_dim)
 
     query_block = queries.reshape(shape4)
-    from_prev = shifted(query_block, "req", -2)
-    from_next = shifted(query_block, "req", 2)
-    mine3 = jnp.concatenate([from_prev, query_block, from_next], axis=0)
+    from_prev = shifted(queries, "req", -2)
+    from_next = shifted(queries, "req", 2)
+    mine3 = jnp.concatenate([from_prev, queries, from_next], axis=0)
     mate3 = swapped(mine3, "req")
+    mine3 = mine3.reshape((3 * per_dev,) + shape4[1:])
+    mate3 = mate3.reshape((3 * per_dev,) + shape4[1:])
     hood = []
     for i in range(3):
         a = mine3[i * per_dev : (i + 1) * per_dev]
@@ -109,13 +131,15 @@
     hood_start = (chip - 1) * chip_beams
     hood_beams = hood_start + jnp.arange(hood_count, dtype=jnp.int32)
     in_range = (hood_beams >= 0) & (hood_beams < beam_count)
-    padded_parents = jnp.pad(parents, (chip_beams, chip_beams))
-    padded_first = jnp.pad(first_beam, (chip_beams, chip_beams))
-    parent = lax.dynamic_slice_in_dim(padded_parents, chip * chip_beams, hood_count)
-    hood_first = lax.dynamic_slice_in_dim(padded_first, chip * chip_beams, hood_count)
+    index_rows = jnp.pad(
+        jnp.stack([parents, first_beam, own_len]), ((0, 0), (chip_beams, chip_beams))
+    )
+    window = lax.dynamic_slice_in_dim(index_rows, chip * chip_beams, hood_count, axis=1)
+    parent = window[0]
+    hood_first = window[1]
 
     parent_here = in_range & (parent // per_dev == dev_index)
-    local_len = lax.dynamic_slice_in_dim(own_len, dev_index * per_dev, per_dev)
+    local_len = lax.dynamic_slice_in_dim(window[2], chip_beams + core * per_dev, per_dev)
     columns = jnp.arange(per_dev * own_size, dtype=jnp.int32)
     column_slot = columns // own_size
     column_len = jnp.repeat(local_len, own_size)
@@ -124,15 +148,17 @@
         & (column_slot[None, :] == (parent % per_dev)[:, None])
         & (columns % own_size < column_len)[None, :]
     )
-    own_keys = own_kv[:, :, 0].reshape(per_dev * own_size, kv_heads_local, head_dim)
-    own_values = own_kv[:, :, 1].reshape(per_dev * own_size, kv_heads_local, head_dim)
+    own_split = jnp.moveaxis(own_kv.reshape(per_dev * own_size, 2, -1), 1, 0)
+    own_keys = own_split[0].reshape(per_dev * own_size, kv_heads_local, head_dim)
+    own_values = own_split[1].reshape(per_dev * own_size, kv_heads_local, head_dim)
     own_part = partial_block(hood_queries, own_keys, own_values, own_allowed)
 
     start = chip_beams
     home_here = in_range[start:] & (hood_first[start:] // per_dev == dev_index)
     prompt_allowed = jnp.broadcast_to(home_here[:, None], (hood_count - start, prompt_size))
-    prompt_keys = prompt_kv[0, :, 0].reshape(prompt_size, kv_heads_local, head_dim)
-    prompt_values = prompt_kv[0, :, 1].reshape(prompt_size, kv_heads_local, head_dim)
+    prompt_split = jnp.moveaxis(prompt_kv[0], 1, 0)
+    prompt_keys = prompt_split[0].reshape(prompt_size, kv_heads_local, head_dim)
+    prompt_values = prompt_split[1].reshape(prompt_size, kv_heads_local, head_dim)
     prompt_part = partial_block(hood_queries[start:], prompt_keys, prompt_values, prompt_allowed)
 
     fresh_keys = new_kv[:, 0].reshape(per_dev, 1, kv_heads_local, head_dim)
@@ -178,15 +204,13 @@
         .reshape(per_dev, q_heads_local * head_dim)
         .astype(jnp.bfloat16)
     )
-    partial_term = jnp.dot(attended, out_weight, preferred_element_type=jnp.float32)
-
     tp_count = lax.axis_size("tp")
     tp_index = lax.axis_index("tp")
-    width = partial_term.shape[1] // tp_count
-    chunks = partial_term.reshape(per_dev, tp_count, width).transpose(1, 0, 2)
+    chunks = project(attended, out_weight, tp_count)
+
     got = lax.all_to_all(chunks.astype(jnp.bfloat16), "tp", 0, 0, tiled=True)
     others = jnp.arange(tp_count, dtype=jnp.int32)[:, None, None] != tp_index
-    mine = lax.dynamic_slice_in_dim(partial_term, tp_index * width, width, axis=1)
+    mine = lax.dynamic_index_in_dim(chunks, tp_index, axis=0, keepdims=False)
     total = mine + jnp.sum(jnp.where(others, got.astype(jnp.float32), 0.0), axis=0)
     return total.astype(jnp.bfloat16)
 

time: 58.7 us -> 61.1 us (1.041)
  Pallas kernels: 0 us -> 4.23 us
  matrix products: 6.07 us -> 2.61 us
  other arithmetic: 3.54 us -> 6.26 us
  local copies, waits for them, and re-layouts: 4.6 us -> 3.44 us
    pallas_call x0 -> x1, Pallas kernels: none -> 4.23 us  [project(): pl.pallas_call(project_kernel, grid=(pieces,), in_specs=[pl.BlockSpec((n,...]
    dot_general x1 -> x0, matrix products: 3.45 us -> none  [local(): jnp.dot(attended, out_weight, preferred_element_type=jnp.float32)]
    slice x2 -> x1, local copies, waits for them, and re-layouts: 2.43 us -> 0.01 us  [local(): window[2]]
    unnamed x18 -> x23, local copies, waits for them, and re-layouts: 0.92 us -> 2.86 us
    convert_element_type x0 -> x1, other arithmetic: none -> 1.46 us  [local(): got = lax.all_to_all(chunks.astype(jnp.bfloat16), 'tp', 0, 0, tiled=True)]
    ppermute x4, waiting for transfers between devices: 7.39 us -> 8.82 us  [shifted(): return lax.ppermute(block, axis, route)]
    ppermute x2, waiting for transfers between devices: 2.12 us -> 0.9 us  [swapped(): return lax.ppermute(block, axis, [(i, i ^ 1) for i in devices])]
    and x1, other arithmetic: 0.85 us -> 0.01 us  [local(): parent_here = in_range & (parent // per_dev == dev_index)]
  transfers between devices with their start and end apart: 7 -> 7, of which waited for: 5 -> 4; matrix products, arithmetic and copies ran while one was open for 8% -> 6% of each run, Pallas kernels for 0% -> 0%
where the time goes in v4:
time: 61.1 us; the launch traced here: 60.5 us
  starting transfers between devices  28.3 us (46%)
  waiting for transfers between devices  15.2 us (25%)
  other arithmetic  6.26 us (10%)
  Pallas kernels  4.23 us (7%)
  local copies, waits for them, and re-layouts  3.44 us (6%)
  matrix products  2.61 us (4%)
    ppermute x4, starting transfers between devices, shifted(): return lax.ppermute(block, axis, route)  19.5 us
    ppermute x4, waiting for transfers between devices, shifted(): return lax.ppermute(block, axis, route)  8.82 us
    all_to_all x1, waiting for transfers between devices, local(): got = lax.all_to_all(chunks.astype(jnp.bfloat16), 'tp', 0, 0, tiled=True)  5.44 us
    all_to_all x1, starting transfers between devices, local(): got = lax.all_to_all(chunks.astype(jnp.bfloat16), 'tp', 0, 0, tiled=True)  4.47 us
    ppermute x2, starting transfers between devices, swapped(): return lax.ppermute(block, axis, [(i, i ^ 1) for i in devices])  4.32 us
    pallas_call x1, Pallas kernels, project(): pl.pallas_call(project_kernel, grid=(pieces,), in_specs=[pl.BlockSpec((n,...  4.23 us
    unnamed x23, local copies, waits for them, and re-layouts  2.86 us
    convert_element_type x1, other arithmetic, local(): got = lax.all_to_all(chunks.astype(jnp.bfloat16), 'tp', 0, 0, tiled=True)  1.46 us
  transfers between devices with their start and end apart: 7, of which 4 were waited for; matrix products, arithmetic and copies ran while one was open for 6% of the time, Pallas kernels for 0%

profile of v4, /device:TPU:6, one launch (start us, length us, event | category | flops | bytes accessed | tf_op | source)
XLA Modules:
  0.0 60.5 jit_solution(11211974791411951759)
XLA Ops:
  0.0 11.8 %collective-permute-start.1 = (bf16[8,1024]{1,0:T(8,128)(2,1)}, bf16[8,1024]{1,0:T(8,128)(2,1)S(1)}, u32[]{:S(2)}, u32[]{:S(2)}) collective-permute-start(bf16[8,1024]{1,0:T(8,128)(2,1)} %param.8), channel_id=1, source_target_pairs={{8,0},{12,4},{16,8},{20,12},{24,16},{28,20},{32,24},{36,28},{40,32... | collective-permute-start | bytes 49160 | tf_op jit(solution)/shard_map/ppermute | solution.py:17
  11.8 1.9 %collective-permute-start = (bf16[8,1024]{1,0:T(8,128)(2,1)}, bf16[8,1024]{1,0:T(8,128)(2,1)S(1)}, u32[]{:S(2)}, u32[]{:S(2)}) collective-permute-start(bf16[8,1024]{1,0:T(8,128)(2,1)} %param.8), channel_id=1, source_target_pairs={{0,8},{4,12},{8,16},{12,20},{16,24},{20,28},{24,32},{28,36},{32,40... | collective-permute-start | bytes 49160 | tf_op jit(solution)/shard_map/ppermute | solution.py:17
  13.8 0.7 %pad_add_fusion = s32[3,1024]{1,0:T(4,128)S(1)} fusion(s32[1,1024]{1,0:T(1,128)} %bitcast.294, s32[1,1024]{1,0:T(1,128)} %bitcast.295, s32[1,1024]{1,0:T(1,128)} %bitcast.296), kind=kLoop, calls=%fused_computation.101 | loop fusion | flops 6144 | bytes 24576 | tf_op jit(solution)/shard_map/stack | solution.py:135
  14.5 0.1 pad_dynamic-slice_fusion
  14.7 0.1 fusion.73
  14.7 0.1 fusion.63
  14.8 0.1 and_and_fusion
  14.9 4.8 %collective-permute-done = bf16[8,1024]{1,0:T(8,128)(2,1)S(1)} collective-permute-done((bf16[8,1024]{1,0:T(8,128)(2,1)}, bf16[8,1024]{1,0:T(8,128)(2,1)S(1)}, u32[]{:S(2)}, u32[]{:S(2)}) %collective-permute-start) | collective-permute-done | bytes 16416 | tf_op jit(solution)/shard_map/ppermute | solution.py:17
  19.8 0.7 %pad_maximum_fusion.1 = bf16[24,1024]{1,0:T(8,128)(2,1)S(1)} fusion(bf16[8,1024]{1,0:T(8,128)(2,1)S(1)} %collective-permute-done.1, bf16[8,1024]{1,0:T(8,128)(2,1)} %param.8, bf16[8,1024]{1,0:T(8,128)(2,1)S(1)} %collective-permute-done), kind=kLoop, calls=%fused_computation.51 | loop fusion | flops 147456 | bytes 98304 | tf_op jit(solution)/shard_map/concatenate | solution.py:119
  20.5 1.9 %collective-permute-start.2 = (bf16[24,1024]{1,0:T(8,128)(2,1)S(1)}, bf16[24,1024]{1,0:T(8,128)(2,1)S(1)}, u32[]{:S(2)}, u32[]{:S(2)}) collective-permute-start(bf16[24,1024]{1,0:T(8,128)(2,1)S(1)} %pad_maximum_fusion.1), channel_id=1, source_target_pairs={{0,4},{4,0},{8,12},{12,8},{16,20},{20,16},{24,28},{28,24},{32,36},... | collective-permute-start | bytes 147464 | tf_op jit(solution)/shard_map/ppermute | solution.py:97
  22.4 0.1 compare_and_fusion
  22.5 1.0 %copy.72 = bf16[1,512,2,128]{3,1,2,0:T(8,128)(2,1)S(1)} copy(bf16[1,512,2,128]{3,2,1,0:T(2,128)(2,1)} %param.11) | data formatting | bytes 524288 | tf_op args[3]
  23.5 1.1 %copy.12 = bf16[8,128,2,128]{3,1,0,2:T(8,128)(2,1)S(1)} copy(bf16[8,128,2,128]{3,2,1,0:T(2,128)(2,1)} %param.10) | data formatting | bytes 1048576 | tf_op args[2]
  24.6 0.0 collective-permute-done.2
  24.7 0.3 fusion.86
  25.0 0.2 fusion.19
  25.3 0.3 fusion.21
  25.6 0.6 fusion.87
  26.2 0.5 fusion.6
  26.8 0.5 fusion.8
  27.3 0.3 fusion.4
  27.6 0.0 copy-start.1
  27.6 0.6 fusion.3
  28.2 0.1 select_bitcast_fusion.1
  28.4 0.1 concatenate.32
  28.5 0.1 concatenate.31
  28.6 0.1 concatenate.30
  28.7 2.4 %collective-permute-start.3 = (f32[24,1040]{1,0:T(8,128)S(1)}, f32[24,1040]{1,0:T(8,128)S(1)}, u32[]{:S(2)}, u32[]{:S(2)}) collective-permute-start(f32[24,1040]{1,0:T(8,128)S(1)} %pad_maximum_fusion), channel_id=1, source_target_pairs={{0,4},{4,0},{8,12},{12,8},{16,20},{20,16},{24,28},{28,24},{32,36},... | collective-permute-start | bytes 299528 | tf_op jit(solution)/shard_map/ppermute | solution.py:97
  31.1 0.9 %collective-permute-done.3 = f32[24,1040]{1,0:T(8,128)S(1)} collective-permute-done((f32[24,1040]{1,0:T(8,128)S(1)}, f32[24,1040]{1,0:T(8,128)S(1)}, u32[]{:S(2)}, u32[]{:S(2)}) %collective-permute-start.3) | collective-permute-done | bytes 99872 | tf_op jit(solution)/shard_map/ppermute | solution.py:97
  32.0 0.1 slice_compare_fusion.4
  32.1 0.1 multiply_add_fusion.1
  32.2 0.1 fusion.46
  32.3 0.1 concatenate.34
  32.4 1.9 %collective-permute-start.4 = (f32[8,1040]{1,0:T(8,128)S(1)}, f32[8,1040]{1,0:T(8,128)S(1)}, u32[]{:S(2)}, u32[]{:S(2)}) collective-permute-start(f32[8,1040]{1,0:T(8,128)S(1)} %concatenate.34), channel_id=1, source_target_pairs={{8,0},{12,4},{16,8},{20,12},{24,16},{28,20},{32,24},{36,28},{40,32... | collective-permute-start | bytes 99848 | tf_op jit(solution)/shard_map/ppermute | solution.py:17
  34.3 0.1 fusion.54
  34.5 0.1 concatenate.35
  34.5 3.9 %collective-permute-start.5 = (f32[8,1040]{1,0:T(8,128)S(1)}, f32[8,1040]{1,0:T(8,128)S(1)}, u32[]{:S(2)}, u32[]{:S(2)}) collective-permute-start(f32[8,1040]{1,0:T(8,128)S(1)} %concatenate.35), channel_id=1, source_target_pairs={{0,8},{4,12},{8,16},{12,20},{16,24},{20,28},{24,32},{28,36},{32,40... | collective-permute-start | bytes 99848 | tf_op jit(solution)/shard_map/ppermute | solution.py:17
  38.5 4.0 %collective-permute-done.5 = f32[8,1040]{1,0:T(8,128)S(1)} collective-permute-done((f32[8,1040]{1,0:T(8,128)S(1)}, f32[8,1040]{1,0:T(8,128)S(1)}, u32[]{:S(2)}, u32[]{:S(2)}) %collective-permute-start.5) | collective-permute-done | bytes 33312 | tf_op jit(solution)/shard_map/ppermute | solution.py:17
  42.5 0.1 maximum_maximum_fusion
  42.6 0.1 multiply_add_fusion
  42.7 0.2 fusion.56
  42.8 0.6 %copy.76 = bf16[1,8,8,128]{3,1,2,0:T(8,128)(2,1)} copy(bf16[1,8,8,128]{3,2,1,0:T(8,128)(2,1)S(1)} %fusion.56) | data formatting | bytes 32768
  43.5 4.2 %shard_map.82 = f32[4,8,512]{2,1,0:T(8,128)} custom-call(bf16[8,1024]{1,0:T(8,128)(2,1)} %bitcast.285, bf16[1024,2048]{1,0:T(8,128)(2,1)} %w_ref.1), custom_call_target="tpu_custom_call" | custom-call | tf_op jit(solution)/shard_map/pallas_call | solution.py:83
  47.7 1.5 %convert_element_type.53 = bf16[4,8,512]{2,1,0:T(8,128)(2,1)} convert(f32[4,8,512]{2,1,0:T(8,128)} %shard_map.82) | non-fusion elementwise | flops 16384 | bytes 98304 | tf_op jit(solution)/shard_map/convert_element_type | solution.py:211
  49.1 4.5 %all-to-all-start = ((bf16[4,8,512]{2,1,0:T(8,128)(2,1)}), bf16[4,8,512]{2,1,0:T(8,128)(2,1)S(1)}, u32[]{:S(2)}, u32[]{:S(2)}) async-start(bf16[4,8,512]{2,1,0:T(8,128)(2,1)} %convert_element_type.53), calls=%async_computation | async-start | bytes 65536 | tf_op jit(solution)/shard_map/all_to_all | solution.py:211
  53.6 5.4 %all-to-all-done = bf16[4,8,512]{2,1,0:T(8,128)(2,1)S(1)} async-done(((bf16[4,8,512]{2,1,0:T(8,128)(2,1)}), bf16[4,8,512]{2,1,0:T(8,128)(2,1)S(1)}, u32[]{:S(2)}, u32[]{:S(2)}) %all-to-all-start) | async-done | bytes 32800 | tf_op jit(solution)/shard_map/all_to_all | solution.py:211
  59.1 0.1 select_reduce_fusion
  59.1 1.3 %fusion.53 = bf16[8,512]{1,0:T(8,128)(2,1)} fusion(f32[8,512]{1,0:T(8,128)S(1)} %select_reduce_fusion, f32[4,8,512]{2,1,0:T(8,128)} %shard_map.82, s32[]{:T(128)S(6)} %select_n.507), kind=kLoop, calls=%fused_computation.103 | loop fusion | flops 8192 | bytes 40964 | tf_op jit(solution)/shard_map/convert_element_type | solution.py:215
  (39 shorter events, 0.3 us)
Async XLA Ops:
  0.0 24.6 %copy-start = (bf16[8,1024]{1,0:T(8,128)(2,1)S(1)}, bf16[8,1024]{1,0:T(8,128)(2,1)}, u32[]{:S(2)}) copy-start(bf16[8,1024]{1,0:T(8,128)(2,1)} %param.8) | copy-start | bytes 49156
  0.0 14.9 %collective-permute-start.1 = (bf16[8,1024]{1,0:T(8,128)(2,1)}, bf16[8,1024]{1,0:T(8,128)(2,1)S(1)}, u32[]{:S(2)}, u32[]{:S(2)}) collective-permute-start(bf16[8,1024]{1,0:T(8,128)(2,1)} %param.8), channel_id=1, source_target_pairs={{8,0},{12,4},{16,8},{20,12},{24,16},{28,20},{32,24},{36,28},{40,32... | collective-permute-start | bytes 49160 | tf_op jit(solution)/shard_map/ppermute | solution.py:17
  11.8 8.0 %collective-permute-start = (bf16[8,1024]{1,0:T(8,128)(2,1)}, bf16[8,1024]{1,0:T(8,128)(2,1)S(1)}, u32[]{:S(2)}, u32[]{:S(2)}) collective-permute-start(bf16[8,1024]{1,0:T(8,128)(2,1)} %param.8), channel_id=1, source_target_pairs={{0,8},{4,12},{8,16},{12,20},{16,24},{20,28},{24,32},{28,36},{32,40... | collective-permute-start | bytes 49160 | tf_op jit(solution)/shard_map/ppermute | solution.py:17
  20.5 4.1 %collective-permute-start.2 = (bf16[24,1024]{1,0:T(8,128)(2,1)S(1)}, bf16[24,1024]{1,0:T(8,128)(2,1)S(1)}, u32[]{:S(2)}, u32[]{:S(2)}) collective-permute-start(bf16[24,1024]{1,0:T(8,128)(2,1)S(1)} %pad_maximum_fusion.1), channel_id=1, source_target_pairs={{0,4},{4,0},{8,12},{12,8},{16,20},{20,16},{24,28},{28,24},{32,36},... | collective-permute-start | bytes 147464 | tf_op jit(solution)/shard_map/ppermute | solution.py:97
  27.6 3.5 %copy-start.1 = (bf16[8,2,128]{2,1,0:T(2,128)(2,1)S(1)}, bf16[8,2,128]{2,1,0:T(2,128)(2,1)}, u32[]{:S(2)}) copy-start(bf16[8,2,128]{2,1,0:T(2,128)(2,1)} %param.9) | copy-start | bytes 12292
  28.7 3.4 %collective-permute-start.3 = (f32[24,1040]{1,0:T(8,128)S(1)}, f32[24,1040]{1,0:T(8,128)S(1)}, u32[]{:S(2)}, u32[]{:S(2)}) collective-permute-start(f32[24,1040]{1,0:T(8,128)S(1)} %pad_maximum_fusion), channel_id=1, source_target_pairs={{0,4},{4,0},{8,12},{12,8},{16,20},{20,16},{24,28},{28,24},{32,36},... | collective-permute-start | bytes 299528 | tf_op jit(solution)/shard_map/ppermute | solution.py:97
  32.4 6.1 %collective-permute-start.4 = (f32[8,1040]{1,0:T(8,128)S(1)}, f32[8,1040]{1,0:T(8,128)S(1)}, u32[]{:S(2)}, u32[]{:S(2)}) collective-permute-start(f32[8,1040]{1,0:T(8,128)S(1)} %concatenate.34), channel_id=1, source_target_pairs={{8,0},{12,4},{16,8},{20,12},{24,16},{28,20},{32,24},{36,28},{40,32... | collective-permute-start | bytes 99848 | tf_op jit(solution)/shard_map/ppermute | solution.py:17
  34.5 8.0 %collective-permute-start.5 = (f32[8,1040]{1,0:T(8,128)S(1)}, f32[8,1040]{1,0:T(8,128)S(1)}, u32[]{:S(2)}, u32[]{:S(2)}) collective-permute-start(f32[8,1040]{1,0:T(8,128)S(1)} %concatenate.35), channel_id=1, source_target_pairs={{0,8},{4,12},{8,16},{12,20},{16,24},{20,28},{24,32},{28,36},{32,40... | collective-permute-start | bytes 99848 | tf_op jit(solution)/shard_map/ppermute | solution.py:17
  49.1 9.9 %all-to-all-start = ((bf16[4,8,512]{2,1,0:T(8,128)(2,1)}), bf16[4,8,512]{2,1,0:T(8,128)(2,1)S(1)}, u32[]{:S(2)}, u32[]{:S(2)}) async-start(bf16[4,8,512]{2,1,0:T(8,128)(2,1)} %convert_element_type.53), calls=%async_computation | async-start | bytes 65536 | tf_op jit(solution)/shard_map/all_to_all | solution.py:211

commit v5 on v4

--- a/solution.py
+++ b/solution.py
@@ -1,7 +1,6 @@
 import jax
 import jax.numpy as jnp
 from jax import lax
-from jax.experimental import pallas as pl
 from jax.sharding import PartitionSpec as P
 
 HD = 128
@@ -71,25 +70,6 @@
     peaks = packed[:, width : width + k * g].reshape(n, k, g)
     totals = packed[:, width + k * g :].reshape(n, k, g)
     return (weighted, peaks, totals)
-
-
-def project_kernel(x_ref, w_ref, o_ref):
-    o_ref[0] = jnp.dot(x_ref[...], w_ref[...], preferred_element_type=jnp.float32)
-
-
-def project(attended, weight, pieces):
-    n, inner = attended.shape
-    width = weight.shape[1] // pieces
-    return pl.pallas_call(
-        project_kernel,
-        grid=(pieces,),
-        in_specs=[
-            pl.BlockSpec((n, inner), lambda j: (0, 0)),
-            pl.BlockSpec((inner, width), lambda j: (0, j)),
-        ],
-        out_specs=pl.BlockSpec((1, n, width), lambda j: (j, 0, 0)),
-        out_shape=jax.ShapeDtypeStruct((pieces, n, width), jnp.float32),
-    )(attended, weight)
 
 
 def swapped(block, axis):
@@ -204,15 +184,23 @@
         .reshape(per_dev, q_heads_local * head_dim)
         .astype(jnp.bfloat16)
     )
+    partial_term = jnp.dot(attended, out_weight, preferred_element_type=jnp.float32)
+
     tp_count = lax.axis_size("tp")
     tp_index = lax.axis_index("tp")
-    chunks = project(attended, out_weight, tp_count)
-
-    got = lax.all_to_all(chunks.astype(jnp.bfloat16), "tp", 0, 0, tiled=True)
-    others = jnp.arange(tp_count, dtype=jnp.int32)[:, None, None] != tp_index
-    mine = lax.dynamic_index_in_dim(chunks, tp_index, axis=0, keepdims=False)
-    total = mine + jnp.sum(jnp.where(others, got.astype(jnp.float32), 0.0), axis=0)
-    return total.astype(jnp.bfloat16)
+    kept = partial_term
+    span = partial_term.shape[1]
+    distance = tp_count // 2
+    while distance >= 1:
+        span //= 2
+        side = (tp_index // distance) % 2
+        mine = lax.dynamic_slice_in_dim(kept, side * span, span, axis=1)
+        other = lax.dynamic_slice_in_dim(kept, (1 - side) * span, span, axis=1)
+        route = [(i, i ^ distance) for i in range(tp_count)]
+        got = lax.ppermute(other.astype(jnp.bfloat16), "tp", route)
+        kept = mine + got.astype(jnp.float32)
+        distance //= 2
+    return kept.astype(jnp.bfloat16)
 
 
 def solution(mesh):

time: 61.1 us -> 59.5 us (0.974)
  Pallas kernels: 4.23 us -> 0 us
  starting transfers between devices: 28.3 us -> 32.4 us
  matrix products: 2.61 us -> 5.46 us
  other arithmetic: 6.26 us -> 4.01 us
  waiting for transfers between devices: 15.2 us -> 13.8 us
    ppermute x0 -> x2, starting transfers between devices: none -> 8.58 us  [local(): got = lax.ppermute(other.astype(jnp.bfloat16), 'tp', route)]
    all_to_all x1 -> x0, waiting for transfers between devices: 5.44 us -> none  [local(): got = lax.all_to_all(chunks.astype(jnp.bfloat16), 'tp', 0, 0, tiled=True)]
    all_to_all x1 -> x0, starting transfers between devices: 4.47 us -> none  [local(): got = lax.all_to_all(chunks.astype(jnp.bfloat16), 'tp', 0, 0, tiled=True)]
    pallas_call x1 -> x0, Pallas kernels: 4.23 us -> none  [project(): pl.pallas_call(project_kernel, grid=(pieces,), in_specs=[pl.BlockSpec((n,...]
    ppermute x0 -> x2, waiting for transfers between devices: none -> 4.05 us  [local(): got = lax.ppermute(other.astype(jnp.bfloat16), 'tp', route)]
    dot_general x0 -> x1, matrix products: none -> 2.84 us  [local(): jnp.dot(attended, out_weight, preferred_element_type=jnp.float32)]
    convert_element_type x2 -> x1, other arithmetic: 2.78 us -> 0.6 us  [local(): return kept.astype(jnp.bfloat16)]
    unnamed x23 -> x22, local copies, waits for them, and re-layouts: 2.86 us -> 2.25 us
  transfers between devices with their start and end apart: 7 -> 8, of which waited for: 4 -> 5; matrix products, arithmetic and copies ran while one was open for 6% -> 6% of each run, Pallas kernels for 0% -> 0%
where the time goes in v5:
time: 59.5 us; the launch traced here: 59 us
  starting transfers between devices  32.4 us (54%)
  waiting for transfers between devices  13.8 us (23%)
  matrix products  5.46 us (9%)
  other arithmetic  4.01 us (7%)
  local copies, waits for them, and re-layouts  2.85 us (5%)
    ppermute x4, starting transfers between devices, shifted(): return lax.ppermute(block, axis, route)  19.5 us
    ppermute x4, waiting for transfers between devices, shifted(): return lax.ppermute(block, axis, route)  8.82 us
    ppermute x2, starting transfers between devices, local(): got = lax.ppermute(other.astype(jnp.bfloat16), 'tp', route)  8.58 us
    ppermute x2, starting transfers between devices, swapped(): return lax.ppermute(block, axis, [(i, i ^ 1) for i in devices])  4.32 us
    ppermute x2, waiting for transfers between devices, local(): got = lax.ppermute(other.astype(jnp.bfloat16), 'tp', route)  4.05 us
    dot_general x1, matrix products, local(): jnp.dot(attended, out_weight, preferred_element_type=jnp.float32)  2.84 us
    unnamed x22, local copies, waits for them, and re-layouts  2.25 us
  transfers between devices with their start and end apart: 8, of which 5 were waited for; matrix products, arithmetic and copies ran while one was open for 6% of the time, Pallas kernels for 0%

profile of v5, /device:TPU:6, one launch (start us, length us, event | category | flops | bytes accessed | tf_op | source)
XLA Modules:
  0.0 59.0 jit_solution(17839400453368770514)
XLA Ops:
  0.0 11.8 %collective-permute-start.1 = (bf16[8,1024]{1,0:T(8,128)(2,1)}, bf16[8,1024]{1,0:T(8,128)(2,1)S(1)}, u32[]{:S(2)}, u32[]{:S(2)}) collective-permute-start(bf16[8,1024]{1,0:T(8,128)(2,1)} %param.8), channel_id=1, source_target_pairs={{8,0},{12,4},{16,8},{20,12},{24,16},{28,20},{32,24},{36,28},{40,32... | collective-permute-start | bytes 49160 | tf_op jit(solution)/shard_map/ppermute | solution.py:16
  11.8 1.9 %collective-permute-start = (bf16[8,1024]{1,0:T(8,128)(2,1)}, bf16[8,1024]{1,0:T(8,128)(2,1)S(1)}, u32[]{:S(2)}, u32[]{:S(2)}) collective-permute-start(bf16[8,1024]{1,0:T(8,128)(2,1)} %param.8), channel_id=1, source_target_pairs={{0,8},{4,12},{8,16},{12,20},{16,24},{20,28},{24,32},{28,36},{32,40... | collective-permute-start | bytes 49160 | tf_op jit(solution)/shard_map/ppermute | solution.py:16
  13.8 0.7 %pad_add_fusion = s32[3,1024]{1,0:T(4,128)S(1)} fusion(s32[1,1024]{1,0:T(1,128)} %bitcast.290, s32[1,1024]{1,0:T(1,128)} %bitcast.291, s32[1,1024]{1,0:T(1,128)} %bitcast.292), kind=kLoop, calls=%fused_computation.104 | loop fusion | flops 6144 | bytes 24576 | tf_op jit(solution)/shard_map/stack | solution.py:115
  14.5 0.1 pad_dynamic-slice_fusion
  14.7 0.1 fusion.75
  14.7 0.1 fusion.65
  14.8 0.1 and_and_fusion
  14.9 4.8 %collective-permute-done = bf16[8,1024]{1,0:T(8,128)(2,1)S(1)} collective-permute-done((bf16[8,1024]{1,0:T(8,128)(2,1)}, bf16[8,1024]{1,0:T(8,128)(2,1)S(1)}, u32[]{:S(2)}, u32[]{:S(2)}) %collective-permute-start) | collective-permute-done | bytes 16416 | tf_op jit(solution)/shard_map/ppermute | solution.py:16
  19.8 0.7 %pad_maximum_fusion.1 = bf16[24,1024]{1,0:T(8,128)(2,1)S(1)} fusion(bf16[8,1024]{1,0:T(8,128)(2,1)S(1)} %collective-permute-done.1, bf16[8,1024]{1,0:T(8,128)(2,1)} %param.8, bf16[8,1024]{1,0:T(8,128)(2,1)S(1)} %collective-permute-done), kind=kLoop, calls=%fused_computation.50 | loop fusion | flops 147456 | bytes 98304 | tf_op jit(solution)/shard_map/concatenate | solution.py:99
  20.5 1.9 %collective-permute-start.2 = (bf16[24,1024]{1,0:T(8,128)(2,1)S(1)}, bf16[24,1024]{1,0:T(8,128)(2,1)S(1)}, u32[]{:S(2)}, u32[]{:S(2)}) collective-permute-start(bf16[24,1024]{1,0:T(8,128)(2,1)S(1)} %pad_maximum_fusion.1), channel_id=1, source_target_pairs={{0,4},{4,0},{8,12},{12,8},{16,20},{20,16},{24,28},{28,24},{32,36},... | collective-permute-start | bytes 147464 | tf_op jit(solution)/shard_map/ppermute | solution.py:77
  22.4 0.1 compare_and_fusion
  22.5 1.0 %copy.75 = bf16[1,512,2,128]{3,1,2,0:T(8,128)(2,1)S(1)} copy(bf16[1,512,2,128]{3,2,1,0:T(2,128)(2,1)} %param.11) | data formatting | bytes 524288 | tf_op args[3]
  23.5 1.1 %copy.12 = bf16[8,128,2,128]{3,1,0,2:T(8,128)(2,1)S(1)} copy(bf16[8,128,2,128]{3,2,1,0:T(2,128)(2,1)} %param.10) | data formatting | bytes 1048576 | tf_op args[2]
  24.6 0.0 collective-permute-done.2
  24.7 0.3 fusion.88
  25.0 0.2 fusion.19
  25.3 0.3 fusion.21
  25.6 0.6 fusion.89
  26.2 0.5 fusion.6
  26.8 0.5 fusion.8
  27.3 0.3 fusion.4
  27.6 0.0 copy-start.1
  27.6 0.6 fusion.3
  28.2 0.1 select_bitcast_fusion.1
  28.4 0.1 concatenate.32
  28.5 0.1 concatenate.31
  28.6 0.1 concatenate.30
  28.7 2.4 %collective-permute-start.3 = (f32[24,1040]{1,0:T(8,128)S(1)}, f32[24,1040]{1,0:T(8,128)S(1)}, u32[]{:S(2)}, u32[]{:S(2)}) collective-permute-start(f32[24,1040]{1,0:T(8,128)S(1)} %pad_maximum_fusion), channel_id=1, source_target_pairs={{0,4},{4,0},{8,12},{12,8},{16,20},{20,16},{24,28},{28,24},{32,36},... | collective-permute-start | bytes 299528 | tf_op jit(solution)/shard_map/ppermute | solution.py:77
  31.1 0.9 %collective-permute-done.3 = f32[24,1040]{1,0:T(8,128)S(1)} collective-permute-done((f32[24,1040]{1,0:T(8,128)S(1)}, f32[24,1040]{1,0:T(8,128)S(1)}, u32[]{:S(2)}, u32[]{:S(2)}) %collective-permute-start.3) | collective-permute-done | bytes 99872 | tf_op jit(solution)/shard_map/ppermute | solution.py:77
  32.0 0.1 slice_compare_fusion.4
  32.1 0.1 multiply_add_fusion.1
  32.2 0.1 fusion.46
  32.3 0.1 concatenate.34
  32.4 1.9 %collective-permute-start.4 = (f32[8,1040]{1,0:T(8,128)S(1)}, f32[8,1040]{1,0:T(8,128)S(1)}, u32[]{:S(2)}, u32[]{:S(2)}) collective-permute-start(f32[8,1040]{1,0:T(8,128)S(1)} %concatenate.34), channel_id=1, source_target_pairs={{8,0},{12,4},{16,8},{20,12},{24,16},{28,20},{32,24},{36,28},{40,32... | collective-permute-start | bytes 99848 | tf_op jit(solution)/shard_map/ppermute | solution.py:16
  34.3 0.1 fusion.56
  34.5 0.1 concatenate.35
  34.5 3.9 %collective-permute-start.5 = (f32[8,1040]{1,0:T(8,128)S(1)}, f32[8,1040]{1,0:T(8,128)S(1)}, u32[]{:S(2)}, u32[]{:S(2)}) collective-permute-start(f32[8,1040]{1,0:T(8,128)S(1)} %concatenate.35), channel_id=1, source_target_pairs={{0,8},{4,12},{8,16},{12,20},{16,24},{20,28},{24,32},{28,36},{32,40... | collective-permute-start | bytes 99848 | tf_op jit(solution)/shard_map/ppermute | solution.py:16
  38.5 0.0 collective-permute-done.4
  38.5 4.0 %collective-permute-done.5 = f32[8,1040]{1,0:T(8,128)S(1)} collective-permute-done((f32[8,1040]{1,0:T(8,128)S(1)}, f32[8,1040]{1,0:T(8,128)S(1)}, u32[]{:S(2)}, u32[]{:S(2)}) %collective-permute-start.5) | collective-permute-done | bytes 33312 | tf_op jit(solution)/shard_map/ppermute | solution.py:16
  42.5 0.1 maximum_maximum_fusion
  42.6 0.1 multiply_add_fusion
  42.7 0.2 fusion.58
  42.8 2.8 %fusion.53 = f32[8,2048]{1,0:T(8,128)S(1)} fusion(bf16[1024,2048]{1,0:T(8,128)(2,1)} %param.12, bf16[1,8,8,128]{3,2,1,0:T(8,128)(2,1)S(1)} %fusion.58), kind=kOutput, calls=%fused_computation.95 | convolution fusion | flops 33554432 | bytes 4276224 | tf_op jit(solution)/shard_map/dot_general | solution.py:187
  45.7 5.1 %collective-permute-start.6 = (bf16[8,1024]{1,0:T(8,128)(2,1)S(1)}, bf16[8,1024]{1,0:T(8,128)(2,1)S(1)}, u32[]{:S(2)}, u32[]{:S(2)}) collective-permute-start(bf16[8,1024]{1,0:T(8,128)(2,1)S(1)} %dynamic-slice_convert_fusion), channel_id=1, source_target_pairs={{0,2},{1,3},{2,0},{3,1},{4,6},{5,7},{6,4},{7,5},{8,10},{9,11},{10,... | collective-permute-start | bytes 49160 | tf_op jit(solution)/shard_map/ppermute | solution.py:200
  50.8 2.0 %collective-permute-done.6 = bf16[8,1024]{1,0:T(8,128)(2,1)S(1)} collective-permute-done((bf16[8,1024]{1,0:T(8,128)(2,1)S(1)}, bf16[8,1024]{1,0:T(8,128)(2,1)S(1)}, u32[]{:S(2)}, u32[]{:S(2)}) %collective-permute-start.6) | collective-permute-done | bytes 16416 | tf_op jit(solution)/shard_map/ppermute | solution.py:200
  52.8 3.5 %collective-permute-start.7 = (bf16[8,512]{1,0:T(8,128)(2,1)S(1)}, bf16[8,512]{1,0:T(8,128)(2,1)S(1)}, u32[]{:S(2)}, u32[]{:S(2)}) collective-permute-start(bf16[8,512]{1,0:T(8,128)(2,1)S(1)} %dynamic-slice_convert_fusion.1), channel_id=1, source_target_pairs={{0,1},{1,0},{2,3},{3,2},{4,5},{5,4},{6,7},{7,6},{8,9},{9,8},{10,11... | collective-permute-start | bytes 24584 | tf_op jit(solution)/shard_map/ppermute | solution.py:200
  56.3 2.0 %collective-permute-done.7 = bf16[8,512]{1,0:T(8,128)(2,1)S(1)} collective-permute-done((bf16[8,512]{1,0:T(8,128)(2,1)S(1)}, bf16[8,512]{1,0:T(8,128)(2,1)S(1)}, u32[]{:S(2)}, u32[]{:S(2)}) %collective-permute-start.7) | collective-permute-done | bytes 8224 | tf_op jit(solution)/shard_map/ppermute | solution.py:200
  58.4 0.6 %add_convert_fusion = bf16[8,512]{1,0:T(8,128)(2,1)} fusion(bf16[8,512]{1,0:T(8,128)(2,1)S(1)} %collective-permute-done.7, f32[8,1024]{1,0:T(8,128)S(1)} %convert_add_fusion, s32[]{:T(128)S(6)} %select_n.528), kind=kLoop, calls=%fused_computation.105 | loop fusion | flops 12288 | bytes 32772 | tf_op jit(solution)/shard_map/convert_element_type | solution.py:203
  (40 shorter events, 0.3 us)
Async XLA Ops:
  0.0 24.6 %copy-start = (bf16[8,1024]{1,0:T(8,128)(2,1)S(1)}, bf16[8,1024]{1,0:T(8,128)(2,1)}, u32[]{:S(2)}) copy-start(bf16[8,1024]{1,0:T(8,128)(2,1)} %param.8) | copy-start | bytes 49156
  0.0 14.9 %collective-permute-start.1 = (bf16[8,1024]{1,0:T(8,128)(2,1)}, bf16[8,1024]{1,0:T(8,128)(2,1)S(1)}, u32[]{:S(2)}, u32[]{:S(2)}) collective-permute-start(bf16[8,1024]{1,0:T(8,128)(2,1)} %param.8), channel_id=1, source_target_pairs={{8,0},{12,4},{16,8},{20,12},{24,16},{28,20},{32,24},{36,28},{40,32... | collective-permute-start | bytes 49160 | tf_op jit(solution)/shard_map/ppermute | solution.py:16
  11.8 8.0 %collective-permute-start = (bf16[8,1024]{1,0:T(8,128)(2,1)}, bf16[8,1024]{1,0:T(8,128)(2,1)S(1)}, u32[]{:S(2)}, u32[]{:S(2)}) collective-permute-start(bf16[8,1024]{1,0:T(8,128)(2,1)} %param.8), channel_id=1, source_target_pairs={{0,8},{4,12},{8,16},{12,20},{16,24},{20,28},{24,32},{28,36},{32,40... | collective-permute-start | bytes 49160 | tf_op jit(solution)/shard_map/ppermute | solution.py:16
  20.5 4.1 %collective-permute-start.2 = (bf16[24,1024]{1,0:T(8,128)(2,1)S(1)}, bf16[24,1024]{1,0:T(8,128)(2,1)S(1)}, u32[]{:S(2)}, u32[]{:S(2)}) collective-permute-start(bf16[24,1024]{1,0:T(8,128)(2,1)S(1)} %pad_maximum_fusion.1), channel_id=1, source_target_pairs={{0,4},{4,0},{8,12},{12,8},{16,20},{20,16},{24,28},{28,24},{32,36},... | collective-permute-start | bytes 147464 | tf_op jit(solution)/shard_map/ppermute | solution.py:77
  27.6 3.5 %copy-start.1 = (bf16[8,2,128]{2,1,0:T(2,128)(2,1)S(1)}, bf16[8,2,128]{2,1,0:T(2,128)(2,1)}, u32[]{:S(2)}) copy-start(bf16[8,2,128]{2,1,0:T(2,128)(2,1)} %param.9) | copy-start | bytes 12292
  28.7 3.4 %collective-permute-start.3 = (f32[24,1040]{1,0:T(8,128)S(1)}, f32[24,1040]{1,0:T(8,128)S(1)}, u32[]{:S(2)}, u32[]{:S(2)}) collective-permute-start(f32[24,1040]{1,0:T(8,128)S(1)} %pad_maximum_fusion), channel_id=1, source_target_pairs={{0,4},{4,0},{8,12},{12,8},{16,20},{20,16},{24,28},{28,24},{32,36},... | collective-permute-start | bytes 299528 | tf_op jit(solution)/shard_map/ppermute | solution.py:77
  32.4 6.1 %collective-permute-start.4 = (f32[8,1040]{1,0:T(8,128)S(1)}, f32[8,1040]{1,0:T(8,128)S(1)}, u32[]{:S(2)}, u32[]{:S(2)}) collective-permute-start(f32[8,1040]{1,0:T(8,128)S(1)} %concatenate.34), channel_id=1, source_target_pairs={{8,0},{12,4},{16,8},{20,12},{24,16},{28,20},{32,24},{36,28},{40,32... | collective-permute-start | bytes 99848 | tf_op jit(solution)/shard_map/ppermute | solution.py:16
  34.5 8.0 %collective-permute-start.5 = (f32[8,1040]{1,0:T(8,128)S(1)}, f32[8,1040]{1,0:T(8,128)S(1)}, u32[]{:S(2)}, u32[]{:S(2)}) collective-permute-start(f32[8,1040]{1,0:T(8,128)S(1)} %concatenate.35), channel_id=1, source_target_pairs={{0,8},{4,12},{8,16},{12,20},{16,24},{20,28},{24,32},{28,36},{32,40... | collective-permute-start | bytes 99848 | tf_op jit(solution)/shard_map/ppermute | solution.py:16
  45.7 7.1 %collective-permute-start.6 = (bf16[8,1024]{1,0:T(8,128)(2,1)S(1)}, bf16[8,1024]{1,0:T(8,128)(2,1)S(1)}, u32[]{:S(2)}, u32[]{:S(2)}) collective-permute-start(bf16[8,1024]{1,0:T(8,128)(2,1)S(1)} %dynamic-slice_convert_fusion), channel_id=1, source_target_pairs={{0,2},{1,3},{2,0},{3,1},{4,6},{5,7},{6,4},{7,5},{8,10},{9,11},{10,... | collective-permute-start | bytes 49160 | tf_op jit(solution)/shard_map/ppermute | solution.py:200
  52.8 5.5 %collective-permute-start.7 = (bf16[8,512]{1,0:T(8,128)(2,1)S(1)}, bf16[8,512]{1,0:T(8,128)(2,1)S(1)}, u32[]{:S(2)}, u32[]{:S(2)}) collective-permute-start(bf16[8,512]{1,0:T(8,128)(2,1)S(1)} %dynamic-slice_convert_fusion.1), channel_id=1, source_target_pairs={{0,1},{1,0},{2,3},{3,2},{4,5},{5,4},{6,7},{7,6},{8,9},{9,8},{10,11... | collective-permute-start | bytes 24584 | tf_op jit(solution)/shard_map/ppermute | solution.py:200

commit v6 on v2

--- a/solution.py
+++ b/solution.py
@@ -72,6 +72,11 @@
     return (weighted, peaks, totals)
 
 
+def swapped(block, axis):
+    devices = range(lax.axis_size(axis))
+    return lax.ppermute(block, axis, [(i, i ^ 1) for i in devices])
+
+
 def local(queries, new_kv, own_kv, prompt_kv, out_weight, parents, own_len, first_beam):
     per_dev = queries.shape[0]
     head_dim = HD
@@ -83,37 +88,75 @@
     req_count = lax.axis_size("req")
     beam_count = per_dev * req_count
     dev_index = lax.axis_index("req")
-    reach_dev = (MOST_BEAMS - 2) // per_dev + 1
-    offsets = list(range(-reach_dev, reach_dev + 1))
+    mate_index = dev_index ^ 1
+    chip = dev_index // 2
     shape4 = (per_dev, kv_heads_local, group_size, head_dim)
-
+    cache_rows = per_dev * own_size
+
+    local_rows = jnp.concatenate(
+        [own_kv.reshape(cache_rows, 2, -1), prompt_kv[0]], axis=0
+    )
+    local_kv = jnp.moveaxis(local_rows, 1, 0)
+    mate_kv = swapped(local_kv, "req")
+
+    from_prev = shifted(queries, "req", -2)
+    from_next = shifted(queries, "req", 2)
+    hood_queries = jnp.concatenate([from_prev, queries, from_next], axis=0)
+    hood_queries = hood_queries.reshape((3 * per_dev,) + shape4[1:])
     query_block = queries.reshape(shape4)
-    hood = [query_block if k == 0 else shifted(query_block, "req", k) for k in offsets]
-    hood_queries = jnp.concatenate(hood, axis=0)
-    hood_count = hood_queries.shape[0]
-    hood_beams = (dev_index - reach_dev) * per_dev + jnp.arange(hood_count, dtype=jnp.int32)
+    hood_count = 3 * per_dev
+    slot_ids = jnp.arange(per_dev, dtype=jnp.int32)
+    hood_beams = jnp.concatenate(
+        [(dev_index + k) * per_dev + slot_ids for k in (-2, 0, 2)]
+    )
     in_range = (hood_beams >= 0) & (hood_beams < beam_count)
-    clipped = jnp.clip(hood_beams, 0, beam_count - 1)
-
-    parent = parents[clipped]
-    lengths = own_len[parent]
-    parent_here = in_range & (parent // per_dev == dev_index)
-    columns = jnp.arange(per_dev * own_size, dtype=jnp.int32)
-    own_allowed = (
-        parent_here[:, None]
-        & (columns[None, :] // own_size == (parent % per_dev)[:, None])
-        & (columns[None, :] % own_size < lengths[:, None])
-    )
-    own_keys = own_kv[:, :, 0].reshape(per_dev * own_size, kv_heads_local, head_dim)
-    own_values = own_kv[:, :, 1].reshape(per_dev * own_size, kv_heads_local, head_dim)
-    own_part = partial_block(hood_queries, own_keys, own_values, own_allowed)
-
-    start = reach_dev * per_dev
-    home_here = in_range[start:] & (first_beam[clipped[start:]] // per_dev == dev_index)
-    prompt_allowed = jnp.broadcast_to(home_here[:, None], (hood_count - start, prompt_size))
-    prompt_keys = prompt_kv[0, :, 0].reshape(prompt_size, kv_heads_local, head_dim)
-    prompt_values = prompt_kv[0, :, 1].reshape(prompt_size, kv_heads_local, head_dim)
-    prompt_part = partial_block(hood_queries[start:], prompt_keys, prompt_values, prompt_allowed)
+    pad = 2 * per_dev
+    index_rows = jnp.pad(jnp.stack([parents, first_beam, own_len]), ((0, 0), (pad, pad)))
+    window = lax.dynamic_slice_in_dim(index_rows, dev_index * per_dev, 5 * per_dev, axis=1)
+    hood_index = jnp.concatenate(
+        [window[:, 0:per_dev], window[:, 2 * per_dev : 3 * per_dev], window[:, 4 * per_dev :]],
+        axis=1,
+    )
+    parent = hood_index[0]
+    home = hood_index[1] // per_dev
+    local_len = window[2, pad : pad + per_dev]
+    mate_len = lax.dynamic_slice_in_dim(
+        window[2], 3 * per_dev - 2 * per_dev * (dev_index % 2), per_dev
+    )
+    parent_dev = parent // per_dev
+    columns = jnp.arange(cache_rows, dtype=jnp.int32)
+    column_slot = columns // own_size
+
+    def own_allowed(holder, lengths):
+        return (
+            (in_range & (parent_dev == holder))[:, None]
+            & (column_slot[None, :] == (parent % per_dev)[:, None])
+            & (columns % own_size < jnp.repeat(lengths, own_size))[None, :]
+        )
+
+    def kv_rows(kv, lo, count):
+        keys = kv[0, lo : lo + count].reshape(count, kv_heads_local, head_dim)
+        values = kv[1, lo : lo + count].reshape(count, kv_heads_local, head_dim)
+        return keys, values
+
+    start = per_dev
+    prompt_queries = hood_queries[start:]
+
+    def prompt_allowed(holder):
+        here = in_range[start:] & (home[start:] == holder)
+        return jnp.broadcast_to(here[:, None], (hood_count - start, prompt_size))
+
+    parts_here = []
+    for kv, holder, lengths in ((local_kv, dev_index, local_len), (mate_kv, mate_index, mate_len)):
+        keys, values = kv_rows(kv, 0, cache_rows)
+        own_part = partial_block(hood_queries, keys, values, own_allowed(holder, lengths))
+        keys, values = kv_rows(kv, cache_rows, prompt_size)
+        prompt_part = partial_block(prompt_queries, keys, values, prompt_allowed(holder))
+        prompt_full = tuple(
+            jnp.concatenate([jnp.zeros_like(x[:start]), x], axis=0) for x in prompt_part
+        )
+        parts_here += [own_part, prompt_full]
+    hood_part = merge_all(parts_here)
 
     fresh_keys = new_kv[:, 0].reshape(per_dev, 1, kv_heads_local, head_dim)
     fresh_values = new_kv[:, 1].reshape(per_dev, 1, kv_heads_local, head_dim)
@@ -126,20 +169,14 @@
         jnp.ones_like(fresh_scores[..., 0]),
     )
 
-    def block_of(part, k, base):
-        lo = (k + reach_dev) * per_dev - base
+    def rows(part, lo):
         return tuple(x[lo : lo + per_dev] for x in part)
 
-    parts = [fresh_part]
-    for k in offsets:
-        own_k = block_of(own_part, k, 0)
-        if k >= 0:
-            own_k = merge_all([own_k, block_of(prompt_part, k, start)])
-        if k == 0:
-            parts.append(own_k)
-        else:
-            parts.append(unpack(shifted(pack(own_k), "req", -k), shape4))
-    weighted, _, totals = merge_all(parts)
+    back_from_next = unpack(shifted(pack(rows(hood_part, 0)), "req", 2), shape4)
+    back_from_prev = unpack(shifted(pack(rows(hood_part, 2 * per_dev)), "req", -2), shape4)
+    weighted, _, totals = merge_all(
+        [fresh_part, rows(hood_part, per_dev), back_from_next, back_from_prev]
+    )
     attended = (
         (weighted / totals[..., None])
         .reshape(per_dev, q_heads_local * head_dim)
@@ -149,13 +186,19 @@
 
     tp_count = lax.axis_size("tp")
     tp_index = lax.axis_index("tp")
-    width = partial_term.shape[1] // tp_count
-    chunks = partial_term.reshape(per_dev, tp_count, width).transpose(1, 0, 2)
-    got = lax.all_to_all(chunks.astype(jnp.bfloat16), "tp", 0, 0, tiled=True)
-    others = jnp.arange(tp_count, dtype=jnp.int32)[:, None, None] != tp_index
-    mine = lax.dynamic_slice_in_dim(partial_term, tp_index * width, width, axis=1)
-    total = mine + jnp.sum(jnp.where(others, got.astype(jnp.float32), 0.0), axis=0)
-    return total.astype(jnp.bfloat16)
+    kept = partial_term
+    span = partial_term.shape[1]
+    distance = tp_count // 2
+    while distance >= 1:
+        span //= 2
+        side = (tp_index // distance) % 2
+        mine = lax.dynamic_slice_in_dim(kept, side * span, span, axis=1)
+        other = lax.dynamic_slice_in_dim(kept, (1 - side) * span, span, axis=1)
+        route = [(i, i ^ distance) for i in range(tp_count)]
+        got = lax.ppermute(other.astype(jnp.bfloat16), "tp", route)
+        kept = mine + got.astype(jnp.float32)
+        distance //= 2
+    return kept.astype(jnp.bfloat16)
 
 
 def solution(mesh):

time: 62.2 us -> 56.3 us (0.905)
  waiting for transfers between devices: 10.7 us -> 5.36 us
  matrix products: 5.84 us -> 10.2 us
  starting transfers between devices: 36 us -> 32.1 us
  local copies, waits for them, and re-layouts: 5.84 us -> 3.56 us
  other arithmetic: 2.92 us -> 4.07 us
    ppermute x0 -> x3, starting transfers between devices: none -> 10.5 us  [the longest x2 8.58 us: local(): got = lax.ppermute(other.astype(jnp.bfloat16), 'tp', route)]
    ppermute x8 -> x4, starting transfers between devices: 31.5 us -> 21.6 us  [shifted(): return lax.ppermute(block, axis, route)]
    all_to_all x1 -> x0, waiting for transfers between devices: 5.44 us -> none  [local(): got = lax.all_to_all(chunks.astype(jnp.bfloat16), 'tp', 0, 0, tiled=True)]
    all_to_all x1 -> x0, starting transfers between devices: 4.47 us -> none  [local(): got = lax.all_to_all(chunks.astype(jnp.bfloat16), 'tp', 0, 0, tiled=True)]
    ppermute x0 -> x3, waiting for transfers between devices: none -> 4.05 us  [the longest x2 4.05 us: local(): got = lax.ppermute(other.astype(jnp.bfloat16), 'tp', route)]
    ppermute x8 -> x4, waiting for transfers between devices: 5.23 us -> 1.31 us  [shifted(): return lax.ppermute(block, axis, route)]
    gather x3 -> x0, local copies, waits for them, and re-layouts: 2.13 us -> none  [the longest x1 0.73 us: local(): lengths = own_len[parent]]
    slice x2 -> x8, local copies, waits for them, and re-layouts: 2.42 us -> 0.5 us  [the longest x6 0.42 us: rows(): return tuple((x[lo:lo + per_dev] for x in part))]
  transfers between devices with their start and end apart: 9 -> 7, of which waited for: 3 -> 3; matrix products, arithmetic and copies ran while one was open for 10% -> 18% of each run, Pallas kernels for 0% -> 0%
where the time goes in v6:
time: 56.3 us; the launch traced here: 55.7 us
  starting transfers between devices  32.1 us (57%)
  matrix products  10.2 us (18%)
  waiting for transfers between devices  5.36 us (10%)
  other arithmetic  4.07 us (7%)
  local copies, waits for them, and re-layouts  3.56 us (6%)
    ppermute x4, starting transfers between devices, shifted(): return lax.ppermute(block, axis, route)  21.6 us
    ppermute x2, starting transfers between devices, local(): got = lax.ppermute(other.astype(jnp.bfloat16), 'tp', route)  8.58 us
    ppermute x2, waiting for transfers between devices, local(): got = lax.ppermute(other.astype(jnp.bfloat16), 'tp', route)  4.05 us
    dot_general x1, matrix products, local(): jnp.dot(attended, out_weight, preferred_element_type=jnp.float32)  2.89 us
    dot_general x4, matrix products, partial_block(): jnp.einsum(formula, low, value_block, preferred_element_type=jnp.float32)  2.68 us
    unnamed x5, local copies, waits for them, and re-layouts  2.14 us
    dot_general x4, matrix products, partial_block(): jnp.einsum('nkgd,skd->nkgs', query_block, key_block, preferred_element_ty...  2.06 us
    ppermute x1, starting transfers between devices, swapped(): return lax.ppermute(block, axis, [(i, i ^ 1) for i in devices])  1.92 us
  transfers between devices with their start and end apart: 7, of which 3 were waited for; matrix products, arithmetic and copies ran while one was open for 18% of the time, Pallas kernels for 0%

profile of v6, /device:TPU:6, one launch (start us, length us, event | category | flops | bytes accessed | tf_op | source)
XLA Modules:
  0.0 55.7 jit_solution(12468675538310351855)
XLA Ops:
  0.0 11.8 %collective-permute-start.1 = (bf16[8,1024]{1,0:T(8,128)(2,1)}, bf16[8,1024]{1,0:T(8,128)(2,1)S(1)}, u32[]{:S(2)}, u32[]{:S(2)}) collective-permute-start(bf16[8,1024]{1,0:T(8,128)(2,1)} %param.8), channel_id=1, source_target_pairs={{8,0},{12,4},{16,8},{20,12},{24,16},{28,20},{32,24},{36,28},{40,32... | collective-permute-start | bytes 49160 | tf_op jit(solution)/shard_map/ppermute | solution.py:16
  11.8 1.9 %collective-permute-start = (bf16[8,1024]{1,0:T(8,128)(2,1)}, bf16[8,1024]{1,0:T(8,128)(2,1)S(1)}, u32[]{:S(2)}, u32[]{:S(2)}) collective-permute-start(bf16[8,1024]{1,0:T(8,128)(2,1)} %param.8), channel_id=1, source_target_pairs={{0,8},{4,12},{8,16},{12,20},{16,24},{20,28},{24,32},{28,36},{32,40... | collective-permute-start | bytes 49160 | tf_op jit(solution)/shard_map/ppermute | solution.py:16
  13.7 1.0 %copy.120 = bf16[1,512,2,128]{3,1,2,0:T(8,128)(2,1)S(1)} copy(bf16[1,512,2,128]{3,2,1,0:T(2,128)(2,1)} %param.11) | data formatting | bytes 524288 | tf_op args[3]
  14.7 1.1 %copy.49 = bf16[8,128,2,128]{3,1,0,2:T(8,128)(2,1)S(1)} copy(bf16[8,128,2,128]{3,2,1,0:T(2,128)(2,1)} %param.10) | data formatting | bytes 1048576 | tf_op args[2]
  15.9 1.9 %collective-permute-start.2 = (bf16[2,1536,128]{2,1,0:T(8,128)(2,1)S(1)}, bf16[2,1536,128]{2,1,0:T(8,128)(2,1)S(1)}, u32[]{:S(2)}, u32[]{:S(2)}) collective-permute-start(bf16[2,1536,128]{2,1,0:T(8,128)(2,1)S(1)} %maximum_bitcast_fusion), channel_id=1, source_target_pairs={{0,4},{4,0},{8,12},{12,8},{16,20},{20,16},{24,28},{28,24},{32,36},... | collective-permute-start | bytes 2359304 | tf_op jit(solution)/shard_map/ppermute | solution.py:77
  17.9 0.7 %pad_add_fusion = s32[3,1024]{1,0:T(4,128)S(1)} fusion(s32[1,1024]{1,0:T(1,128)} %bitcast.345, s32[1,1024]{1,0:T(1,128)} %bitcast.346, s32[1,1024]{1,0:T(1,128)} %bitcast.347), kind=kLoop, calls=%fused_computation.116 | loop fusion | flops 6144 | bytes 24576 | tf_op jit(solution)/shard_map/stack | solution.py:114
  18.6 0.1 pad_dynamic-slice_fusion
  18.9 0.8 %slice_convert_fusion = (f32[8,1,128]{2,1,0:T(1,128)S(1)}, bf16[8,1,128]{2,1,0:T(2,128)(2,1)S(1)}) fusion(bf16[8,2,128]{2,1,0:T(2,128)(2,1)} %param.9), kind=kLoop, calls=%fused_computation.169 | loop fusion | flops 1024 | bytes 10240 | tf_op jit(solution)/shard_map/convert_element_type | solution.py:167
  19.7 0.1 pad_add_fusion.1
  19.7 0.1 compare_and_fusion.3
  19.8 0.8 %fusion.94 = f32[8,1,8]{2,1,0:T(1,128)S(1)} fusion(bf16[8,8,128]{2,0,1:T(8,128)(2,1)} %bitcast.352, bf16[8,128,1]{1,0,2:T(8,128)(2,1)S(1)} %bitcast.351), kind=kOutput, calls=%fused_computation.126 | convolution fusion | flops 16384 | bytes 18688 | tf_op jit(solution)/shard_map/nkgd,nskd->nkgs/dot_general | solution.py:163
  20.7 0.1 fusion.102
  20.8 0.1 fusion.70
  20.9 0.1 compare_and_fusion.2
  21.0 1.0 %fusion.134 = (f32[16,8]{0,1:T(8,128)S(1)}, f32[16,1,8,512]{3,0,2,1:T(8,128)S(1)}) fusion(bf16[2,1536,128]{2,1,0:T(8,128)(2,1)S(1)} %maximum_bitcast_fusion, pred[16]{0:T(512)(128)(4,1)S(1)} %get-tuple-element.42, bf16[8,1024]{1,0:T(8,128)(2,1)S(1)} %collective-permute-done.1, bf16[8,1024]{1,0:T(8,128)(2,1)} %param.8), kind=kOutput, calls=%fused_computation.224 | convolution fusion | flops 17039232 | bytes 427008 | tf_op jit(solution)/shard_map/nkgd,skd->nkgs/dot_general | solution.py:27
  22.0 0.2 fusion.51
  22.3 0.9 %fusion.20 = f32[16,1,8,128]{3,0,2,1:T(8,128)} fusion(f32[128,16,8]{0,1,2:T(8,128)S(1)} %fusion.51, f32[16,1,8,512]{3,0,2,1:T(8,128)S(1)} %get-tuple-element.50, f32[16,8]{0,1:T(8,128)S(1)} %get-tuple-element.49, pred[16]{0:T(512)(128)(4,1)S(1)} %get-tuple-element.42, bf16[2,1536,128]{2,1,0:T(8,128)(2,1)S(1)} %maximum_bitcast_fusion), kind=kOutput, calls=%fused_computation.28 | convolution fusion | flops 17186816 | bytes 528896 | tf_op jit(solution)/shard_map/nkgs,skd->nkgd/dot_general | solution.py:40
  23.1 0.2 fusion.46
  23.3 0.4 fusion.132
  23.7 0.3 fusion.22
  24.0 1.0 %fusion.27 = f32[128,24,8]{0,1,2:T(8,128)} fusion(f32[24,1,8,1024]{3,0,2,1:T(8,128)S(1)} %get-tuple-element.46, f32[24,8]{0,1:T(8,128)S(1)} %get-tuple-element.45, pred[24,1024]{1,0:T(8,128)(4,1)S(1)} %get-tuple-element.27, bf16[2,1536,128]{2,1,0:T(8,128)(2,1)S(1)} %maximum_bitcast_fusion), kind=kOutput, calls=%fused_computation.40 | convolution fusion | flops 50921472 | bytes 1175552 | tf_op jit(solution)/shard_map/nkgs,skd->nkgd/dot_general | solution.py:38
  25.0 0.3 fusion.133
  25.3 0.2 fusion.48
  25.5 0.4 fusion.131
  25.9 0.3 fusion.24
  26.2 0.1 fusion.108
  26.3 0.1 fusion.115
  26.7 1.2 %fusion.18 = f32[24,1,8,128]{3,0,2,1:T(8,128)S(1)} fusion(f32[128,24,8]{0,1,2:T(8,128)} %fusion.27, f32[24,1,8,1024]{3,0,2,1:T(8,128)S(1)} %get-tuple-element.46, f32[24,8]{0,1:T(8,128)S(1)} %get-tuple-element.45, pred[24,1024]{1,0:T(8,128)(4,1)S(1)} %get-tuple-element.27, bf16[2,1536,128]{2,1,0:T(8,128)(2,1)S(1)} %maximum_bitcast_fusion, ...), kind=kOutput, calls=%fused_computation.24 | convolution fusion | flops 51609600 | bytes 1347584 | tf_op jit(solution)/shard_map/nkgs,skd->nkgd/dot_general | solution.py:40
  27.9 0.2 fusion.63
  28.1 0.3 fusion.39
  28.5 0.2 fusion.19
  28.7 0.3 fusion.14
  29.1 0.1 concatenate.63
  29.2 1.9 %collective-permute-start.4 = (f32[8,1040]{1,0:T(8,128)S(1)}, f32[8,1040]{1,0:T(8,128)S(1)}, u32[]{:S(2)}, u32[]{:S(2)}) collective-permute-start(f32[8,1040]{1,0:T(8,128)S(1)} %concatenate.63), channel_id=1, source_target_pairs={{0,8},{4,12},{8,16},{12,20},{16,24},{20,28},{24,32},{28,36},{32,40... | collective-permute-start | bytes 99848 | tf_op jit(solution)/shard_map/ppermute | solution.py:16
  31.3 0.1 concatenate.62
  31.4 6.0 %collective-permute-start.3 = (f32[8,1040]{1,0:T(8,128)S(1)}, f32[8,1040]{1,0:T(8,128)S(1)}, u32[]{:S(2)}, u32[]{:S(2)}) collective-permute-start(f32[8,1040]{1,0:T(8,128)S(1)} %concatenate.62), channel_id=1, source_target_pairs={{8,0},{12,4},{16,8},{20,12},{24,16},{28,20},{32,24},{36,28},{40,32... | collective-permute-start | bytes 99848 | tf_op jit(solution)/shard_map/ppermute | solution.py:16
  37.5 0.1 fusion.105
  37.6 0.1 copy.72
  37.8 1.3 %collective-permute-done.3 = f32[8,1040]{1,0:T(8,128)S(1)} collective-permute-done((f32[8,1040]{1,0:T(8,128)S(1)}, f32[8,1040]{1,0:T(8,128)S(1)}, u32[]{:S(2)}, u32[]{:S(2)}) %collective-permute-start.3) | collective-permute-done | bytes 33312 | tf_op jit(solution)/shard_map/ppermute | solution.py:16
  39.2 0.1 copy.68
  39.4 0.1 fusion.111
  39.4 0.1 fusion.119
  39.5 2.9 %fusion.86 = f32[8,2048]{1,0:T(8,128)S(1)} fusion(bf16[1024,2048]{1,0:T(8,128)(2,1)} %param.12, f32[8,1040]{1,0:T(8,128)S(1)} %collective-permute-done.4, f32[8,1040]{1,0:T(8,128)S(1)} %collective-permute-done.3, f32[24,1,8,128]{3,0,2,1:T(8,128)S(1)} %fusion.14, f32[8,8]{0,1:T(8,128)S(1)} %get-tuple-element.23, f32[8,8]{0,1:T(8,128)S(1)} %get-tuple-element.24, ...), kind=kOutput, calls=%fused_computation.117 | convolution fusion | flops 33628160 | bytes 4382720 | tf_op jit(solution)/shard_map/dot_general | solution.py:185
  42.4 5.1 %collective-permute-start.5 = (bf16[8,1024]{1,0:T(8,128)(2,1)S(1)}, bf16[8,1024]{1,0:T(8,128)(2,1)S(1)}, u32[]{:S(2)}, u32[]{:S(2)}) collective-permute-start(bf16[8,1024]{1,0:T(8,128)(2,1)S(1)} %dynamic-slice_convert_fusion), channel_id=1, source_target_pairs={{0,2},{1,3},{2,0},{3,1},{4,6},{5,7},{6,4},{7,5},{8,10},{9,11},{10,... | collective-permute-start | bytes 49160 | tf_op jit(solution)/shard_map/ppermute | solution.py:198
  47.5 2.0 %collective-permute-done.5 = bf16[8,1024]{1,0:T(8,128)(2,1)S(1)} collective-permute-done((bf16[8,1024]{1,0:T(8,128)(2,1)S(1)}, bf16[8,1024]{1,0:T(8,128)(2,1)S(1)}, u32[]{:S(2)}, u32[]{:S(2)}) %collective-permute-start.5) | collective-permute-done | bytes 16416 | tf_op jit(solution)/shard_map/ppermute | solution.py:198
  49.6 3.5 %collective-permute-start.6 = (bf16[8,512]{1,0:T(8,128)(2,1)S(1)}, bf16[8,512]{1,0:T(8,128)(2,1)S(1)}, u32[]{:S(2)}, u32[]{:S(2)}) collective-permute-start(bf16[8,512]{1,0:T(8,128)(2,1)S(1)} %dynamic-slice_convert_fusion.1), channel_id=1, source_target_pairs={{0,1},{1,0},{2,3},{3,2},{4,5},{5,4},{6,7},{7,6},{8,9},{9,8},{10,11... | collective-permute-start | bytes 24584 | tf_op jit(solution)/shard_map/ppermute | solution.py:198
  53.1 2.0 %collective-permute-done.6 = bf16[8,512]{1,0:T(8,128)(2,1)S(1)} collective-permute-done((bf16[8,512]{1,0:T(8,128)(2,1)S(1)}, bf16[8,512]{1,0:T(8,128)(2,1)S(1)}, u32[]{:S(2)}, u32[]{:S(2)}) %collective-permute-start.6) | collective-permute-done | bytes 8224 | tf_op jit(solution)/shard_map/ppermute | solution.py:198
  55.1 0.6 %add_convert_fusion = bf16[8,512]{1,0:T(8,128)(2,1)} fusion(bf16[8,512]{1,0:T(8,128)(2,1)S(1)} %collective-permute-done.6, f32[8,1024]{1,0:T(8,128)S(1)} %convert_add_fusion, s32[]{:T(128)S(6)} %select_n.230), kind=kLoop, calls=%fused_computation.119 | loop fusion | flops 12288 | bytes 32772 | tf_op jit(solution)/shard_map/convert_element_type | solution.py:201
  (35 shorter events, 1.2 us)
Async XLA Ops:
  0.0 23.3 %copy-start = (bf16[8,1024]{1,0:T(8,128)(2,1)S(1)}, bf16[8,1024]{1,0:T(8,128)(2,1)}, u32[]{:S(2)}) copy-start(bf16[8,1024]{1,0:T(8,128)(2,1)} %param.8) | copy-start | bytes 49156
  0.0 21.0 %collective-permute-start.1 = (bf16[8,1024]{1,0:T(8,128)(2,1)}, bf16[8,1024]{1,0:T(8,128)(2,1)S(1)}, u32[]{:S(2)}, u32[]{:S(2)}) collective-permute-start(bf16[8,1024]{1,0:T(8,128)(2,1)} %param.8), channel_id=1, source_target_pairs={{8,0},{12,4},{16,8},{20,12},{24,16},{28,20},{32,24},{36,28},{40,32... | collective-permute-start | bytes 49160 | tf_op jit(solution)/shard_map/ppermute | solution.py:16
  11.8 11.5 %collective-permute-start = (bf16[8,1024]{1,0:T(8,128)(2,1)}, bf16[8,1024]{1,0:T(8,128)(2,1)S(1)}, u32[]{:S(2)}, u32[]{:S(2)}) collective-permute-start(bf16[8,1024]{1,0:T(8,128)(2,1)} %param.8), channel_id=1, source_target_pairs={{0,8},{4,12},{8,16},{12,20},{16,24},{20,28},{24,32},{28,36},{32,40... | collective-permute-start | bytes 49160 | tf_op jit(solution)/shard_map/ppermute | solution.py:16
  15.9 9.1 %collective-permute-start.2 = (bf16[2,1536,128]{2,1,0:T(8,128)(2,1)S(1)}, bf16[2,1536,128]{2,1,0:T(8,128)(2,1)S(1)}, u32[]{:S(2)}, u32[]{:S(2)}) collective-permute-start(bf16[2,1536,128]{2,1,0:T(8,128)(2,1)S(1)} %maximum_bitcast_fusion), channel_id=1, source_target_pairs={{0,4},{4,0},{8,12},{12,8},{16,20},{20,16},{24,28},{28,24},{32,36},... | collective-permute-start | bytes 2359304 | tf_op jit(solution)/shard_map/ppermute | solution.py:77
  29.2 8.3 %collective-permute-start.4 = (f32[8,1040]{1,0:T(8,128)S(1)}, f32[8,1040]{1,0:T(8,128)S(1)}, u32[]{:S(2)}, u32[]{:S(2)}) collective-permute-start(f32[8,1040]{1,0:T(8,128)S(1)} %concatenate.63), channel_id=1, source_target_pairs={{0,8},{4,12},{8,16},{12,20},{16,24},{20,28},{24,32},{28,36},{32,40... | collective-permute-start | bytes 99848 | tf_op jit(solution)/shard_map/ppermute | solution.py:16
  31.4 7.6 %collective-permute-start.3 = (f32[8,1040]{1,0:T(8,128)S(1)}, f32[8,1040]{1,0:T(8,128)S(1)}, u32[]{:S(2)}, u32[]{:S(2)}) collective-permute-start(f32[8,1040]{1,0:T(8,128)S(1)} %concatenate.62), channel_id=1, source_target_pairs={{8,0},{12,4},{16,8},{20,12},{24,16},{28,20},{32,24},{36,28},{40,32... | collective-permute-start | bytes 99848 | tf_op jit(solution)/shard_map/ppermute | solution.py:16
  42.4 7.1 %collective-permute-start.5 = (bf16[8,1024]{1,0:T(8,128)(2,1)S(1)}, bf16[8,1024]{1,0:T(8,128)(2,1)S(1)}, u32[]{:S(2)}, u32[]{:S(2)}) collective-permute-start(bf16[8,1024]{1,0:T(8,128)(2,1)S(1)} %dynamic-slice_convert_fusion), channel_id=1, source_target_pairs={{0,2},{1,3},{2,0},{3,1},{4,6},{5,7},{6,4},{7,5},{8,10},{9,11},{10,... | collective-permute-start | bytes 49160 | tf_op jit(solution)/shard_map/ppermute | solution.py:198
  49.6 5.5 %collective-permute-start.6 = (bf16[8,512]{1,0:T(8,128)(2,1)S(1)}, bf16[8,512]{1,0:T(8,128)(2,1)S(1)}, u32[]{:S(2)}, u32[]{:S(2)}) collective-permute-start(bf16[8,512]{1,0:T(8,128)(2,1)S(1)} %dynamic-slice_convert_fusion.1), channel_id=1, source_target_pairs={{0,1},{1,0},{2,3},{3,2},{4,5},{5,4},{6,7},{7,6},{8,9},{9,8},{10,11... | collective-permute-start | bytes 24584 | tf_op jit(solution)/shard_map/ppermute | solution.py:198

commit v7 on v6

--- a/solution.py
+++ b/solution.py
@@ -186,19 +186,13 @@
 
     tp_count = lax.axis_size("tp")
     tp_index = lax.axis_index("tp")
-    kept = partial_term
-    span = partial_term.shape[1]
-    distance = tp_count // 2
-    while distance >= 1:
-        span //= 2
-        side = (tp_index // distance) % 2
-        mine = lax.dynamic_slice_in_dim(kept, side * span, span, axis=1)
-        other = lax.dynamic_slice_in_dim(kept, (1 - side) * span, span, axis=1)
-        route = [(i, i ^ distance) for i in range(tp_count)]
-        got = lax.ppermute(other.astype(jnp.bfloat16), "tp", route)
-        kept = mine + got.astype(jnp.float32)
-        distance //= 2
-    return kept.astype(jnp.bfloat16)
+    width = partial_term.shape[1] // tp_count
+    chunks = partial_term.reshape(per_dev, tp_count, width).transpose(1, 0, 2)
+    got = lax.all_to_all(chunks.astype(jnp.bfloat16), "tp", 0, 0, tiled=True)
+    others = jnp.arange(tp_count, dtype=jnp.int32)[:, None, None] != tp_index
+    mine = lax.dynamic_slice_in_dim(partial_term, tp_index * width, width, axis=1)
+    total = mine + jnp.sum(jnp.where(others, got.astype(jnp.float32), 0.0), axis=0)
+    return total.astype(jnp.bfloat16)
 
 
 def solution(mesh):

time: 56.3 us -> 54.2 us (0.963)
  starting transfers between devices: 32.1 us -> 28 us
  waiting for transfers between devices: 5.36 us -> 6.76 us
  matrix products: 10.2 us -> 10.9 us
    ppermute x2 -> x0, starting transfers between devices: 8.58 us -> none  [local(): got = lax.ppermute(other.astype(jnp.bfloat16), 'tp', route)]
    all_to_all x0 -> x1, waiting for transfers between devices: none -> 5.44 us  [local(): got = lax.all_to_all(chunks.astype(jnp.bfloat16), 'tp', 0, 0, tiled=True)]
    all_to_all x0 -> x1, starting transfers between devices: none -> 4.46 us  [local(): got = lax.all_to_all(chunks.astype(jnp.bfloat16), 'tp', 0, 0, tiled=True)]
    ppermute x2 -> x0, waiting for transfers between devices: 4.05 us -> none  [local(): got = lax.ppermute(other.astype(jnp.bfloat16), 'tp', route)]
    dot_general x1, matrix products: 2.89 us -> 3.51 us  [local(): jnp.dot(attended, out_weight, preferred_element_type=jnp.float32)]
  transfers between devices with their start and end apart: 7 -> 6, of which waited for: 3 -> 2; matrix products, arithmetic and copies ran while one was open for 18% -> 18% of each run, Pallas kernels for 0% -> 0%
where the time goes in v7:
time: 54.2 us; the launch traced here: 53.6 us
  starting transfers between devices  28 us (52%)
  matrix products  10.9 us (20%)
  waiting for transfers between devices  6.76 us (12%)
  other arithmetic  4.15 us (8%)
  local copies, waits for them, and re-layouts  3.54 us (7%)
    ppermute x4, starting transfers between devices, shifted(): return lax.ppermute(block, axis, route)  21.6 us
    all_to_all x1, waiting for transfers between devices, local(): got = lax.all_to_all(chunks.astype(jnp.bfloat16), 'tp', 0, 0, tiled=True)  5.44 us
    all_to_all x1, starting transfers between devices, local(): got = lax.all_to_all(chunks.astype(jnp.bfloat16), 'tp', 0, 0, tiled=True)  4.46 us
    dot_general x1, matrix products, local(): jnp.dot(attended, out_weight, preferred_element_type=jnp.float32)  3.51 us
    dot_general x4, matrix products, partial_block(): jnp.einsum(formula, low, value_block, preferred_element_type=jnp.float32)  2.68 us
    unnamed x5, local copies, waits for them, and re-layouts  2.13 us
    dot_general x4, matrix products, partial_block(): jnp.einsum('nkgd,skd->nkgs', query_block, key_block, preferred_element_ty...  2.06 us
    ppermute x1, starting transfers between devices, swapped(): return lax.ppermute(block, axis, [(i, i ^ 1) for i in devices])  1.92 us
  transfers between devices with their start and end apart: 6, of which 2 were waited for; matrix products, arithmetic and copies ran while one was open for 18% of the time, Pallas kernels for 0%

profile of v7, /device:TPU:6, one launch (start us, length us, event | category | flops | bytes accessed | tf_op | source)
XLA Modules:
  0.0 53.6 jit_solution(8719387537516685461)
XLA Ops:
  0.0 11.8 %collective-permute-start.1 = (bf16[8,1024]{1,0:T(8,128)(2,1)}, bf16[8,1024]{1,0:T(8,128)(2,1)S(1)}, u32[]{:S(2)}, u32[]{:S(2)}) collective-permute-start(bf16[8,1024]{1,0:T(8,128)(2,1)} %param.8), channel_id=1, source_target_pairs={{8,0},{12,4},{16,8},{20,12},{24,16},{28,20},{32,24},{36,28},{40,32... | collective-permute-start | bytes 49160 | tf_op jit(solution)/shard_map/ppermute | solution.py:16
  11.8 1.9 %collective-permute-start = (bf16[8,1024]{1,0:T(8,128)(2,1)}, bf16[8,1024]{1,0:T(8,128)(2,1)S(1)}, u32[]{:S(2)}, u32[]{:S(2)}) collective-permute-start(bf16[8,1024]{1,0:T(8,128)(2,1)} %param.8), channel_id=1, source_target_pairs={{0,8},{4,12},{8,16},{12,20},{16,24},{20,28},{24,32},{28,36},{32,40... | collective-permute-start | bytes 49160 | tf_op jit(solution)/shard_map/ppermute | solution.py:16
  13.7 1.0 %copy.120 = bf16[1,512,2,128]{3,1,2,0:T(8,128)(2,1)S(1)} copy(bf16[1,512,2,128]{3,2,1,0:T(2,128)(2,1)} %param.11) | data formatting | bytes 524288 | tf_op args[3]
  14.7 1.1 %copy.49 = bf16[8,128,2,128]{3,1,0,2:T(8,128)(2,1)S(1)} copy(bf16[8,128,2,128]{3,2,1,0:T(2,128)(2,1)} %param.10) | data formatting | bytes 1048576 | tf_op args[2]
  15.9 1.9 %collective-permute-start.2 = (bf16[2,1536,128]{2,1,0:T(8,128)(2,1)S(1)}, bf16[2,1536,128]{2,1,0:T(8,128)(2,1)S(1)}, u32[]{:S(2)}, u32[]{:S(2)}) collective-permute-start(bf16[2,1536,128]{2,1,0:T(8,128)(2,1)S(1)} %maximum_bitcast_fusion), channel_id=1, source_target_pairs={{0,4},{4,0},{8,12},{12,8},{16,20},{20,16},{24,28},{28,24},{32,36},... | collective-permute-start | bytes 2359304 | tf_op jit(solution)/shard_map/ppermute | solution.py:77
  17.9 0.7 %pad_add_fusion = s32[3,1024]{1,0:T(4,128)S(1)} fusion(s32[1,1024]{1,0:T(1,128)} %bitcast.354, s32[1,1024]{1,0:T(1,128)} %bitcast.355, s32[1,1024]{1,0:T(1,128)} %bitcast.356), kind=kLoop, calls=%fused_computation.115 | loop fusion | flops 6144 | bytes 24576 | tf_op jit(solution)/shard_map/stack | solution.py:114
  18.6 0.1 pad_dynamic-slice_fusion
  18.9 0.8 %slice_convert_fusion = (f32[8,1,128]{2,1,0:T(1,128)S(1)}, bf16[8,1,128]{2,1,0:T(2,128)(2,1)S(1)}) fusion(bf16[8,2,128]{2,1,0:T(2,128)(2,1)} %param.9), kind=kLoop, calls=%fused_computation.167 | loop fusion | flops 1024 | bytes 10240 | tf_op jit(solution)/shard_map/convert_element_type | solution.py:167
  19.7 0.1 pad_add_fusion.1
  19.7 0.1 compare_and_fusion.3
  19.8 0.8 %fusion.94 = f32[8,1,8]{2,1,0:T(1,128)S(1)} fusion(bf16[8,8,128]{2,0,1:T(8,128)(2,1)} %bitcast.361, bf16[8,128,1]{1,0,2:T(8,128)(2,1)S(1)} %bitcast.360), kind=kOutput, calls=%fused_computation.124 | convolution fusion | flops 16384 | bytes 18688 | tf_op jit(solution)/shard_map/nkgd,nskd->nkgs/dot_general | solution.py:163
  20.7 0.1 fusion.102
  20.8 0.1 fusion.70
  20.9 0.1 compare_and_fusion.2
  21.0 1.0 %fusion.134 = (f32[16,8]{0,1:T(8,128)S(1)}, f32[16,1,8,512]{3,0,2,1:T(8,128)S(1)}) fusion(bf16[2,1536,128]{2,1,0:T(8,128)(2,1)S(1)} %maximum_bitcast_fusion, pred[16]{0:T(512)(128)(4,1)S(1)} %get-tuple-element.42, bf16[8,1024]{1,0:T(8,128)(2,1)S(1)} %collective-permute-done.1, bf16[8,1024]{1,0:T(8,128)(2,1)} %param.8), kind=kOutput, calls=%fused_computation.223 | convolution fusion | flops 17039232 | bytes 427008 | tf_op jit(solution)/shard_map/nkgd,skd->nkgs/dot_general | solution.py:27
  22.0 0.2 fusion.51
  22.3 0.9 %fusion.20 = f32[16,1,8,128]{3,0,2,1:T(8,128)} fusion(f32[128,16,8]{0,1,2:T(8,128)S(1)} %fusion.51, f32[16,1,8,512]{3,0,2,1:T(8,128)S(1)} %get-tuple-element.50, f32[16,8]{0,1:T(8,128)S(1)} %get-tuple-element.49, pred[16]{0:T(512)(128)(4,1)S(1)} %get-tuple-element.42, bf16[2,1536,128]{2,1,0:T(8,128)(2,1)S(1)} %maximum_bitcast_fusion), kind=kOutput, calls=%fused_computation.28 | convolution fusion | flops 17186816 | bytes 528896 | tf_op jit(solution)/shard_map/nkgs,skd->nkgd/dot_general | solution.py:40
  23.1 0.2 fusion.46
  23.3 0.4 fusion.132
  23.8 0.3 fusion.22
  24.1 1.0 %fusion.27 = f32[128,24,8]{0,1,2:T(8,128)} fusion(f32[24,1,8,1024]{3,0,2,1:T(8,128)S(1)} %get-tuple-element.46, f32[24,8]{0,1:T(8,128)S(1)} %get-tuple-element.45, pred[24,1024]{1,0:T(8,128)(4,1)S(1)} %get-tuple-element.27, bf16[2,1536,128]{2,1,0:T(8,128)(2,1)S(1)} %maximum_bitcast_fusion), kind=kOutput, calls=%fused_computation.40 | convolution fusion | flops 50921472 | bytes 1175552 | tf_op jit(solution)/shard_map/nkgs,skd->nkgd/dot_general | solution.py:38
  25.0 0.3 fusion.133
  25.3 0.2 fusion.48
  25.5 0.4 fusion.131
  25.9 0.3 fusion.24
  26.2 0.1 fusion.108
  26.3 0.1 fusion.115
  26.7 1.2 %fusion.18 = f32[24,1,8,128]{3,0,2,1:T(8,128)S(1)} fusion(f32[128,24,8]{0,1,2:T(8,128)} %fusion.27, f32[24,1,8,1024]{3,0,2,1:T(8,128)S(1)} %get-tuple-element.46, f32[24,8]{0,1:T(8,128)S(1)} %get-tuple-element.45, pred[24,1024]{1,0:T(8,128)(4,1)S(1)} %get-tuple-element.27, bf16[2,1536,128]{2,1,0:T(8,128)(2,1)S(1)} %maximum_bitcast_fusion, ...), kind=kOutput, calls=%fused_computation.24 | convolution fusion | flops 51609600 | bytes 1347584 | tf_op jit(solution)/shard_map/nkgs,skd->nkgd/dot_general | solution.py:40
  27.9 0.2 fusion.63
  28.1 0.3 fusion.39
  28.5 0.2 fusion.19
  28.7 0.3 fusion.14
  29.1 0.1 concatenate.63
  29.2 1.9 %collective-permute-start.4 = (f32[8,1040]{1,0:T(8,128)S(1)}, f32[8,1040]{1,0:T(8,128)S(1)}, u32[]{:S(2)}, u32[]{:S(2)}) collective-permute-start(f32[8,1040]{1,0:T(8,128)S(1)} %concatenate.63), channel_id=1, source_target_pairs={{0,8},{4,12},{8,16},{12,20},{16,24},{20,28},{24,32},{28,36},{32,40... | collective-permute-start | bytes 99848 | tf_op jit(solution)/shard_map/ppermute | solution.py:16
  31.3 0.1 concatenate.62
  31.4 6.0 %collective-permute-start.3 = (f32[8,1040]{1,0:T(8,128)S(1)}, f32[8,1040]{1,0:T(8,128)S(1)}, u32[]{:S(2)}, u32[]{:S(2)}) collective-permute-start(f32[8,1040]{1,0:T(8,128)S(1)} %concatenate.62), channel_id=1, source_target_pairs={{8,0},{12,4},{16,8},{20,12},{24,16},{28,20},{32,24},{36,28},{40,32... | collective-permute-start | bytes 99848 | tf_op jit(solution)/shard_map/ppermute | solution.py:16
  37.4 0.1 fusion.105
  37.6 0.1 copy.72
  37.7 1.3 %collective-permute-done.3 = f32[8,1040]{1,0:T(8,128)S(1)} collective-permute-done((f32[8,1040]{1,0:T(8,128)S(1)}, f32[8,1040]{1,0:T(8,128)S(1)}, u32[]{:S(2)}, u32[]{:S(2)}) %collective-permute-start.3) | collective-permute-done | bytes 33312 | tf_op jit(solution)/shard_map/ppermute | solution.py:16
  39.0 0.1 fusion.106
  39.2 0.1 copy.68
  39.3 0.1 fusion.111
  39.4 0.1 fusion.119
  39.5 3.5 %fusion.135 = (bf16[8,2048]{1,0:T(8,128)(2,1)}, f32[8,2048]{1,0:T(8,128)S(1)}) fusion(bf16[1024,2048]{1,0:T(8,128)(2,1)} %param.12, f32[8,8]{0,1:T(8,128)S(1)} %get-tuple-element.23, f32[8,1040]{1,0:T(8,128)S(1)} %collective-permute-done.4, f32[8,1040]{1,0:T(8,128)S(1)} %collective-permute-done.3, f32[24,1,8,128]{3,0,2,1:T(8,128)S(1)} %fusion.14, ...), kind=kOutput, calls=%fused_computation.224 | convolution fusion | flops 33644544 | bytes 4415488 | tf_op jit(solution)/shard_map/dot_general | solution.py:185
  43.0 4.5 %all-to-all-start = ((bf16[4,8,512]{2,1,0:T(8,128)(2,1)}), bf16[4,8,512]{2,1,0:T(8,128)(2,1)S(1)}, u32[]{:S(2)}, u32[]{:S(2)}) async-start(bf16[4,8,512]{2,1,0:T(8,128)(2,1)} %bitcast.92), calls=%async_computation | async-start | bytes 65536 | tf_op jit(solution)/shard_map/all_to_all | solution.py:191
  47.5 5.4 %all-to-all-done = bf16[4,8,512]{2,1,0:T(8,128)(2,1)S(1)} async-done(((bf16[4,8,512]{2,1,0:T(8,128)(2,1)}), bf16[4,8,512]{2,1,0:T(8,128)(2,1)S(1)}, u32[]{:S(2)}, u32[]{:S(2)}) %all-to-all-start) | async-done | bytes 32800 | tf_op jit(solution)/shard_map/all_to_all | solution.py:191
  52.9 0.1 select_reduce_fusion
  53.0 0.6 %add_convert_fusion = bf16[8,512]{1,0:T(8,128)(2,1)} fusion(f32[8,512]{1,0:T(8,128)S(1)} %select_reduce_fusion, f32[8,2048]{1,0:T(8,128)S(1)} %get-tuple-element.52, s32[]{:T(128)S(6)} %select_n.207), kind=kLoop, calls=%fused_computation.118 | loop fusion | flops 8192 | bytes 40964 | tf_op jit(solution)/shard_map/convert_element_type | solution.py:195
  (32 shorter events, 1.1 us)
Async XLA Ops:
  0.0 23.3 %copy-start = (bf16[8,1024]{1,0:T(8,128)(2,1)S(1)}, bf16[8,1024]{1,0:T(8,128)(2,1)}, u32[]{:S(2)}) copy-start(bf16[8,1024]{1,0:T(8,128)(2,1)} %param.8) | copy-start | bytes 49156
  0.0 21.0 %collective-permute-start.1 = (bf16[8,1024]{1,0:T(8,128)(2,1)}, bf16[8,1024]{1,0:T(8,128)(2,1)S(1)}, u32[]{:S(2)}, u32[]{:S(2)}) collective-permute-start(bf16[8,1024]{1,0:T(8,128)(2,1)} %param.8), channel_id=1, source_target_pairs={{8,0},{12,4},{16,8},{20,12},{24,16},{28,20},{32,24},{36,28},{40,32... | collective-permute-start | bytes 49160 | tf_op jit(solution)/shard_map/ppermute | solution.py:16
  11.8 11.5 %collective-permute-start = (bf16[8,1024]{1,0:T(8,128)(2,1)}, bf16[8,1024]{1,0:T(8,128)(2,1)S(1)}, u32[]{:S(2)}, u32[]{:S(2)}) collective-permute-start(bf16[8,1024]{1,0:T(8,128)(2,1)} %param.8), channel_id=1, source_target_pairs={{0,8},{4,12},{8,16},{12,20},{16,24},{20,28},{24,32},{28,36},{32,40... | collective-permute-start | bytes 49160 | tf_op jit(solution)/shard_map/ppermute | solution.py:16
  15.9 9.1 %collective-permute-start.2 = (bf16[2,1536,128]{2,1,0:T(8,128)(2,1)S(1)}, bf16[2,1536,128]{2,1,0:T(8,128)(2,1)S(1)}, u32[]{:S(2)}, u32[]{:S(2)}) collective-permute-start(bf16[2,1536,128]{2,1,0:T(8,128)(2,1)S(1)} %maximum_bitcast_fusion), channel_id=1, source_target_pairs={{0,4},{4,0},{8,12},{12,8},{16,20},{20,16},{24,28},{28,24},{32,36},... | collective-permute-start | bytes 2359304 | tf_op jit(solution)/shard_map/ppermute | solution.py:77
  29.2 8.2 %collective-permute-start.4 = (f32[8,1040]{1,0:T(8,128)S(1)}, f32[8,1040]{1,0:T(8,128)S(1)}, u32[]{:S(2)}, u32[]{:S(2)}) collective-permute-start(f32[8,1040]{1,0:T(8,128)S(1)} %concatenate.63), channel_id=1, source_target_pairs={{0,8},{4,12},{8,16},{12,20},{16,24},{20,28},{24,32},{28,36},{32,40... | collective-permute-start | bytes 99848 | tf_op jit(solution)/shard_map/ppermute | solution.py:16
  31.4 7.6 %collective-permute-start.3 = (f32[8,1040]{1,0:T(8,128)S(1)}, f32[8,1040]{1,0:T(8,128)S(1)}, u32[]{:S(2)}, u32[]{:S(2)}) collective-permute-start(f32[8,1040]{1,0:T(8,128)S(1)} %concatenate.62), channel_id=1, source_target_pairs={{8,0},{12,4},{16,8},{20,12},{24,16},{28,20},{32,24},{36,28},{40,32... | collective-permute-start | bytes 99848 | tf_op jit(solution)/shard_map/ppermute | solution.py:16
  43.0 9.9 %all-to-all-start = ((bf16[4,8,512]{2,1,0:T(8,128)(2,1)}), bf16[4,8,512]{2,1,0:T(8,128)(2,1)S(1)}, u32[]{:S(2)}, u32[]{:S(2)}) async-start(bf16[4,8,512]{2,1,0:T(8,128)(2,1)} %bitcast.92), calls=%async_computation | async-start | bytes 65536 | tf_op jit(solution)/shard_map/all_to_all | solution.py:191

commit v8 on v7

--- a/solution.py
+++ b/solution.py
@@ -94,7 +94,7 @@
     cache_rows = per_dev * own_size
 
     local_rows = jnp.concatenate(
-        [own_kv.reshape(cache_rows, 2, -1), prompt_kv[0]], axis=0
+        [own_kv.reshape(cache_rows, 2, -1), prompt_kv[0], new_kv], axis=0
     )
     local_kv = jnp.moveaxis(local_rows, 1, 0)
     mate_kv = swapped(local_kv, "req")
@@ -103,7 +103,6 @@
     from_next = shifted(queries, "req", 2)
     hood_queries = jnp.concatenate([from_prev, queries, from_next], axis=0)
     hood_queries = hood_queries.reshape((3 * per_dev,) + shape4[1:])
-    query_block = queries.reshape(shape4)
     hood_count = 3 * per_dev
     slot_ids = jnp.arange(per_dev, dtype=jnp.int32)
     hood_beams = jnp.concatenate(
@@ -127,47 +126,38 @@
     columns = jnp.arange(cache_rows, dtype=jnp.int32)
     column_slot = columns // own_size
 
-    def own_allowed(holder, lengths):
-        return (
+    kv_count = cache_rows + prompt_size + per_dev
+    all_columns = jnp.arange(kv_count, dtype=jnp.int32)
+    is_cache = all_columns < cache_rows
+    is_prompt = (all_columns >= cache_rows) & (all_columns < cache_rows + prompt_size)
+    is_fresh = all_columns >= cache_rows + prompt_size
+    column_slot = jnp.where(is_cache, all_columns // own_size, all_columns - cache_rows - prompt_size)
+    column_pos = all_columns % own_size
+    hood_slot = hood_beams % per_dev
+
+    def allowed_for(holder, lengths):
+        column_len = jnp.repeat(lengths, own_size, total_repeat_length=cache_rows)
+        column_len = jnp.pad(column_len, (0, kv_count - cache_rows))
+        own_ok = (
             (in_range & (parent_dev == holder))[:, None]
+            & is_cache[None, :]
             & (column_slot[None, :] == (parent % per_dev)[:, None])
-            & (columns % own_size < jnp.repeat(lengths, own_size))[None, :]
+            & (column_pos < column_len)[None, :]
         )
-
-    def kv_rows(kv, lo, count):
-        keys = kv[0, lo : lo + count].reshape(count, kv_heads_local, head_dim)
-        values = kv[1, lo : lo + count].reshape(count, kv_heads_local, head_dim)
-        return keys, values
-
-    start = per_dev
-    prompt_queries = hood_queries[start:]
-
-    def prompt_allowed(holder):
-        here = in_range[start:] & (home[start:] == holder)
-        return jnp.broadcast_to(here[:, None], (hood_count - start, prompt_size))
+        prompt_ok = (in_range & (home == holder))[:, None] & is_prompt[None, :]
+        fresh_ok = (
+            (in_range & (hood_beams // per_dev == holder))[:, None]
+            & is_fresh[None, :]
+            & (column_slot[None, :] == hood_slot[:, None])
+        )
+        return own_ok | prompt_ok | fresh_ok
 
     parts_here = []
     for kv, holder, lengths in ((local_kv, dev_index, local_len), (mate_kv, mate_index, mate_len)):
-        keys, values = kv_rows(kv, 0, cache_rows)
-        own_part = partial_block(hood_queries, keys, values, own_allowed(holder, lengths))
-        keys, values = kv_rows(kv, cache_rows, prompt_size)
-        prompt_part = partial_block(prompt_queries, keys, values, prompt_allowed(holder))
-        prompt_full = tuple(
-            jnp.concatenate([jnp.zeros_like(x[:start]), x], axis=0) for x in prompt_part
-        )
-        parts_here += [own_part, prompt_full]
+        keys = kv[0].reshape(kv_count, kv_heads_local, head_dim)
+        values = kv[1].reshape(kv_count, kv_heads_local, head_dim)
+        parts_here.append(partial_block(hood_queries, keys, values, allowed_for(holder, lengths)))
     hood_part = merge_all(parts_here)
-
-    fresh_keys = new_kv[:, 0].reshape(per_dev, 1, kv_heads_local, head_dim)
-    fresh_values = new_kv[:, 1].reshape(per_dev, 1, kv_heads_local, head_dim)
-    fresh_scores = jnp.einsum(
-        "nkgd,nskd->nkgs", query_block, fresh_keys, preferred_element_type=jnp.float32
-    ) * (head_dim ** (-0.5))
-    fresh_part = (
-        fresh_values[:, 0, :, None, :].astype(jnp.float32) * jnp.ones_like(fresh_scores),
-        fresh_scores[..., 0],
-        jnp.ones_like(fresh_scores[..., 0]),
-    )
 
     def rows(part, lo):
         return tuple(x[lo : lo + per_dev] for x in part)
@@ -175,7 +165,7 @@
     back_from_next = unpack(shifted(pack(rows(hood_part, 0)), "req", 2), shape4)
     back_from_prev = unpack(shifted(pack(rows(hood_part, 2 * per_dev)), "req", -2), shape4)
     weighted, _, totals = merge_all(
-        [fresh_part, rows(hood_part, per_dev), back_from_next, back_from_prev]
+        [rows(hood_part, per_dev), back_from_next, back_from_prev]
     )
     attended = (
         (weighted / totals[..., None])

time: 54.2 us -> 64.3 us (1.19)
  other arithmetic: 4.15 us -> 12.5 us
  matrix products: 10.9 us -> 6.18 us
  waiting for transfers between devices: 6.76 us -> 11.2 us
  local copies, waits for them, and re-layouts: 3.54 us -> 5.57 us
    select_n x2 -> x6, other arithmetic: 0.01 us -> 10.2 us  [the longest x2 10.2 us: allowed_for(): column_len = jnp.repeat(lengths, own_size, total_repeat_length=cache_rows)]
    ppermute x4, waiting for transfers between devices: 1.31 us -> 5.8 us  [shifted(): return lax.ppermute(block, axis, route)]
    dot_general x4 -> x2, matrix products: 2.68 us -> 0.85 us  [partial_block(): jnp.einsum(formula, low, value_block, preferred_element_type=jnp.float32)]
    gather x0 -> x2, local copies, waits for them, and re-layouts: none -> 1.37 us  [allowed_for(): column_len = jnp.repeat(lengths, own_size, total_repeat_length=cache_rows)]
    dot_general x4 -> x2, matrix products: 2.06 us -> 1.04 us  [partial_block(): jnp.einsum('nkgd,skd->nkgs', query_block, key_block, preferred_element_ty...]
    dot_general x4 -> x2, matrix products: 1.77 us -> 0.78 us  [partial_block(): jnp.einsum(formula, high, value_block, preferred_element_type=jnp.float32)]
    dot_general x1 -> x0, matrix products: 0.84 us -> none  [local(): jnp.einsum('nkgd,nskd->nkgs', query_block, fresh_keys, preferred_element_...]
    convert_element_type x1 -> x0, other arithmetic: 0.77 us -> none  [local(): fresh_values[:, 0, :, None, :].astype(jnp.float32)]
  transfers between devices with their start and end apart: 6 -> 6, of which waited for: 2 -> 2; matrix products, arithmetic and copies ran while one was open for 18% -> 27% of each run, Pallas kernels for 0% -> 0%
where the time goes in v8:
time: 64.3 us; the launch traced here: 63.8 us
  starting transfers between devices  27.9 us (43%)
  other arithmetic  12.5 us (19%)
  waiting for transfers between devices  11.2 us (17%)
  matrix products  6.18 us (10%)
  local copies, waits for them, and re-layouts  5.57 us (9%)
    ppermute x4, starting transfers between devices, shifted(): return lax.ppermute(block, axis, route)  21.5 us
    select_n x2, other arithmetic, allowed_for(): column_len = jnp.repeat(lengths, own_size, total_repeat_length=cache_rows)  10.2 us
    ppermute x4, waiting for transfers between devices, shifted(): return lax.ppermute(block, axis, route)  5.8 us
    all_to_all x1, waiting for transfers between devices, local(): got = lax.all_to_all(chunks.astype(jnp.bfloat16), 'tp', 0, 0, tiled=True)  5.44 us
    all_to_all x1, starting transfers between devices, local(): got = lax.all_to_all(chunks.astype(jnp.bfloat16), 'tp', 0, 0, tiled=True)  4.46 us
    dot_general x1, matrix products, local(): jnp.dot(attended, out_weight, preferred_element_type=jnp.float32)  3.52 us
    unnamed x11, local copies, waits for them, and re-layouts  2.86 us
    ppermute x1, starting transfers between devices, swapped(): return lax.ppermute(block, axis, [(i, i ^ 1) for i in devices])  1.92 us
  transfers between devices with their start and end apart: 6, of which 2 were waited for; matrix products, arithmetic and copies ran while one was open for 27% of the time, Pallas kernels for 0%

profile of v8, /device:TPU:6, one launch (start us, length us, event | category | flops | bytes accessed | tf_op | source)
XLA Modules:
  0.0 63.8 jit_solution(17133716623093750134)
XLA Ops:
  0.0 11.7 %collective-permute-start.1 = (bf16[8,1024]{1,0:T(8,128)(2,1)}, bf16[8,1024]{1,0:T(8,128)(2,1)S(1)}, u32[]{:S(2)}, u32[]{:S(2)}) collective-permute-start(bf16[8,1024]{1,0:T(8,128)(2,1)} %param.14), channel_id=1, source_target_pairs={{8,0},{12,4},{16,8},{20,12},{24,16},{28,20},{32,24},{36,28},{40,32... | collective-permute-start | bytes 49160 | tf_op jit(solution)/shard_map/ppermute | solution.py:16
  11.7 1.9 %collective-permute-start = (bf16[8,1024]{1,0:T(8,128)(2,1)}, bf16[8,1024]{1,0:T(8,128)(2,1)S(1)}, u32[]{:S(2)}, u32[]{:S(2)}) collective-permute-start(bf16[8,1024]{1,0:T(8,128)(2,1)} %param.14), channel_id=1, source_target_pairs={{0,8},{4,12},{8,16},{12,20},{16,24},{20,28},{24,32},{28,36},{32,40... | collective-permute-start | bytes 49160 | tf_op jit(solution)/shard_map/ppermute | solution.py:16
  13.6 0.7 %copy.35 = bf16[8,2,128]{2,0,1:T(8,128)(2,1)S(1)} copy(bf16[8,2,128]{2,1,0:T(2,128)(2,1)} %param.15) | data formatting | bytes 8192 | tf_op args[1]
  14.3 1.0 %copy.76 = bf16[1,512,2,128]{3,1,2,0:T(8,128)(2,1)S(1)} copy(bf16[1,512,2,128]{3,2,1,0:T(2,128)(2,1)} %param.17) | data formatting | bytes 524288 | tf_op args[3]
  15.3 1.2 %copy.33 = bf16[8,128,2,128]{3,1,0,2:T(8,128)(2,1)S(1)} copy(bf16[8,128,2,128]{3,2,1,0:T(2,128)(2,1)} %param.16) | data formatting | bytes 1048576 | tf_op args[2]
  16.5 1.9 %collective-permute-start.2 = (bf16[2,1544,128]{2,1,0:T(8,128)(2,1)S(1)}, bf16[2,1544,128]{2,1,0:T(8,128)(2,1)S(1)}, u32[]{:S(2)}, u32[]{:S(2)}) collective-permute-start(bf16[2,1544,128]{2,1,0:T(8,128)(2,1)S(1)} %maximum_bitcast_fusion), channel_id=1, source_target_pairs={{0,4},{4,0},{8,12},{12,8},{16,20},{20,16},{24,28},{28,24},{32,36},... | collective-permute-start | bytes 2371592 | tf_op jit(solution)/shard_map/ppermute | solution.py:77
  18.6 0.1 pad_dynamic-slice_fusion
  18.6 0.1 fusion.95
  18.7 0.1 slice_bitcast_fusion.16
  18.9 0.1 fusion.87
  18.9 0.7 %fusion.96 = (s32[1]{0:T(128)}, s32[1]{0:T(128)}, s32[1]{0:T(128)}, s32[1]{0:T(128)}, s32[1]{0:T(128)}, /*index=5*/s32[1]{0:T(128)}, s32[1]{0:T(128)}, s32[1]{0:T(128)}) fusion(s32[8]{0:T(128)S(1)} %fusion.87), kind=kLoop, calls=%fused_computation.185 | loop fusion | bytes 64 | tf_op jit(solution)/shard_map/jit(_take)/gather | solution.py:139
  19.6 0.7 %fusion.97 = (s32[1]{0:T(128)}, s32[1]{0:T(128)}, s32[1]{0:T(128)}, s32[1]{0:T(128)}, s32[1]{0:T(128)}, /*index=5*/s32[1]{0:T(128)}, s32[1]{0:T(128)}, s32[1]{0:T(128)}) fusion(s32[8]{0:T(128)S(1)} %slice_bitcast_fusion.16), kind=kLoop, calls=%fused_computation.186 | loop fusion | bytes 64 | tf_op jit(solution)/shard_map/jit(_take)/gather | solution.py:139
  20.3 0.1 pad_add_fusion.1
  20.4 0.1 compare_and_fusion.6
  20.5 5.1 %select_select_fusion = s32[1024]{0:T(1024)S(1)} fusion(s32[]{:T(128)} %bitcast.35, s32[]{:T(128)} %bitcast.34, s32[]{:T(128)} %bitcast.33, s32[]{:T(128)} %bitcast.32, s32[]{:T(128)} %bitcast.31, s32[]{:T(128)} %bitcast.30, s32[]{:T(128)} %bitcast.29, s32[]{:T(128)} %bitcast.28), kind=kLoop, calls=%fused_computation.117 | loop fusion | flops 23552 | bytes 4128 | tf_op jit(solution)/shard_map/jit(_take)/select_n | solution.py:139
  25.6 5.1 %select_select_fusion.1 = s32[1024]{0:T(1024)S(1)} fusion(s32[]{:T(128)} %bitcast.18, s32[]{:T(128)} %bitcast.17, s32[]{:T(128)} %bitcast.16, s32[]{:T(128)} %bitcast.15, s32[]{:T(128)} %bitcast.14, s32[]{:T(128)} %bitcast.13, s32[]{:T(128)} %bitcast.12, s32[]{:T(128)} %bitcast.11), kind=kLoop, calls=%fused_computation.118 | loop fusion | flops 23552 | bytes 4128 | tf_op jit(solution)/shard_map/jit(_take)/select_n | solution.py:139
  30.8 0.2 fusion.39
  31.0 0.5 fusion.99
  31.5 0.4 fusion.10
  31.9 0.4 fusion.16
  32.3 0.5 fusion.98
  32.8 0.4 fusion.13
  33.3 0.4 fusion.7
  33.7 0.4 fusion.28
  34.1 0.4 fusion.9
  34.6 0.1 fusion.94
  34.6 0.1 copy.38
  34.7 0.1 fusion.93
  34.8 0.1 copy.39
  34.8 0.1 concatenate.90
  34.9 6.0 %collective-permute-start.3 = (f32[8,1040]{1,0:T(8,128)S(1)}, f32[8,1040]{1,0:T(8,128)S(1)}, u32[]{:S(2)}, u32[]{:S(2)}) collective-permute-start(f32[8,1040]{1,0:T(8,128)S(1)} %concatenate.90), channel_id=1, source_target_pairs={{8,0},{12,4},{16,8},{20,12},{24,16},{28,20},{32,24},{36,28},{40,32... | collective-permute-start | bytes 99848 | tf_op jit(solution)/shard_map/ppermute | solution.py:16
  40.9 0.1 copy.41
  41.1 0.1 concatenate.91
  41.2 1.9 %collective-permute-start.4 = (f32[8,1040]{1,0:T(8,128)S(1)}, f32[8,1040]{1,0:T(8,128)S(1)}, u32[]{:S(2)}, u32[]{:S(2)}) collective-permute-start(f32[8,1040]{1,0:T(8,128)S(1)} %concatenate.91), channel_id=1, source_target_pairs={{0,8},{4,12},{8,16},{12,20},{16,24},{20,28},{24,32},{28,36},{32,40... | collective-permute-start | bytes 99848 | tf_op jit(solution)/shard_map/ppermute | solution.py:16
  43.1 0.1 fusion.72
  43.2 0.1 copy.47
  43.3 5.8 %collective-permute-done.4 = f32[8,1040]{1,0:T(8,128)S(1)} collective-permute-done((f32[8,1040]{1,0:T(8,128)S(1)}, f32[8,1040]{1,0:T(8,128)S(1)}, u32[]{:S(2)}, u32[]{:S(2)}) %collective-permute-start.4) | collective-permute-done | bytes 33312 | tf_op jit(solution)/shard_map/ppermute | solution.py:16
  49.1 0.1 fusion.71
  49.2 0.1 copy.43
  49.3 0.1 copy.51
  49.4 0.1 copy.54
  49.5 0.1 fusion.88
  49.6 0.1 fusion.85
  49.6 3.5 %fusion.100 = (bf16[8,2048]{1,0:T(8,128)(2,1)}, f32[8,2048]{1,0:T(8,128)S(1)}) fusion(bf16[1024,2048]{1,0:T(8,128)(2,1)} %param.18, f32[8,8]{0,1:T(8,128)S(1)} %get-tuple-element.53, f32[8,1040]{1,0:T(8,128)S(1)} %collective-permute-done.4, f32[8,1040]{1,0:T(8,128)S(1)} %collective-permute-done.3, f32[24,1,8,128]{3,0,2,1:T(8,128)S(1)} %fusion.9, ...), kind=kOutput, calls=%fused_computation.189 | convolution fusion | flops 33628160 | bytes 4407296 | tf_op jit(solution)/shard_map/dot_general | solution.py:175
  53.2 4.5 %all-to-all-start = ((bf16[4,8,512]{2,1,0:T(8,128)(2,1)}), bf16[4,8,512]{2,1,0:T(8,128)(2,1)S(1)}, u32[]{:S(2)}, u32[]{:S(2)}) async-start(bf16[4,8,512]{2,1,0:T(8,128)(2,1)} %bitcast.70), calls=%async_computation | async-start | bytes 65536 | tf_op jit(solution)/shard_map/all_to_all | solution.py:181
  57.6 5.4 %all-to-all-done = bf16[4,8,512]{2,1,0:T(8,128)(2,1)S(1)} async-done(((bf16[4,8,512]{2,1,0:T(8,128)(2,1)}), bf16[4,8,512]{2,1,0:T(8,128)(2,1)S(1)}, u32[]{:S(2)}, u32[]{:S(2)}) %all-to-all-start) | async-done | bytes 32800 | tf_op jit(solution)/shard_map/all_to_all | solution.py:181
  63.1 0.1 select_reduce_fusion
  63.1 0.6 add_convert_fusion
  (34 shorter events, 0.5 us)
Async XLA Ops:
  0.0 31.0 %collective-permute-start.1 = (bf16[8,1024]{1,0:T(8,128)(2,1)}, bf16[8,1024]{1,0:T(8,128)(2,1)S(1)}, u32[]{:S(2)}, u32[]{:S(2)}) collective-permute-start(bf16[8,1024]{1,0:T(8,128)(2,1)} %param.14), channel_id=1, source_target_pairs={{8,0},{12,4},{16,8},{20,12},{24,16},{28,20},{32,24},{36,28},{40,32... | collective-permute-start | bytes 49160 | tf_op jit(solution)/shard_map/ppermute | solution.py:16
  11.7 19.3 %collective-permute-start = (bf16[8,1024]{1,0:T(8,128)(2,1)}, bf16[8,1024]{1,0:T(8,128)(2,1)S(1)}, u32[]{:S(2)}, u32[]{:S(2)}) collective-permute-start(bf16[8,1024]{1,0:T(8,128)(2,1)} %param.14), channel_id=1, source_target_pairs={{0,8},{4,12},{8,16},{12,20},{16,24},{20,28},{24,32},{28,36},{32,40... | collective-permute-start | bytes 49160 | tf_op jit(solution)/shard_map/ppermute | solution.py:16
  15.3 3.2 %copy-start = (s32[1024]{0:T(1024)S(1)}, s32[1024]{0:T(1024)}, u32[]{:S(2)}) copy-start(s32[1024]{0:T(1024)} %param.20) | copy-start | bytes 12292
  15.3 3.2 %copy-start.1 = (s32[1024]{0:T(1024)S(1)}, s32[1024]{0:T(1024)}, u32[]{:S(2)}) copy-start(s32[1024]{0:T(1024)} %param.21) | copy-start | bytes 12292
  15.3 3.2 %copy-start.2 = (s32[1024]{0:T(1024)S(1)}, s32[1024]{0:T(1024)}, u32[]{:S(2)}) copy-start(s32[1024]{0:T(1024)} %param.19) | copy-start | bytes 12292
  15.3 15.7 %copy-start.3 = (bf16[8,1024]{1,0:T(8,128)(2,1)S(1)}, bf16[8,1024]{1,0:T(8,128)(2,1)}, u32[]{:S(2)}) copy-start(bf16[8,1024]{1,0:T(8,128)(2,1)} %param.14) | copy-start | bytes 49156
  16.5 15.8 %collective-permute-start.2 = (bf16[2,1544,128]{2,1,0:T(8,128)(2,1)S(1)}, bf16[2,1544,128]{2,1,0:T(8,128)(2,1)S(1)}, u32[]{:S(2)}, u32[]{:S(2)}) collective-permute-start(bf16[2,1544,128]{2,1,0:T(8,128)(2,1)S(1)} %maximum_bitcast_fusion), channel_id=1, source_target_pairs={{0,4},{4,0},{8,12},{12,8},{16,20},{20,16},{24,28},{28,24},{32,36},... | collective-permute-start | bytes 2371592 | tf_op jit(solution)/shard_map/ppermute | solution.py:77
  34.9 8.2 %collective-permute-start.3 = (f32[8,1040]{1,0:T(8,128)S(1)}, f32[8,1040]{1,0:T(8,128)S(1)}, u32[]{:S(2)}, u32[]{:S(2)}) collective-permute-start(f32[8,1040]{1,0:T(8,128)S(1)} %concatenate.90), channel_id=1, source_target_pairs={{8,0},{12,4},{16,8},{20,12},{24,16},{28,20},{32,24},{36,28},{40,32... | collective-permute-start | bytes 99848 | tf_op jit(solution)/shard_map/ppermute | solution.py:16
  41.2 8.0 %collective-permute-start.4 = (f32[8,1040]{1,0:T(8,128)S(1)}, f32[8,1040]{1,0:T(8,128)S(1)}, u32[]{:S(2)}, u32[]{:S(2)}) collective-permute-start(f32[8,1040]{1,0:T(8,128)S(1)} %concatenate.91), channel_id=1, source_target_pairs={{0,8},{4,12},{8,16},{12,20},{16,24},{20,28},{24,32},{28,36},{32,40... | collective-permute-start | bytes 99848 | tf_op jit(solution)/shard_map/ppermute | solution.py:16
  53.2 9.9 %all-to-all-start = ((bf16[4,8,512]{2,1,0:T(8,128)(2,1)}), bf16[4,8,512]{2,1,0:T(8,128)(2,1)S(1)}, u32[]{:S(2)}, u32[]{:S(2)}) async-start(bf16[4,8,512]{2,1,0:T(8,128)(2,1)} %bitcast.70), calls=%async_computation | async-start | bytes 65536 | tf_op jit(solution)/shard_map/all_to_all | solution.py:181

commit v9 on v8

--- a/solution.py
+++ b/solution.py
@@ -94,7 +94,7 @@
     cache_rows = per_dev * own_size
 
     local_rows = jnp.concatenate(
-        [own_kv.reshape(cache_rows, 2, -1), prompt_kv[0], new_kv], axis=0
+        [own_kv.reshape(cache_rows, 2, -1), prompt_kv[0]], axis=0
     )
     local_kv = jnp.moveaxis(local_rows, 1, 0)
     mate_kv = swapped(local_kv, "req")
@@ -103,6 +103,7 @@
     from_next = shifted(queries, "req", 2)
     hood_queries = jnp.concatenate([from_prev, queries, from_next], axis=0)
     hood_queries = hood_queries.reshape((3 * per_dev,) + shape4[1:])
+    query_block = queries.reshape(shape4)
     hood_count = 3 * per_dev
     slot_ids = jnp.arange(per_dev, dtype=jnp.int32)
     hood_beams = jnp.concatenate(
@@ -126,31 +127,24 @@
     columns = jnp.arange(cache_rows, dtype=jnp.int32)
     column_slot = columns // own_size
 
-    kv_count = cache_rows + prompt_size + per_dev
+    kv_count = cache_rows + prompt_size
     all_columns = jnp.arange(kv_count, dtype=jnp.int32)
     is_cache = all_columns < cache_rows
-    is_prompt = (all_columns >= cache_rows) & (all_columns < cache_rows + prompt_size)
-    is_fresh = all_columns >= cache_rows + prompt_size
-    column_slot = jnp.where(is_cache, all_columns // own_size, all_columns - cache_rows - prompt_size)
+    column_slot = all_columns // own_size
     column_pos = all_columns % own_size
-    hood_slot = hood_beams % per_dev
 
     def allowed_for(holder, lengths):
-        column_len = jnp.repeat(lengths, own_size, total_repeat_length=cache_rows)
-        column_len = jnp.pad(column_len, (0, kv_count - cache_rows))
+        column_len = jnp.pad(
+            jnp.repeat(lengths, own_size, total_repeat_length=cache_rows), (0, prompt_size)
+        )
         own_ok = (
             (in_range & (parent_dev == holder))[:, None]
             & is_cache[None, :]
             & (column_slot[None, :] == (parent % per_dev)[:, None])
             & (column_pos < column_len)[None, :]
         )
-        prompt_ok = (in_range & (home == holder))[:, None] & is_prompt[None, :]
-        fresh_ok = (
-            (in_range & (hood_beams // per_dev == holder))[:, None]
-            & is_fresh[None, :]
-            & (column_slot[None, :] == hood_slot[:, None])
-        )
-        return own_ok | prompt_ok | fresh_ok
+        prompt_ok = (in_range & (home == holder))[:, None] & ~is_cache[None, :]
+        return own_ok | prompt_ok
 
     parts_here = []
     for kv, holder, lengths in ((local_kv, dev_index, local_len), (mate_kv, mate_index, mate_len)):
@@ -159,13 +153,24 @@
         parts_here.append(partial_block(hood_queries, keys, values, allowed_for(holder, lengths)))
     hood_part = merge_all(parts_here)
 
+    fresh_keys = new_kv[:, 0].reshape(per_dev, 1, kv_heads_local, head_dim)
+    fresh_values = new_kv[:, 1].reshape(per_dev, 1, kv_heads_local, head_dim)
+    fresh_scores = jnp.einsum(
+        "nkgd,nskd->nkgs", query_block, fresh_keys, preferred_element_type=jnp.float32
+    ) * (head_dim ** (-0.5))
+    fresh_part = (
+        fresh_values[:, 0, :, None, :].astype(jnp.float32) * jnp.ones_like(fresh_scores),
+        fresh_scores[..., 0],
+        jnp.ones_like(fresh_scores[..., 0]),
+    )
+
     def rows(part, lo):
         return tuple(x[lo : lo + per_dev] for x in part)
 
     back_from_next = unpack(shifted(pack(rows(hood_part, 0)), "req", 2), shape4)
     back_from_prev = unpack(shifted(pack(rows(hood_part, 2 * per_dev)), "req", -2), shape4)
     weighted, _, totals = merge_all(
-        [rows(hood_part, per_dev), back_from_next, back_from_prev]
+        [fresh_part, rows(hood_part, per_dev), back_from_next, back_from_prev]
     )
     attended = (
         (weighted / totals[..., None])

time: 64.3 us -> 59.2 us (0.921)
  waiting for transfers between devices: 11.2 us -> 6.91 us
    ppermute x4, waiting for transfers between devices: 5.8 us -> 1.46 us  [shifted(): return lax.ppermute(block, axis, route)]
    unnamed x11 -> x13, local copies, waits for them, and re-layouts: 2.86 us -> 2.18 us
  transfers between devices with their start and end apart: 6 -> 6, of which waited for: 2 -> 2; matrix products, arithmetic and copies ran while one was open for 27% -> 28% of each run, Pallas kernels for 0% -> 0%
where the time goes in v9:
time: 59.2 us; the launch traced here: 58.7 us
  starting transfers between devices  27.9 us (47%)
  other arithmetic  12.4 us (21%)
  waiting for transfers between devices  6.91 us (12%)
  matrix products  6.23 us (11%)
  local copies, waits for them, and re-layouts  4.94 us (8%)
    ppermute x4, starting transfers between devices, shifted(): return lax.ppermute(block, axis, route)  21.5 us
    select_n x2, other arithmetic, allowed_for(): jnp.repeat(lengths, own_size, total_repeat_length=cache_rows)  10.2 us
    all_to_all x1, waiting for transfers between devices, local(): got = lax.all_to_all(chunks.astype(jnp.bfloat16), 'tp', 0, 0, tiled=True)  5.44 us
    all_to_all x1, starting transfers between devices, local(): got = lax.all_to_all(chunks.astype(jnp.bfloat16), 'tp', 0, 0, tiled=True)  4.46 us
    dot_general x1, matrix products, local(): jnp.dot(attended, out_weight, preferred_element_type=jnp.float32)  3.51 us
    unnamed x13, local copies, waits for them, and re-layouts  2.18 us
    ppermute x1, starting transfers between devices, swapped(): return lax.ppermute(block, axis, [(i, i ^ 1) for i in devices])  1.92 us
    ppermute x4, waiting for transfers between devices, shifted(): return lax.ppermute(block, axis, route)  1.46 us
  transfers between devices with their start and end apart: 6, of which 2 were waited for; matrix products, arithmetic and copies ran while one was open for 28% of the time, Pallas kernels for 0%

profile of v9, /device:TPU:6, one launch (start us, length us, event | category | flops | bytes accessed | tf_op | source)
XLA Modules:
  0.0 58.7 jit_solution(9364800627086773816)
XLA Ops:
  0.0 11.7 %collective-permute-start.1 = (bf16[8,1024]{1,0:T(8,128)(2,1)}, bf16[8,1024]{1,0:T(8,128)(2,1)S(1)}, u32[]{:S(2)}, u32[]{:S(2)}) collective-permute-start(bf16[8,1024]{1,0:T(8,128)(2,1)} %param.14), channel_id=1, source_target_pairs={{8,0},{12,4},{16,8},{20,12},{24,16},{28,20},{32,24},{36,28},{40,32... | collective-permute-start | bytes 49160 | tf_op jit(solution)/shard_map/ppermute | solution.py:16
  11.7 1.9 %collective-permute-start = (bf16[8,1024]{1,0:T(8,128)(2,1)}, bf16[8,1024]{1,0:T(8,128)(2,1)S(1)}, u32[]{:S(2)}, u32[]{:S(2)}) collective-permute-start(bf16[8,1024]{1,0:T(8,128)(2,1)} %param.14), channel_id=1, source_target_pairs={{0,8},{4,12},{8,16},{12,20},{16,24},{20,28},{24,32},{28,36},{32,40... | collective-permute-start | bytes 49160 | tf_op jit(solution)/shard_map/ppermute | solution.py:16
  13.6 1.0 %copy.91 = bf16[1,512,2,128]{3,1,2,0:T(8,128)(2,1)S(1)} copy(bf16[1,512,2,128]{3,2,1,0:T(2,128)(2,1)} %param.17) | data formatting | bytes 524288 | tf_op args[3]
  14.6 1.2 %copy.35 = bf16[8,128,2,128]{3,1,0,2:T(8,128)(2,1)S(1)} copy(bf16[8,128,2,128]{3,2,1,0:T(2,128)(2,1)} %param.16) | data formatting | bytes 1048576 | tf_op args[2]
  15.9 1.9 %collective-permute-start.2 = (bf16[2,1536,128]{2,1,0:T(8,128)(2,1)S(1)}, bf16[2,1536,128]{2,1,0:T(8,128)(2,1)S(1)}, u32[]{:S(2)}, u32[]{:S(2)}) collective-permute-start(bf16[2,1536,128]{2,1,0:T(8,128)(2,1)S(1)} %maximum_bitcast_fusion), channel_id=1, source_target_pairs={{0,4},{4,0},{8,12},{12,8},{16,20},{20,16},{24,28},{28,24},{32,36},... | collective-permute-start | bytes 2359304 | tf_op jit(solution)/shard_map/ppermute | solution.py:77
  17.9 0.1 pad_dynamic-slice_fusion
  18.0 0.1 fusion.99
  18.0 0.1 slice_bitcast_fusion.16
  18.2 0.1 pad_add_fusion.1
  18.2 0.1 compare_and_fusion.3
  18.3 0.1 fusion.91
  18.4 0.7 %fusion.100 = (s32[1]{0:T(128)}, s32[1]{0:T(128)}, s32[1]{0:T(128)}, s32[1]{0:T(128)}, s32[1]{0:T(128)}, /*index=5*/s32[1]{0:T(128)}, s32[1]{0:T(128)}, s32[1]{0:T(128)}) fusion(s32[8]{0:T(128)S(1)} %fusion.91), kind=kLoop, calls=%fused_computation.179 | loop fusion | bytes 64 | tf_op jit(solution)/shard_map/jit(_take)/gather | solution.py:138
  19.1 0.7 %fusion.101 = (s32[1]{0:T(128)}, s32[1]{0:T(128)}, s32[1]{0:T(128)}, s32[1]{0:T(128)}, s32[1]{0:T(128)}, /*index=5*/s32[1]{0:T(128)}, s32[1]{0:T(128)}, s32[1]{0:T(128)}) fusion(s32[8]{0:T(128)S(1)} %slice_bitcast_fusion.16), kind=kLoop, calls=%fused_computation.180 | loop fusion | bytes 64 | tf_op jit(solution)/shard_map/jit(_take)/gather | solution.py:138
  19.8 5.1 %select_select_fusion = s32[1024]{0:T(1024)S(1)} fusion(s32[]{:T(128)} %bitcast.39, s32[]{:T(128)} %bitcast.38, s32[]{:T(128)} %bitcast.37, s32[]{:T(128)} %bitcast.36, s32[]{:T(128)} %bitcast.35, s32[]{:T(128)} %bitcast.34, s32[]{:T(128)} %bitcast.33, s32[]{:T(128)} %bitcast.32), kind=kLoop, calls=%fused_computation.112 | loop fusion | flops 23552 | bytes 4128 | tf_op jit(solution)/shard_map/jit(_take)/select_n | solution.py:138
  24.9 5.1 %select_select_fusion.1 = s32[1024]{0:T(1024)S(1)} fusion(s32[]{:T(128)} %bitcast.20, s32[]{:T(128)} %bitcast.19, s32[]{:T(128)} %bitcast.18, s32[]{:T(128)} %bitcast.17, s32[]{:T(128)} %bitcast.16, s32[]{:T(128)} %bitcast.15, s32[]{:T(128)} %bitcast.14, s32[]{:T(128)} %bitcast.13), kind=kLoop, calls=%fused_computation.113 | loop fusion | flops 23552 | bytes 4128 | tf_op jit(solution)/shard_map/jit(_take)/select_n | solution.py:138
  30.0 0.2 fusion.37
  30.1 0.1 fusion.61
  30.3 0.5 fusion.103
  30.8 0.4 fusion.11
  31.1 0.4 fusion.16
  31.5 0.5 fusion.102
  32.0 0.4 fusion.13
  32.4 0.4 fusion.9
  32.8 0.4 fusion.28
  33.2 0.4 fusion.7
  33.7 0.1 fusion.98
  33.8 0.1 copy.43
  33.9 0.1 fusion.97
  33.9 0.1 copy.44
  34.0 0.1 concatenate.51
  34.1 1.9 %collective-permute-start.4 = (f32[8,1040]{1,0:T(8,128)S(1)}, f32[8,1040]{1,0:T(8,128)S(1)}, u32[]{:S(2)}, u32[]{:S(2)}) collective-permute-start(f32[8,1040]{1,0:T(8,128)S(1)} %concatenate.51), channel_id=1, source_target_pairs={{0,8},{4,12},{8,16},{12,20},{16,24},{20,28},{24,32},{28,36},{32,40... | collective-permute-start | bytes 99848 | tf_op jit(solution)/shard_map/ppermute | solution.py:16
  36.0 0.1 copy.46
  36.2 0.1 concatenate.50
  36.3 6.0 %collective-permute-start.3 = (f32[8,1040]{1,0:T(8,128)S(1)}, f32[8,1040]{1,0:T(8,128)S(1)}, u32[]{:S(2)}, u32[]{:S(2)}) collective-permute-start(f32[8,1040]{1,0:T(8,128)S(1)} %concatenate.50), channel_id=1, source_target_pairs={{8,0},{12,4},{16,8},{20,12},{24,16},{28,20},{32,24},{36,28},{40,32... | collective-permute-start | bytes 99848 | tf_op jit(solution)/shard_map/ppermute | solution.py:16
  42.3 0.1 fusion.72
  42.4 0.1 copy.45
  42.5 1.5 %collective-permute-done.3 = f32[8,1040]{1,0:T(8,128)S(1)} collective-permute-done((f32[8,1040]{1,0:T(8,128)S(1)}, f32[8,1040]{1,0:T(8,128)S(1)}, u32[]{:S(2)}, u32[]{:S(2)}) %collective-permute-start.3) | collective-permute-done | bytes 33312 | tf_op jit(solution)/shard_map/ppermute | solution.py:16
  43.9 0.1 fusion.73
  44.0 0.1 copy.42
  44.2 0.1 copy.56
  44.3 0.1 copy.52
  44.4 0.1 fusion.88
  44.5 0.1 fusion.92
  44.6 3.5 %fusion.104 = (bf16[8,2048]{1,0:T(8,128)(2,1)}, f32[8,2048]{1,0:T(8,128)S(1)}) fusion(bf16[1024,2048]{1,0:T(8,128)(2,1)} %param.18, f32[8,8]{0,1:T(8,128)S(1)} %get-tuple-element.51, f32[8,1040]{1,0:T(8,128)S(1)} %collective-permute-done.4, f32[8,1040]{1,0:T(8,128)S(1)} %collective-permute-done.3, f32[24,1,8,128]{3,0,2,1:T(8,128)S(1)} %fusion.7, ...), kind=kOutput, calls=%fused_computation.183 | convolution fusion | flops 33644544 | bytes 4415488 | tf_op jit(solution)/shard_map/dot_general | solution.py:180
  48.1 4.5 %all-to-all-start = ((bf16[4,8,512]{2,1,0:T(8,128)(2,1)}), bf16[4,8,512]{2,1,0:T(8,128)(2,1)S(1)}, u32[]{:S(2)}, u32[]{:S(2)}) async-start(bf16[4,8,512]{2,1,0:T(8,128)(2,1)} %bitcast.78), calls=%async_computation | async-start | bytes 65536 | tf_op jit(solution)/shard_map/all_to_all | solution.py:186
  52.5 5.4 %all-to-all-done = bf16[4,8,512]{2,1,0:T(8,128)(2,1)S(1)} async-done(((bf16[4,8,512]{2,1,0:T(8,128)(2,1)}), bf16[4,8,512]{2,1,0:T(8,128)(2,1)S(1)}, u32[]{:S(2)}, u32[]{:S(2)}) %all-to-all-start) | async-done | bytes 32800 | tf_op jit(solution)/shard_map/all_to_all | solution.py:186
  58.0 0.1 select_reduce_fusion
  58.1 0.6 %add_convert_fusion = bf16[8,512]{1,0:T(8,128)(2,1)} fusion(f32[8,512]{1,0:T(8,128)S(1)} %select_reduce_fusion, f32[8,2048]{1,0:T(8,128)S(1)} %get-tuple-element.85, s32[]{:T(128)S(6)} %select_n.238), kind=kLoop, calls=%fused_computation.72 | loop fusion | flops 8192 | bytes 40964 | tf_op jit(solution)/shard_map/convert_element_type | solution.py:190
  (37 shorter events, 0.5 us)
Async XLA Ops:
  0.0 30.3 %collective-permute-start.1 = (bf16[8,1024]{1,0:T(8,128)(2,1)}, bf16[8,1024]{1,0:T(8,128)(2,1)S(1)}, u32[]{:S(2)}, u32[]{:S(2)}) collective-permute-start(bf16[8,1024]{1,0:T(8,128)(2,1)} %param.14), channel_id=1, source_target_pairs={{8,0},{12,4},{16,8},{20,12},{24,16},{28,20},{32,24},{36,28},{40,32... | collective-permute-start | bytes 49160 | tf_op jit(solution)/shard_map/ppermute | solution.py:16
  11.7 18.6 %collective-permute-start = (bf16[8,1024]{1,0:T(8,128)(2,1)}, bf16[8,1024]{1,0:T(8,128)(2,1)S(1)}, u32[]{:S(2)}, u32[]{:S(2)}) collective-permute-start(bf16[8,1024]{1,0:T(8,128)(2,1)} %param.14), channel_id=1, source_target_pairs={{0,8},{4,12},{8,16},{12,20},{16,24},{20,28},{24,32},{28,36},{32,40... | collective-permute-start | bytes 49160 | tf_op jit(solution)/shard_map/ppermute | solution.py:16
  14.6 3.2 %copy-start.1 = (s32[1024]{0:T(1024)S(1)}, s32[1024]{0:T(1024)}, u32[]{:S(2)}) copy-start(s32[1024]{0:T(1024)} %param.20) | copy-start | bytes 12292
  14.6 3.2 %copy-start.2 = (s32[1024]{0:T(1024)S(1)}, s32[1024]{0:T(1024)}, u32[]{:S(2)}) copy-start(s32[1024]{0:T(1024)} %param.21) | copy-start | bytes 12292
  14.6 3.2 %copy-start.3 = (s32[1024]{0:T(1024)S(1)}, s32[1024]{0:T(1024)}, u32[]{:S(2)}) copy-start(s32[1024]{0:T(1024)} %param.19) | copy-start | bytes 12292
  14.6 3.5 %copy-start = (bf16[8,2,128]{2,1,0:T(2,128)(2,1)S(1)}, bf16[8,2,128]{2,1,0:T(2,128)(2,1)}, u32[]{:S(2)}) copy-start(bf16[8,2,128]{2,1,0:T(2,128)(2,1)} %param.15) | copy-start | bytes 12292
  15.8 14.3 %copy-start.4 = (bf16[8,1024]{1,0:T(8,128)(2,1)S(1)}, bf16[8,1024]{1,0:T(8,128)(2,1)}, u32[]{:S(2)}) copy-start(bf16[8,1024]{1,0:T(8,128)(2,1)} %param.14) | copy-start | bytes 49156
  15.9 15.6 %collective-permute-start.2 = (bf16[2,1536,128]{2,1,0:T(8,128)(2,1)S(1)}, bf16[2,1536,128]{2,1,0:T(8,128)(2,1)S(1)}, u32[]{:S(2)}, u32[]{:S(2)}) collective-permute-start(bf16[2,1536,128]{2,1,0:T(8,128)(2,1)S(1)} %maximum_bitcast_fusion), channel_id=1, source_target_pairs={{0,4},{4,0},{8,12},{12,8},{16,20},{20,16},{24,28},{28,24},{32,36},... | collective-permute-start | bytes 2359304 | tf_op jit(solution)/shard_map/ppermute | solution.py:77
  34.1 8.2 %collective-permute-start.4 = (f32[8,1040]{1,0:T(8,128)S(1)}, f32[8,1040]{1,0:T(8,128)S(1)}, u32[]{:S(2)}, u32[]{:S(2)}) collective-permute-start(f32[8,1040]{1,0:T(8,128)S(1)} %concatenate.51), channel_id=1, source_target_pairs={{0,8},{4,12},{8,16},{12,20},{16,24},{20,28},{24,32},{28,36},{32,40... | collective-permute-start | bytes 99848 | tf_op jit(solution)/shard_map/ppermute | solution.py:16
  36.3 7.6 %collective-permute-start.3 = (f32[8,1040]{1,0:T(8,128)S(1)}, f32[8,1040]{1,0:T(8,128)S(1)}, u32[]{:S(2)}, u32[]{:S(2)}) collective-permute-start(f32[8,1040]{1,0:T(8,128)S(1)} %concatenate.50), channel_id=1, source_target_pairs={{8,0},{12,4},{16,8},{20,12},{24,16},{28,20},{32,24},{36,28},{40,32... | collective-permute-start | bytes 99848 | tf_op jit(solution)/shard_map/ppermute | solution.py:16
  48.1 9.9 %all-to-all-start = ((bf16[4,8,512]{2,1,0:T(8,128)(2,1)}), bf16[4,8,512]{2,1,0:T(8,128)(2,1)S(1)}, u32[]{:S(2)}, u32[]{:S(2)}) async-start(bf16[4,8,512]{2,1,0:T(8,128)(2,1)} %bitcast.78), calls=%async_computation | async-start | bytes 65536 | tf_op jit(solution)/shard_map/all_to_all | solution.py:186

commit v10 on v9

--- a/solution.py
+++ b/solution.py
@@ -134,9 +134,8 @@
     column_pos = all_columns % own_size
 
     def allowed_for(holder, lengths):
-        column_len = jnp.pad(
-            jnp.repeat(lengths, own_size, total_repeat_length=cache_rows), (0, prompt_size)
-        )
+        per_column = jnp.broadcast_to(lengths[:, None], (per_dev, own_size)).reshape(-1)
+        column_len = jnp.pad(per_column, (0, prompt_size))
         own_ok = (
             (in_range & (parent_dev == holder))[:, None]
             & is_cache[None, :]

time: 59.2 us -> 48.4 us (0.82)
  other arithmetic: 12.4 us -> 2.2 us
  local copies, waits for them, and re-layouts: 4.94 us -> 3.73 us
  waiting for transfers between devices: 6.91 us -> 7.64 us
    select_n x2 -> x0, other arithmetic: 10.2 us -> none  [allowed_for(): jnp.repeat(lengths, own_size, total_repeat_length=cache_rows)]
    gather x2 -> x0, local copies, waits for them, and re-layouts: 1.35 us -> none  [allowed_for(): jnp.repeat(lengths, own_size, total_repeat_length=cache_rows)]
    ppermute x4, waiting for transfers between devices: 1.46 us -> 2.19 us  [shifted(): return lax.ppermute(block, axis, route)]
  transfers between devices with their start and end apart: 6 -> 6, of which waited for: 2 -> 3; matrix products, arithmetic and copies ran while one was open for 28% -> 10% of each run, Pallas kernels for 0% -> 0%
where the time goes in v10:
time: 48.4 us; the launch traced here: 48 us
  starting transfers between devices  27.9 us (58%)
  waiting for transfers between devices  7.64 us (16%)
  matrix products  6.23 us (13%)
  local copies, waits for them, and re-layouts  3.73 us (8%)
  other arithmetic  2.2 us (5%)
    ppermute x4, starting transfers between devices, shifted(): return lax.ppermute(block, axis, route)  21.5 us
    all_to_all x1, waiting for transfers between devices, local(): got = lax.all_to_all(chunks.astype(jnp.bfloat16), 'tp', 0, 0, tiled=True)  5.44 us
    all_to_all x1, starting transfers between devices, local(): got = lax.all_to_all(chunks.astype(jnp.bfloat16), 'tp', 0, 0, tiled=True)  4.46 us
    dot_general x1, matrix products, local(): jnp.dot(attended, out_weight, preferred_element_type=jnp.float32)  3.5 us
    ppermute x4, waiting for transfers between devices, shifted(): return lax.ppermute(block, axis, route)  2.19 us
    unnamed x13, local copies, waits for them, and re-layouts  2.18 us
    ppermute x1, starting transfers between devices, swapped(): return lax.ppermute(block, axis, [(i, i ^ 1) for i in devices])  1.92 us
    dot_general x2, matrix products, partial_block(): jnp.einsum('nkgd,skd->nkgs', query_block, key_block, preferred_element_ty...  0.97 us
  transfers between devices with their start and end apart: 6, of which 3 were waited for; matrix products, arithmetic and copies ran while one was open for 10% of the time, Pallas kernels for 0%

profile of v10, /device:TPU:6, one launch (start us, length us, event | category | flops | bytes accessed | tf_op | source)
XLA Modules:
  0.0 48.0 jit_solution(6574984158576158077)
XLA Ops:
  0.0 11.7 %collective-permute-start.1 = (bf16[8,1024]{1,0:T(8,128)(2,1)}, bf16[8,1024]{1,0:T(8,128)(2,1)S(1)}, u32[]{:S(2)}, u32[]{:S(2)}) collective-permute-start(bf16[8,1024]{1,0:T(8,128)(2,1)} %param.8), channel_id=1, source_target_pairs={{8,0},{12,4},{16,8},{20,12},{24,16},{28,20},{32,24},{36,28},{40,32... | collective-permute-start | bytes 49160 | tf_op jit(solution)/shard_map/ppermute | solution.py:16
  11.7 1.9 %collective-permute-start = (bf16[8,1024]{1,0:T(8,128)(2,1)}, bf16[8,1024]{1,0:T(8,128)(2,1)S(1)}, u32[]{:S(2)}, u32[]{:S(2)}) collective-permute-start(bf16[8,1024]{1,0:T(8,128)(2,1)} %param.8), channel_id=1, source_target_pairs={{0,8},{4,12},{8,16},{12,20},{16,24},{20,28},{24,32},{28,36},{32,40... | collective-permute-start | bytes 49160 | tf_op jit(solution)/shard_map/ppermute | solution.py:16
  13.6 1.0 %copy.91 = bf16[1,512,2,128]{3,1,2,0:T(8,128)(2,1)S(1)} copy(bf16[1,512,2,128]{3,2,1,0:T(2,128)(2,1)} %param.11) | data formatting | bytes 524288 | tf_op args[3]
  14.6 1.2 %copy.35 = bf16[8,128,2,128]{3,1,0,2:T(8,128)(2,1)S(1)} copy(bf16[8,128,2,128]{3,2,1,0:T(2,128)(2,1)} %param.10) | data formatting | bytes 1048576 | tf_op args[2]
  15.9 1.9 %collective-permute-start.2 = (bf16[2,1536,128]{2,1,0:T(8,128)(2,1)S(1)}, bf16[2,1536,128]{2,1,0:T(8,128)(2,1)S(1)}, u32[]{:S(2)}, u32[]{:S(2)}) collective-permute-start(bf16[2,1536,128]{2,1,0:T(8,128)(2,1)S(1)} %maximum_bitcast_fusion), channel_id=1, source_target_pairs={{0,4},{4,0},{8,12},{12,8},{16,20},{20,16},{24,28},{28,24},{32,36},... | collective-permute-start | bytes 2359304 | tf_op jit(solution)/shard_map/ppermute | solution.py:77
  17.9 0.1 pad_dynamic-slice_fusion
  18.0 0.1 fusion.89
  18.0 0.1 slice_bitcast_fusion.16
  18.2 0.1 pad_add_fusion.1
  18.2 0.1 compare_and_fusion.3
  18.3 0.1 fusion.81
  18.4 0.1 broadcast_bitcast_fusion
  18.6 0.2 fusion.37
  18.8 0.1 fusion.61
  18.9 0.7 %collective-permute-done = bf16[8,1024]{1,0:T(8,128)(2,1)S(1)} collective-permute-done((bf16[8,1024]{1,0:T(8,128)(2,1)}, bf16[8,1024]{1,0:T(8,128)(2,1)S(1)}, u32[]{:S(2)}, u32[]{:S(2)}) %collective-permute-start) | collective-permute-done | bytes 16416 | tf_op jit(solution)/shard_map/ppermute | solution.py:16
  19.6 0.5 %fusion.91 = (f32[24,8]{0,1:T(8,128)S(1)}, f32[24,1,8,1536]{3,0,2,1:T(8,128)S(1)}) fusion(bf16[2,1536,128]{2,1,0:T(8,128)(2,1)S(1)} %maximum_bitcast_fusion, pred[24,1536]{1,0:T(8,128)(4,1)S(1)} %get-tuple-element.28, bf16[8,1024]{1,0:T(8,128)(2,1)S(1)} %collective-permute-done.1, bf16[8,1024]{1,0:T(8,128)(2,1)S(1)} %copy-done.4, ...), kind=kOutput, calls=%fused_computation.169 | convolution fusion | flops 76529472 | bytes 1659648 | tf_op jit(solution)/shard_map/nkgd,skd->nkgs/dot_general | solution.py:27
  20.1 0.4 fusion.11
  20.5 0.4 fusion.16
  20.9 0.5 %fusion.90 = (f32[24,8]{0,1:T(8,128)S(1)}, f32[24,1,8,1536]{3,0,2,1:T(8,128)S(1)}) fusion(bf16[2,1536,128]{2,1,0:T(8,128)(2,1)S(1)} %collective-permute-done.2, pred[24,1536]{1,0:T(8,128)(4,1)S(1)} %get-tuple-element.27, bf16[8,1024]{1,0:T(8,128)(2,1)S(1)} %collective-permute-done.1, bf16[8,1024]{1,0:T(8,128)(2,1)S(1)} %copy-done.4, ...), kind=kOutput, calls=%fused_computation.168 | convolution fusion | flops 76529472 | bytes 1659648 | tf_op jit(solution)/shard_map/nkgd,skd->nkgs/dot_general | solution.py:27
  21.4 0.4 fusion.13
  21.8 0.4 fusion.9
  22.2 0.4 fusion.28
  22.6 0.4 fusion.7
  23.1 0.1 fusion.88
  23.1 0.1 copy.43
  23.2 0.1 fusion.87
  23.3 0.1 copy.44
  23.3 0.1 concatenate.45
  23.4 1.9 %collective-permute-start.4 = (f32[8,1040]{1,0:T(8,128)S(1)}, f32[8,1040]{1,0:T(8,128)S(1)}, u32[]{:S(2)}, u32[]{:S(2)}) collective-permute-start(f32[8,1040]{1,0:T(8,128)S(1)} %concatenate.45), channel_id=1, source_target_pairs={{0,8},{4,12},{8,16},{12,20},{16,24},{20,28},{24,32},{28,36},{32,40... | collective-permute-start | bytes 99848 | tf_op jit(solution)/shard_map/ppermute | solution.py:16
  25.4 0.1 copy.46
  25.4 0.1 copy.40
  25.6 0.1 concatenate.44
  25.6 6.0 %collective-permute-start.3 = (f32[8,1040]{1,0:T(8,128)S(1)}, f32[8,1040]{1,0:T(8,128)S(1)}, u32[]{:S(2)}, u32[]{:S(2)}) collective-permute-start(f32[8,1040]{1,0:T(8,128)S(1)} %concatenate.44), channel_id=1, source_target_pairs={{8,0},{12,4},{16,8},{20,12},{24,16},{28,20},{32,24},{36,28},{40,32... | collective-permute-start | bytes 99848 | tf_op jit(solution)/shard_map/ppermute | solution.py:16
  31.7 0.1 fusion.72
  31.8 0.1 copy.45
  31.8 1.5 %collective-permute-done.3 = f32[8,1040]{1,0:T(8,128)S(1)} collective-permute-done((f32[8,1040]{1,0:T(8,128)S(1)}, f32[8,1040]{1,0:T(8,128)S(1)}, u32[]{:S(2)}, u32[]{:S(2)}) %collective-permute-start.3) | collective-permute-done | bytes 33312 | tf_op jit(solution)/shard_map/ppermute | solution.py:16
  33.3 0.1 fusion.73
  33.4 0.1 copy.42
  33.4 0.1 copy.60
  33.5 0.1 copy.56
  33.7 0.1 copy.52
  33.7 0.1 fusion.78
  33.8 0.1 fusion.82
  33.9 3.5 %fusion.92 = (bf16[8,2048]{1,0:T(8,128)(2,1)}, f32[8,2048]{1,0:T(8,128)S(1)}) fusion(bf16[1024,2048]{1,0:T(8,128)(2,1)} %param.12, f32[8,8]{0,1:T(8,128)S(1)} %get-tuple-element.30, f32[8,1040]{1,0:T(8,128)S(1)} %collective-permute-done.4, f32[8,1040]{1,0:T(8,128)S(1)} %collective-permute-done.3, f32[24,1,8,128]{3,0,2,1:T(8,128)S(1)} %fusion.7, ...), kind=kOutput, calls=%fused_computation.170 | convolution fusion | flops 33644544 | bytes 4415488 | tf_op jit(solution)/shard_map/dot_general | solution.py:179
  37.4 4.5 %all-to-all-start = ((bf16[4,8,512]{2,1,0:T(8,128)(2,1)}), bf16[4,8,512]{2,1,0:T(8,128)(2,1)S(1)}, u32[]{:S(2)}, u32[]{:S(2)}) async-start(bf16[4,8,512]{2,1,0:T(8,128)(2,1)} %bitcast.63), calls=%async_computation | async-start | bytes 65536 | tf_op jit(solution)/shard_map/all_to_all | solution.py:185
  41.9 5.4 %all-to-all-done = bf16[4,8,512]{2,1,0:T(8,128)(2,1)S(1)} async-done(((bf16[4,8,512]{2,1,0:T(8,128)(2,1)}), bf16[4,8,512]{2,1,0:T(8,128)(2,1)S(1)}, u32[]{:S(2)}, u32[]{:S(2)}) %all-to-all-start) | async-done | bytes 32800 | tf_op jit(solution)/shard_map/all_to_all | solution.py:185
  47.3 0.1 select_reduce_fusion
  47.4 0.6 %add_convert_fusion = bf16[8,512]{1,0:T(8,128)(2,1)} fusion(f32[8,512]{1,0:T(8,128)S(1)} %select_reduce_fusion, f32[8,2048]{1,0:T(8,128)S(1)} %get-tuple-element.48, s32[]{:T(128)S(6)} %select_n.228), kind=kLoop, calls=%fused_computation.72 | loop fusion | flops 8192 | bytes 40964 | tf_op jit(solution)/shard_map/convert_element_type | solution.py:189
  (35 shorter events, 0.4 us)
Async XLA Ops:
  0.0 18.9 %collective-permute-start.1 = (bf16[8,1024]{1,0:T(8,128)(2,1)}, bf16[8,1024]{1,0:T(8,128)(2,1)S(1)}, u32[]{:S(2)}, u32[]{:S(2)}) collective-permute-start(bf16[8,1024]{1,0:T(8,128)(2,1)} %param.8), channel_id=1, source_target_pairs={{8,0},{12,4},{16,8},{20,12},{24,16},{28,20},{32,24},{36,28},{40,32... | collective-permute-start | bytes 49160 | tf_op jit(solution)/shard_map/ppermute | solution.py:16
  11.7 8.0 %collective-permute-start = (bf16[8,1024]{1,0:T(8,128)(2,1)}, bf16[8,1024]{1,0:T(8,128)(2,1)S(1)}, u32[]{:S(2)}, u32[]{:S(2)}) collective-permute-start(bf16[8,1024]{1,0:T(8,128)(2,1)} %param.8), channel_id=1, source_target_pairs={{0,8},{4,12},{8,16},{12,20},{16,24},{20,28},{24,32},{28,36},{32,40... | collective-permute-start | bytes 49160 | tf_op jit(solution)/shard_map/ppermute | solution.py:16
  14.6 3.2 %copy-start.1 = (s32[1024]{0:T(1024)S(1)}, s32[1024]{0:T(1024)}, u32[]{:S(2)}) copy-start(s32[1024]{0:T(1024)} %param.14) | copy-start | bytes 12292
  14.6 3.2 %copy-start.2 = (s32[1024]{0:T(1024)S(1)}, s32[1024]{0:T(1024)}, u32[]{:S(2)}) copy-start(s32[1024]{0:T(1024)} %param.15) | copy-start | bytes 12292
  14.6 3.2 %copy-start.3 = (s32[1024]{0:T(1024)S(1)}, s32[1024]{0:T(1024)}, u32[]{:S(2)}) copy-start(s32[1024]{0:T(1024)} %param.13) | copy-start | bytes 12292
  14.6 3.5 %copy-start = (bf16[8,2,128]{2,1,0:T(2,128)(2,1)S(1)}, bf16[8,2,128]{2,1,0:T(2,128)(2,1)}, u32[]{:S(2)}) copy-start(bf16[8,2,128]{2,1,0:T(2,128)(2,1)} %param.9) | copy-start | bytes 12292
  15.8 3.0 %copy-start.4 = (bf16[8,1024]{1,0:T(8,128)(2,1)S(1)}, bf16[8,1024]{1,0:T(8,128)(2,1)}, u32[]{:S(2)}) copy-start(bf16[8,1024]{1,0:T(8,128)(2,1)} %param.8) | copy-start | bytes 49156
  15.9 5.0 %collective-permute-start.2 = (bf16[2,1536,128]{2,1,0:T(8,128)(2,1)S(1)}, bf16[2,1536,128]{2,1,0:T(8,128)(2,1)S(1)}, u32[]{:S(2)}, u32[]{:S(2)}) collective-permute-start(bf16[2,1536,128]{2,1,0:T(8,128)(2,1)S(1)} %maximum_bitcast_fusion), channel_id=1, source_target_pairs={{0,4},{4,0},{8,12},{12,8},{16,20},{20,16},{24,28},{28,24},{32,36},... | collective-permute-start | bytes 2359304 | tf_op jit(solution)/shard_map/ppermute | solution.py:77
  23.4 8.2 %collective-permute-start.4 = (f32[8,1040]{1,0:T(8,128)S(1)}, f32[8,1040]{1,0:T(8,128)S(1)}, u32[]{:S(2)}, u32[]{:S(2)}) collective-permute-start(f32[8,1040]{1,0:T(8,128)S(1)} %concatenate.45), channel_id=1, source_target_pairs={{0,8},{4,12},{8,16},{12,20},{16,24},{20,28},{24,32},{28,36},{32,40... | collective-permute-start | bytes 99848 | tf_op jit(solution)/shard_map/ppermute | solution.py:16
  25.6 7.6 %collective-permute-start.3 = (f32[8,1040]{1,0:T(8,128)S(1)}, f32[8,1040]{1,0:T(8,128)S(1)}, u32[]{:S(2)}, u32[]{:S(2)}) collective-permute-start(f32[8,1040]{1,0:T(8,128)S(1)} %concatenate.44), channel_id=1, source_target_pairs={{8,0},{12,4},{16,8},{20,12},{24,16},{28,20},{32,24},{36,28},{40,32... | collective-permute-start | bytes 99848 | tf_op jit(solution)/shard_map/ppermute | solution.py:16
  37.4 9.9 %all-to-all-start = ((bf16[4,8,512]{2,1,0:T(8,128)(2,1)}), bf16[4,8,512]{2,1,0:T(8,128)(2,1)S(1)}, u32[]{:S(2)}, u32[]{:S(2)}) async-start(bf16[4,8,512]{2,1,0:T(8,128)(2,1)} %bitcast.63), calls=%async_computation | async-start | bytes 65536 | tf_op jit(solution)/shard_map/all_to_all | solution.py:185

commit v11 on v10

--- a/solution.py
+++ b/solution.py
@@ -16,12 +16,6 @@
     return lax.ppermute(block, axis, route)
 
 
-def split_weights(weights):
-    high = weights.astype(jnp.bfloat16)
-    low = (weights - high.astype(jnp.float32)).astype(jnp.bfloat16)
-    return high, low
-
-
 def partial_block(query_block, key_block, value_block, allowed):
     score_scale = query_block.shape[-1] ** (-0.5)
     scores = jnp.einsum(
@@ -33,11 +27,10 @@
     peaks = jnp.max(scores, axis=-1)
     weights = jnp.where(masked, jnp.exp(scores - peaks[..., None]), 0.0)
     totals = jnp.sum(weights, axis=-1)
-    high, low = split_weights(weights)
-    formula = "nkgs,skd->nkgd"
     weighted = jnp.einsum(
-        formula, high, value_block, preferred_element_type=jnp.float32
-    ) + jnp.einsum(formula, low, value_block, preferred_element_type=jnp.float32)
+        "nkgs,skd->nkgd", weights.astype(jnp.bfloat16), value_block,
+        preferred_element_type=jnp.float32,
+    )
     return (weighted, peaks, totals)
 
 

time: 48.4 us -> 47.5 us (0.981)
  matrix products: 6.23 us -> 5.35 us
    dot_general x4 -> x2, matrix products: 1.63 us -> 0.75 us  [partial_block(): jnp.einsum('nkgs,skd->nkgd', weights.astype(jnp.bfloat16), value_block, p...]
  transfers between devices with their start and end apart: 6 -> 6, of which waited for: 3 -> 3; matrix products, arithmetic and copies ran while one was open for 10% -> 9% of each run, Pallas kernels for 0% -> 0%
where the time goes in v11:
time: 47.5 us; the launch traced here: 47.1 us
  starting transfers between devices  27.9 us (59%)
  waiting for transfers between devices  7.65 us (16%)
  matrix products  5.35 us (11%)
  local copies, waits for them, and re-layouts  3.73 us (8%)
  other arithmetic  2.2 us (5%)
    ppermute x4, starting transfers between devices, shifted(): return lax.ppermute(block, axis, route)  21.5 us
    all_to_all x1, waiting for transfers between devices, local(): got = lax.all_to_all(chunks.astype(jnp.bfloat16), 'tp', 0, 0, tiled=True)  5.44 us
    all_to_all x1, starting transfers between devices, local(): got = lax.all_to_all(chunks.astype(jnp.bfloat16), 'tp', 0, 0, tiled=True)  4.47 us
    dot_general x1, matrix products, local(): jnp.dot(attended, out_weight, preferred_element_type=jnp.float32)  3.5 us
    ppermute x4, waiting for transfers between devices, shifted(): return lax.ppermute(block, axis, route)  2.2 us
    unnamed x13, local copies, waits for them, and re-layouts  2.17 us
    ppermute x1, starting transfers between devices, swapped(): return lax.ppermute(block, axis, [(i, i ^ 1) for i in devices])  1.92 us
    dot_general x2, matrix products, partial_block(): jnp.einsum('nkgd,skd->nkgs', query_block, key_block, preferred_element_ty...  0.98 us
  transfers between devices with their start and end apart: 6, of which 3 were waited for; matrix products, arithmetic and copies ran while one was open for 9% of the time, Pallas kernels for 0%

profile of v11, /device:TPU:6, one launch (start us, length us, event | category | flops | bytes accessed | tf_op | source)
XLA Modules:
  0.0 47.1 jit_solution(1646819854279863704)
XLA Ops:
  0.0 11.7 %collective-permute-start.1 = (bf16[8,1024]{1,0:T(8,128)(2,1)}, bf16[8,1024]{1,0:T(8,128)(2,1)S(1)}, u32[]{:S(2)}, u32[]{:S(2)}) collective-permute-start(bf16[8,1024]{1,0:T(8,128)(2,1)} %param.8), channel_id=1, source_target_pairs={{8,0},{12,4},{16,8},{20,12},{24,16},{28,20},{32,24},{36,28},{40,32... | collective-permute-start | bytes 49160 | tf_op jit(solution)/shard_map/ppermute | solution.py:16
  11.7 1.9 %collective-permute-start = (bf16[8,1024]{1,0:T(8,128)(2,1)}, bf16[8,1024]{1,0:T(8,128)(2,1)S(1)}, u32[]{:S(2)}, u32[]{:S(2)}) collective-permute-start(bf16[8,1024]{1,0:T(8,128)(2,1)} %param.8), channel_id=1, source_target_pairs={{0,8},{4,12},{8,16},{12,20},{16,24},{20,28},{24,32},{28,36},{32,40... | collective-permute-start | bytes 49160 | tf_op jit(solution)/shard_map/ppermute | solution.py:16
  13.6 1.0 %copy.91 = bf16[1,512,2,128]{3,1,2,0:T(8,128)(2,1)S(1)} copy(bf16[1,512,2,128]{3,2,1,0:T(2,128)(2,1)} %param.11) | data formatting | bytes 524288 | tf_op args[3]
  14.6 1.2 %copy.35 = bf16[8,128,2,128]{3,1,0,2:T(8,128)(2,1)S(1)} copy(bf16[8,128,2,128]{3,2,1,0:T(2,128)(2,1)} %param.10) | data formatting | bytes 1048576 | tf_op args[2]
  15.9 1.9 %collective-permute-start.2 = (bf16[2,1536,128]{2,1,0:T(8,128)(2,1)S(1)}, bf16[2,1536,128]{2,1,0:T(8,128)(2,1)S(1)}, u32[]{:S(2)}, u32[]{:S(2)}) collective-permute-start(bf16[2,1536,128]{2,1,0:T(8,128)(2,1)S(1)} %maximum_bitcast_fusion), channel_id=1, source_target_pairs={{0,4},{4,0},{8,12},{12,8},{16,20},{20,16},{24,28},{28,24},{32,36},... | collective-permute-start | bytes 2359304 | tf_op jit(solution)/shard_map/ppermute | solution.py:70
  17.9 0.1 pad_dynamic-slice_fusion
  18.0 0.1 fusion.75
  18.0 0.1 slice_bitcast_fusion.14
  18.1 0.1 pad_add_fusion.1
  18.2 0.1 compare_and_fusion.3
  18.3 0.1 fusion.69
  18.4 0.1 broadcast_bitcast_fusion
  18.4 0.1 broadcast_bitcast_fusion.1
  18.5 0.2 fusion.25
  18.8 0.1 fusion.49
  18.9 0.7 %collective-permute-done = bf16[8,1024]{1,0:T(8,128)(2,1)S(1)} collective-permute-done((bf16[8,1024]{1,0:T(8,128)(2,1)}, bf16[8,1024]{1,0:T(8,128)(2,1)S(1)}, u32[]{:S(2)}, u32[]{:S(2)}) %collective-permute-start) | collective-permute-done | bytes 16416 | tf_op jit(solution)/shard_map/ppermute | solution.py:16
  19.6 0.5 %fusion.77 = (f32[24,8]{0,1:T(8,128)S(1)}, f32[24,1,8,1536]{3,0,2,1:T(8,128)S(1)}) fusion(bf16[2,1536,128]{2,1,0:T(8,128)(2,1)S(1)} %maximum_bitcast_fusion, pred[24,1536]{1,0:T(8,128)(4,1)S(1)} %get-tuple-element.28, bf16[8,1024]{1,0:T(8,128)(2,1)S(1)} %collective-permute-done.1, bf16[8,1024]{1,0:T(8,128)(2,1)S(1)} %copy-done.4, ...), kind=kOutput, calls=%fused_computation.155 | convolution fusion | flops 76529472 | bytes 1659648 | tf_op jit(solution)/shard_map/nkgd,skd->nkgs/dot_general | solution.py:21
  20.1 0.4 fusion.9
  20.5 0.5 %fusion.76 = (f32[24,8]{0,1:T(8,128)S(1)}, f32[24,1,8,1536]{3,0,2,1:T(8,128)S(1)}) fusion(bf16[2,1536,128]{2,1,0:T(8,128)(2,1)S(1)} %collective-permute-done.2, pred[24,1536]{1,0:T(8,128)(4,1)S(1)} %get-tuple-element.27, bf16[8,1024]{1,0:T(8,128)(2,1)S(1)} %collective-permute-done.1, bf16[8,1024]{1,0:T(8,128)(2,1)S(1)} %copy-done.4, ...), kind=kOutput, calls=%fused_computation.154 | convolution fusion | flops 76529472 | bytes 1659648 | tf_op jit(solution)/shard_map/nkgd,skd->nkgs/dot_general | solution.py:21
  21.0 0.4 fusion.11
  21.4 0.4 fusion.7
  21.8 0.4 fusion.6
  22.2 0.1 fusion.74
  22.2 0.1 copy.43
  22.3 0.1 fusion.73
  22.4 0.1 copy.44
  22.4 0.1 concatenate.45
  22.5 1.9 %collective-permute-start.4 = (f32[8,1040]{1,0:T(8,128)S(1)}, f32[8,1040]{1,0:T(8,128)S(1)}, u32[]{:S(2)}, u32[]{:S(2)}) collective-permute-start(f32[8,1040]{1,0:T(8,128)S(1)} %concatenate.45), channel_id=1, source_target_pairs={{0,8},{4,12},{8,16},{12,20},{16,24},{20,28},{24,32},{28,36},{32,40... | collective-permute-start | bytes 99848 | tf_op jit(solution)/shard_map/ppermute | solution.py:16
  24.5 0.1 copy.46
  24.5 0.1 copy.40
  24.6 0.1 copy.41
  24.7 0.1 concatenate.44
  24.7 6.0 %collective-permute-start.3 = (f32[8,1040]{1,0:T(8,128)S(1)}, f32[8,1040]{1,0:T(8,128)S(1)}, u32[]{:S(2)}, u32[]{:S(2)}) collective-permute-start(f32[8,1040]{1,0:T(8,128)S(1)} %concatenate.44), channel_id=1, source_target_pairs={{8,0},{12,4},{16,8},{20,12},{24,16},{28,20},{32,24},{36,28},{40,32... | collective-permute-start | bytes 99848 | tf_op jit(solution)/shard_map/ppermute | solution.py:16
  30.8 0.1 fusion.60
  30.9 0.1 copy.45
  30.9 1.5 %collective-permute-done.3 = f32[8,1040]{1,0:T(8,128)S(1)} collective-permute-done((f32[8,1040]{1,0:T(8,128)S(1)}, f32[8,1040]{1,0:T(8,128)S(1)}, u32[]{:S(2)}, u32[]{:S(2)}) %collective-permute-start.3) | collective-permute-done | bytes 33312 | tf_op jit(solution)/shard_map/ppermute | solution.py:16
  32.4 0.1 fusion.61
  32.5 0.1 copy.42
  32.6 0.1 copy.56
  32.7 0.1 copy.59
  32.8 0.1 copy.52
  32.8 0.1 fusion.66
  32.9 0.1 fusion.70
  33.0 3.5 %fusion.78 = (bf16[8,2048]{1,0:T(8,128)(2,1)}, f32[8,2048]{1,0:T(8,128)S(1)}) fusion(bf16[1024,2048]{1,0:T(8,128)(2,1)} %param.12, f32[8,8]{0,1:T(8,128)S(1)} %get-tuple-element.30, f32[8,1040]{1,0:T(8,128)S(1)} %collective-permute-done.4, f32[8,1040]{1,0:T(8,128)S(1)} %collective-permute-done.3, f32[24,1,8,128]{3,0,2,1:T(8,128)S(1)} %fusion.6, ...), kind=kOutput, calls=%fused_computation.156 | convolution fusion | flops 33644544 | bytes 4415488 | tf_op jit(solution)/shard_map/dot_general | solution.py:172
  36.5 4.5 %all-to-all-start = ((bf16[4,8,512]{2,1,0:T(8,128)(2,1)}), bf16[4,8,512]{2,1,0:T(8,128)(2,1)S(1)}, u32[]{:S(2)}, u32[]{:S(2)}) async-start(bf16[4,8,512]{2,1,0:T(8,128)(2,1)} %bitcast.61), calls=%async_computation | async-start | bytes 65536 | tf_op jit(solution)/shard_map/all_to_all | solution.py:178
  41.0 5.4 %all-to-all-done = bf16[4,8,512]{2,1,0:T(8,128)(2,1)S(1)} async-done(((bf16[4,8,512]{2,1,0:T(8,128)(2,1)}), bf16[4,8,512]{2,1,0:T(8,128)(2,1)S(1)}, u32[]{:S(2)}, u32[]{:S(2)}) %all-to-all-start) | async-done | bytes 32800 | tf_op jit(solution)/shard_map/all_to_all | solution.py:178
  46.4 0.1 select_reduce_fusion
  46.5 0.6 %add_convert_fusion = bf16[8,512]{1,0:T(8,128)(2,1)} fusion(f32[8,512]{1,0:T(8,128)S(1)} %select_reduce_fusion, f32[8,2048]{1,0:T(8,128)S(1)} %get-tuple-element.48, s32[]{:T(128)S(6)} %select_n.228), kind=kLoop, calls=%fused_computation.60 | loop fusion | flops 8192 | bytes 40964 | tf_op jit(solution)/shard_map/convert_element_type | solution.py:182
  (33 shorter events, 0.3 us)
Async XLA Ops:
  0.0 18.9 %collective-permute-start.1 = (bf16[8,1024]{1,0:T(8,128)(2,1)}, bf16[8,1024]{1,0:T(8,128)(2,1)S(1)}, u32[]{:S(2)}, u32[]{:S(2)}) collective-permute-start(bf16[8,1024]{1,0:T(8,128)(2,1)} %param.8), channel_id=1, source_target_pairs={{8,0},{12,4},{16,8},{20,12},{24,16},{28,20},{32,24},{36,28},{40,32... | collective-permute-start | bytes 49160 | tf_op jit(solution)/shard_map/ppermute | solution.py:16
  11.7 8.0 %collective-permute-start = (bf16[8,1024]{1,0:T(8,128)(2,1)}, bf16[8,1024]{1,0:T(8,128)(2,1)S(1)}, u32[]{:S(2)}, u32[]{:S(2)}) collective-permute-start(bf16[8,1024]{1,0:T(8,128)(2,1)} %param.8), channel_id=1, source_target_pairs={{0,8},{4,12},{8,16},{12,20},{16,24},{20,28},{24,32},{28,36},{32,40... | collective-permute-start | bytes 49160 | tf_op jit(solution)/shard_map/ppermute | solution.py:16
  14.6 3.2 %copy-start.1 = (s32[1024]{0:T(1024)S(1)}, s32[1024]{0:T(1024)}, u32[]{:S(2)}) copy-start(s32[1024]{0:T(1024)} %param.14) | copy-start | bytes 12292
  14.6 3.2 %copy-start.2 = (s32[1024]{0:T(1024)S(1)}, s32[1024]{0:T(1024)}, u32[]{:S(2)}) copy-start(s32[1024]{0:T(1024)} %param.15) | copy-start | bytes 12292
  14.6 3.2 %copy-start.3 = (s32[1024]{0:T(1024)S(1)}, s32[1024]{0:T(1024)}, u32[]{:S(2)}) copy-start(s32[1024]{0:T(1024)} %param.13) | copy-start | bytes 12292
  15.8 2.9 %copy-start = (bf16[8,2,128]{2,1,0:T(2,128)(2,1)S(1)}, bf16[8,2,128]{2,1,0:T(2,128)(2,1)}, u32[]{:S(2)}) copy-start(bf16[8,2,128]{2,1,0:T(2,128)(2,1)} %param.9) | copy-start | bytes 12292
  15.8 3.0 %copy-start.4 = (bf16[8,1024]{1,0:T(8,128)(2,1)S(1)}, bf16[8,1024]{1,0:T(8,128)(2,1)}, u32[]{:S(2)}) copy-start(bf16[8,1024]{1,0:T(8,128)(2,1)} %param.8) | copy-start | bytes 49156
  15.9 4.6 %collective-permute-start.2 = (bf16[2,1536,128]{2,1,0:T(8,128)(2,1)S(1)}, bf16[2,1536,128]{2,1,0:T(8,128)(2,1)S(1)}, u32[]{:S(2)}, u32[]{:S(2)}) collective-permute-start(bf16[2,1536,128]{2,1,0:T(8,128)(2,1)S(1)} %maximum_bitcast_fusion), channel_id=1, source_target_pairs={{0,4},{4,0},{8,12},{12,8},{16,20},{20,16},{24,28},{28,24},{32,36},... | collective-permute-start | bytes 2359304 | tf_op jit(solution)/shard_map/ppermute | solution.py:70
  22.5 8.2 %collective-permute-start.4 = (f32[8,1040]{1,0:T(8,128)S(1)}, f32[8,1040]{1,0:T(8,128)S(1)}, u32[]{:S(2)}, u32[]{:S(2)}) collective-permute-start(f32[8,1040]{1,0:T(8,128)S(1)} %concatenate.45), channel_id=1, source_target_pairs={{0,8},{4,12},{8,16},{12,20},{16,24},{20,28},{24,32},{28,36},{32,40... | collective-permute-start | bytes 99848 | tf_op jit(solution)/shard_map/ppermute | solution.py:16
  24.7 7.6 %collective-permute-start.3 = (f32[8,1040]{1,0:T(8,128)S(1)}, f32[8,1040]{1,0:T(8,128)S(1)}, u32[]{:S(2)}, u32[]{:S(2)}) collective-permute-start(f32[8,1040]{1,0:T(8,128)S(1)} %concatenate.44), channel_id=1, source_target_pairs={{8,0},{12,4},{16,8},{20,12},{24,16},{28,20},{32,24},{36,28},{40,32... | collective-permute-start | bytes 99848 | tf_op jit(solution)/shard_map/ppermute | solution.py:16
  36.5 9.9 %all-to-all-start = ((bf16[4,8,512]{2,1,0:T(8,128)(2,1)}), bf16[4,8,512]{2,1,0:T(8,128)(2,1)S(1)}, u32[]{:S(2)}, u32[]{:S(2)}) async-start(bf16[4,8,512]{2,1,0:T(8,128)(2,1)} %bitcast.61), calls=%async_computation | async-start | bytes 65536 | tf_op jit(solution)/shard_map/all_to_all | solution.py:178

commit v12 on v8

--- a/solution.py
+++ b/solution.py
@@ -16,12 +16,6 @@
     return lax.ppermute(block, axis, route)
 
 
-def split_weights(weights):
-    high = weights.astype(jnp.bfloat16)
-    low = (weights - high.astype(jnp.float32)).astype(jnp.bfloat16)
-    return high, low
-
-
 def partial_block(query_block, key_block, value_block, allowed):
     score_scale = query_block.shape[-1] ** (-0.5)
     scores = jnp.einsum(
@@ -33,11 +27,10 @@
     peaks = jnp.max(scores, axis=-1)
     weights = jnp.where(masked, jnp.exp(scores - peaks[..., None]), 0.0)
     totals = jnp.sum(weights, axis=-1)
-    high, low = split_weights(weights)
-    formula = "nkgs,skd->nkgd"
     weighted = jnp.einsum(
-        formula, high, value_block, preferred_element_type=jnp.float32
-    ) + jnp.einsum(formula, low, value_block, preferred_element_type=jnp.float32)
+        "nkgs,skd->nkgd", weights.astype(jnp.bfloat16), value_block,
+        preferred_element_type=jnp.float32,
+    )
     return (weighted, peaks, totals)
 
 
@@ -136,8 +129,8 @@
     hood_slot = hood_beams % per_dev
 
     def allowed_for(holder, lengths):
-        column_len = jnp.repeat(lengths, own_size, total_repeat_length=cache_rows)
-        column_len = jnp.pad(column_len, (0, kv_count - cache_rows))
+        per_column = jnp.broadcast_to(lengths[:, None], (per_dev, own_size)).reshape(-1)
+        column_len = jnp.pad(per_column, (0, kv_count - cache_rows))
         own_ok = (
             (in_range & (parent_dev == holder))[:, None]
             & is_cache[None, :]

time: 64.3 us -> 52.1 us (0.81)
  other arithmetic: 12.5 us -> 2.31 us
  local copies, waits for them, and re-layouts: 5.57 us -> 4.34 us
  matrix products: 6.18 us -> 5.31 us
    select_n x2 -> x0, other arithmetic: 10.2 us -> none  [allowed_for(): column_len = jnp.repeat(lengths, own_size, total_repeat_length=cache_rows)]
    gather x2 -> x0, local copies, waits for them, and re-layouts: 1.37 us -> none  [allowed_for(): column_len = jnp.repeat(lengths, own_size, total_repeat_length=cache_rows)]
    dot_general x4 -> x2, matrix products: 1.63 us -> 0.77 us  [partial_block(): jnp.einsum('nkgs,skd->nkgd', weights.astype(jnp.bfloat16), value_block, p...]
  transfers between devices with their start and end apart: 6 -> 6, of which waited for: 2 -> 4; matrix products, arithmetic and copies ran while one was open for 27% -> 10% of each run, Pallas kernels for 0% -> 0%
where the time goes in v12:
time: 52.1 us; the launch traced here: 51.7 us
  starting transfers between devices  27.9 us (54%)
  waiting for transfers between devices  11.5 us (22%)
  matrix products  5.31 us (10%)
  local copies, waits for them, and re-layouts  4.34 us (8%)
  other arithmetic  2.31 us (4%)
    ppermute x4, starting transfers between devices, shifted(): return lax.ppermute(block, axis, route)  21.5 us
    ppermute x4, waiting for transfers between devices, shifted(): return lax.ppermute(block, axis, route)  5.87 us
    all_to_all x1, waiting for transfers between devices, local(): got = lax.all_to_all(chunks.astype(jnp.bfloat16), 'tp', 0, 0, tiled=True)  5.44 us
    all_to_all x1, starting transfers between devices, local(): got = lax.all_to_all(chunks.astype(jnp.bfloat16), 'tp', 0, 0, tiled=True)  4.47 us
    dot_general x1, matrix products, local(): jnp.dot(attended, out_weight, preferred_element_type=jnp.float32)  3.51 us
    unnamed x11, local copies, waits for them, and re-layouts  2.86 us
    ppermute x1, starting transfers between devices, swapped(): return lax.ppermute(block, axis, [(i, i ^ 1) for i in devices])  1.92 us
  transfers between devices with their start and end apart: 6, of which 4 were waited for; matrix products, arithmetic and copies ran while one was open for 10% of the time, Pallas kernels for 0%

profile of v12, /device:TPU:6, one launch (start us, length us, event | category | flops | bytes accessed | tf_op | source)
XLA Modules:
  0.0 51.7 jit_solution(10195210436738535463)
XLA Ops:
  0.0 11.7 %collective-permute-start.1 = (bf16[8,1024]{1,0:T(8,128)(2,1)}, bf16[8,1024]{1,0:T(8,128)(2,1)S(1)}, u32[]{:S(2)}, u32[]{:S(2)}) collective-permute-start(bf16[8,1024]{1,0:T(8,128)(2,1)} %param.8), channel_id=1, source_target_pairs={{8,0},{12,4},{16,8},{20,12},{24,16},{28,20},{32,24},{36,28},{40,32... | collective-permute-start | bytes 49160 | tf_op jit(solution)/shard_map/ppermute | solution.py:16
  11.7 1.9 %collective-permute-start = (bf16[8,1024]{1,0:T(8,128)(2,1)}, bf16[8,1024]{1,0:T(8,128)(2,1)S(1)}, u32[]{:S(2)}, u32[]{:S(2)}) collective-permute-start(bf16[8,1024]{1,0:T(8,128)(2,1)} %param.8), channel_id=1, source_target_pairs={{0,8},{4,12},{8,16},{12,20},{16,24},{20,28},{24,32},{28,36},{32,40... | collective-permute-start | bytes 49160 | tf_op jit(solution)/shard_map/ppermute | solution.py:16
  13.6 0.7 %copy.35 = bf16[8,2,128]{2,0,1:T(8,128)(2,1)S(1)} copy(bf16[8,2,128]{2,1,0:T(2,128)(2,1)} %param.9) | data formatting | bytes 8192 | tf_op args[1]
  14.3 1.0 %copy.76 = bf16[1,512,2,128]{3,1,2,0:T(8,128)(2,1)S(1)} copy(bf16[1,512,2,128]{3,2,1,0:T(2,128)(2,1)} %param.11) | data formatting | bytes 524288 | tf_op args[3]
  15.3 1.2 %copy.33 = bf16[8,128,2,128]{3,1,0,2:T(8,128)(2,1)S(1)} copy(bf16[8,128,2,128]{3,2,1,0:T(2,128)(2,1)} %param.10) | data formatting | bytes 1048576 | tf_op args[2]
  16.5 1.9 %collective-permute-start.2 = (bf16[2,1544,128]{2,1,0:T(8,128)(2,1)S(1)}, bf16[2,1544,128]{2,1,0:T(8,128)(2,1)S(1)}, u32[]{:S(2)}, u32[]{:S(2)}) collective-permute-start(bf16[2,1544,128]{2,1,0:T(8,128)(2,1)S(1)} %maximum_bitcast_fusion), channel_id=1, source_target_pairs={{0,4},{4,0},{8,12},{12,8},{16,20},{20,16},{24,28},{28,24},{32,36},... | collective-permute-start | bytes 2371592 | tf_op jit(solution)/shard_map/ppermute | solution.py:70
  18.6 0.1 pad_dynamic-slice_fusion
  18.6 0.1 fusion.71
  18.7 0.1 slice_bitcast_fusion.14
  18.9 0.1 fusion.65
  18.9 0.1 broadcast_bitcast_fusion
  19.0 0.1 broadcast_bitcast_fusion.1
  19.1 0.1 pad_add_fusion.1
  19.1 0.1 compare_and_fusion.6
  19.3 0.2 fusion.27
  19.5 0.1 collective-permute-done
  19.6 0.5 fusion.73
  20.1 0.4 fusion.8
  20.5 0.2 collective-permute-done.2
  20.7 0.5 %fusion.72 = (f32[24,8]{0,1:T(8,128)S(1)}, f32[24,1,8,1544]{3,0,2,1:T(8,128)S(1)}) fusion(bf16[2,1544,128]{2,1,0:T(8,128)(2,1)S(1)} %collective-permute-done.2, pred[24,1544]{1,0:T(8,128)(4,1)S(1)} %get-tuple-element.29, bf16[8,1024]{1,0:T(8,128)(2,1)S(1)} %collective-permute-done.1, bf16[8,1024]{1,0:T(8,128)(2,1)S(1)} %copy-done.3, ...), kind=kOutput, calls=%fused_computation.160 | convolution fusion | flops 76927296 | bytes 1670912 | tf_op jit(solution)/shard_map/nkgd,skd->nkgs/dot_general | solution.py:21
  21.3 0.4 fusion.11
  21.7 0.4 fusion.7
  22.1 0.4 fusion.6
  22.5 0.1 fusion.70
  22.6 0.1 copy.38
  22.6 0.1 fusion.69
  22.7 0.1 copy.39
  22.8 0.1 concatenate.84
  22.8 6.0 %collective-permute-start.3 = (f32[8,1040]{1,0:T(8,128)S(1)}, f32[8,1040]{1,0:T(8,128)S(1)}, u32[]{:S(2)}, u32[]{:S(2)}) collective-permute-start(f32[8,1040]{1,0:T(8,128)S(1)} %concatenate.84), channel_id=1, source_target_pairs={{8,0},{12,4},{16,8},{20,12},{24,16},{28,20},{32,24},{36,28},{40,32... | collective-permute-start | bytes 99848 | tf_op jit(solution)/shard_map/ppermute | solution.py:16
  28.9 0.1 copy.41
  28.9 0.1 copy.42
  29.0 0.1 concatenate.85
  29.1 1.9 %collective-permute-start.4 = (f32[8,1040]{1,0:T(8,128)S(1)}, f32[8,1040]{1,0:T(8,128)S(1)}, u32[]{:S(2)}, u32[]{:S(2)}) collective-permute-start(f32[8,1040]{1,0:T(8,128)S(1)} %concatenate.85), channel_id=1, source_target_pairs={{0,8},{4,12},{8,16},{12,20},{16,24},{20,28},{24,32},{28,36},{32,40... | collective-permute-start | bytes 99848 | tf_op jit(solution)/shard_map/ppermute | solution.py:16
  31.0 0.1 fusion.60
  31.1 0.1 copy.47
  31.2 0.1 copy.40
  31.3 5.8 %collective-permute-done.4 = f32[8,1040]{1,0:T(8,128)S(1)} collective-permute-done((f32[8,1040]{1,0:T(8,128)S(1)}, f32[8,1040]{1,0:T(8,128)S(1)}, u32[]{:S(2)}, u32[]{:S(2)}) %collective-permute-start.4) | collective-permute-done | bytes 33312 | tf_op jit(solution)/shard_map/ppermute | solution.py:16
  37.0 0.1 fusion.59
  37.1 0.1 copy.43
  37.2 0.1 copy.55
  37.3 0.1 copy.51
  37.4 0.1 fusion.66
  37.5 0.1 fusion.63
  37.6 3.5 %fusion.74 = (bf16[8,2048]{1,0:T(8,128)(2,1)}, f32[8,2048]{1,0:T(8,128)S(1)}) fusion(bf16[1024,2048]{1,0:T(8,128)(2,1)} %param.12, f32[8,8]{0,1:T(8,128)S(1)} %get-tuple-element.32, f32[8,1040]{1,0:T(8,128)S(1)} %collective-permute-done.4, f32[8,1040]{1,0:T(8,128)S(1)} %collective-permute-done.3, f32[24,1,8,128]{3,0,2,1:T(8,128)S(1)} %fusion.6, ...), kind=kOutput, calls=%fused_computation.162 | convolution fusion | flops 33628160 | bytes 4407296 | tf_op jit(solution)/shard_map/dot_general | solution.py:168
  41.1 4.5 %all-to-all-start = ((bf16[4,8,512]{2,1,0:T(8,128)(2,1)}), bf16[4,8,512]{2,1,0:T(8,128)(2,1)S(1)}, u32[]{:S(2)}, u32[]{:S(2)}) async-start(bf16[4,8,512]{2,1,0:T(8,128)(2,1)} %bitcast.53), calls=%async_computation | async-start | bytes 65536 | tf_op jit(solution)/shard_map/all_to_all | solution.py:174
  45.5 5.4 %all-to-all-done = bf16[4,8,512]{2,1,0:T(8,128)(2,1)S(1)} async-done(((bf16[4,8,512]{2,1,0:T(8,128)(2,1)}), bf16[4,8,512]{2,1,0:T(8,128)(2,1)S(1)}, u32[]{:S(2)}, u32[]{:S(2)}) %all-to-all-start) | async-done | bytes 32800 | tf_op jit(solution)/shard_map/all_to_all | solution.py:174
  51.0 0.1 select_reduce_fusion
  51.1 0.6 %add_convert_fusion = bf16[8,512]{1,0:T(8,128)(2,1)} fusion(f32[8,512]{1,0:T(8,128)S(1)} %select_reduce_fusion, f32[8,2048]{1,0:T(8,128)S(1)} %get-tuple-element.48, s32[]{:T(128)S(6)} %select_n.259), kind=kLoop, calls=%fused_computation.71 | loop fusion | flops 8192 | bytes 40964 | tf_op jit(solution)/shard_map/convert_element_type | solution.py:178
  (30 shorter events, 0.3 us)
Async XLA Ops:
  0.0 19.5 %collective-permute-start.1 = (bf16[8,1024]{1,0:T(8,128)(2,1)}, bf16[8,1024]{1,0:T(8,128)(2,1)S(1)}, u32[]{:S(2)}, u32[]{:S(2)}) collective-permute-start(bf16[8,1024]{1,0:T(8,128)(2,1)} %param.8), channel_id=1, source_target_pairs={{8,0},{12,4},{16,8},{20,12},{24,16},{28,20},{32,24},{36,28},{40,32... | collective-permute-start | bytes 49160 | tf_op jit(solution)/shard_map/ppermute | solution.py:16
  11.7 8.0 %collective-permute-start = (bf16[8,1024]{1,0:T(8,128)(2,1)}, bf16[8,1024]{1,0:T(8,128)(2,1)S(1)}, u32[]{:S(2)}, u32[]{:S(2)}) collective-permute-start(bf16[8,1024]{1,0:T(8,128)(2,1)} %param.8), channel_id=1, source_target_pairs={{0,8},{4,12},{8,16},{12,20},{16,24},{20,28},{24,32},{28,36},{32,40... | collective-permute-start | bytes 49160 | tf_op jit(solution)/shard_map/ppermute | solution.py:16
  15.3 3.2 %copy-start = (s32[1024]{0:T(1024)S(1)}, s32[1024]{0:T(1024)}, u32[]{:S(2)}) copy-start(s32[1024]{0:T(1024)} %param.14) | copy-start | bytes 12292
  15.3 3.2 %copy-start.1 = (s32[1024]{0:T(1024)S(1)}, s32[1024]{0:T(1024)}, u32[]{:S(2)}) copy-start(s32[1024]{0:T(1024)} %param.15) | copy-start | bytes 12292
  15.3 3.2 %copy-start.2 = (s32[1024]{0:T(1024)S(1)}, s32[1024]{0:T(1024)}, u32[]{:S(2)}) copy-start(s32[1024]{0:T(1024)} %param.13) | copy-start | bytes 12292
  15.3 4.3 %copy-start.3 = (bf16[8,1024]{1,0:T(8,128)(2,1)S(1)}, bf16[8,1024]{1,0:T(8,128)(2,1)}, u32[]{:S(2)}) copy-start(bf16[8,1024]{1,0:T(8,128)(2,1)} %param.8) | copy-start | bytes 49156
  16.5 4.2 %collective-permute-start.2 = (bf16[2,1544,128]{2,1,0:T(8,128)(2,1)S(1)}, bf16[2,1544,128]{2,1,0:T(8,128)(2,1)S(1)}, u32[]{:S(2)}, u32[]{:S(2)}) collective-permute-start(bf16[2,1544,128]{2,1,0:T(8,128)(2,1)S(1)} %maximum_bitcast_fusion), channel_id=1, source_target_pairs={{0,4},{4,0},{8,12},{12,8},{16,20},{20,16},{24,28},{28,24},{32,36},... | collective-permute-start | bytes 2371592 | tf_op jit(solution)/shard_map/ppermute | solution.py:70
  22.8 8.2 %collective-permute-start.3 = (f32[8,1040]{1,0:T(8,128)S(1)}, f32[8,1040]{1,0:T(8,128)S(1)}, u32[]{:S(2)}, u32[]{:S(2)}) collective-permute-start(f32[8,1040]{1,0:T(8,128)S(1)} %concatenate.84), channel_id=1, source_target_pairs={{8,0},{12,4},{16,8},{20,12},{24,16},{28,20},{32,24},{36,28},{40,32... | collective-permute-start | bytes 99848 | tf_op jit(solution)/shard_map/ppermute | solution.py:16
  29.1 8.0 %collective-permute-start.4 = (f32[8,1040]{1,0:T(8,128)S(1)}, f32[8,1040]{1,0:T(8,128)S(1)}, u32[]{:S(2)}, u32[]{:S(2)}) collective-permute-start(f32[8,1040]{1,0:T(8,128)S(1)} %concatenate.85), channel_id=1, source_target_pairs={{0,8},{4,12},{8,16},{12,20},{16,24},{20,28},{24,32},{28,36},{32,40... | collective-permute-start | bytes 99848 | tf_op jit(solution)/shard_map/ppermute | solution.py:16
  41.1 9.9 %all-to-all-start = ((bf16[4,8,512]{2,1,0:T(8,128)(2,1)}), bf16[4,8,512]{2,1,0:T(8,128)(2,1)S(1)}, u32[]{:S(2)}, u32[]{:S(2)}) async-start(bf16[4,8,512]{2,1,0:T(8,128)(2,1)} %bitcast.53), calls=%async_computation | async-start | bytes 65536 | tf_op jit(solution)/shard_map/all_to_all | solution.py:174

commit v13 on v11

--- a/solution.py
+++ b/solution.py
@@ -1,6 +1,9 @@
+import functools
+
 import jax
 import jax.numpy as jnp
 from jax import lax
+from jax.experimental import pallas as pl
 from jax.sharding import PartitionSpec as P
 
 HD = 128
@@ -63,6 +66,60 @@
     peaks = packed[:, width : width + k * g].reshape(n, k, g)
     totals = packed[:, width + k * g :].reshape(n, k, g)
     return (weighted, peaks, totals)
+
+
+def attend_kernel(q_ref, local_ref, mate_ref, row_ref, w_ref, peak_ref, total_ref, *, cache_rows, slot_shift):
+    queries = q_ref[...]
+    rows = row_ref[...]
+    shape = (queries.shape[0], local_ref.shape[1])
+    columns = lax.broadcasted_iota(jnp.int32, shape, 1)
+    is_cache = columns < cache_rows
+    column_slot = jnp.right_shift(columns, slot_shift)
+    column_pos = jnp.bitwise_and(columns, (1 << slot_shift) - 1)
+    score_scale = queries.shape[-1] ** (-0.5)
+
+    def part(kv_ref, base):
+        scores = lax.dot_general(
+            queries, kv_ref[0], (((1,), (1,)), ((), ())), preferred_element_type=jnp.float32
+        ) * score_scale
+        slot = rows[:, base : base + 1]
+        length = rows[:, base + 1 : base + 2]
+        prompt_ok = rows[:, base + 2 : base + 3] > 0
+        allowed = (is_cache & (column_slot == slot) & (column_pos < length)) | (
+            jnp.logical_not(is_cache) & prompt_ok
+        )
+        scores = jnp.where(allowed, scores, MASKED_SCORE)
+        peak = jnp.max(scores, axis=1, keepdims=True)
+        weights = jnp.where(allowed, jnp.exp(scores - peak), 0.0)
+        total = jnp.sum(weights, axis=1, keepdims=True)
+        weighted = jnp.dot(
+            weights.astype(jnp.bfloat16), kv_ref[1], preferred_element_type=jnp.float32
+        )
+        return weighted, jnp.where(total > 0, peak, MASKED_SCORE), total
+
+    w_local, p_local, t_local = part(local_ref, 0)
+    w_mate, p_mate, t_mate = part(mate_ref, 3)
+    top = jnp.maximum(p_local, p_mate)
+    s_local = jnp.where(t_local > 0, jnp.exp(p_local - top), 0.0)
+    s_mate = jnp.where(t_mate > 0, jnp.exp(p_mate - top), 0.0)
+    w_ref[...] = w_local * s_local + w_mate * s_mate
+    peak_ref[...] = jnp.broadcast_to(top, peak_ref.shape)
+    total_ref[...] = jnp.broadcast_to(t_local * s_local + t_mate * s_mate, total_ref.shape)
+
+
+def attend(queries, local_kv, mate_kv, row_params, cache_rows, own_size):
+    count, width = queries.shape
+    slot_shift = own_size.bit_length() - 1
+    assert 1 << slot_shift == own_size
+    body = functools.partial(attend_kernel, cache_rows=cache_rows, slot_shift=slot_shift)
+    return pl.pallas_call(
+        body,
+        out_shape=(
+            jax.ShapeDtypeStruct((count, width), jnp.float32),
+            jax.ShapeDtypeStruct((count, 128), jnp.float32),
+            jax.ShapeDtypeStruct((count, 128), jnp.float32),
+        ),
+    )(queries, local_kv, mate_kv, row_params)
 
 
 def swapped(block, axis):
@@ -117,33 +174,30 @@
         window[2], 3 * per_dev - 2 * per_dev * (dev_index % 2), per_dev
     )
     parent_dev = parent // per_dev
-    columns = jnp.arange(cache_rows, dtype=jnp.int32)
-    column_slot = columns // own_size
-
-    kv_count = cache_rows + prompt_size
-    all_columns = jnp.arange(kv_count, dtype=jnp.int32)
-    is_cache = all_columns < cache_rows
-    column_slot = all_columns // own_size
-    column_pos = all_columns % own_size
-
-    def allowed_for(holder, lengths):
-        per_column = jnp.broadcast_to(lengths[:, None], (per_dev, own_size)).reshape(-1)
-        column_len = jnp.pad(per_column, (0, prompt_size))
-        own_ok = (
-            (in_range & (parent_dev == holder))[:, None]
-            & is_cache[None, :]
-            & (column_slot[None, :] == (parent % per_dev)[:, None])
-            & (column_pos < column_len)[None, :]
-        )
-        prompt_ok = (in_range & (home == holder))[:, None] & ~is_cache[None, :]
-        return own_ok | prompt_ok
-
-    parts_here = []
-    for kv, holder, lengths in ((local_kv, dev_index, local_len), (mate_kv, mate_index, mate_len)):
-        keys = kv[0].reshape(kv_count, kv_heads_local, head_dim)
-        values = kv[1].reshape(kv_count, kv_heads_local, head_dim)
-        parts_here.append(partial_block(hood_queries, keys, values, allowed_for(holder, lengths)))
-    hood_part = merge_all(parts_here)
+    assert kv_heads_local == 1
+    slot_onehot = (parent % per_dev)[:, None] == slot_ids[None, :]
+    params = []
+    for holder, lengths in ((dev_index, local_len), (mate_index, mate_len)):
+        held = in_range & (parent_dev == holder)
+        params += [
+            jnp.where(held, parent % per_dev, -1),
+            jnp.sum(jnp.where(slot_onehot, lengths[None, :], 0), axis=1),
+            (in_range & (home == holder)).astype(jnp.int32),
+        ]
+    params += [jnp.zeros_like(parent), jnp.zeros_like(parent)]
+    beam_params = jnp.stack(params, axis=1)
+    row_params = jnp.broadcast_to(
+        beam_params[:, None, :], (hood_count, group_size, beam_params.shape[1])
+    ).reshape(hood_count * group_size, -1)
+    weighted_rows, peak_rows, total_rows = attend(
+        hood_queries.reshape(hood_count * group_size, head_dim),
+        local_kv, mate_kv, row_params, cache_rows, own_size,
+    )
+    hood_part = (
+        weighted_rows.reshape(hood_count, kv_heads_local, group_size, head_dim),
+        peak_rows[:, 0].reshape(hood_count, kv_heads_local, group_size),
+        total_rows[:, 0].reshape(hood_count, kv_heads_local, group_size),
+    )
 
     fresh_keys = new_kv[:, 0].reshape(per_dev, 1, kv_heads_local, head_dim)
     fresh_values = new_kv[:, 1].reshape(per_dev, 1, kv_heads_local, head_dim)

time: 47.5 us -> 57.1 us (1.20)
  local copies, waits for them, and re-layouts: 3.73 us -> 8.37 us
  Pallas kernels: 0 us -> 3.67 us
  waiting for transfers between devices: 7.65 us -> 11.2 us
  starting transfers between devices: 27.9 us -> 25.9 us
  matrix products: 5.35 us -> 3.61 us
  other arithmetic: 2.2 us -> 3.42 us
    pallas_call x0 -> x1, Pallas kernels: none -> 3.67 us  [attend(): pl.pallas_call(body, out_shape=(jax.ShapeDtypeStruct((count, width), jnp....]
    ppermute x4, waiting for transfers between devices: 2.2 us -> 5.72 us  [shifted(): return lax.ppermute(block, axis, route)]
    slice x6, local copies, waits for them, and re-layouts: 0.43 us -> 2.86 us  [rows(): return tuple((x[lo:lo + per_dev] for x in part))]
    ppermute x4, starting transfers between devices: 21.5 us -> 19.6 us  [shifted(): return lax.ppermute(block, axis, route)]
    dot_general x4 -> x0, matrix products: 1.73 us -> none  [the longest x2 0.98 us: partial_block(): jnp.einsum('nkgd,skd->nkgs', query_block, key_block, preferred_element_ty...]
    unnamed x13 -> x9, local copies, waits for them, and re-layouts: 2.17 us -> 3.05 us
    convert_element_type x1, other arithmetic: 0.01 us -> 0.77 us  [local(): fresh_values[:, 0, :, None, :].astype(jnp.float32)]
    another operation x0 -> x4, local copies, waits for them, and re-layouts: none -> 0.75 us  [the longest x1 0.65 us: local(): hood_queries.reshape(hood_count * group_size, head_dim)]
  transfers between devices with their start and end apart: 6 -> 6, of which waited for: 3 -> 2; matrix products, arithmetic and copies ran while one was open for 9% -> 12% of each run, Pallas kernels for 0% -> 0%
where the time goes in v13:
time: 57.1 us; the launch traced here: 56.3 us
  starting transfers between devices  25.9 us (45%)
  waiting for transfers between devices  11.2 us (20%)
  local copies, waits for them, and re-layouts  8.37 us (15%)
  Pallas kernels  3.67 us (6%)
  matrix products  3.61 us (6%)
  other arithmetic  3.42 us (6%)
    ppermute x4, starting transfers between devices, shifted(): return lax.ppermute(block, axis, route)  19.6 us
    ppermute x4, waiting for transfers between devices, shifted(): return lax.ppermute(block, axis, route)  5.72 us
    all_to_all x1, waiting for transfers between devices, local(): got = lax.all_to_all(chunks.astype(jnp.bfloat16), 'tp', 0, 0, tiled=True)  5.44 us
    all_to_all x1, starting transfers between devices, local(): got = lax.all_to_all(chunks.astype(jnp.bfloat16), 'tp', 0, 0, tiled=True)  4.46 us
    pallas_call x1, Pallas kernels, attend(): pl.pallas_call(body, out_shape=(jax.ShapeDtypeStruct((count, width), jnp....  3.67 us
    dot_general x1, matrix products, local(): jnp.dot(attended, out_weight, preferred_element_type=jnp.float32)  3.49 us
    unnamed x9, local copies, waits for them, and re-layouts  3.05 us
    slice x6, local copies, waits for them, and re-layouts, rows(): return tuple((x[lo:lo + per_dev] for x in part))  2.86 us
  transfers between devices with their start and end apart: 6, of which 2 were waited for; matrix products, arithmetic and copies ran while one was open for 12% of the time, Pallas kernels for 0%

profile of v13, /device:TPU:6, one launch (start us, length us, event | category | flops | bytes accessed | tf_op | source)
XLA Modules:
  0.0 56.3 jit_solution(5920897207666937452)
XLA Ops:
  0.0 3.9 %collective-permute-start = (bf16[8,1024]{1,0:T(8,128)(2,1)}, bf16[8,1024]{1,0:T(8,128)(2,1)S(1)}, u32[]{:S(2)}, u32[]{:S(2)}) collective-permute-start(bf16[8,1024]{1,0:T(8,128)(2,1)} %param.8), channel_id=1, source_target_pairs={{0,8},{4,12},{8,16},{12,20},{16,24},{20,28},{24,32},{28,36},{32,40... | collective-permute-start | bytes 49160 | tf_op jit(solution)/shard_map/ppermute | solution.py:19
  4.0 9.8 %collective-permute-start.1 = (bf16[8,1024]{1,0:T(8,128)(2,1)}, bf16[8,1024]{1,0:T(8,128)(2,1)S(1)}, u32[]{:S(2)}, u32[]{:S(2)}) collective-permute-start(bf16[8,1024]{1,0:T(8,128)(2,1)} %param.8), channel_id=1, source_target_pairs={{8,0},{12,4},{16,8},{20,12},{24,16},{28,20},{32,24},{36,28},{40,32... | collective-permute-start | bytes 49160 | tf_op jit(solution)/shard_map/ppermute | solution.py:19
  13.7 1.1 %copy.46 = bf16[8,128,2,128]{3,1,0,2:T(8,128)(2,1)S(1)} copy(bf16[8,128,2,128]{3,2,1,0:T(2,128)(2,1)} %param.10) | data formatting | bytes 1048576 | tf_op args[2]
  14.9 1.0 %copy.64 = bf16[1,512,2,128]{3,1,2,0:T(8,128)(2,1)S(1)} copy(bf16[1,512,2,128]{3,2,1,0:T(2,128)(2,1)} %param.11) | data formatting | bytes 524288 | tf_op args[3]
  15.9 0.1 maximum_bitcast_fusion.local_ref
  15.9 1.9 %collective-permute-start.2 = (bf16[2,1536,128]{2,1,0:T(8,128)(2,1)S(1)}, bf16[2,1536,128]{2,1,0:T(8,128)(2,1)S(1)}, u32[]{:S(2)}, u32[]{:S(2)}) collective-permute-start(bf16[2,1536,128]{2,1,0:T(8,128)(2,1)S(1)} %maximum_bitcast_fusion.local_ref), channel_id=1, source_target_pairs={{0,4},{4,0},{8,12},{12,8},{16,20},{20,16},{24,28},{28,24},{32,36},... | collective-permute-start | bytes 2359304 | tf_op jit(solution)/shard_map/ppermute | solution.py:127
  17.9 0.7 %pad_add_fusion = s32[3,1024]{1,0:T(4,128)S(1)} fusion(s32[1,1024]{1,0:T(1,128)} %bitcast.104, s32[1,1024]{1,0:T(1,128)} %bitcast.105, s32[1,1024]{1,0:T(1,128)} %bitcast.106), kind=kLoop, calls=%fused_computation.21 | loop fusion | flops 6144 | bytes 24576 | tf_op jit(solution)/shard_map/stack | solution.py:164
  18.6 0.1 pad_dynamic-slice_fusion
  18.7 0.1 fusion.19
  18.8 0.1 pad_add_fusion.1
  18.9 0.1 and_convert_fusion
  19.0 0.1 fusion.16
  19.1 0.1 select_reduce_fusion.1
  19.2 0.1 copy.48
  19.3 0.6 %broadcast_bitcast_fusion.row_ref = s32[192,8]{1,0:T(8,128)} fusion(s32[24,8]{1,0:T(8,128)S(1)} %copy.48), kind=kLoop, calls=%fused_computation.4 | loop fusion | bytes 6912 | tf_op jit(solution)/shard_map/reshape | solution.py:191
  19.9 0.8 %slice_convert_fusion = (f32[8,1,128]{2,1,0:T(1,128)S(1)}, bf16[8,1,128]{2,1,0:T(2,128)(2,1)S(1)}) fusion(bf16[8,2,128]{2,1,0:T(2,128)(2,1)} %param.9), kind=kLoop, calls=%fused_computation.42 | loop fusion | flops 1024 | bytes 10240 | tf_op jit(solution)/shard_map/convert_element_type | solution.py:208
  20.7 0.0 collective-permute-done
  20.7 0.7 %pad_maximum_fusion = bf16[24,1024]{1,0:T(8,128)(2,1)S(1)} fusion(bf16[8,1024]{1,0:T(8,128)(2,1)S(1)} %collective-permute-done.1, bf16[8,1024]{1,0:T(8,128)(2,1)} %param.8, bf16[8,1024]{1,0:T(8,128)(2,1)S(1)} %collective-permute-done), kind=kLoop, calls=%fused_computation.3 | loop fusion | flops 147456 | bytes 98304 | tf_op jit(solution)/shard_map/concatenate | solution.py:154
  21.4 0.6 %reshape_reshape.3.q_ref = bf16[192,128]{1,0:T(8,128)(2,1)} reshape(bf16[24,1024]{1,0:T(8,128)(2,1)S(1)} %pad_maximum_fusion) | data formatting | bytes 98304 | tf_op jit(solution)/shard_map/reshape;reshape | solution.py:193
  22.1 0.9 %copy-done.1 = bf16[2,1536,128]{2,1,0:T(8,128)(2,1)} copy-done((bf16[2,1536,128]{2,1,0:T(8,128)(2,1)}, bf16[2,1536,128]{2,1,0:T(8,128)(2,1)S(1)}, u32[]{:S(2)}) %copy-start.1) | copy-done | bytes 786456
  23.0 3.7 %shard_map.82 = (f32[192,128]{1,0:T(8,128)}, f32[192,128]{1,0:T(8,128)}, f32[192,128]{1,0:T(8,128)}) custom-call(bf16[192,128]{1,0:T(8,128)(2,1)} %reshape_reshape.3.q_ref, bf16[2,1536,128]{2,1,0:T(8,128)(2,1)} %copy-done, bf16[2,1536,128]{2,1,0:T(8,128)(2,1)} %copy-done.1, s32[192,8]{1,0:T(8,128)} %broadcast_bitcast_fusion.row_ref), custom_call_target="tpu_custom_call" | custom-call | tf_op jit(solution)/shard_map/pallas_call | solution.py:115
  26.7 0.8 %fusion.18 = (f32[64,128]{1,0:T(8,128)S(1)}, f32[64,128]{1,0:T(8,128)S(1)}, f32[64,128]{1,0:T(8,128)S(1)}) fusion(f32[192,128]{1,0:T(8,128)} %get-tuple-element.10), kind=kLoop, calls=%fused_computation.76 | loop fusion | bytes 196608 | tf_op jit(solution)/shard_map/slice | solution.py:214
  27.5 0.9 %slice_reduce_fusion.4 = (f32[64]{0:T(128)S(1)}, f32[64]{0:T(128)S(1)}, f32[64]{0:T(128)S(1)}) fusion(f32[192,128]{1,0:T(8,128)} %get-tuple-element.9), kind=kLoop, calls=%fused_computation.16 | loop fusion | bytes 1536 | tf_op jit(solution)/shard_map/slice | solution.py:214
  28.4 0.1 reshape.516
  28.5 0.9 %slice_reduce_fusion.5 = (f32[64]{0:T(128)S(1)}, f32[64]{0:T(128)S(1)}, f32[64]{0:T(128)S(1)}) fusion(f32[192,128]{1,0:T(8,128)} %get-tuple-element.8), kind=kLoop, calls=%fused_computation.17 | loop fusion | bytes 1536 | tf_op jit(solution)/shard_map/slice | solution.py:214
  29.5 0.1 reshape.517
  29.5 0.1 concatenate.65
  29.6 3.9 %collective-permute-start.3 = (f32[8,1040]{1,0:T(8,128)S(1)}, f32[8,1040]{1,0:T(8,128)S(1)}, u32[]{:S(2)}, u32[]{:S(2)}) collective-permute-start(f32[8,1040]{1,0:T(8,128)S(1)} %concatenate.65), channel_id=1, source_target_pairs={{8,0},{12,4},{16,8},{20,12},{24,16},{28,20},{32,24},{36,28},{40,32... | collective-permute-start | bytes 99848 | tf_op jit(solution)/shard_map/ppermute | solution.py:19
  33.6 0.1 reshape.519
  33.6 0.1 reshape.520
  33.7 0.1 concatenate.66
  33.8 1.9 %collective-permute-start.4 = (f32[8,1040]{1,0:T(8,128)S(1)}, f32[8,1040]{1,0:T(8,128)S(1)}, u32[]{:S(2)}, u32[]{:S(2)}) collective-permute-start(f32[8,1040]{1,0:T(8,128)S(1)} %concatenate.66), channel_id=1, source_target_pairs={{0,8},{4,12},{8,16},{12,20},{16,24},{20,28},{24,32},{28,36},{32,40... | collective-permute-start | bytes 99848 | tf_op jit(solution)/shard_map/ppermute | solution.py:19
  35.7 0.1 fusion.13
  35.9 0.1 slice.105
  35.9 0.1 slice.107
  36.0 5.7 %collective-permute-done.4 = f32[8,1040]{1,0:T(8,128)S(1)} collective-permute-done((f32[8,1040]{1,0:T(8,128)S(1)}, f32[8,1040]{1,0:T(8,128)S(1)}, u32[]{:S(2)}, u32[]{:S(2)}) %collective-permute-start.4) | collective-permute-done | bytes 33312 | tf_op jit(solution)/shard_map/ppermute | solution.py:19
  41.8 0.1 maximum_maximum_fusion
  41.8 0.1 multiply_add_fusion
  41.9 0.1 copy.49
  42.0 0.1 copy.50
  42.0 0.1 copy.51
  42.1 0.1 copy.52
  42.2 0.1 copy.53
  42.3 3.5 %fusion.20 = (bf16[8,2048]{1,0:T(8,128)(2,1)}, f32[8,2048]{1,0:T(8,128)S(1)}) fusion(bf16[1024,2048]{1,0:T(8,128)(2,1)} %param.12, f32[8,1040]{1,0:T(8,128)S(1)} %collective-permute-done.4, f32[8,1040]{1,0:T(8,128)S(1)} %collective-permute-done.3, f32[8,1024]{1,0:T(8,128)S(1)} %slice.119, f32[8,8]{0,1:T(8,128)S(1)} %copy.53, f32[8,8]{0,1:T(8,128)S(1)} %copy.52, ...), kind=kOutput, calls=%fused_computation.78 | convolution fusion | flops 33644544 | bytes 4415488 | tf_op jit(solution)/shard_map/dot_general | solution.py:226
  45.7 4.5 %all-to-all-start = ((bf16[4,8,512]{2,1,0:T(8,128)(2,1)}), bf16[4,8,512]{2,1,0:T(8,128)(2,1)S(1)}, u32[]{:S(2)}, u32[]{:S(2)}) async-start(bf16[4,8,512]{2,1,0:T(8,128)(2,1)} %bitcast.29), calls=%async_computation | async-start | bytes 65536 | tf_op jit(solution)/shard_map/all_to_all | solution.py:232
  50.2 5.4 %all-to-all-done = bf16[4,8,512]{2,1,0:T(8,128)(2,1)S(1)} async-done(((bf16[4,8,512]{2,1,0:T(8,128)(2,1)}), bf16[4,8,512]{2,1,0:T(8,128)(2,1)S(1)}, u32[]{:S(2)}, u32[]{:S(2)}) %all-to-all-start) | async-done | bytes 32800 | tf_op jit(solution)/shard_map/all_to_all | solution.py:232
  55.7 0.1 select_reduce_fusion
  55.7 0.6 %add_convert_fusion = bf16[8,512]{1,0:T(8,128)(2,1)} fusion(f32[8,512]{1,0:T(8,128)S(1)} %select_reduce_fusion, f32[8,2048]{1,0:T(8,128)S(1)} %get-tuple-element.43, s32[]{:T(128)S(6)} %select_n.148), kind=kLoop, calls=%fused_computation.22 | loop fusion | flops 8192 | bytes 40964 | tf_op jit(solution)/shard_map/convert_element_type | solution.py:236
  (22 shorter events, 0.2 us)
Async XLA Ops:
  0.0 35.7 %copy-start.2 = (bf16[8,1024]{1,0:T(8,128)(2,1)S(1)}, bf16[8,1024]{1,0:T(8,128)(2,1)}, u32[]{:S(2)}) copy-start(bf16[8,1024]{1,0:T(8,128)(2,1)} %param.8) | copy-start | bytes 49156
  0.0 20.7 %collective-permute-start = (bf16[8,1024]{1,0:T(8,128)(2,1)}, bf16[8,1024]{1,0:T(8,128)(2,1)S(1)}, u32[]{:S(2)}, u32[]{:S(2)}) collective-permute-start(bf16[8,1024]{1,0:T(8,128)(2,1)} %param.8), channel_id=1, source_target_pairs={{0,8},{4,12},{8,16},{12,20},{16,24},{20,28},{24,32},{28,36},{32,40... | collective-permute-start | bytes 49160 | tf_op jit(solution)/shard_map/ppermute | solution.py:19
  4.0 16.8 %collective-permute-start.1 = (bf16[8,1024]{1,0:T(8,128)(2,1)}, bf16[8,1024]{1,0:T(8,128)(2,1)S(1)}, u32[]{:S(2)}, u32[]{:S(2)}) collective-permute-start(bf16[8,1024]{1,0:T(8,128)(2,1)} %param.8), channel_id=1, source_target_pairs={{8,0},{12,4},{16,8},{20,12},{24,16},{28,20},{32,24},{36,28},{40,32... | collective-permute-start | bytes 49160 | tf_op jit(solution)/shard_map/ppermute | solution.py:19
  15.9 6.2 %copy-start = (bf16[2,1536,128]{2,1,0:T(8,128)(2,1)}, bf16[2,1536,128]{2,1,0:T(8,128)(2,1)S(1)}, u32[]{:S(2)}) copy-start(bf16[2,1536,128]{2,1,0:T(8,128)(2,1)S(1)} %maximum_bitcast_fusion.local_ref) | copy-start | bytes 2359300
  15.9 6.2 %collective-permute-start.2 = (bf16[2,1536,128]{2,1,0:T(8,128)(2,1)S(1)}, bf16[2,1536,128]{2,1,0:T(8,128)(2,1)S(1)}, u32[]{:S(2)}, u32[]{:S(2)}) collective-permute-start(bf16[2,1536,128]{2,1,0:T(8,128)(2,1)S(1)} %maximum_bitcast_fusion.local_ref), channel_id=1, source_target_pairs={{0,4},{4,0},{8,12},{12,8},{16,20},{20,16},{24,28},{28,24},{32,36},... | collective-permute-start | bytes 2359304 | tf_op jit(solution)/shard_map/ppermute | solution.py:127
  22.1 0.9 %copy-start.1 = (bf16[2,1536,128]{2,1,0:T(8,128)(2,1)}, bf16[2,1536,128]{2,1,0:T(8,128)(2,1)S(1)}, u32[]{:S(2)}) copy-start(bf16[2,1536,128]{2,1,0:T(8,128)(2,1)S(1)} %collective-permute-done.2.mate_ref) | copy-start | bytes 2359300
  29.6 6.4 %collective-permute-start.3 = (f32[8,1040]{1,0:T(8,128)S(1)}, f32[8,1040]{1,0:T(8,128)S(1)}, u32[]{:S(2)}, u32[]{:S(2)}) collective-permute-start(f32[8,1040]{1,0:T(8,128)S(1)} %concatenate.65), channel_id=1, source_target_pairs={{8,0},{12,4},{16,8},{20,12},{24,16},{28,20},{32,24},{36,28},{40,32... | collective-permute-start | bytes 99848 | tf_op jit(solution)/shard_map/ppermute | solution.py:19
  33.8 8.0 %collective-permute-start.4 = (f32[8,1040]{1,0:T(8,128)S(1)}, f32[8,1040]{1,0:T(8,128)S(1)}, u32[]{:S(2)}, u32[]{:S(2)}) collective-permute-start(f32[8,1040]{1,0:T(8,128)S(1)} %concatenate.66), channel_id=1, source_target_pairs={{0,8},{4,12},{8,16},{12,20},{16,24},{20,28},{24,32},{28,36},{32,40... | collective-permute-start | bytes 99848 | tf_op jit(solution)/shard_map/ppermute | solution.py:19
  45.7 9.9 %all-to-all-start = ((bf16[4,8,512]{2,1,0:T(8,128)(2,1)}), bf16[4,8,512]{2,1,0:T(8,128)(2,1)S(1)}, u32[]{:S(2)}, u32[]{:S(2)}) async-start(bf16[4,8,512]{2,1,0:T(8,128)(2,1)} %bitcast.29), calls=%async_computation | async-start | bytes 65536 | tf_op jit(solution)/shard_map/all_to_all | solution.py:232

commit v14 on v11

--- a/solution.py
+++ b/solution.py
@@ -138,12 +138,22 @@
         prompt_ok = (in_range & (home == holder))[:, None] & ~is_cache[None, :]
         return own_ok | prompt_ok
 
-    parts_here = []
+    def pick_rows(x, groups):
+        return jnp.concatenate([x[g * per_dev : (g + 1) * per_dev] for g in groups], axis=0)
+
+    send_parts = []
+    own_parts = []
     for kv, holder, lengths in ((local_kv, dev_index, local_len), (mate_kv, mate_index, mate_len)):
         keys = kv[0].reshape(kv_count, kv_heads_local, head_dim)
         values = kv[1].reshape(kv_count, kv_heads_local, head_dim)
-        parts_here.append(partial_block(hood_queries, keys, values, allowed_for(holder, lengths)))
-    hood_part = merge_all(parts_here)
+        allowed = allowed_for(holder, lengths)
+        send_parts.append(
+            partial_block(pick_rows(hood_queries, (0, 2)), keys, values, pick_rows(allowed, (0, 2)))
+        )
+        own_parts.append(
+            partial_block(pick_rows(hood_queries, (1,)), keys, values, pick_rows(allowed, (1,)))
+        )
+    send_part = merge_all(send_parts)
 
     fresh_keys = new_kv[:, 0].reshape(per_dev, 1, kv_heads_local, head_dim)
     fresh_values = new_kv[:, 1].reshape(per_dev, 1, kv_heads_local, head_dim)
@@ -159,10 +169,10 @@
     def rows(part, lo):
         return tuple(x[lo : lo + per_dev] for x in part)
 
-    back_from_next = unpack(shifted(pack(rows(hood_part, 0)), "req", 2), shape4)
-    back_from_prev = unpack(shifted(pack(rows(hood_part, 2 * per_dev)), "req", -2), shape4)
+    back_from_next = unpack(shifted(pack(rows(send_part, 0)), "req", 2), shape4)
+    back_from_prev = unpack(shifted(pack(rows(send_part, per_dev)), "req", -2), shape4)
     weighted, _, totals = merge_all(
-        [fresh_part, rows(hood_part, per_dev), back_from_next, back_from_prev]
+        [fresh_part] + own_parts + [back_from_next, back_from_prev]
     )
     attended = (
         (weighted / totals[..., None])

time: 47.5 us -> 53.4 us (1.12)
  matrix products: 5.35 us -> 9.45 us
  waiting for transfers between devices: 7.65 us -> 9.9 us
  starting transfers between devices: 27.9 us -> 26.1 us
  other arithmetic: 2.2 us -> 3.83 us
  local copies, waits for them, and re-layouts: 3.73 us -> 3.19 us
    dot_general x2 -> x4, matrix products: 0.98 us -> 4.11 us  [partial_block(): jnp.einsum('nkgd,skd->nkgs', query_block, key_block, preferred_element_ty...]
    dot_general x2 -> x4, matrix products: 0.75 us -> 3.23 us  [partial_block(): jnp.einsum('nkgs,skd->nkgd', weights.astype(jnp.bfloat16), value_block, p...]
    ppermute x4, waiting for transfers between devices: 2.2 us -> 4.45 us  [shifted(): return lax.ppermute(block, axis, route)]
    dot_general x1, matrix products: 3.5 us -> 1.27 us  [local(): jnp.dot(attended, out_weight, preferred_element_type=jnp.float32)]
    ppermute x4, starting transfers between devices: 21.5 us -> 19.7 us  [shifted(): return lax.ppermute(block, axis, route)]
    convert_element_type x1, other arithmetic: 0.01 us -> 0.77 us  [local(): fresh_values[:, 0, :, None, :].astype(jnp.float32)]
    another operation x1, other arithmetic: 0.02 us -> 0.74 us  [local(): jnp.stack([parents, first_beam, own_len])]
    dot_general x1, matrix products: 0.12 us -> 0.84 us  [local(): jnp.einsum('nkgd,nskd->nkgs', query_block, fresh_keys, preferred_element_...]
  transfers between devices with their start and end apart: 6 -> 6, of which waited for: 3 -> 2; matrix products, arithmetic and copies ran while one was open for 9% -> 17% of each run, Pallas kernels for 0% -> 0%
where the time goes in v14:
time: 53.4 us; the launch traced here: 52.7 us
  starting transfers between devices  26.1 us (49%)
  waiting for transfers between devices  9.9 us (19%)
  matrix products  9.45 us (18%)
  other arithmetic  3.83 us (7%)
  local copies, waits for them, and re-layouts  3.19 us (6%)
    ppermute x4, starting transfers between devices, shifted(): return lax.ppermute(block, axis, route)  19.7 us
    all_to_all x1, waiting for transfers between devices, local(): got = lax.all_to_all(chunks.astype(jnp.bfloat16), 'tp', 0, 0, tiled=True)  5.44 us
    all_to_all x1, starting transfers between devices, local(): got = lax.all_to_all(chunks.astype(jnp.bfloat16), 'tp', 0, 0, tiled=True)  4.47 us
    ppermute x4, waiting for transfers between devices, shifted(): return lax.ppermute(block, axis, route)  4.45 us
    dot_general x4, matrix products, partial_block(): jnp.einsum('nkgd,skd->nkgs', query_block, key_block, preferred_element_ty...  4.11 us
    dot_general x4, matrix products, partial_block(): jnp.einsum('nkgs,skd->nkgd', weights.astype(jnp.bfloat16), value_block, p...  3.23 us
    unnamed x9, local copies, waits for them, and re-layouts  2.15 us
    ppermute x1, starting transfers between devices, swapped(): return lax.ppermute(block, axis, [(i, i ^ 1) for i in devices])  1.92 us
  transfers between devices with their start and end apart: 6, of which 2 were waited for; matrix products, arithmetic and copies ran while one was open for 17% of the time, Pallas kernels for 0%

profile of v14, /device:TPU:6, one launch (start us, length us, event | category | flops | bytes accessed | tf_op | source)
XLA Modules:
  0.0 52.7 jit_solution(940686001311859849)
XLA Ops:
  0.0 3.8 %collective-permute-start.1 = (bf16[8,1024]{1,0:T(8,128)(2,1)}, bf16[8,1024]{1,0:T(8,128)(2,1)S(1)}, u32[]{:S(2)}, u32[]{:S(2)}) collective-permute-start(bf16[8,1024]{1,0:T(8,128)(2,1)} %param.8), channel_id=1, source_target_pairs={{0,8},{4,12},{8,16},{12,20},{16,24},{20,28},{24,32},{28,36},{32,40... | collective-permute-start | bytes 49160 | tf_op jit(solution)/shard_map/ppermute | solution.py:16
  3.8 9.8 %collective-permute-start.2 = (bf16[8,1024]{1,0:T(8,128)(2,1)}, bf16[8,1024]{1,0:T(8,128)(2,1)S(1)}, u32[]{:S(2)}, u32[]{:S(2)}) collective-permute-start(bf16[8,1024]{1,0:T(8,128)(2,1)} %param.8), channel_id=1, source_target_pairs={{8,0},{12,4},{16,8},{20,12},{24,16},{28,20},{32,24},{36,28},{40,32... | collective-permute-start | bytes 49160 | tf_op jit(solution)/shard_map/ppermute | solution.py:16
  13.6 1.1 %copy.18 = bf16[8,128,2,128]{3,1,0,2:T(8,128)(2,1)S(1)} copy(bf16[8,128,2,128]{3,2,1,0:T(2,128)(2,1)} %param.10) | data formatting | bytes 1048576 | tf_op args[2]
  14.7 1.0 %copy.54 = bf16[1,512,2,128]{3,1,2,0:T(8,128)(2,1)S(1)} copy(bf16[1,512,2,128]{3,2,1,0:T(2,128)(2,1)} %param.11) | data formatting | bytes 524288 | tf_op args[3]
  15.7 0.1 maximum_bitcast_fusion
  15.8 1.9 %collective-permute-start = (bf16[2,1536,128]{2,1,0:T(8,128)(2,1)S(1)}, bf16[2,1536,128]{2,1,0:T(8,128)(2,1)}, u32[]{:S(2)}, u32[]{:S(2)}) collective-permute-start(bf16[2,1536,128]{2,1,0:T(8,128)(2,1)S(1)} %maximum_bitcast_fusion), channel_id=1, source_target_pairs={{0,4},{4,0},{8,12},{12,8},{16,20},{20,16},{24,28},{28,24},{32,36},... | collective-permute-start | bytes 2359304 | tf_op jit(solution)/shard_map/ppermute | solution.py:70
  17.7 0.7 %pad_add_fusion.2 = s32[3,1024]{1,0:T(4,128)S(1)} fusion(s32[1,1024]{1,0:T(1,128)} %bitcast.262, s32[1,1024]{1,0:T(1,128)} %bitcast.263, s32[1,1024]{1,0:T(1,128)} %bitcast.264), kind=kLoop, calls=%fused_computation.85 | loop fusion | flops 6144 | bytes 24576 | tf_op jit(solution)/shard_map/stack | solution.py:107
  18.5 0.1 pad_dynamic-slice_fusion
  18.6 0.1 fusion.90
  18.6 0.1 slice_bitcast_fusion.16
  18.7 0.1 pad_add_fusion.3
  18.8 0.1 compare_and_fusion.3
  18.9 0.1 fusion.79
  19.0 0.1 broadcast_bitcast_fusion
  19.1 0.1 broadcast_bitcast_fusion.1
  19.2 0.2 fusion.54
  19.4 0.8 %slice_convert_fusion = (f32[8,1,128]{2,1,0:T(1,128)S(1)}, bf16[8,1,128]{2,1,0:T(2,128)(2,1)S(1)}) fusion(bf16[8,2,128]{2,1,0:T(2,128)(2,1)} %param.9), kind=kLoop, calls=%fused_computation.127 | loop fusion | flops 1024 | bytes 10240 | tf_op jit(solution)/shard_map/convert_element_type | solution.py:164
  20.2 0.8 %fusion.63 = f32[8,1,8]{2,1,0:T(1,128)S(1)} fusion(bf16[8,8,128]{2,0,1:T(8,128)(2,1)} %bitcast.267, bf16[8,128,1]{1,0,2:T(8,128)(2,1)S(1)} %bitcast.266), kind=kOutput, calls=%fused_computation.95 | convolution fusion | flops 16384 | bytes 18688 | tf_op jit(solution)/shard_map/nkgd,nskd->nkgs/dot_general | solution.py:160
  21.0 1.1 %fusion.93 = (f32[8,8]{1,0:T(8,128)S(1)}, f32[8,1,8,1536]{3,2,0,1:T(8,128)S(1)}) fusion(bf16[8,8,128]{2,0,1:T(8,128)(2,1)} %bitcast.268, bf16[2,1536,128]{2,1,0:T(8,128)(2,1)S(1)} %maximum_bitcast_fusion, pred[8,1536]{1,0:T(8,128)(4,1)S(1)} %get-tuple-element.32), kind=kOutput, calls=%fused_computation.177 | convolution fusion | flops 25460672 | bytes 815360 | tf_op jit(solution)/shard_map/nkgd,skd->nkgs/dot_general | solution.py:21
  22.1 0.2 fusion.38
  22.3 0.3 fusion.92
  22.7 0.3 fusion.23
  22.9 1.4 %fusion.91 = (f32[16,8]{0,1:T(8,128)S(1)}, f32[16,1,8,1536]{3,0,2,1:T(8,128)S(1)}) fusion(bf16[8,1,8,128]{3,0,2,1:T(8,128)(2,1)S(1)} %bitcast.273, bf16[8,1,8,128]{3,0,2,1:T(8,128)(2,1)S(1)} %bitcast.271, bf16[2,1536,128]{2,1,0:T(8,128)(2,1)} %collective-permute-done, pred[16,1536]{1,0:T(8,128)(4,1)S(1)} %pad_add_fusion.1), kind=kOutput, calls=%fused_computation.175 | convolution fusion | flops 50986880 | bytes 1237504 | tf_op jit(solution)/shard_map/nkgd,skd->nkgs/dot_general | solution.py:21
  24.3 0.3 fusion.26
  24.6 0.1 fusion.89
  24.7 0.1 copy.22
  24.8 0.1 fusion.88
  24.8 0.1 copy.23
  24.9 0.3 fusion.11
  25.3 1.3 %fusion.10 = f32[16,1,8,128]{3,0,2,1:T(8,128)S(1)} fusion(f32[1,128,16,8]{1,2,3,0:T(8,128)S(1)} %fusion.11, f32[16,1,8,1536]{3,0,2,1:T(8,128)S(1)} %get-tuple-element.48, f32[16,8]{0,1:T(8,128)S(1)} %get-tuple-element.47, pred[16,1536]{1,0:T(8,128)(4,1)S(1)} %pad_add_fusion.1, bf16[2,1536,128]{2,1,0:T(8,128)(2,1)} %collective-permute-done, ...), kind=kOutput, calls=%fused_computation.15 | convolution fusion | flops 50954240 | bytes 1336320 | tf_op jit(solution)/shard_map/nkgs,skd->nkgd/dot_general | solution.py:30
  26.6 0.1 concatenate.54
  26.7 3.9 %collective-permute-start.3 = (f32[8,1040]{1,0:T(8,128)S(1)}, f32[8,1040]{1,0:T(8,128)S(1)}, u32[]{:S(2)}, u32[]{:S(2)}) collective-permute-start(f32[8,1040]{1,0:T(8,128)S(1)} %concatenate.54), channel_id=1, source_target_pairs={{8,0},{12,4},{16,8},{20,12},{24,16},{28,20},{32,24},{36,28},{40,32... | collective-permute-start | bytes 99848 | tf_op jit(solution)/shard_map/ppermute | solution.py:16
  30.6 0.1 copy.24
  30.7 0.1 copy.25
  30.8 0.1 concatenate.55
  30.9 2.2 %collective-permute-start.4 = (f32[8,1040]{1,0:T(8,128)S(1)}, f32[8,1040]{1,0:T(8,128)S(1)}, u32[]{:S(2)}, u32[]{:S(2)}) collective-permute-start(f32[8,1040]{1,0:T(8,128)S(1)} %concatenate.55), channel_id=1, source_target_pairs={{0,8},{4,12},{8,16},{12,20},{16,24},{20,28},{24,32},{28,36},{32,40... | collective-permute-start | bytes 99848 | tf_op jit(solution)/shard_map/ppermute | solution.py:16
  33.0 1.3 %fusion.94 = (f32[8,8]{1,0:T(8,128)S(1)}, f32[8,1,8,1536]{3,2,0,1:T(8,128)S(1)}) fusion(bf16[8,8,128]{2,0,1:T(8,128)(2,1)S(1)} %bitcast.269, bf16[2,1536,128]{2,1,0:T(8,128)(2,1)} %collective-permute-done, pred[8,1536]{1,0:T(8,128)(4,1)S(1)} %get-tuple-element.29), kind=kOutput, calls=%fused_computation.178 | convolution fusion | flops 25460672 | bytes 815360 | tf_op jit(solution)/shard_map/nkgd,skd->nkgs/dot_general | solution.py:21
  34.4 0.2 fusion.40
  34.6 4.4 %collective-permute-done.4 = f32[8,1040]{1,0:T(8,128)S(1)} collective-permute-done((f32[8,1040]{1,0:T(8,128)S(1)}, f32[8,1040]{1,0:T(8,128)S(1)}, u32[]{:S(2)}, u32[]{:S(2)}) %collective-permute-start.4) | collective-permute-done | bytes 33312 | tf_op jit(solution)/shard_map/ppermute | solution.py:16
  39.1 0.1 maximum_maximum_fusion
  39.1 0.1 multiply_add_fusion
  39.2 0.3 fusion.16
  39.5 1.3 %fusion.22 = bf16[1,8,8,128]{3,2,1,0:T(8,128)(2,1)S(1)} fusion(f32[8,1,8,128]{3,2,0,1:T(8,128)S(1)} %fusion.16, bf16[2,1536,128]{2,1,0:T(8,128)(2,1)} %collective-permute-done, f32[8,1,8,1536]{3,2,0,1:T(8,128)S(1)} %get-tuple-element.54, f32[8,8]{1,0:T(8,128)S(1)} %get-tuple-element.53, pred[8,1536]{1,0:T(8,128)(4,1)S(1)} %get-tuple-element.29, ...), kind=kOutput, calls=%fused_computation.30 | convolution fusion | flops 25526272 | bytes 914688 | tf_op jit(solution)/shard_map/nkgs,skd->nkgd/dot_general | solution.py:30
  40.8 1.3 %fusion.95 = (bf16[8,2048]{1,0:T(8,128)(2,1)}, f32[8,2048]{1,0:T(8,128)S(1)}) fusion(bf16[1024,2048]{1,0:T(8,128)(2,1)S(1)} %copy-done, bf16[1,8,8,128]{3,2,1,0:T(8,128)(2,1)S(1)} %fusion.22), kind=kOutput, calls=%fused_computation.179 | convolution fusion | flops 33570816 | bytes 4308992 | tf_op jit(solution)/shard_map/dot_general | solution.py:182
  42.1 4.5 %all-to-all-start = ((bf16[4,8,512]{2,1,0:T(8,128)(2,1)}), bf16[4,8,512]{2,1,0:T(8,128)(2,1)S(1)}, u32[]{:S(2)}, u32[]{:S(2)}) async-start(bf16[4,8,512]{2,1,0:T(8,128)(2,1)} %bitcast.59), calls=%async_computation | async-start | bytes 65536 | tf_op jit(solution)/shard_map/all_to_all | solution.py:188
  46.6 5.4 %all-to-all-done = bf16[4,8,512]{2,1,0:T(8,128)(2,1)S(1)} async-done(((bf16[4,8,512]{2,1,0:T(8,128)(2,1)}), bf16[4,8,512]{2,1,0:T(8,128)(2,1)S(1)}, u32[]{:S(2)}, u32[]{:S(2)}) %all-to-all-start) | async-done | bytes 32800 | tf_op jit(solution)/shard_map/all_to_all | solution.py:188
  52.0 0.1 select_reduce_fusion
  52.1 0.6 %add_convert_fusion = bf16[8,512]{1,0:T(8,128)(2,1)} fusion(f32[8,512]{1,0:T(8,128)S(1)} %select_reduce_fusion, f32[8,2048]{1,0:T(8,128)S(1)} %get-tuple-element.56, s32[]{:T(128)S(6)} %select_n.253), kind=kLoop, calls=%fused_computation.86 | loop fusion | flops 8192 | bytes 40964 | tf_op jit(solution)/shard_map/convert_element_type | solution.py:192
  (29 shorter events, 0.2 us)
Async XLA Ops:
  0.0 22.3 %collective-permute-start.1 = (bf16[8,1024]{1,0:T(8,128)(2,1)}, bf16[8,1024]{1,0:T(8,128)(2,1)S(1)}, u32[]{:S(2)}, u32[]{:S(2)}) collective-permute-start(bf16[8,1024]{1,0:T(8,128)(2,1)} %param.8), channel_id=1, source_target_pairs={{0,8},{4,12},{8,16},{12,20},{16,24},{20,28},{24,32},{28,36},{32,40... | collective-permute-start | bytes 49160 | tf_op jit(solution)/shard_map/ppermute | solution.py:16
  3.8 18.5 %collective-permute-start.2 = (bf16[8,1024]{1,0:T(8,128)(2,1)}, bf16[8,1024]{1,0:T(8,128)(2,1)S(1)}, u32[]{:S(2)}, u32[]{:S(2)}) collective-permute-start(bf16[8,1024]{1,0:T(8,128)(2,1)} %param.8), channel_id=1, source_target_pairs={{8,0},{12,4},{16,8},{20,12},{24,16},{28,20},{32,24},{36,28},{40,32... | collective-permute-start | bytes 49160 | tf_op jit(solution)/shard_map/ppermute | solution.py:16
  15.8 7.1 %collective-permute-start = (bf16[2,1536,128]{2,1,0:T(8,128)(2,1)S(1)}, bf16[2,1536,128]{2,1,0:T(8,128)(2,1)}, u32[]{:S(2)}, u32[]{:S(2)}) collective-permute-start(bf16[2,1536,128]{2,1,0:T(8,128)(2,1)S(1)} %maximum_bitcast_fusion), channel_id=1, source_target_pairs={{0,4},{4,0},{8,12},{12,8},{16,20},{20,16},{24,28},{28,24},{32,36},... | collective-permute-start | bytes 2359304 | tf_op jit(solution)/shard_map/ppermute | solution.py:70
  22.1 11.0 %copy-start.1 = (bf16[8,1024]{1,0:T(8,128)(2,1)S(1)}, bf16[8,1024]{1,0:T(8,128)(2,1)}, u32[]{:S(2)}) copy-start(bf16[8,1024]{1,0:T(8,128)(2,1)} %param.8) | copy-start | bytes 49156
  26.7 7.9 %collective-permute-start.3 = (f32[8,1040]{1,0:T(8,128)S(1)}, f32[8,1040]{1,0:T(8,128)S(1)}, u32[]{:S(2)}, u32[]{:S(2)}) collective-permute-start(f32[8,1040]{1,0:T(8,128)S(1)} %concatenate.54), channel_id=1, source_target_pairs={{8,0},{12,4},{16,8},{20,12},{24,16},{28,20},{32,24},{36,28},{40,32... | collective-permute-start | bytes 99848 | tf_op jit(solution)/shard_map/ppermute | solution.py:16
  30.8 10.0 %copy-start = (bf16[1024,2048]{1,0:T(8,128)(2,1)S(1)}, bf16[1024,2048]{1,0:T(8,128)(2,1)}, u32[]{:S(2)}) copy-start(bf16[1024,2048]{1,0:T(8,128)(2,1)} %param.12) | copy-start | bytes 12582916
  30.9 8.2 %collective-permute-start.4 = (f32[8,1040]{1,0:T(8,128)S(1)}, f32[8,1040]{1,0:T(8,128)S(1)}, u32[]{:S(2)}, u32[]{:S(2)}) collective-permute-start(f32[8,1040]{1,0:T(8,128)S(1)} %concatenate.55), channel_id=1, source_target_pairs={{0,8},{4,12},{8,16},{12,20},{16,24},{20,28},{24,32},{28,36},{32,40... | collective-permute-start | bytes 99848 | tf_op jit(solution)/shard_map/ppermute | solution.py:16
  42.1 9.9 %all-to-all-start = ((bf16[4,8,512]{2,1,0:T(8,128)(2,1)}), bf16[4,8,512]{2,1,0:T(8,128)(2,1)S(1)}, u32[]{:S(2)}, u32[]{:S(2)}) async-start(bf16[4,8,512]{2,1,0:T(8,128)(2,1)} %bitcast.59), calls=%async_computation | async-start | bytes 65536 | tf_op jit(solution)/shard_map/all_to_all | solution.py:188

commit v15 on v14

--- a/solution.py
+++ b/solution.py
@@ -94,20 +94,20 @@
 
     from_prev = shifted(queries, "req", -2)
     from_next = shifted(queries, "req", 2)
-    hood_queries = jnp.concatenate([from_prev, queries, from_next], axis=0)
+    hood_queries = jnp.concatenate([from_prev, from_next, queries], axis=0)
     hood_queries = hood_queries.reshape((3 * per_dev,) + shape4[1:])
     query_block = queries.reshape(shape4)
     hood_count = 3 * per_dev
     slot_ids = jnp.arange(per_dev, dtype=jnp.int32)
     hood_beams = jnp.concatenate(
-        [(dev_index + k) * per_dev + slot_ids for k in (-2, 0, 2)]
+        [(dev_index + k) * per_dev + slot_ids for k in (-2, 2, 0)]
     )
     in_range = (hood_beams >= 0) & (hood_beams < beam_count)
     pad = 2 * per_dev
     index_rows = jnp.pad(jnp.stack([parents, first_beam, own_len]), ((0, 0), (pad, pad)))
     window = lax.dynamic_slice_in_dim(index_rows, dev_index * per_dev, 5 * per_dev, axis=1)
     hood_index = jnp.concatenate(
-        [window[:, 0:per_dev], window[:, 2 * per_dev : 3 * per_dev], window[:, 4 * per_dev :]],
+        [window[:, 0:per_dev], window[:, 4 * per_dev :], window[:, 2 * per_dev : 3 * per_dev]],
         axis=1,
     )
     parent = hood_index[0]
@@ -138,8 +138,7 @@
         prompt_ok = (in_range & (home == holder))[:, None] & ~is_cache[None, :]
         return own_ok | prompt_ok
 
-    def pick_rows(x, groups):
-        return jnp.concatenate([x[g * per_dev : (g + 1) * per_dev] for g in groups], axis=0)
+    sent = 2 * per_dev
 
     send_parts = []
     own_parts = []
@@ -147,12 +146,8 @@
         keys = kv[0].reshape(kv_count, kv_heads_local, head_dim)
         values = kv[1].reshape(kv_count, kv_heads_local, head_dim)
         allowed = allowed_for(holder, lengths)
-        send_parts.append(
-            partial_block(pick_rows(hood_queries, (0, 2)), keys, values, pick_rows(allowed, (0, 2)))
-        )
-        own_parts.append(
-            partial_block(pick_rows(hood_queries, (1,)), keys, values, pick_rows(allowed, (1,)))
-        )
+        send_parts.append(partial_block(hood_queries[:sent], keys, values, allowed[:sent]))
+        own_parts.append(partial_block(hood_queries[sent:], keys, values, allowed[sent:]))
     send_part = merge_all(send_parts)
 
     fresh_keys = new_kv[:, 0].reshape(per_dev, 1, kv_heads_local, head_dim)

time: 53.4 us -> 53.3 us (level)
  no operation moved by 1% of the time
where the time goes in v15:
time: 53.3 us; the launch traced here: 52.7 us
  starting transfers between devices  26 us (49%)
  waiting for transfers between devices  9.9 us (19%)
  matrix products  9.45 us (18%)
  other arithmetic  3.82 us (7%)
  local copies, waits for them, and re-layouts  3.19 us (6%)
    ppermute x4, starting transfers between devices, shifted(): return lax.ppermute(block, axis, route)  19.7 us
    all_to_all x1, waiting for transfers between devices, local(): got = lax.all_to_all(chunks.astype(jnp.bfloat16), 'tp', 0, 0, tiled=True)  5.44 us
    all_to_all x1, starting transfers between devices, local(): got = lax.all_to_all(chunks.astype(jnp.bfloat16), 'tp', 0, 0, tiled=True)  4.46 us
    ppermute x4, waiting for transfers between devices, shifted(): return lax.ppermute(block, axis, route)  4.45 us
    dot_general x4, matrix products, partial_block(): jnp.einsum('nkgd,skd->nkgs', query_block, key_block, preferred_element_ty...  4.11 us
    dot_general x4, matrix products, partial_block(): jnp.einsum('nkgs,skd->nkgd', weights.astype(jnp.bfloat16), value_block, p...  3.23 us
    unnamed x9, local copies, waits for them, and re-layouts  2.15 us
    ppermute x1, starting transfers between devices, swapped(): return lax.ppermute(block, axis, [(i, i ^ 1) for i in devices])  1.92 us
  transfers between devices with their start and end apart: 6, of which 2 were waited for; matrix products, arithmetic and copies ran while one was open for 17% of the time, Pallas kernels for 0%

profile of v15, /device:TPU:6, one launch (start us, length us, event | category | flops | bytes accessed | tf_op | source)
XLA Modules:
  0.0 52.7 jit_solution(15394865651331786646)
XLA Ops:
  0.0 3.8 %collective-permute-start.1 = (bf16[8,1024]{1,0:T(8,128)(2,1)}, bf16[8,1024]{1,0:T(8,128)(2,1)S(1)}, u32[]{:S(2)}, u32[]{:S(2)}) collective-permute-start(bf16[8,1024]{1,0:T(8,128)(2,1)} %param.8), channel_id=1, source_target_pairs={{0,8},{4,12},{8,16},{12,20},{16,24},{20,28},{24,32},{28,36},{32,40... | collective-permute-start | bytes 49160 | tf_op jit(solution)/shard_map/ppermute | solution.py:16
  3.8 9.8 %collective-permute-start.2 = (bf16[8,1024]{1,0:T(8,128)(2,1)}, bf16[8,1024]{1,0:T(8,128)(2,1)S(1)}, u32[]{:S(2)}, u32[]{:S(2)}) collective-permute-start(bf16[8,1024]{1,0:T(8,128)(2,1)} %param.8), channel_id=1, source_target_pairs={{8,0},{12,4},{16,8},{20,12},{24,16},{28,20},{32,24},{36,28},{40,32... | collective-permute-start | bytes 49160 | tf_op jit(solution)/shard_map/ppermute | solution.py:16
  13.6 1.1 %copy.18 = bf16[8,128,2,128]{3,1,0,2:T(8,128)(2,1)S(1)} copy(bf16[8,128,2,128]{3,2,1,0:T(2,128)(2,1)} %param.10) | data formatting | bytes 1048576 | tf_op args[2]
  14.7 1.0 %copy.69 = bf16[1,512,2,128]{3,1,2,0:T(8,128)(2,1)S(1)} copy(bf16[1,512,2,128]{3,2,1,0:T(2,128)(2,1)} %param.11) | data formatting | bytes 524288 | tf_op args[3]
  15.7 0.1 maximum_bitcast_fusion
  15.8 1.9 %collective-permute-start = (bf16[2,1536,128]{2,1,0:T(8,128)(2,1)S(1)}, bf16[2,1536,128]{2,1,0:T(8,128)(2,1)}, u32[]{:S(2)}, u32[]{:S(2)}) collective-permute-start(bf16[2,1536,128]{2,1,0:T(8,128)(2,1)S(1)} %maximum_bitcast_fusion), channel_id=1, source_target_pairs={{0,4},{4,0},{8,12},{12,8},{16,20},{20,16},{24,28},{28,24},{32,36},... | collective-permute-start | bytes 2359304 | tf_op jit(solution)/shard_map/ppermute | solution.py:70
  17.7 0.7 %pad_add_fusion = s32[3,1024]{1,0:T(4,128)S(1)} fusion(s32[1,1024]{1,0:T(1,128)} %bitcast.267, s32[1,1024]{1,0:T(1,128)} %bitcast.268, s32[1,1024]{1,0:T(1,128)} %bitcast.269), kind=kLoop, calls=%fused_computation.87 | loop fusion | flops 6144 | bytes 24576 | tf_op jit(solution)/shard_map/stack | solution.py:107
  18.5 0.1 pad_dynamic-slice_fusion
  18.6 0.1 fusion.90
  18.6 0.1 slice_bitcast_fusion.16
  18.7 0.1 pad_add_fusion.1
  18.8 0.1 compare_and_fusion.3
  18.9 0.1 fusion.83
  19.0 0.1 broadcast_bitcast_fusion
  19.1 0.1 broadcast_bitcast_fusion.1
  19.2 0.2 fusion.54
  19.4 0.8 %slice_convert_fusion = (f32[8,1,128]{2,1,0:T(1,128)S(1)}, bf16[8,1,128]{2,1,0:T(2,128)(2,1)S(1)}) fusion(bf16[8,2,128]{2,1,0:T(2,128)(2,1)} %param.9), kind=kLoop, calls=%fused_computation.129 | loop fusion | flops 1024 | bytes 10240 | tf_op jit(solution)/shard_map/convert_element_type | solution.py:159
  20.1 0.8 %fusion.67 = f32[8,1,8]{2,1,0:T(1,128)S(1)} fusion(bf16[8,8,128]{2,0,1:T(8,128)(2,1)} %bitcast.272, bf16[8,128,1]{1,0,2:T(8,128)(2,1)S(1)} %bitcast.271), kind=kOutput, calls=%fused_computation.97 | convolution fusion | flops 16384 | bytes 18688 | tf_op jit(solution)/shard_map/nkgd,nskd->nkgs/dot_general | solution.py:155
  21.0 1.1 %fusion.93 = (f32[8,8]{1,0:T(8,128)S(1)}, f32[8,1,8,1536]{3,2,0,1:T(8,128)S(1)}) fusion(bf16[8,8,128]{2,0,1:T(8,128)(2,1)} %bitcast.273, bf16[2,1536,128]{2,1,0:T(8,128)(2,1)S(1)} %maximum_bitcast_fusion, pred[8,1536]{1,0:T(8,128)(4,1)S(1)} %slice.123), kind=kOutput, calls=%fused_computation.175 | convolution fusion | flops 25460672 | bytes 815360 | tf_op jit(solution)/shard_map/nkgd,skd->nkgs/dot_general | solution.py:21
  22.0 0.2 fusion.38
  22.3 0.3 fusion.92
  22.7 0.3 fusion.23
  22.9 1.4 %fusion.91 = (f32[16,8]{0,1:T(8,128)S(1)}, f32[16,1,8,1536]{3,0,2,1:T(8,128)S(1)}) fusion(bf16[2,1536,128]{2,1,0:T(8,128)(2,1)} %collective-permute-done, pred[16,1536]{1,0:T(8,128)(4,1)S(1)} %slice.129, bf16[8,1024]{1,0:T(8,128)(2,1)S(1)} %collective-permute-done.2, bf16[8,1024]{1,0:T(8,128)(2,1)S(1)} %collective-permute-done.1), kind=kOutput, calls=%fused_computation.173 | convolution fusion | flops 50986880 | bytes 1237504 | tf_op jit(solution)/shard_map/nkgd,skd->nkgs/dot_general | solution.py:21
  24.3 0.3 fusion.26
  24.6 0.1 fusion.89
  24.7 0.1 copy.24
  24.8 0.1 fusion.88
  24.8 0.1 copy.25
  24.9 0.3 fusion.11
  25.3 1.3 %fusion.10 = f32[16,1,8,128]{3,0,2,1:T(8,128)S(1)} fusion(f32[1,128,16,8]{1,2,3,0:T(8,128)S(1)} %fusion.11, f32[16,1,8,1536]{3,0,2,1:T(8,128)S(1)} %get-tuple-element.42, f32[16,8]{0,1:T(8,128)S(1)} %get-tuple-element.41, pred[16,1536]{1,0:T(8,128)(4,1)S(1)} %slice.129, bf16[2,1536,128]{2,1,0:T(8,128)(2,1)} %collective-permute-done, ...), kind=kOutput, calls=%fused_computation.15 | convolution fusion | flops 50954240 | bytes 1336320 | tf_op jit(solution)/shard_map/nkgs,skd->nkgd/dot_general | solution.py:30
  26.6 0.1 concatenate.45
  26.7 3.9 %collective-permute-start.3 = (f32[8,1040]{1,0:T(8,128)S(1)}, f32[8,1040]{1,0:T(8,128)S(1)}, u32[]{:S(2)}, u32[]{:S(2)}) collective-permute-start(f32[8,1040]{1,0:T(8,128)S(1)} %concatenate.45), channel_id=1, source_target_pairs={{8,0},{12,4},{16,8},{20,12},{24,16},{28,20},{32,24},{36,28},{40,32... | collective-permute-start | bytes 99848 | tf_op jit(solution)/shard_map/ppermute | solution.py:16
  30.6 0.1 copy.26
  30.7 0.1 copy.27
  30.8 0.1 concatenate.46
  30.8 2.2 %collective-permute-start.4 = (f32[8,1040]{1,0:T(8,128)S(1)}, f32[8,1040]{1,0:T(8,128)S(1)}, u32[]{:S(2)}, u32[]{:S(2)}) collective-permute-start(f32[8,1040]{1,0:T(8,128)S(1)} %concatenate.46), channel_id=1, source_target_pairs={{0,8},{4,12},{8,16},{12,20},{16,24},{20,28},{24,32},{28,36},{32,40... | collective-permute-start | bytes 99848 | tf_op jit(solution)/shard_map/ppermute | solution.py:16
  33.0 1.3 %fusion.94 = (f32[8,8]{1,0:T(8,128)S(1)}, f32[8,1,8,1536]{3,2,0,1:T(8,128)S(1)}) fusion(bf16[8,8,128]{2,0,1:T(8,128)(2,1)S(1)} %bitcast.274, bf16[2,1536,128]{2,1,0:T(8,128)(2,1)} %collective-permute-done, pred[8,1536]{1,0:T(8,128)(4,1)S(1)} %slice.125), kind=kOutput, calls=%fused_computation.176 | convolution fusion | flops 25460672 | bytes 815360 | tf_op jit(solution)/shard_map/nkgd,skd->nkgs/dot_general | solution.py:21
  34.4 0.2 fusion.40
  34.6 4.4 %collective-permute-done.4 = f32[8,1040]{1,0:T(8,128)S(1)} collective-permute-done((f32[8,1040]{1,0:T(8,128)S(1)}, f32[8,1040]{1,0:T(8,128)S(1)}, u32[]{:S(2)}, u32[]{:S(2)}) %collective-permute-start.4) | collective-permute-done | bytes 33312 | tf_op jit(solution)/shard_map/ppermute | solution.py:16
  39.1 0.1 maximum_maximum_fusion
  39.1 0.1 multiply_add_fusion
  39.2 0.3 fusion.16
  39.5 1.3 %fusion.22 = bf16[1,8,8,128]{3,2,1,0:T(8,128)(2,1)S(1)} fusion(f32[8,1,8,128]{3,2,0,1:T(8,128)S(1)} %fusion.16, bf16[2,1536,128]{2,1,0:T(8,128)(2,1)} %collective-permute-done, f32[8,1,8,1536]{3,2,0,1:T(8,128)S(1)} %get-tuple-element.48, f32[8,8]{1,0:T(8,128)S(1)} %get-tuple-element.47, pred[8,1536]{1,0:T(8,128)(4,1)S(1)} %slice.125, ...), kind=kOutput, calls=%fused_computation.30 | convolution fusion | flops 25526272 | bytes 914688 | tf_op jit(solution)/shard_map/nkgs,skd->nkgd/dot_general | solution.py:30
  40.8 1.3 %fusion.95 = (bf16[8,2048]{1,0:T(8,128)(2,1)}, f32[8,2048]{1,0:T(8,128)S(1)}) fusion(bf16[1024,2048]{1,0:T(8,128)(2,1)S(1)} %copy-done, bf16[1,8,8,128]{3,2,1,0:T(8,128)(2,1)S(1)} %fusion.22), kind=kOutput, calls=%fused_computation.177 | convolution fusion | flops 33570816 | bytes 4308992 | tf_op jit(solution)/shard_map/dot_general | solution.py:177
  42.1 4.5 %all-to-all-start = ((bf16[4,8,512]{2,1,0:T(8,128)(2,1)}), bf16[4,8,512]{2,1,0:T(8,128)(2,1)S(1)}, u32[]{:S(2)}, u32[]{:S(2)}) async-start(bf16[4,8,512]{2,1,0:T(8,128)(2,1)} %bitcast.56), calls=%async_computation | async-start | bytes 65536 | tf_op jit(solution)/shard_map/all_to_all | solution.py:183
  46.5 5.4 %all-to-all-done = bf16[4,8,512]{2,1,0:T(8,128)(2,1)S(1)} async-done(((bf16[4,8,512]{2,1,0:T(8,128)(2,1)}), bf16[4,8,512]{2,1,0:T(8,128)(2,1)S(1)}, u32[]{:S(2)}, u32[]{:S(2)}) %all-to-all-start) | async-done | bytes 32800 | tf_op jit(solution)/shard_map/all_to_all | solution.py:183
  52.0 0.1 select_reduce_fusion
  52.1 0.6 %add_convert_fusion = bf16[8,512]{1,0:T(8,128)(2,1)} fusion(f32[8,512]{1,0:T(8,128)S(1)} %select_reduce_fusion, f32[8,2048]{1,0:T(8,128)S(1)} %get-tuple-element.50, s32[]{:T(128)S(6)} %select_n.253), kind=kLoop, calls=%fused_computation.88 | loop fusion | flops 8192 | bytes 40964 | tf_op jit(solution)/shard_map/convert_element_type | solution.py:187
  (29 shorter events, 0.2 us)
Async XLA Ops:
  0.0 22.3 %collective-permute-start.1 = (bf16[8,1024]{1,0:T(8,128)(2,1)}, bf16[8,1024]{1,0:T(8,128)(2,1)S(1)}, u32[]{:S(2)}, u32[]{:S(2)}) collective-permute-start(bf16[8,1024]{1,0:T(8,128)(2,1)} %param.8), channel_id=1, source_target_pairs={{0,8},{4,12},{8,16},{12,20},{16,24},{20,28},{24,32},{28,36},{32,40... | collective-permute-start | bytes 49160 | tf_op jit(solution)/shard_map/ppermute | solution.py:16
  3.8 18.5 %collective-permute-start.2 = (bf16[8,1024]{1,0:T(8,128)(2,1)}, bf16[8,1024]{1,0:T(8,128)(2,1)S(1)}, u32[]{:S(2)}, u32[]{:S(2)}) collective-permute-start(bf16[8,1024]{1,0:T(8,128)(2,1)} %param.8), channel_id=1, source_target_pairs={{8,0},{12,4},{16,8},{20,12},{24,16},{28,20},{32,24},{36,28},{40,32... | collective-permute-start | bytes 49160 | tf_op jit(solution)/shard_map/ppermute | solution.py:16
  15.8 7.1 %collective-permute-start = (bf16[2,1536,128]{2,1,0:T(8,128)(2,1)S(1)}, bf16[2,1536,128]{2,1,0:T(8,128)(2,1)}, u32[]{:S(2)}, u32[]{:S(2)}) collective-permute-start(bf16[2,1536,128]{2,1,0:T(8,128)(2,1)S(1)} %maximum_bitcast_fusion), channel_id=1, source_target_pairs={{0,4},{4,0},{8,12},{12,8},{16,20},{20,16},{24,28},{28,24},{32,36},... | collective-permute-start | bytes 2359304 | tf_op jit(solution)/shard_map/ppermute | solution.py:70
  22.0 11.0 %copy-start.1 = (bf16[8,1024]{1,0:T(8,128)(2,1)S(1)}, bf16[8,1024]{1,0:T(8,128)(2,1)}, u32[]{:S(2)}) copy-start(bf16[8,1024]{1,0:T(8,128)(2,1)} %param.8) | copy-start | bytes 49156
  26.7 7.9 %collective-permute-start.3 = (f32[8,1040]{1,0:T(8,128)S(1)}, f32[8,1040]{1,0:T(8,128)S(1)}, u32[]{:S(2)}, u32[]{:S(2)}) collective-permute-start(f32[8,1040]{1,0:T(8,128)S(1)} %concatenate.45), channel_id=1, source_target_pairs={{8,0},{12,4},{16,8},{20,12},{24,16},{28,20},{32,24},{36,28},{40,32... | collective-permute-start | bytes 99848 | tf_op jit(solution)/shard_map/ppermute | solution.py:16
  30.8 10.0 %copy-start = (bf16[1024,2048]{1,0:T(8,128)(2,1)S(1)}, bf16[1024,2048]{1,0:T(8,128)(2,1)}, u32[]{:S(2)}) copy-start(bf16[1024,2048]{1,0:T(8,128)(2,1)} %param.12) | copy-start | bytes 12582916
  30.8 8.2 %collective-permute-start.4 = (f32[8,1040]{1,0:T(8,128)S(1)}, f32[8,1040]{1,0:T(8,128)S(1)}, u32[]{:S(2)}, u32[]{:S(2)}) collective-permute-start(f32[8,1040]{1,0:T(8,128)S(1)} %concatenate.46), channel_id=1, source_target_pairs={{0,8},{4,12},{8,16},{12,20},{16,24},{20,28},{24,32},{28,36},{32,40... | collective-permute-start | bytes 99848 | tf_op jit(solution)/shard_map/ppermute | solution.py:16
  42.1 9.9 %all-to-all-start = ((bf16[4,8,512]{2,1,0:T(8,128)(2,1)}), bf16[4,8,512]{2,1,0:T(8,128)(2,1)S(1)}, u32[]{:S(2)}, u32[]{:S(2)}) async-start(bf16[4,8,512]{2,1,0:T(8,128)(2,1)} %bitcast.56), calls=%async_computation | async-start | bytes 65536 | tf_op jit(solution)/shard_map/all_to_all | solution.py:183

commit v16 on v15

--- a/solution.py
+++ b/solution.py
@@ -14,6 +14,23 @@
     devices = range(lax.axis_size(axis))
     route = [(i + distance, i) for i in devices if i + distance in devices]
     return lax.ppermute(block, axis, route)
+
+
+def softmax_block(query_block, key_block, allowed):
+    score_scale = query_block.shape[-1] ** (-0.5)
+    scores = jnp.einsum(
+        "nkgd,skd->nkgs", query_block, key_block, preferred_element_type=jnp.float32
+    )
+    scores = scores * score_scale
+    masked = allowed[:, None, None, :]
+    scores = jnp.where(masked, scores, MASKED_SCORE)
+    peaks = jnp.max(scores, axis=-1)
+    weights = jnp.where(masked, jnp.exp(scores - peaks[..., None]), 0.0)
+    return weights.astype(jnp.bfloat16), peaks, jnp.sum(weights, axis=-1)
+
+
+def weigh(weights, value_block):
+    return jnp.einsum("nkgs,skd->nkgd", weights, value_block, preferred_element_type=jnp.float32)
 
 
 def partial_block(query_block, key_block, value_block, allowed):
@@ -146,8 +163,9 @@
         keys = kv[0].reshape(kv_count, kv_heads_local, head_dim)
         values = kv[1].reshape(kv_count, kv_heads_local, head_dim)
         allowed = allowed_for(holder, lengths)
-        send_parts.append(partial_block(hood_queries[:sent], keys, values, allowed[:sent]))
-        own_parts.append(partial_block(hood_queries[sent:], keys, values, allowed[sent:]))
+        weights, peaks, totals = softmax_block(hood_queries, keys, allowed)
+        send_parts.append((weigh(weights[:sent], values), peaks[:sent], totals[:sent]))
+        own_parts.append((weigh(weights[sent:], values), peaks[sent:], totals[sent:]))
     send_part = merge_all(send_parts)
 
     fresh_keys = new_kv[:, 0].reshape(per_dev, 1, kv_heads_local, head_dim)
@@ -174,7 +192,14 @@
         .reshape(per_dev, q_heads_local * head_dim)
         .astype(jnp.bfloat16)
     )
-    partial_term = jnp.dot(attended, out_weight, preferred_element_type=jnp.float32)
+    half = out_weight.shape[1] // 2
+    partial_term = jnp.concatenate(
+        [
+            jnp.dot(attended, out_weight[:, :half], preferred_element_type=jnp.float32),
+            jnp.dot(attended, out_weight[:, half:], preferred_element_type=jnp.float32),
+        ],
+        axis=1,
+    )
 
     tp_count = lax.axis_size("tp")
     tp_index = lax.axis_index("tp")

time: 53.3 us -> 48.8 us (0.916)
  matrix products: 9.45 us -> 4.63 us
  waiting for transfers between devices: 9.9 us -> 11.4 us
  other arithmetic: 3.82 us -> 2.69 us
    dot_general x9 -> x8, matrix products: 8.61 us -> 4.51 us  [the longest x1 2.21 us: local(): jnp.dot(attended, out_weight[:, half:], preferred_element_type=jnp.float32)]
    ppermute x4, waiting for transfers between devices: 4.45 us -> 5.81 us  [shifted(): return lax.ppermute(block, axis, route)]
    convert_element_type x0 -> x2, other arithmetic: none -> 1 us  [the longest x1 0.62 us: local(): got = lax.all_to_all(chunks.astype(jnp.bfloat16), 'tp', 0, 0, tiled=True)]
    convert_element_type x1, other arithmetic: 0.77 us -> 0.01 us  [local(): fresh_values[:, 0, :, None, :].astype(jnp.float32)]
    another operation x1, other arithmetic: 0.74 us -> 0.02 us  [local(): jnp.stack([parents, first_beam, own_len])]
    dot_general x1, matrix products: 0.84 us -> 0.12 us  [local(): jnp.einsum('nkgd,nskd->nkgs', query_block, fresh_keys, preferred_element_...]
    reduce_sum x4 -> x1, other arithmetic: 1 us -> 0.38 us  [softmax_block(): return (weights.astype(jnp.bfloat16), peaks, jnp.sum(weights, axis=-1))]
    unnamed x9 -> x23, local copies, waits for them, and re-layouts: 2.15 us -> 1.67 us
  transfers between devices with their start and end apart: 6 -> 6, of which waited for: 2 -> 3; matrix products, arithmetic and copies ran while one was open for 17% -> 7% of each run, Pallas kernels for 0% -> 0%
where the time goes in v16:
time: 48.8 us; the launch traced here: 48.4 us
  starting transfers between devices  25.9 us (53%)
  waiting for transfers between devices  11.4 us (23%)
  matrix products  4.63 us (9%)
  local copies, waits for them, and re-layouts  3.37 us (7%)
  other arithmetic  2.69 us (6%)
    ppermute x4, starting transfers between devices, shifted(): return lax.ppermute(block, axis, route)  19.5 us
    ppermute x4, waiting for transfers between devices, shifted(): return lax.ppermute(block, axis, route)  5.81 us
    all_to_all x1, waiting for transfers between devices, local(): got = lax.all_to_all(chunks.astype(jnp.bfloat16), 'tp', 0, 0, tiled=True)  5.44 us
    all_to_all x1, starting transfers between devices, local(): got = lax.all_to_all(chunks.astype(jnp.bfloat16), 'tp', 0, 0, tiled=True)  4.46 us
    dot_general x1, matrix products, local(): jnp.dot(attended, out_weight[:, half:], preferred_element_type=jnp.float32)  2.21 us
    ppermute x1, starting transfers between devices, swapped(): return lax.ppermute(block, axis, [(i, i ^ 1) for i in devices])  1.92 us
    unnamed x23, local copies, waits for them, and re-layouts  1.67 us
    dot_general x2, matrix products, softmax_block(): jnp.einsum('nkgd,skd->nkgs', query_block, key_block, preferred_element_ty...  0.98 us
  transfers between devices with their start and end apart: 6, of which 3 were waited for; matrix products, arithmetic and copies ran while one was open for 7% of the time, Pallas kernels for 0%

profile of v16, /device:TPU:6, one launch (start us, length us, event | category | flops | bytes accessed | tf_op | source)
XLA Modules:
  0.0 48.4 jit_solution(951477019385460205)
XLA Ops:
  0.0 3.9 %collective-permute-start = (bf16[8,1024]{1,0:T(8,128)(2,1)}, bf16[8,1024]{1,0:T(8,128)(2,1)S(1)}, u32[]{:S(2)}, u32[]{:S(2)}) collective-permute-start(bf16[8,1024]{1,0:T(8,128)(2,1)} %param.8), channel_id=1, source_target_pairs={{0,8},{4,12},{8,16},{12,20},{16,24},{20,28},{24,32},{28,36},{32,40... | collective-permute-start | bytes 49160 | tf_op jit(solution)/shard_map/ppermute | solution.py:16
  4.0 9.8 %collective-permute-start.1 = (bf16[8,1024]{1,0:T(8,128)(2,1)}, bf16[8,1024]{1,0:T(8,128)(2,1)S(1)}, u32[]{:S(2)}, u32[]{:S(2)}) collective-permute-start(bf16[8,1024]{1,0:T(8,128)(2,1)} %param.8), channel_id=1, source_target_pairs={{8,0},{12,4},{16,8},{20,12},{24,16},{28,20},{32,24},{36,28},{40,32... | collective-permute-start | bytes 49160 | tf_op jit(solution)/shard_map/ppermute | solution.py:16
  13.7 1.1 %copy.50 = bf16[8,128,2,128]{3,1,0,2:T(8,128)(2,1)S(1)} copy(bf16[8,128,2,128]{3,2,1,0:T(2,128)(2,1)} %param.10) | data formatting | bytes 1048576 | tf_op args[2]
  15.1 1.9 %collective-permute-start.2 = (bf16[2,1536,128]{2,1,0:T(8,128)(2,1)S(1)}, bf16[2,1536,128]{2,1,0:T(8,128)(2,1)S(1)}, u32[]{:S(2)}, u32[]{:S(2)}) collective-permute-start(bf16[2,1536,128]{2,1,0:T(8,128)(2,1)S(1)} %maximum_bitcast_fusion), channel_id=1, source_target_pairs={{0,4},{4,0},{8,12},{12,8},{16,20},{20,16},{24,28},{28,24},{32,36},... | collective-permute-start | bytes 2359304 | tf_op jit(solution)/shard_map/ppermute | solution.py:87
  17.0 0.1 pad_dynamic-slice_fusion.2
  17.1 0.1 fusion.65
  17.2 0.1 slice_bitcast_fusion.20
  17.3 0.1 pad_add_fusion.1
  17.4 0.1 compare_and_fusion.3
  17.5 0.1 fusion.59
  17.6 0.1 broadcast_bitcast_fusion
  17.8 0.2 fusion.32
  18.0 0.1 fusion.47
  18.1 0.1 copy.72
  18.2 0.5 %fusion.67 = (f32[24,8]{0,1:T(8,128)S(1)}, f32[24,1,8,1536]{3,0,2,1:T(8,128)S(1)}) fusion(bf16[2,1536,128]{2,1,0:T(8,128)(2,1)S(1)} %maximum_bitcast_fusion, pred[24,1536]{1,0:T(8,128)(4,1)S(1)} %get-tuple-element.37, bf16[8,1024]{1,0:T(8,128)(2,1)S(1)} %copy-done.6, bf16[8,1024]{1,0:T(8,128)(2,1)S(1)} %collective-permute-done.1, ...), kind=kOutput, calls=%fused_computation.152 | convolution fusion | flops 76529472 | bytes 1659648 | tf_op jit(solution)/shard_map/nkgd,skd->nkgs/dot_general | solution.py:21
  18.7 0.4 fusion.24
  19.1 0.2 collective-permute-done.2
  19.2 0.5 %fusion.66 = (f32[24,8]{0,1:T(8,128)S(1)}, f32[24,1,8,1536]{3,0,2,1:T(8,128)S(1)}) fusion(bf16[2,1536,128]{2,1,0:T(8,128)(2,1)S(1)} %collective-permute-done.2, pred[24,1536]{1,0:T(8,128)(4,1)S(1)} %get-tuple-element.36, bf16[8,1024]{1,0:T(8,128)(2,1)S(1)} %copy-done.6, bf16[8,1024]{1,0:T(8,128)(2,1)S(1)} %collective-permute-done.1, ...), kind=kOutput, calls=%fused_computation.151 | convolution fusion | flops 76529472 | bytes 1659648 | tf_op jit(solution)/shard_map/nkgd,skd->nkgs/dot_general | solution.py:21
  19.7 0.4 fusion.25
  20.1 0.3 fusion.11
  20.4 0.3 fusion.10
  20.7 0.1 fusion.64
  20.7 0.1 copy.54
  20.8 0.1 fusion.63
  20.9 0.1 copy.55
  21.0 0.1 concatenate.47
  21.0 3.9 %collective-permute-start.3 = (f32[8,1040]{1,0:T(8,128)S(1)}, f32[8,1040]{1,0:T(8,128)S(1)}, u32[]{:S(2)}, u32[]{:S(2)}) collective-permute-start(f32[8,1040]{1,0:T(8,128)S(1)} %concatenate.47), channel_id=1, source_target_pairs={{8,0},{12,4},{16,8},{20,12},{24,16},{28,20},{32,24},{36,28},{40,32... | collective-permute-start | bytes 99848 | tf_op jit(solution)/shard_map/ppermute | solution.py:16
  25.0 0.1 copy.58
  25.0 0.1 copy.59
  25.1 0.1 concatenate.48
  25.2 1.9 %collective-permute-start.4 = (f32[8,1040]{1,0:T(8,128)S(1)}, f32[8,1040]{1,0:T(8,128)S(1)}, u32[]{:S(2)}, u32[]{:S(2)}) collective-permute-start(f32[8,1040]{1,0:T(8,128)S(1)} %concatenate.48), channel_id=1, source_target_pairs={{0,8},{4,12},{8,16},{12,20},{16,24},{20,28},{24,32},{28,36},{32,40... | collective-permute-start | bytes 99848 | tf_op jit(solution)/shard_map/ppermute | solution.py:16
  27.1 0.1 fusion.61
  27.2 0.1 copy.74
  27.3 5.8 %collective-permute-done.4 = f32[8,1040]{1,0:T(8,128)S(1)} collective-permute-done((f32[8,1040]{1,0:T(8,128)S(1)}, f32[8,1040]{1,0:T(8,128)S(1)}, u32[]{:S(2)}, u32[]{:S(2)}) %collective-permute-start.4) | collective-permute-done | bytes 33312 | tf_op jit(solution)/shard_map/ppermute | solution.py:16
  33.1 0.1 fusion.62
  33.2 0.1 copy.76
  33.4 0.1 maximum_maximum_fusion
  33.4 0.1 multiply_add_fusion
  33.9 0.2 fusion.16
  34.2 0.2 fusion.22
  34.4 2.2 %fusion.4 = f32[8,1024]{1,0:T(8,128)S(1)} fusion(bf16[1024,2048]{1,0:T(8,128)(2,1)} %param.12, bf16[1,8,8,128]{3,2,1,0:T(8,128)(2,1)S(1)} %fusion.22), kind=kOutput, calls=%fused_computation.6 | convolution fusion | flops 16777216 | bytes 2146304 | tf_op jit(solution)/shard_map/dot_general | solution.py:199
  36.6 0.2 copy-done
  36.8 0.4 fusion.6
  37.1 0.6 %fusion.33 = bf16[8,2048]{1,0:T(8,128)(2,1)} fusion(f32[8,1024]{1,0:T(8,128)S(1)} %fusion.4, f32[8,1024]{1,0:T(8,128)S(1)} %fusion.6), kind=kLoop, calls=%fused_computation.56 | loop fusion | flops 65536 | bytes 98304 | tf_op jit(solution)/shard_map/convert_element_type | solution.py:208
  37.8 4.5 %all-to-all-start = ((bf16[4,8,512]{2,1,0:T(8,128)(2,1)}), bf16[4,8,512]{2,1,0:T(8,128)(2,1)S(1)}, u32[]{:S(2)}, u32[]{:S(2)}) async-start(bf16[4,8,512]{2,1,0:T(8,128)(2,1)} %bitcast.43), calls=%async_computation | async-start | bytes 65536 | tf_op jit(solution)/shard_map/all_to_all | solution.py:208
  42.2 5.4 %all-to-all-done = bf16[4,8,512]{2,1,0:T(8,128)(2,1)S(1)} async-done(((bf16[4,8,512]{2,1,0:T(8,128)(2,1)}), bf16[4,8,512]{2,1,0:T(8,128)(2,1)S(1)}, u32[]{:S(2)}, u32[]{:S(2)}) %all-to-all-start) | async-done | bytes 32800 | tf_op jit(solution)/shard_map/all_to_all | solution.py:208
  47.7 0.1 select_reduce_fusion
  47.8 0.6 %fusion.40 = bf16[8,512]{1,0:T(8,128)(2,1)} fusion(f32[8,512]{1,0:T(8,128)S(1)} %select_reduce_fusion, s32[]{:T(128)S(6)} %select_n.160, f32[8,1024]{1,0:T(8,128)S(1)} %fusion.6, f32[8,1024]{1,0:T(8,128)S(1)} %fusion.4), kind=kLoop, calls=%fused_computation.72 | loop fusion | flops 12288 | bytes 90116 | tf_op jit(solution)/shard_map/convert_element_type | solution.py:212
  (46 shorter events, 0.9 us)
Async XLA Ops:
  0.0 14.9 %copy-start.1 = (bf16[1,512,2,128]{3,2,1,0:T(2,128)(2,1)S(1)}, bf16[1,512,2,128]{3,2,1,0:T(2,128)(2,1)}, u32[]{:S(2)}) copy-start(bf16[1,512,2,128]{3,2,1,0:T(2,128)(2,1)} %param.11) | copy-start | bytes 786436
  0.0 18.1 %collective-permute-start = (bf16[8,1024]{1,0:T(8,128)(2,1)}, bf16[8,1024]{1,0:T(8,128)(2,1)S(1)}, u32[]{:S(2)}, u32[]{:S(2)}) collective-permute-start(bf16[8,1024]{1,0:T(8,128)(2,1)} %param.8), channel_id=1, source_target_pairs={{0,8},{4,12},{8,16},{12,20},{16,24},{20,28},{24,32},{28,36},{32,40... | collective-permute-start | bytes 49160 | tf_op jit(solution)/shard_map/ppermute | solution.py:16
  4.0 14.2 %collective-permute-start.1 = (bf16[8,1024]{1,0:T(8,128)(2,1)}, bf16[8,1024]{1,0:T(8,128)(2,1)S(1)}, u32[]{:S(2)}, u32[]{:S(2)}) collective-permute-start(bf16[8,1024]{1,0:T(8,128)(2,1)} %param.8), channel_id=1, source_target_pairs={{8,0},{12,4},{16,8},{20,12},{24,16},{28,20},{32,24},{36,28},{40,32... | collective-permute-start | bytes 49160 | tf_op jit(solution)/shard_map/ppermute | solution.py:16
  14.9 2.1 %copy-start.3 = (s32[1024]{0:T(1024)S(1)}, s32[1024]{0:T(1024)}, u32[]{:S(2)}) copy-start(s32[1024]{0:T(1024)} %param.14) | copy-start | bytes 12292
  14.9 2.1 %copy-start.4 = (s32[1024]{0:T(1024)S(1)}, s32[1024]{0:T(1024)}, u32[]{:S(2)}) copy-start(s32[1024]{0:T(1024)} %param.15) | copy-start | bytes 12292
  14.9 2.1 %copy-start.5 = (s32[1024]{0:T(1024)S(1)}, s32[1024]{0:T(1024)}, u32[]{:S(2)}) copy-start(s32[1024]{0:T(1024)} %param.13) | copy-start | bytes 12292
  14.9 2.8 %copy-start.2 = (bf16[8,2,128]{2,1,0:T(2,128)(2,1)S(1)}, bf16[8,2,128]{2,1,0:T(2,128)(2,1)}, u32[]{:S(2)}) copy-start(bf16[8,2,128]{2,1,0:T(2,128)(2,1)} %param.9) | copy-start | bytes 12292
  14.9 3.0 %copy-start.6 = (bf16[8,1024]{1,0:T(8,128)(2,1)S(1)}, bf16[8,1024]{1,0:T(8,128)(2,1)}, u32[]{:S(2)}) copy-start(bf16[8,1024]{1,0:T(8,128)(2,1)} %param.8) | copy-start | bytes 49156
  15.1 4.2 %collective-permute-start.2 = (bf16[2,1536,128]{2,1,0:T(8,128)(2,1)S(1)}, bf16[2,1536,128]{2,1,0:T(8,128)(2,1)S(1)}, u32[]{:S(2)}, u32[]{:S(2)}) collective-permute-start(bf16[2,1536,128]{2,1,0:T(8,128)(2,1)S(1)} %maximum_bitcast_fusion), channel_id=1, source_target_pairs={{0,4},{4,0},{8,12},{12,8},{16,20},{20,16},{24,28},{28,24},{32,36},... | collective-permute-start | bytes 2359304 | tf_op jit(solution)/shard_map/ppermute | solution.py:87
  21.0 6.1 %collective-permute-start.3 = (f32[8,1040]{1,0:T(8,128)S(1)}, f32[8,1040]{1,0:T(8,128)S(1)}, u32[]{:S(2)}, u32[]{:S(2)}) collective-permute-start(f32[8,1040]{1,0:T(8,128)S(1)} %concatenate.47), channel_id=1, source_target_pairs={{8,0},{12,4},{16,8},{20,12},{24,16},{28,20},{32,24},{36,28},{40,32... | collective-permute-start | bytes 99848 | tf_op jit(solution)/shard_map/ppermute | solution.py:16
  25.2 8.0 %collective-permute-start.4 = (f32[8,1040]{1,0:T(8,128)S(1)}, f32[8,1040]{1,0:T(8,128)S(1)}, u32[]{:S(2)}, u32[]{:S(2)}) collective-permute-start(f32[8,1040]{1,0:T(8,128)S(1)} %concatenate.48), channel_id=1, source_target_pairs={{0,8},{4,12},{8,16},{12,20},{16,24},{20,28},{24,32},{28,36},{32,40... | collective-permute-start | bytes 99848 | tf_op jit(solution)/shard_map/ppermute | solution.py:16
  33.9 2.8 %copy-start = (bf16[1024,2048]{1,0:T(8,128)(2,1)S(1)}, bf16[1024,2048]{1,0:T(8,128)(2,1)}, u32[]{:S(2)}) copy-start(bf16[1024,2048]{1,0:T(8,128)(2,1)} %param.12) | copy-start | bytes 12582916
  37.8 9.9 %all-to-all-start = ((bf16[4,8,512]{2,1,0:T(8,128)(2,1)}), bf16[4,8,512]{2,1,0:T(8,128)(2,1)S(1)}, u32[]{:S(2)}, u32[]{:S(2)}) async-start(bf16[4,8,512]{2,1,0:T(8,128)(2,1)} %bitcast.43), calls=%async_computation | async-start | bytes 65536 | tf_op jit(solution)/shard_map/all_to_all | solution.py:208

commit v17 on v11

--- a/solution.py
+++ b/solution.py
@@ -172,14 +172,10 @@
     partial_term = jnp.dot(attended, out_weight, preferred_element_type=jnp.float32)
 
     tp_count = lax.axis_size("tp")
-    tp_index = lax.axis_index("tp")
     width = partial_term.shape[1] // tp_count
-    chunks = partial_term.reshape(per_dev, tp_count, width).transpose(1, 0, 2)
-    got = lax.all_to_all(chunks.astype(jnp.bfloat16), "tp", 0, 0, tiled=True)
-    others = jnp.arange(tp_count, dtype=jnp.int32)[:, None, None] != tp_index
-    mine = lax.dynamic_slice_in_dim(partial_term, tp_index * width, width, axis=1)
-    total = mine + jnp.sum(jnp.where(others, got.astype(jnp.float32), 0.0), axis=0)
-    return total.astype(jnp.bfloat16)
+    chunks = partial_term.astype(jnp.bfloat16).reshape(per_dev, tp_count, width)
+    got = lax.all_to_all(chunks, "tp", 1, 1, tiled=True)
+    return jnp.sum(got.astype(jnp.float32), axis=1).astype(jnp.bfloat16)
 
 
 def solution(mesh):

time: 47.5 us -> 46.6 us (0.981)
  blocking collectives: 0 us -> 9.71 us
  waiting for transfers between devices: 7.65 us -> 2.21 us
  starting transfers between devices: 27.9 us -> 23.4 us
  matrix products: 5.35 us -> 4.74 us
    all_to_all x0 -> x1, blocking collectives: none -> 9.71 us  [local(): got = lax.all_to_all(chunks, 'tp', 1, 1, tiled=True)]
    all_to_all x1 -> x0, waiting for transfers between devices: 5.44 us -> none  [local(): got = lax.all_to_all(chunks.astype(jnp.bfloat16), 'tp', 0, 0, tiled=True)]
    all_to_all x1 -> x0, starting transfers between devices: 4.47 us -> none  [local(): got = lax.all_to_all(chunks.astype(jnp.bfloat16), 'tp', 0, 0, tiled=True)]
    dot_general x1, matrix products: 3.5 us -> 2.89 us  [local(): jnp.dot(attended, out_weight, preferred_element_type=jnp.float32)]
    convert_element_type x1 -> x0, other arithmetic: 0.61 us -> none  [local(): return total.astype(jnp.bfloat16)]
    reduce_sum x1, other arithmetic: 0.08 us -> 0.61 us  [local(): return jnp.sum(got.astype(jnp.float32), axis=1).astype(jnp.bfloat16)]
  transfers between devices with their start and end apart: 6 -> 5, of which waited for: 3 -> 2; matrix products, arithmetic and copies ran while one was open for 9% -> 10% of each run, Pallas kernels for 0% -> 0%
where the time goes in v17:
time: 46.6 us; the launch traced here: 46.2 us
  starting transfers between devices  23.4 us (50%)
  blocking collectives  9.71 us (21%)
  matrix products  4.74 us (10%)
  local copies, waits for them, and re-layouts  3.73 us (8%)
  waiting for transfers between devices  2.21 us (5%)
  other arithmetic  2.12 us (5%)
    ppermute x4, starting transfers between devices, shifted(): return lax.ppermute(block, axis, route)  21.5 us
    all_to_all x1, blocking collectives, local(): got = lax.all_to_all(chunks, 'tp', 1, 1, tiled=True)  9.71 us
    dot_general x1, matrix products, local(): jnp.dot(attended, out_weight, preferred_element_type=jnp.float32)  2.89 us
    ppermute x4, waiting for transfers between devices, shifted(): return lax.ppermute(block, axis, route)  2.2 us
    unnamed x13, local copies, waits for them, and re-layouts  2.17 us
    ppermute x1, starting transfers between devices, swapped(): return lax.ppermute(block, axis, [(i, i ^ 1) for i in devices])  1.92 us
    dot_general x2, matrix products, partial_block(): jnp.einsum('nkgd,skd->nkgs', query_block, key_block, preferred_element_ty...  0.98 us
  transfers between devices with their start and end apart: 5, of which 2 were waited for; matrix products, arithmetic and copies ran while one was open for 10% of the time, Pallas kernels for 0%

profile of v17, /device:TPU:6, one launch (start us, length us, event | category | flops | bytes accessed | tf_op | source)
XLA Modules:
  0.0 46.2 jit_solution(8107401812827111745)
XLA Ops:
  0.0 11.7 %collective-permute-start.1 = (bf16[8,1024]{1,0:T(8,128)(2,1)}, bf16[8,1024]{1,0:T(8,128)(2,1)S(1)}, u32[]{:S(2)}, u32[]{:S(2)}) collective-permute-start(bf16[8,1024]{1,0:T(8,128)(2,1)} %param.8), channel_id=1, source_target_pairs={{8,0},{12,4},{16,8},{20,12},{24,16},{28,20},{32,24},{36,28},{40,32... | collective-permute-start | bytes 49160 | tf_op jit(solution)/shard_map/ppermute | solution.py:16
  11.7 1.9 %collective-permute-start = (bf16[8,1024]{1,0:T(8,128)(2,1)}, bf16[8,1024]{1,0:T(8,128)(2,1)S(1)}, u32[]{:S(2)}, u32[]{:S(2)}) collective-permute-start(bf16[8,1024]{1,0:T(8,128)(2,1)} %param.8), channel_id=1, source_target_pairs={{0,8},{4,12},{8,16},{12,20},{16,24},{20,28},{24,32},{28,36},{32,40... | collective-permute-start | bytes 49160 | tf_op jit(solution)/shard_map/ppermute | solution.py:16
  13.6 1.0 %copy.91 = bf16[1,512,2,128]{3,1,2,0:T(8,128)(2,1)S(1)} copy(bf16[1,512,2,128]{3,2,1,0:T(2,128)(2,1)} %param.11) | data formatting | bytes 524288 | tf_op args[3]
  14.6 1.2 %copy.35 = bf16[8,128,2,128]{3,1,0,2:T(8,128)(2,1)S(1)} copy(bf16[8,128,2,128]{3,2,1,0:T(2,128)(2,1)} %param.10) | data formatting | bytes 1048576 | tf_op args[2]
  15.8 0.1 maximum_bitcast_fusion
  15.9 1.9 %collective-permute-start.2 = (bf16[2,1536,128]{2,1,0:T(8,128)(2,1)S(1)}, bf16[2,1536,128]{2,1,0:T(8,128)(2,1)S(1)}, u32[]{:S(2)}, u32[]{:S(2)}) collective-permute-start(bf16[2,1536,128]{2,1,0:T(8,128)(2,1)S(1)} %maximum_bitcast_fusion), channel_id=1, source_target_pairs={{0,4},{4,0},{8,12},{12,8},{16,20},{20,16},{24,28},{28,24},{32,36},... | collective-permute-start | bytes 2359304 | tf_op jit(solution)/shard_map/ppermute | solution.py:70
  17.9 0.1 pad_dynamic-slice_fusion
  17.9 0.1 fusion.73
  18.0 0.1 slice_bitcast_fusion.14
  18.1 0.1 pad_add_fusion.1
  18.2 0.1 compare_and_fusion.3
  18.3 0.1 dynamic-slice_bitcast_fusion
  18.4 0.1 broadcast_bitcast_fusion
  18.4 0.1 broadcast_bitcast_fusion.1
  18.5 0.2 fusion.25
  18.8 0.1 fusion.48
  18.9 0.7 %collective-permute-done = bf16[8,1024]{1,0:T(8,128)(2,1)S(1)} collective-permute-done((bf16[8,1024]{1,0:T(8,128)(2,1)}, bf16[8,1024]{1,0:T(8,128)(2,1)S(1)}, u32[]{:S(2)}, u32[]{:S(2)}) %collective-permute-start) | collective-permute-done | bytes 16416 | tf_op jit(solution)/shard_map/ppermute | solution.py:16
  19.6 0.5 %fusion.75 = (f32[24,8]{0,1:T(8,128)S(1)}, f32[24,1,8,1536]{3,0,2,1:T(8,128)S(1)}) fusion(bf16[2,1536,128]{2,1,0:T(8,128)(2,1)S(1)} %maximum_bitcast_fusion, pred[24,1536]{1,0:T(8,128)(4,1)S(1)} %get-tuple-element.28, bf16[8,1024]{1,0:T(8,128)(2,1)S(1)} %collective-permute-done.1, bf16[8,1024]{1,0:T(8,128)(2,1)S(1)} %copy-done.4, ...), kind=kOutput, calls=%fused_computation.151 | convolution fusion | flops 76529472 | bytes 1659648 | tf_op jit(solution)/shard_map/nkgd,skd->nkgs/dot_general | solution.py:21
  20.1 0.4 fusion.9
  20.5 0.5 %fusion.74 = (f32[24,8]{0,1:T(8,128)S(1)}, f32[24,1,8,1536]{3,0,2,1:T(8,128)S(1)}) fusion(bf16[2,1536,128]{2,1,0:T(8,128)(2,1)S(1)} %collective-permute-done.2, pred[24,1536]{1,0:T(8,128)(4,1)S(1)} %get-tuple-element.27, bf16[8,1024]{1,0:T(8,128)(2,1)S(1)} %collective-permute-done.1, bf16[8,1024]{1,0:T(8,128)(2,1)S(1)} %copy-done.4, ...), kind=kOutput, calls=%fused_computation.150 | convolution fusion | flops 76529472 | bytes 1659648 | tf_op jit(solution)/shard_map/nkgd,skd->nkgs/dot_general | solution.py:21
  21.0 0.4 fusion.11
  21.4 0.4 fusion.7
  21.8 0.4 fusion.6
  22.2 0.1 fusion.72
  22.2 0.1 copy.43
  22.3 0.1 fusion.71
  22.4 0.1 copy.44
  22.4 0.1 concatenate.45
  22.5 1.9 %collective-permute-start.4 = (f32[8,1040]{1,0:T(8,128)S(1)}, f32[8,1040]{1,0:T(8,128)S(1)}, u32[]{:S(2)}, u32[]{:S(2)}) collective-permute-start(f32[8,1040]{1,0:T(8,128)S(1)} %concatenate.45), channel_id=1, source_target_pairs={{0,8},{4,12},{8,16},{12,20},{16,24},{20,28},{24,32},{28,36},{32,40... | collective-permute-start | bytes 99848 | tf_op jit(solution)/shard_map/ppermute | solution.py:16
  24.5 0.1 copy.46
  24.5 0.1 copy.40
  24.6 0.1 copy.41
  24.7 0.1 concatenate.44
  24.7 6.0 %collective-permute-start.3 = (f32[8,1040]{1,0:T(8,128)S(1)}, f32[8,1040]{1,0:T(8,128)S(1)}, u32[]{:S(2)}, u32[]{:S(2)}) collective-permute-start(f32[8,1040]{1,0:T(8,128)S(1)} %concatenate.44), channel_id=1, source_target_pairs={{8,0},{12,4},{16,8},{20,12},{24,16},{28,20},{32,24},{36,28},{40,32... | collective-permute-start | bytes 99848 | tf_op jit(solution)/shard_map/ppermute | solution.py:16
  30.8 0.1 fusion.59
  30.9 0.1 copy.45
  30.9 1.5 %collective-permute-done.3 = f32[8,1040]{1,0:T(8,128)S(1)} collective-permute-done((f32[8,1040]{1,0:T(8,128)S(1)}, f32[8,1040]{1,0:T(8,128)S(1)}, u32[]{:S(2)}, u32[]{:S(2)}) %collective-permute-start.3) | collective-permute-done | bytes 33312 | tf_op jit(solution)/shard_map/ppermute | solution.py:16
  32.4 0.1 fusion.60
  32.5 0.1 copy.42
  32.5 0.1 copy.60
  32.6 0.1 copy.56
  32.7 0.1 copy.59
  32.8 0.1 copy.52
  32.8 0.1 fusion.65
  32.9 0.1 fusion.68
  33.0 2.9 %convolution_convert_fusion = bf16[8,2048]{1,0:T(8,128)(2,1)S(1)} fusion(bf16[1024,2048]{1,0:T(8,128)(2,1)} %param.12, f32[8,1040]{1,0:T(8,128)S(1)} %collective-permute-done.4, f32[8,1040]{1,0:T(8,128)S(1)} %collective-permute-done.3, f32[24,1,8,128]{3,0,2,1:T(8,128)S(1)} %fusion.6, f32[8,8]{0,1:T(8,128)S(1)} %get-tuple-element.30, ...), kind=kOutput, calls=%fused_computation.6 | convolution fusion | flops 33644544 | bytes 4349952 | tf_op jit(solution)/shard_map/dot_general | solution.py:172
  35.9 9.7 %all_to_all.5 = bf16[8,4,512]{2,0,1:T(8,128)(2,1)S(1)} all-to-all(bf16[8,4,512]{2,0,1:T(8,128)(2,1)S(1)} %bitcast.215), channel_id=1, replica_groups=mesh['req'=128,'tp'=4] {'tp'}, dimensions={1} | all-to-all | bytes 65536 | tf_op jit(solution)/shard_map/all_to_all | solution.py:177
  45.6 0.6 %reduce_sum.38 = bf16[8,512]{1,0:T(8,128)(2,1)} reduce(bf16[8,4,512]{2,0,1:T(8,128)(2,1)S(1)} %all_to_all.5, bf16[]{:T(256)} %constant.113.clone.1), dimensions={1}, to_apply=%region_4.5 | reduce | flops 12288 | bytes 40962 | tf_op jit(solution)/shard_map/reduce_sum | solution.py:178
  (30 shorter events, 0.2 us)
Async XLA Ops:
  0.0 18.9 %collective-permute-start.1 = (bf16[8,1024]{1,0:T(8,128)(2,1)}, bf16[8,1024]{1,0:T(8,128)(2,1)S(1)}, u32[]{:S(2)}, u32[]{:S(2)}) collective-permute-start(bf16[8,1024]{1,0:T(8,128)(2,1)} %param.8), channel_id=1, source_target_pairs={{8,0},{12,4},{16,8},{20,12},{24,16},{28,20},{32,24},{36,28},{40,32... | collective-permute-start | bytes 49160 | tf_op jit(solution)/shard_map/ppermute | solution.py:16
  11.7 8.0 %collective-permute-start = (bf16[8,1024]{1,0:T(8,128)(2,1)}, bf16[8,1024]{1,0:T(8,128)(2,1)S(1)}, u32[]{:S(2)}, u32[]{:S(2)}) collective-permute-start(bf16[8,1024]{1,0:T(8,128)(2,1)} %param.8), channel_id=1, source_target_pairs={{0,8},{4,12},{8,16},{12,20},{16,24},{20,28},{24,32},{28,36},{32,40... | collective-permute-start | bytes 49160 | tf_op jit(solution)/shard_map/ppermute | solution.py:16
  14.6 3.2 %copy-start.1 = (s32[1024]{0:T(1024)S(1)}, s32[1024]{0:T(1024)}, u32[]{:S(2)}) copy-start(s32[1024]{0:T(1024)} %param.14) | copy-start | bytes 12292
  14.6 3.2 %copy-start.2 = (s32[1024]{0:T(1024)S(1)}, s32[1024]{0:T(1024)}, u32[]{:S(2)}) copy-start(s32[1024]{0:T(1024)} %param.15) | copy-start | bytes 12292
  14.6 3.2 %copy-start.3 = (s32[1024]{0:T(1024)S(1)}, s32[1024]{0:T(1024)}, u32[]{:S(2)}) copy-start(s32[1024]{0:T(1024)} %param.13) | copy-start | bytes 12292
  15.8 2.9 %copy-start = (bf16[8,2,128]{2,1,0:T(2,128)(2,1)S(1)}, bf16[8,2,128]{2,1,0:T(2,128)(2,1)}, u32[]{:S(2)}) copy-start(bf16[8,2,128]{2,1,0:T(2,128)(2,1)} %param.9) | copy-start | bytes 12292
  15.8 3.0 %copy-start.4 = (bf16[8,1024]{1,0:T(8,128)(2,1)S(1)}, bf16[8,1024]{1,0:T(8,128)(2,1)}, u32[]{:S(2)}) copy-start(bf16[8,1024]{1,0:T(8,128)(2,1)} %param.8) | copy-start | bytes 49156
  15.9 4.6 %collective-permute-start.2 = (bf16[2,1536,128]{2,1,0:T(8,128)(2,1)S(1)}, bf16[2,1536,128]{2,1,0:T(8,128)(2,1)S(1)}, u32[]{:S(2)}, u32[]{:S(2)}) collective-permute-start(bf16[2,1536,128]{2,1,0:T(8,128)(2,1)S(1)} %maximum_bitcast_fusion), channel_id=1, source_target_pairs={{0,4},{4,0},{8,12},{12,8},{16,20},{20,16},{24,28},{28,24},{32,36},... | collective-permute-start | bytes 2359304 | tf_op jit(solution)/shard_map/ppermute | solution.py:70
  22.5 8.2 %collective-permute-start.4 = (f32[8,1040]{1,0:T(8,128)S(1)}, f32[8,1040]{1,0:T(8,128)S(1)}, u32[]{:S(2)}, u32[]{:S(2)}) collective-permute-start(f32[8,1040]{1,0:T(8,128)S(1)} %concatenate.45), channel_id=1, source_target_pairs={{0,8},{4,12},{8,16},{12,20},{16,24},{20,28},{24,32},{28,36},{32,40... | collective-permute-start | bytes 99848 | tf_op jit(solution)/shard_map/ppermute | solution.py:16
  24.7 7.6 %collective-permute-start.3 = (f32[8,1040]{1,0:T(8,128)S(1)}, f32[8,1040]{1,0:T(8,128)S(1)}, u32[]{:S(2)}, u32[]{:S(2)}) collective-permute-start(f32[8,1040]{1,0:T(8,128)S(1)} %concatenate.44), channel_id=1, source_target_pairs={{8,0},{12,4},{16,8},{20,12},{24,16},{28,20},{32,24},{36,28},{40,32... | collective-permute-start | bytes 99848 | tf_op jit(solution)/shard_map/ppermute | solution.py:16
